TPU v7x, 128 devices: a whole 4x4x4 slice. The times are simulated.
128 devices in a mesh: tm: 32 (over y_lo, z, x), rows: 4 (over y_hi, core).
Axes of the slice: x: 4, y: 4 (y_hi: 2, y_lo: 2; y = y_hi * 2 + y_lo), z: 4, core: 2. Of those that a mesh axis runs over, the one named last changes fastest.
Arguments:
- features: bfloat16 [128, 96, 16, 256], P('tm', None, 'rows'), may hold values from -6 to 6
- first_kernel: bfloat16 [3, 3, 3, 96, 96], replicated, may hold values from -0.125 to 0.125
- first_bias: float32 [96], replicated, may hold values from -3 to 3
- first_gain: float32 [96], replicated, may hold values from 0.1 to 1.9
- second_kernel: bfloat16 [3, 3, 3, 96, 96], replicated, may hold values from -0.125 to 0.125
- latent_weight: bfloat16 [4, 16, 96], replicated, may hold values from -0.3125 to 0.3125
- decode_kernel: bfloat16 [3, 3, 3, 96, 16], replicated, may hold values from -0.3125 to 0.3125
- decode_bias: float32 [96], replicated, may hold values from -3 to 3
- decode_gain: float32 [96], replicated, may hold values from 0.1 to 1.9
- upsample_weight: bfloat16 [4, 96, 96], replicated, may hold values from -0.625 to 0.625
- final_kernel: bfloat16 [3, 3, 3, 96, 96], replicated, may hold values from -0.125 to 0.125
Outputs:
- latents: bfloat16 [32, 16, 16, 256], P('tm', None, 'rows')
- rebuilt: bfloat16 [128, 96, 16, 256], P('tm', None, 'rows')
All inputs are finite; a program needn't handle non-finite values.
Results may differ from a plain program's by a relative error of at most 0.01.
Values may be sent and summed in bfloat16 or wider, within the bound.
No kernel may reach another device: no remote copies, remote signals or barrier semaphores. Data moves between devices by JAX's collectives and lax.ppermute only.
A program may use at most 64 MiB of HBM per device.

v0:
```python
import functools

import jax
import jax.numpy as jnp
from jax import lax
from jax.experimental import pallas as pl
from jax.experimental.pallas import tpu as pltpu
from jax.sharding import PartitionSpec as P


def shift(x, dt, dr):
    nt = lax.axis_size("tm")
    nr = lax.axis_size("rows")
    if dt == 0:
        pairs = [(r, r + dr) for r in range(nr) if 0 <= r + dr < nr]
        return lax.ppermute(x, "rows", pairs)
    if dr == 0:
        pairs = [(t, t + dt) for t in range(nt) if 0 <= t + dt < nt]
        return lax.ppermute(x, "tm", pairs)
    pairs = [
        (t * nr + r, (t + dt) * nr + r + dr)
        for t in range(nt)
        for r in range(nr)
        if 0 <= t + dt < nt and 0 <= r + dr < nr
    ]
    return lax.ppermute(x, ("tm", "rows"), pairs)


def haloed_rows_first(v):
    prev = shift(v[-2:], 1, 0)
    top = shift(v[:, -1:], 0, 1)
    bottom = shift(v[:, :1], 0, -1)
    top_corner = shift(v[-2:, -1:], 1, 1)
    bottom_corner = shift(v[-2:, :1], 1, -1)
    own = jnp.concatenate([top, v, bottom], 1)
    before = jnp.concatenate([top_corner, prev, bottom_corner], 1)
    return jnp.concatenate([before, own], 0)


def merged_kernel(kernel):
    o, c = kernel.shape[3], kernel.shape[4]
    return kernel.transpose(2, 3, 0, 1, 4).reshape(3 * o, 9 * c)


def tap_sum(x_ref, k_ref, t, rows, columns):
    pieces = []
    for a in range(3):
        for b in range(3):
            pieces.append(
                jnp.concatenate([x_ref[t + a, r + b] for r in range(rows)], axis=1)
            )
    stacked = jnp.concatenate(pieces, axis=0)
    acc = jnp.dot(k_ref[...], stacked, preferred_element_type=jnp.float32)
    out_channels = acc.shape[0] // 3
    width = rows * columns
    lane = lax.broadcasted_iota(jnp.int32, (out_channels, width), 1) % columns
    left = pltpu.roll(acc[:out_channels], 1, 1)
    right = pltpu.roll(acc[2 * out_channels :], width - 1, 1)
    left = jnp.where(lane == 0, 0.0, left)
    right = jnp.where(lane == columns - 1, 0.0, right)
    return left + acc[out_channels : 2 * out_channels] + right


def gate_kernel(x_ref, k_ref, bias_ref, gain_ref, o_ref, *, frames, rows, columns):
    bias = bias_ref[...]
    gain = gain_ref[...]
    for t in range(frames):
        y = tap_sum(x_ref, k_ref, t, rows, columns) + bias
        scale = lax.rsqrt(jnp.mean(y * y, axis=0, keepdims=True) + 1e-06)
        z = y * scale * gain
        g = (z / (1.0 + jnp.exp(-z))).astype(o_ref.dtype)
        for r in range(rows):
            o_ref[t, r] = g[:, r * columns : (r + 1) * columns]


def latent_kernel(x_ref, k_ref, res_ref, w_ref, o_ref, *, frames, rows, columns):
    total = None
    for t in range(frames):
        y = tap_sum(x_ref, k_ref, t, rows, columns)
        res = jnp.concatenate([res_ref[t, r] for r in range(rows)], axis=1)
        hidden = (res.astype(jnp.float32) + y).astype(jnp.bfloat16)
        part = jnp.dot(w_ref[t], hidden, preferred_element_type=jnp.float32)
        total = part if total is None else total + part
    o_ref[...] = total.astype(o_ref.dtype)


def rebuild_kernel(x_ref, k_ref, o_ref, *, frames, rows, columns):
    for t in range(frames):
        y = tap_sum(x_ref, k_ref, t, rows, columns)
        res = jnp.concatenate([x_ref[t + 2, r + 1] for r in range(rows)], axis=1)
        o_ref[t] = (res.astype(jnp.float32) + y).astype(o_ref.dtype)


def normed_silu(values, gain):
    scale = lax.rsqrt(jnp.mean(values * values, axis=1, keepdims=True) + 1e-06)
    return jax.nn.silu(values * scale * gain[None, :, None, None])


def conv_valid(v, kernel):
    out = lax.conv_general_dilated(
        v[None],
        kernel,
        (1, 1, 1),
        [(0, 0), (0, 0), (1, 1)],
        dimension_numbers=("NDCHW", "DHWOI", "NDCHW"),
        preferred_element_type=jnp.float32,
    )
    return out[0]


def body(
    features,
    first_kernel,
    first_bias,
    first_gain,
    second_kernel,
    latent_weight,
    decode_kernel,
    decode_bias,
    decode_gain,
    upsample_weight,
    final_kernel,
):
    frames, channels, rows, columns = features.shape
    z_count = latent_weight.shape[1]
    dims = dict(frames=frames, rows=rows, columns=columns)
    own = features.transpose(0, 2, 1, 3)
    gated = pl.pallas_call(
        functools.partial(gate_kernel, **dims),
        out_shape=jax.ShapeDtypeStruct((frames, rows, channels, columns), jnp.bfloat16),
    )(
        haloed_rows_first(own),
        merged_kernel(first_kernel),
        first_bias[:, None],
        first_gain[:, None],
    )
    latent_flat = pl.pallas_call(
        functools.partial(latent_kernel, **dims),
        out_shape=jax.ShapeDtypeStruct((z_count, rows * columns), jnp.bfloat16),
    )(haloed_rows_first(gated), merged_kernel(second_kernel), own, latent_weight)
    latent = latent_flat.reshape(1, z_count, rows, columns)
    lat_rows = jnp.concatenate(
        [shift(latent[:, :, -2:], 0, 1), latent, shift(latent[:, :, :2], 0, -1)], 2
    )
    stacked = jnp.concatenate(
        [shift(lat_rows, 3, 0), shift(lat_rows, 2, 0), shift(lat_rows, 1, 0), lat_rows], 0
    )
    decoded = conv_valid(stacked, decode_kernel) + decode_bias[None, :, None, None]
    activated = normed_silu(decoded, decode_gain).astype(jnp.bfloat16)
    upsampled = jnp.einsum(
        "joc,kcrw->kjrow", upsample_weight, activated, preferred_element_type=jnp.float32
    )
    upsampled = upsampled.reshape(-1, rows + 2, channels, columns).astype(jnp.bfloat16)
    band = lax.axis_index("rows")
    bands = lax.axis_size("rows")
    row_ids = lax.broadcasted_iota(jnp.int32, (1, rows + 2, 1, 1), 1)
    inside = ((row_ids > 0) | (band > 0)) & ((row_ids < rows + 1) | (band < bands - 1))
    upsampled = jnp.where(inside, upsampled, jnp.zeros_like(upsampled))
    previous = upsampled[frames - 2 : frames]
    previous = jnp.where(lax.axis_index("tm") > 0, previous, jnp.zeros_like(previous))
    rebuilt_flat = pl.pallas_call(
        functools.partial(rebuild_kernel, **dims),
        out_shape=jax.ShapeDtypeStruct((frames, channels, rows * columns), jnp.bfloat16),
    )(jnp.concatenate([previous, upsampled[frames:]], 0), merged_kernel(final_kernel))
    rebuilt = rebuilt_flat.reshape(frames, channels, rows, columns)
    return (latent, rebuilt)


def solution(mesh):
    return jax.shard_map(
        body,
        mesh=mesh,
        in_specs=(P("tm", None, "rows", None), P(), P(), P(), P(), P(), P(), P(), P(), P(), P()),
        out_specs=(P("tm", None, "rows", None), P("tm", None, "rows", None)),
        check_vma=False,
    )
```

profile of v0, /device:TPU:24, one launch (start us, length us, event | category | flops | bytes accessed | tf_op | source)
XLA Modules:
  0.0 128.9 jit_solution(9642782492212785890)
XLA Ops:
  0.6 0.0 copy-start
  0.7 1.3 %copy.38 = bf16[4,96,4,256]{3,1,2,0:T(8,128)(2,1)S(1)} copy(bf16[4,96,4,256]{3,2,1,0:T(4,128)(2,1)} %param.11) | data formatting | bytes 1572864 | tf_op args[0]
  2.0 3.4 %collective-permute-start.1 = (bf16[2,4,96,256]{3,2,1,0:T(8,128)(2,1)S(1)}, bf16[2,4,96,256]{3,2,1,0:T(8,128)(2,1)S(1)}, u32[]{:S(2)}, u32[]{:S(2)}) collective-permute-start(bf16[2,4,96,256]{3,2,1,0:T(8,128)(2,1)S(1)} %slice.57), channel_id=1, source_target_pairs={{0,4},{4,8},{8,12},{12,16},{16,20},{20,24},{24,28},{28,32},{32,36}... | collective-permute-start | bytes 1179656 | tf_op jit(solution)/shard_map/ppermute | solution.py:19
  5.5 0.0 copy-start.7
  5.5 1.9 %collective-permute-start.3 = (bf16[4,1,96,256]{3,2,1,0:T(8,128)(2,1)S(1)}, bf16[4,1,96,256]{3,2,1,0:T(8,128)(2,1)S(1)}, u32[]{:S(2)}, u32[]{:S(2)}) collective-permute-start(bf16[4,1,96,256]{3,2,1,0:T(8,128)(2,1)S(1)} %get-tuple-element.8), channel_id=1, source_target_pairs={{0,1},{1,2},{2,3},{4,5},{5,6},{6,7},{8,9},{9,10},{10,11},{12,13},{... | collective-permute-start | bytes 589832 | tf_op jit(solution)/shard_map/ppermute | solution.py:16
  7.4 5.1 %collective-permute-start.4 = (bf16[4,1,96,256]{3,2,1,0:T(8,128)(2,1)S(1)}, bf16[4,1,96,256]{3,2,1,0:T(8,128)(2,1)S(1)}, u32[]{:S(2)}, u32[]{:S(2)}) collective-permute-start(bf16[4,1,96,256]{3,2,1,0:T(8,128)(2,1)S(1)} %get-tuple-element.9), channel_id=1, source_target_pairs={{1,0},{2,1},{3,2},{5,4},{6,5},{7,6},{9,8},{10,9},{11,10},{13,12},{... | collective-permute-start | bytes 589832 | tf_op jit(solution)/shard_map/ppermute | solution.py:16
  12.6 0.7 fusion.8
  13.3 1.9 %collective-permute-start = (bf16[2,1,96,256]{3,2,1,0:T(8,128)(2,1)}, bf16[2,1,96,256]{3,2,1,0:T(8,128)(2,1)S(1)}, u32[]{:S(2)}, u32[]{:S(2)}) collective-permute-start(bf16[2,1,96,256]{3,2,1,0:T(8,128)(2,1)} %get-tuple-element.6), channel_id=1, source_target_pairs={{0,5},{1,6},{2,7},{4,9},{5,10},{6,11},{8,13},{9,14},{10,15},{12,17... | collective-permute-start | bytes 294920 | tf_op jit(solution)/shard_map/ppermute | solution.py:26
  15.2 6.7 %collective-permute-start.2 = (bf16[2,1,96,256]{3,2,1,0:T(8,128)(2,1)}, bf16[2,1,96,256]{3,2,1,0:T(8,128)(2,1)S(1)}, u32[]{:S(2)}, u32[]{:S(2)}) collective-permute-start(bf16[2,1,96,256]{3,2,1,0:T(8,128)(2,1)} %get-tuple-element.7), channel_id=1, source_target_pairs={{1,4},{2,5},{3,6},{5,8},{6,9},{7,10},{9,12},{10,13},{11,14},{13,16... | collective-permute-start | bytes 294920 | tf_op jit(solution)/shard_map/ppermute | solution.py:26
  21.9 0.5 copy.25
  22.4 1.3 %reshape.46.k_ref = bf16[288,864]{1,0:T(8,128)(2,1)} reshape(bf16[3,96,3,3,96]{4,3,2,1,0:T(4,128)(2,1)S(1)} %copy.25) | data formatting | bytes 995328 | tf_op jit(solution)/shard_map/reshape | solution.py:42
  23.7 0.7 copy.26.bias_ref
  24.4 1.4 %copy.27.gain_ref = f32[96,1]{1,0:T(8,128)} copy(f32[96,1]{0,1:T(1,128)} %bitcast.38) | data formatting | bytes 768 | tf_op jit(solution)/shard_map/broadcast_in_dim | solution.py:135
  25.8 0.0 collective-permute-done
  25.8 0.1 collective-permute-done.2
  25.9 0.0 collective-permute-done.3
  25.9 0.0 collective-permute-done.4
  25.9 0.0 collective-permute-done.1
  25.9 1.5 %maximum_maximum_fusion.x_ref = bf16[6,6,96,256]{3,2,1,0:T(8,128)(2,1)} fusion(bf16[4,1,96,256]{3,2,1,0:T(8,128)(2,1)S(1)} %collective-permute-done.4, bf16[4,4,96,256]{3,2,1,0:T(8,128)(2,1)S(1)} %bitcast.30, bf16[4,1,96,256]{3,2,1,0:T(8,128)(2,1)S(1)} %collective-permute-done.3, bf16[2,1,96,256]{3,2,1,0:T(8,128)(2,1)S(1)} %collective-permute-done.2, ...), kind=kLoop, calls=%fused_computation.2 | loop fusion | flops 4423680 | bytes 3538944 | tf_op jit(solution)/shard_map/concatenate | solution.py:37
  27.4 5.4 %shard_map.122 = bf16[4,4,96,256]{3,2,1,0:T(8,128)(2,1)} custom-call(bf16[6,6,96,256]{3,2,1,0:T(8,128)(2,1)} %maximum_maximum_fusion.x_ref, bf16[288,864]{1,0:T(8,128)(2,1)} %reshape.46.k_ref, f32[96,1]{1,0:T(8,128)} %copy.26.bias_ref, f32[96,1]{1,0:T(8,128)} %copy.27.gain_ref), custom_call_target="tpu_custom_call" | custom-call | tf_op jit(solution)/shard_map/pallas_call | solution.py:128
  32.8 1.1 slice.62
  33.9 3.6 %collective-permute-start.6 = (bf16[2,4,96,256]{3,2,1,0:T(8,128)(2,1)S(1)}, bf16[2,4,96,256]{3,2,1,0:T(8,128)(2,1)S(1)}, u32[]{:S(2)}, u32[]{:S(2)}) collective-permute-start(bf16[2,4,96,256]{3,2,1,0:T(8,128)(2,1)S(1)} %slice.62), channel_id=1, source_target_pairs={{0,4},{4,8},{8,12},{12,16},{16,20},{20,24},{24,28},{28,32},{32,36}... | collective-permute-start | bytes 1179656 | tf_op jit(solution)/shard_map/ppermute | solution.py:19
  37.5 1.1 fusion.7
  38.6 0.0 copy-start.2
  38.6 2.1 %collective-permute-start.8 = (bf16[4,1,96,256]{3,2,1,0:T(8,128)(2,1)S(1)}, bf16[4,1,96,256]{3,2,1,0:T(8,128)(2,1)S(1)}, u32[]{:S(2)}, u32[]{:S(2)}) collective-permute-start(bf16[4,1,96,256]{3,2,1,0:T(8,128)(2,1)S(1)} %get-tuple-element.4), channel_id=1, source_target_pairs={{0,1},{1,2},{2,3},{4,5},{5,6},{6,7},{8,9},{9,10},{10,11},{12,13},{... | collective-permute-start | bytes 589832 | tf_op jit(solution)/shard_map/ppermute | solution.py:16
  40.6 5.1 %collective-permute-start.9 = (bf16[4,1,96,256]{3,2,1,0:T(8,128)(2,1)S(1)}, bf16[4,1,96,256]{3,2,1,0:T(8,128)(2,1)S(1)}, u32[]{:S(2)}, u32[]{:S(2)}) collective-permute-start(bf16[4,1,96,256]{3,2,1,0:T(8,128)(2,1)S(1)} %get-tuple-element.5), channel_id=1, source_target_pairs={{1,0},{2,1},{3,2},{5,4},{6,5},{7,6},{9,8},{10,9},{11,10},{13,12},{... | collective-permute-start | bytes 589832 | tf_op jit(solution)/shard_map/ppermute | solution.py:16
  45.8 1.7 %fusion.6 = (bf16[2,1,96,256]{3,2,1,0:T(8,128)(2,1)}, bf16[2,1,96,256]{3,2,1,0:T(8,128)(2,1)}) fusion(bf16[4,4,96,256]{3,2,1,0:T(8,128)(2,1)} %shard_map.122), kind=kLoop, calls=%fused_computation.19 | loop fusion | bytes 393216 | tf_op jit(solution)/shard_map/slice | solution.py:33
  47.5 1.9 %collective-permute-start.5 = (bf16[2,1,96,256]{3,2,1,0:T(8,128)(2,1)}, bf16[2,1,96,256]{3,2,1,0:T(8,128)(2,1)S(1)}, u32[]{:S(2)}, u32[]{:S(2)}) collective-permute-start(bf16[2,1,96,256]{3,2,1,0:T(8,128)(2,1)} %get-tuple-element.2), channel_id=1, source_target_pairs={{0,5},{1,6},{2,7},{4,9},{5,10},{6,11},{8,13},{9,14},{10,15},{12,17... | collective-permute-start | bytes 294920 | tf_op jit(solution)/shard_map/ppermute | solution.py:26
  49.4 7.0 %collective-permute-start.7 = (bf16[2,1,96,256]{3,2,1,0:T(8,128)(2,1)}, bf16[2,1,96,256]{3,2,1,0:T(8,128)(2,1)S(1)}, u32[]{:S(2)}, u32[]{:S(2)}) collective-permute-start(bf16[2,1,96,256]{3,2,1,0:T(8,128)(2,1)} %get-tuple-element.3), channel_id=1, source_target_pairs={{1,4},{2,5},{3,6},{5,8},{6,9},{7,10},{9,12},{10,13},{11,14},{13,16... | collective-permute-start | bytes 294920 | tf_op jit(solution)/shard_map/ppermute | solution.py:26
  56.4 0.5 copy.28
  56.9 1.3 %reshape.47.k_ref = bf16[288,864]{1,0:T(8,128)(2,1)} reshape(bf16[3,96,3,3,96]{4,3,2,1,0:T(4,128)(2,1)S(1)} %copy.28) | data formatting | bytes 995328 | tf_op jit(solution)/shard_map/reshape | solution.py:42
  58.2 1.2 collective-permute-done.5
  59.4 0.7 collective-permute-done.7
  60.1 0.0 collective-permute-done.8
  60.1 0.0 collective-permute-done.9
  60.1 0.0 collective-permute-done.6
  60.1 1.5 %maximum_maximum_fusion.1.x_ref = bf16[6,6,96,256]{3,2,1,0:T(8,128)(2,1)} fusion(bf16[4,1,96,256]{3,2,1,0:T(8,128)(2,1)S(1)} %collective-permute-done.9, bf16[4,4,96,256]{3,2,1,0:T(8,128)(2,1)S(1)} %copy-done.2, bf16[4,1,96,256]{3,2,1,0:T(8,128)(2,1)S(1)} %collective-permute-done.8, bf16[2,1,96,256]{3,2,1,0:T(8,128)(2,1)S(1)} %collective-permute-done.7, ...), kind=kLoop, calls=%fused_computation.3 | loop fusion | flops 4423680 | bytes 3538944 | tf_op jit(solution)/shard_map/concatenate | solution.py:37
  61.6 5.9 %shard_map.123 = bf16[16,1024]{1,0:T(8,128)(2,1)} custom-call(bf16[6,6,96,256]{3,2,1,0:T(8,128)(2,1)} %maximum_maximum_fusion.1.x_ref, bf16[288,864]{1,0:T(8,128)(2,1)} %reshape.47.k_ref, bf16[4,4,96,256]{3,2,1,0:T(8,128)(2,1)} %bitcast.31, bf16[4,16,96]{2,1,0:T(8,128)(2,1)} %w_ref.1), custom_call_target="tpu_custom_call" | custom-call | tf_op jit(solution)/shard_map/pallas_call | solution.py:137
  67.5 0.8 reshape.48
  68.2 0.0 copy-start.6
  68.3 1.9 %collective-permute-start.10 = (bf16[1,16,2,256]{3,2,1,0:T(2,128)(2,1)S(1)}, bf16[1,16,2,256]{3,2,1,0:T(2,128)(2,1)S(1)}, u32[]{:S(2)}, u32[]{:S(2)}) collective-permute-start(bf16[1,16,2,256]{3,2,1,0:T(2,128)(2,1)S(1)} %get-tuple-element.10), channel_id=1, source_target_pairs={{0,1},{1,2},{2,3},{4,5},{5,6},{6,7},{8,9},{9,10},{10,11},{12,13},{... | collective-permute-start | bytes 49160 | tf_op jit(solution)/shard_map/ppermute | solution.py:16
  70.2 5.7 %collective-permute-start.11 = (bf16[1,16,2,256]{3,2,1,0:T(2,128)(2,1)S(1)}, bf16[1,16,2,256]{3,2,1,0:T(2,128)(2,1)S(1)}, u32[]{:S(2)}, u32[]{:S(2)}) collective-permute-start(bf16[1,16,2,256]{3,2,1,0:T(2,128)(2,1)S(1)} %get-tuple-element.11), channel_id=1, source_target_pairs={{1,0},{2,1},{3,2},{5,4},{6,5},{7,6},{9,8},{10,9},{11,10},{13,12},{... | collective-permute-start | bytes 49160 | tf_op jit(solution)/shard_map/ppermute | solution.py:16
  76.0 0.5 copy.32
  76.4 1.3 %reshape.49.k_ref = bf16[288,864]{1,0:T(8,128)(2,1)} reshape(bf16[3,96,3,3,96]{4,3,2,1,0:T(4,128)(2,1)S(1)} %copy.32) | data formatting | bytes 995328 | tf_op jit(solution)/shard_map/reshape | solution.py:42
  77.7 0.0 collective-permute-done.10
  77.7 0.0 collective-permute-done.11
  77.7 0.1 pad_maximum_fusion.1
  77.8 3.2 %collective-permute-start.12 = (bf16[1,16,8,256]{3,2,1,0:T(8,128)(2,1)S(1)}, bf16[1,16,8,256]{3,2,1,0:T(8,128)(2,1)S(1)}, u32[]{:S(2)}, u32[]{:S(2)}) collective-permute-start(bf16[1,16,8,256]{3,2,1,0:T(8,128)(2,1)S(1)} %pad_maximum_fusion.1), channel_id=1, source_target_pairs={{0,12},{4,16},{8,20},{12,24},{16,28},{20,32},{24,36},{28,40},{32,4... | collective-permute-start | bytes 196616 | tf_op jit(solution)/shard_map/ppermute | solution.py:19
  81.0 4.1 %collective-permute-start.13 = (bf16[1,16,8,256]{3,2,1,0:T(8,128)(2,1)S(1)}, bf16[1,16,8,256]{3,2,1,0:T(8,128)(2,1)S(1)}, u32[]{:S(2)}, u32[]{:S(2)}) collective-permute-start(bf16[1,16,8,256]{3,2,1,0:T(8,128)(2,1)S(1)} %pad_maximum_fusion.1), channel_id=1, source_target_pairs={{0,8},{4,12},{8,16},{12,20},{16,24},{20,28},{24,32},{28,36},{32,40... | collective-permute-start | bytes 196616 | tf_op jit(solution)/shard_map/ppermute | solution.py:19
  85.2 2.8 %collective-permute-start.14 = (bf16[1,16,8,256]{3,2,1,0:T(8,128)(2,1)S(1)}, bf16[1,16,8,256]{3,2,1,0:T(8,128)(2,1)S(1)}, u32[]{:S(2)}, u32[]{:S(2)}) collective-permute-start(bf16[1,16,8,256]{3,2,1,0:T(8,128)(2,1)S(1)} %pad_maximum_fusion.1), channel_id=1, source_target_pairs={{0,4},{4,8},{8,12},{12,16},{16,20},{20,24},{24,28},{28,32},{32,36}... | collective-permute-start | bytes 196616 | tf_op jit(solution)/shard_map/ppermute | solution.py:19
  88.0 0.0 collective-permute-done.12
  88.0 3.9 %collective-permute-done.13 = bf16[1,16,8,256]{3,2,1,0:T(8,128)(2,1)S(1)} collective-permute-done((bf16[1,16,8,256]{3,2,1,0:T(8,128)(2,1)S(1)}, bf16[1,16,8,256]{3,2,1,0:T(8,128)(2,1)S(1)}, u32[]{:S(2)}, u32[]{:S(2)}) %collective-permute-start.13) | collective-permute-done | bytes 65568 | tf_op jit(solution)/shard_map/ppermute | solution.py:19
  91.8 3.7 %collective-permute-done.14 = bf16[1,16,8,256]{3,2,1,0:T(8,128)(2,1)S(1)} collective-permute-done((bf16[1,16,8,256]{3,2,1,0:T(8,128)(2,1)S(1)}, bf16[1,16,8,256]{3,2,1,0:T(8,128)(2,1)S(1)}, u32[]{:S(2)}, u32[]{:S(2)}) %collective-permute-start.14) | collective-permute-done | bytes 65568 | tf_op jit(solution)/shard_map/ppermute | solution.py:19
  95.6 0.1 maximum_bitcast_fusion
  95.6 4.7 %copy.29 = bf16[1,4,16,8,256]{2,0,4,3,1:T(2,128)(2,1)} copy(bf16[1,4,16,8,256]{4,3,2,1,0:T(8,128)(2,1)S(1)} %maximum_bitcast_fusion) | data formatting | bytes 524288 | tf_op jit(solution)/shard_map/broadcast_in_dim | solution.py:101
  100.3 16.9 %fusion.11 = f32[1,2,96,6,256]{2,0,4,3,1:T(1,128)S(1)} fusion(bf16[1,4,16,8,256]{2,0,4,3,1:T(2,128)(2,1)} %copy.29, bf16[3,3,3,96,16]{3,4,2,1,0:T(8,128)(2,1)S(1)} %copy-done), kind=kOutput, calls=%fused_computation.24 | convolution fusion | flops 254140416 | bytes 1524736 | tf_op jit(solution)/shard_map/conv_general_dilated | solution.py:100
  117.3 0.5 multiply_reduce_fusion
  117.8 1.3 convert_bitcast_fusion
  119.0 0.2 copy.31
  119.2 0.3 bitcast_select_fusion
  119.5 0.1 slice.69
  119.7 1.4 %pad_maximum_fusion.x_ref = bf16[6,6,96,256]{3,2,1,0:T(8,128)(2,1)} fusion(bf16[4,6,96,256]{3,2,1,0:T(8,128)(2,1)S(1)} %slice.69, bf16[2,6,96,256]{3,2,1,0:T(8,128)(2,1)S(1)} %slice_select_fusion), kind=kLoop, calls=%fused_computation.4 | loop fusion | flops 884736 | bytes 3538944 | tf_op jit(solution)/shard_map/concatenate | solution.py:164
  121.1 5.2 %shard_map.124 = bf16[4,96,1024]{2,1,0:T(8,128)(2,1)} custom-call(bf16[6,6,96,256]{3,2,1,0:T(8,128)(2,1)} %pad_maximum_fusion.x_ref, bf16[288,864]{1,0:T(8,128)(2,1)} %reshape.49.k_ref), custom_call_target="tpu_custom_call" | custom-call | tf_op jit(solution)/shard_map/pallas_call | solution.py:161
  126.3 2.6 %reshape.50 = bf16[4,96,4,256]{3,2,1,0:T(4,128)(2,1)} reshape(bf16[4,96,1024]{2,1,0:T(8,128)(2,1)} %shard_map.124) | data formatting | bytes 1572864 | tf_op jit(solution)/shard_map/reshape | solution.py:165
  (24 shorter events, 0.2 us)
Async XLA Ops:
  0.6 99.7 %copy-start = (bf16[3,3,3,96,16]{3,4,2,1,0:T(8,128)(2,1)S(1)}, bf16[3,3,3,96,16]{3,4,2,1,0:T(8,128)(2,1)}, u32[]{:S(2)}) copy-start(bf16[3,3,3,96,16]{3,4,2,1,0:T(8,128)(2,1)} %param.17) | copy-start | bytes 248836
  0.6 21.3 %copy-start.3 = (bf16[3,3,3,96,96]{4,3,2,1,0:T(8,128)(2,1)S(1)}, bf16[3,3,3,96,96]{4,3,2,1,0:T(8,128)(2,1)}, u32[]{:S(2)}) copy-start(bf16[3,3,3,96,96]{4,3,2,1,0:T(8,128)(2,1)} %param.12) | copy-start | bytes 1492996
  2.0 23.9 %copy-start.1 = (bf16[4,96,4,256]{3,1,2,0:T(8,128)(2,1)}, bf16[4,96,4,256]{3,1,2,0:T(8,128)(2,1)S(1)}, u32[]{:S(2)}) copy-start(bf16[4,96,4,256]{3,1,2,0:T(8,128)(2,1)S(1)} %copy.38) | copy-start | bytes 2359300
  2.0 23.9 %collective-permute-start.1 = (bf16[2,4,96,256]{3,2,1,0:T(8,128)(2,1)S(1)}, bf16[2,4,96,256]{3,2,1,0:T(8,128)(2,1)S(1)}, u32[]{:S(2)}, u32[]{:S(2)}) collective-permute-start(bf16[2,4,96,256]{3,2,1,0:T(8,128)(2,1)S(1)} %slice.57), channel_id=1, source_target_pairs={{0,4},{4,8},{8,12},{12,16},{16,20},{20,24},{24,28},{28,32},{32,36}... | collective-permute-start | bytes 1179656 | tf_op jit(solution)/shard_map/ppermute | solution.py:19
  5.5 18.2 %copy-start.7 = (f32[96]{0:T(128)S(1)}, f32[96]{0:T(128)}, u32[]{:S(2)}) copy-start(f32[96]{0:T(128)} %param.13) | copy-start | bytes 1156
  5.5 20.4 %collective-permute-start.3 = (bf16[4,1,96,256]{3,2,1,0:T(8,128)(2,1)S(1)}, bf16[4,1,96,256]{3,2,1,0:T(8,128)(2,1)S(1)}, u32[]{:S(2)}, u32[]{:S(2)}) collective-permute-start(bf16[4,1,96,256]{3,2,1,0:T(8,128)(2,1)S(1)} %get-tuple-element.8), channel_id=1, source_target_pairs={{0,1},{1,2},{2,3},{4,5},{5,6},{6,7},{8,9},{9,10},{10,11},{12,13},{... | collective-permute-start | bytes 589832 | tf_op jit(solution)/shard_map/ppermute | solution.py:16
  7.4 18.5 %collective-permute-start.4 = (bf16[4,1,96,256]{3,2,1,0:T(8,128)(2,1)S(1)}, bf16[4,1,96,256]{3,2,1,0:T(8,128)(2,1)S(1)}, u32[]{:S(2)}, u32[]{:S(2)}) collective-permute-start(bf16[4,1,96,256]{3,2,1,0:T(8,128)(2,1)S(1)} %get-tuple-element.9), channel_id=1, source_target_pairs={{1,0},{2,1},{3,2},{5,4},{6,5},{7,6},{9,8},{10,9},{11,10},{13,12},{... | collective-permute-start | bytes 589832 | tf_op jit(solution)/shard_map/ppermute | solution.py:16
  13.3 12.5 %collective-permute-start = (bf16[2,1,96,256]{3,2,1,0:T(8,128)(2,1)}, bf16[2,1,96,256]{3,2,1,0:T(8,128)(2,1)S(1)}, u32[]{:S(2)}, u32[]{:S(2)}) collective-permute-start(bf16[2,1,96,256]{3,2,1,0:T(8,128)(2,1)} %get-tuple-element.6), channel_id=1, source_target_pairs={{0,5},{1,6},{2,7},{4,9},{5,10},{6,11},{8,13},{9,14},{10,15},{12,17... | collective-permute-start | bytes 294920 | tf_op jit(solution)/shard_map/ppermute | solution.py:26
  15.2 10.7 %collective-permute-start.2 = (bf16[2,1,96,256]{3,2,1,0:T(8,128)(2,1)}, bf16[2,1,96,256]{3,2,1,0:T(8,128)(2,1)S(1)}, u32[]{:S(2)}, u32[]{:S(2)}) collective-permute-start(bf16[2,1,96,256]{3,2,1,0:T(8,128)(2,1)} %get-tuple-element.7), channel_id=1, source_target_pairs={{1,4},{2,5},{3,6},{5,8},{6,9},{7,10},{9,12},{10,13},{11,14},{13,16... | collective-permute-start | bytes 294920 | tf_op jit(solution)/shard_map/ppermute | solution.py:26
  32.8 23.6 %copy-start.4 = (bf16[3,3,3,96,96]{4,3,2,1,0:T(8,128)(2,1)S(1)}, bf16[3,3,3,96,96]{4,3,2,1,0:T(8,128)(2,1)}, u32[]{:S(2)}) copy-start(bf16[3,3,3,96,96]{4,3,2,1,0:T(8,128)(2,1)} %param.15) | copy-start | bytes 1492996
  33.9 26.2 %collective-permute-start.6 = (bf16[2,4,96,256]{3,2,1,0:T(8,128)(2,1)S(1)}, bf16[2,4,96,256]{3,2,1,0:T(8,128)(2,1)S(1)}, u32[]{:S(2)}, u32[]{:S(2)}) collective-permute-start(bf16[2,4,96,256]{3,2,1,0:T(8,128)(2,1)S(1)} %slice.62), channel_id=1, source_target_pairs={{0,4},{4,8},{8,12},{12,16},{16,20},{20,24},{24,28},{28,32},{32,36}... | collective-permute-start | bytes 1179656 | tf_op jit(solution)/shard_map/ppermute | solution.py:19
  38.6 21.5 %copy-start.2 = (bf16[4,4,96,256]{3,2,1,0:T(8,128)(2,1)S(1)}, bf16[4,4,96,256]{3,2,1,0:T(8,128)(2,1)}, u32[]{:S(2)}) copy-start(bf16[4,4,96,256]{3,2,1,0:T(8,128)(2,1)} %shard_map.122) | copy-start | bytes 2359300
  38.6 21.5 %collective-permute-start.8 = (bf16[4,1,96,256]{3,2,1,0:T(8,128)(2,1)S(1)}, bf16[4,1,96,256]{3,2,1,0:T(8,128)(2,1)S(1)}, u32[]{:S(2)}, u32[]{:S(2)}) collective-permute-start(bf16[4,1,96,256]{3,2,1,0:T(8,128)(2,1)S(1)} %get-tuple-element.4), channel_id=1, source_target_pairs={{0,1},{1,2},{2,3},{4,5},{5,6},{6,7},{8,9},{9,10},{10,11},{12,13},{... | collective-permute-start | bytes 589832 | tf_op jit(solution)/shard_map/ppermute | solution.py:16
  40.6 19.4 %collective-permute-start.9 = (bf16[4,1,96,256]{3,2,1,0:T(8,128)(2,1)S(1)}, bf16[4,1,96,256]{3,2,1,0:T(8,128)(2,1)S(1)}, u32[]{:S(2)}, u32[]{:S(2)}) collective-permute-start(bf16[4,1,96,256]{3,2,1,0:T(8,128)(2,1)S(1)} %get-tuple-element.5), channel_id=1, source_target_pairs={{1,0},{2,1},{3,2},{5,4},{6,5},{7,6},{9,8},{10,9},{11,10},{13,12},{... | collective-permute-start | bytes 589832 | tf_op jit(solution)/shard_map/ppermute | solution.py:16
  47.5 11.9 %collective-permute-start.5 = (bf16[2,1,96,256]{3,2,1,0:T(8,128)(2,1)}, bf16[2,1,96,256]{3,2,1,0:T(8,128)(2,1)S(1)}, u32[]{:S(2)}, u32[]{:S(2)}) collective-permute-start(bf16[2,1,96,256]{3,2,1,0:T(8,128)(2,1)} %get-tuple-element.2), channel_id=1, source_target_pairs={{0,5},{1,6},{2,7},{4,9},{5,10},{6,11},{8,13},{9,14},{10,15},{12,17... | collective-permute-start | bytes 294920 | tf_op jit(solution)/shard_map/ppermute | solution.py:26
  49.4 10.7 %collective-permute-start.7 = (bf16[2,1,96,256]{3,2,1,0:T(8,128)(2,1)}, bf16[2,1,96,256]{3,2,1,0:T(8,128)(2,1)S(1)}, u32[]{:S(2)}, u32[]{:S(2)}) collective-permute-start(bf16[2,1,96,256]{3,2,1,0:T(8,128)(2,1)} %get-tuple-element.3), channel_id=1, source_target_pairs={{1,4},{2,5},{3,6},{5,8},{6,9},{7,10},{9,12},{10,13},{11,14},{13,16... | collective-permute-start | bytes 294920 | tf_op jit(solution)/shard_map/ppermute | solution.py:26
  61.6 14.4 %copy-start.5 = (bf16[3,3,3,96,96]{4,3,2,1,0:T(8,128)(2,1)S(1)}, bf16[3,3,3,96,96]{4,3,2,1,0:T(8,128)(2,1)}, u32[]{:S(2)}) copy-start(bf16[3,3,3,96,96]{4,3,2,1,0:T(8,128)(2,1)} %param.21) | copy-start | bytes 1492996
  68.2 27.4 %copy-start.6 = (bf16[1,16,4,256]{3,2,1,0:T(4,128)(2,1)}, bf16[1,16,4,256]{3,2,1,0:T(4,128)(2,1)S(1)}, u32[]{:S(2)}) copy-start(bf16[1,16,4,256]{3,2,1,0:T(4,128)(2,1)S(1)} %reshape.48) | copy-start | bytes 98308
  68.3 9.5 %collective-permute-start.10 = (bf16[1,16,2,256]{3,2,1,0:T(2,128)(2,1)S(1)}, bf16[1,16,2,256]{3,2,1,0:T(2,128)(2,1)S(1)}, u32[]{:S(2)}, u32[]{:S(2)}) collective-permute-start(bf16[1,16,2,256]{3,2,1,0:T(2,128)(2,1)S(1)} %get-tuple-element.10), channel_id=1, source_target_pairs={{0,1},{1,2},{2,3},{4,5},{5,6},{6,7},{8,9},{9,10},{10,11},{12,13},{... | collective-permute-start | bytes 49160 | tf_op jit(solution)/shard_map/ppermute | solution.py:16
  70.2 7.5 %collective-permute-start.11 = (bf16[1,16,2,256]{3,2,1,0:T(2,128)(2,1)S(1)}, bf16[1,16,2,256]{3,2,1,0:T(2,128)(2,1)S(1)}, u32[]{:S(2)}, u32[]{:S(2)}) collective-permute-start(bf16[1,16,2,256]{3,2,1,0:T(2,128)(2,1)S(1)} %get-tuple-element.11), channel_id=1, source_target_pairs={{1,0},{2,1},{3,2},{5,4},{6,5},{7,6},{9,8},{10,9},{11,10},{13,12},{... | collective-permute-start | bytes 49160 | tf_op jit(solution)/shard_map/ppermute | solution.py:16
  77.8 10.2 %collective-permute-start.12 = (bf16[1,16,8,256]{3,2,1,0:T(8,128)(2,1)S(1)}, bf16[1,16,8,256]{3,2,1,0:T(8,128)(2,1)S(1)}, u32[]{:S(2)}, u32[]{:S(2)}) collective-permute-start(bf16[1,16,8,256]{3,2,1,0:T(8,128)(2,1)S(1)} %pad_maximum_fusion.1), channel_id=1, source_target_pairs={{0,12},{4,16},{8,20},{12,24},{16,28},{20,32},{24,36},{28,40},{32,4... | collective-permute-start | bytes 196616 | tf_op jit(solution)/shard_map/ppermute | solution.py:19
  81.0 10.8 %collective-permute-start.13 = (bf16[1,16,8,256]{3,2,1,0:T(8,128)(2,1)S(1)}, bf16[1,16,8,256]{3,2,1,0:T(8,128)(2,1)S(1)}, u32[]{:S(2)}, u32[]{:S(2)}) collective-permute-start(bf16[1,16,8,256]{3,2,1,0:T(8,128)(2,1)S(1)} %pad_maximum_fusion.1), channel_id=1, source_target_pairs={{0,8},{4,12},{8,16},{12,20},{16,24},{20,28},{24,32},{28,36},{32,40... | collective-permute-start | bytes 196616 | tf_op jit(solution)/shard_map/ppermute | solution.py:19
  85.2 10.4 %collective-permute-start.14 = (bf16[1,16,8,256]{3,2,1,0:T(8,128)(2,1)S(1)}, bf16[1,16,8,256]{3,2,1,0:T(8,128)(2,1)S(1)}, u32[]{:S(2)}, u32[]{:S(2)}) collective-permute-start(bf16[1,16,8,256]{3,2,1,0:T(8,128)(2,1)S(1)} %pad_maximum_fusion.1), channel_id=1, source_target_pairs={{0,4},{4,8},{8,12},{12,16},{16,20},{20,24},{24,28},{28,32},{32,36}... | collective-permute-start | bytes 196616 | tf_op jit(solution)/shard_map/ppermute | solution.py:19
  100.3 16.9 %copy-start.8 = (f32[96]{0:T(128)S(1)}, f32[96]{0:T(128)}, u32[]{:S(2)}) copy-start(f32[96]{0:T(128)} %param.18) | copy-start | bytes 1156
  100.3 17.4 %copy-start.9 = (bf16[4,96,96]{2,1,0:T(8,128)(2,1)S(1)}, bf16[4,96,96]{2,1,0:T(8,128)(2,1)}, u32[]{:S(2)}) copy-start(bf16[4,96,96]{2,1,0:T(8,128)(2,1)} %param.20) | copy-start | bytes 221188
  100.3 17.4 %copy-start.10 = (f32[96]{0:T(128)S(1)}, f32[96]{0:T(128)}, u32[]{:S(2)}) copy-start(f32[96]{0:T(128)} %param.19) | copy-start | bytes 1156
where the time goes:
time: 130 us; the launch traced here: 129 us
  starting transfers between devices  56.6 us (44%)
  local copies, waits for them, and re-layouts  21.7 us (17%)
  matrix products  18.2 us (14%)
  Pallas kernels  16.5 us (13%)
  waiting for transfers between devices  9.64 us (7%)
  other arithmetic  5.3 us (4%)
    ppermute x6, starting transfers between devices, shift(): return lax.ppermute(x, 'rows', pairs)  21.9 us
    ppermute x4, starting transfers between devices, shift(): return lax.ppermute(x, ('tm', 'rows'), pairs)  17.5 us
    ppermute x5, starting transfers between devices, shift(): return lax.ppermute(x, 'tm', pairs)  17.2 us
    conv_general_dilated x1, matrix products, conv_valid(): lax.conv_general_dilated(v[None], kernel, (1, 1, 1), [(0, 0), (0, 0), (1,...  16.9 us
    ppermute x5, waiting for transfers between devices, shift(): return lax.ppermute(x, 'tm', pairs)  7.6 us
    pallas_call x1, Pallas kernels, body(): pl.pallas_call(functools.partial(latent_kernel, **dims), out_shape=jax.Sh...  5.89 us
    pallas_call x1, Pallas kernels, body(): pl.pallas_call(functools.partial(gate_kernel, **dims), out_shape=jax.Shap...  5.4 us
    pallas_call x1, Pallas kernels, body(): pl.pallas_call(functools.partial(rebuild_kernel, **dims), out_shape=jax.S...  5.19 us
  transfers between devices with their start and end apart: 15, of which 5 were waited for; matrix products, arithmetic and copies ran while one was open for 8% of the time, Pallas kernels for 0%

commit v1 on v0

--- a/solution.py
+++ b/solution.py
@@ -81,13 +81,32 @@
         hidden = (res.astype(jnp.float32) + y).astype(jnp.bfloat16)
         part = jnp.dot(w_ref[t], hidden, preferred_element_type=jnp.float32)
         total = part if total is None else total + part
-    o_ref[...] = total.astype(o_ref.dtype)
-
-
-def rebuild_kernel(x_ref, k_ref, o_ref, *, frames, rows, columns):
+    for r in range(rows):
+        o_ref[r] = total[:, r * columns : (r + 1) * columns].astype(o_ref.dtype)
+
+
+def decode_kernel_body(
+    lat_ref, dk_ref, bias_ref, gain_ref, up_ref, mask_ref, fk_ref, o_ref, ext_ref,
+    *, frames, rows, columns
+):
+    wide = rows + 2
+    bias = bias_ref[...]
+    gain = gain_ref[...]
+    for f in range(2):
+        y = tap_sum(lat_ref, dk_ref, f, wide, columns) + bias
+        scale = lax.rsqrt(jnp.mean(y * y, axis=0, keepdims=True) + 1e-06)
+        z = y * scale * gain
+        act = (z / (1.0 + jnp.exp(-z))).astype(jnp.bfloat16)
+        first_j = frames - 2 if f == 0 else 0
+        for j in range(first_j, frames):
+            up = jnp.dot(up_ref[j], act, preferred_element_type=jnp.float32)
+            slot = j - first_j if f == 0 else j + 2
+            for r in range(wide):
+                piece = up[:, r * columns : (r + 1) * columns] * mask_ref[slot, r]
+                ext_ref[slot, r] = piece.astype(ext_ref.dtype)
     for t in range(frames):
-        y = tap_sum(x_ref, k_ref, t, rows, columns)
-        res = jnp.concatenate([x_ref[t + 2, r + 1] for r in range(rows)], axis=1)
+        y = tap_sum(ext_ref, fk_ref, t, rows, columns)
+        res = jnp.concatenate([ext_ref[t + 2, r + 1] for r in range(rows)], axis=1)
         o_ref[t] = (res.astype(jnp.float32) + y).astype(o_ref.dtype)
 
 
@@ -134,34 +153,43 @@
         first_bias[:, None],
         first_gain[:, None],
     )
-    latent_flat = pl.pallas_call(
+    lat = pl.pallas_call(
         functools.partial(latent_kernel, **dims),
-        out_shape=jax.ShapeDtypeStruct((z_count, rows * columns), jnp.bfloat16),
+        out_shape=jax.ShapeDtypeStruct((rows, z_count, columns), jnp.bfloat16),
     )(haloed_rows_first(gated), merged_kernel(second_kernel), own, latent_weight)
-    latent = latent_flat.reshape(1, z_count, rows, columns)
-    lat_rows = jnp.concatenate(
-        [shift(latent[:, :, -2:], 0, 1), latent, shift(latent[:, :, :2], 0, -1)], 2
-    )
-    stacked = jnp.concatenate(
-        [shift(lat_rows, 3, 0), shift(lat_rows, 2, 0), shift(lat_rows, 1, 0), lat_rows], 0
-    )
-    decoded = conv_valid(stacked, decode_kernel) + decode_bias[None, :, None, None]
-    activated = normed_silu(decoded, decode_gain).astype(jnp.bfloat16)
-    upsampled = jnp.einsum(
-        "joc,kcrw->kjrow", upsample_weight, activated, preferred_element_type=jnp.float32
-    )
-    upsampled = upsampled.reshape(-1, rows + 2, channels, columns).astype(jnp.bfloat16)
+    latent = lat.transpose(1, 0, 2)[None]
+    stacked = jnp.stack(
+        [
+            jnp.concatenate(
+                [shift(lat[-2:], dt, 1), lat if dt == 0 else shift(lat, dt, 0), shift(lat[:2], dt, -1)],
+                0,
+            )
+            for dt in (3, 2, 1, 0)
+        ],
+        0,
+    )
     band = lax.axis_index("rows")
     bands = lax.axis_size("rows")
-    row_ids = lax.broadcasted_iota(jnp.int32, (1, rows + 2, 1, 1), 1)
+    row_ids = lax.broadcasted_iota(jnp.int32, (frames + 2, rows + 2), 1)
+    frame_ids = lax.broadcasted_iota(jnp.int32, (frames + 2, rows + 2), 0)
     inside = ((row_ids > 0) | (band > 0)) & ((row_ids < rows + 1) | (band < bands - 1))
-    upsampled = jnp.where(inside, upsampled, jnp.zeros_like(upsampled))
-    previous = upsampled[frames - 2 : frames]
-    previous = jnp.where(lax.axis_index("tm") > 0, previous, jnp.zeros_like(previous))
+    inside = inside & ((frame_ids >= 2) | (lax.axis_index("tm") > 0))
+    mask = inside.astype(jnp.float32)
+    vmem = pl.BlockSpec(memory_space=pltpu.VMEM)
     rebuilt_flat = pl.pallas_call(
-        functools.partial(rebuild_kernel, **dims),
+        functools.partial(decode_kernel_body, **dims),
         out_shape=jax.ShapeDtypeStruct((frames, channels, rows * columns), jnp.bfloat16),
-    )(jnp.concatenate([previous, upsampled[frames:]], 0), merged_kernel(final_kernel))
+        in_specs=[vmem] * 5 + [pl.BlockSpec(memory_space=pltpu.SMEM), vmem],
+        scratch_shapes=[pltpu.VMEM((frames + 2, rows + 2, channels, columns), jnp.bfloat16)],
+    )(
+        stacked,
+        merged_kernel(decode_kernel),
+        decode_bias[:, None],
+        decode_gain[:, None],
+        upsample_weight,
+        mask,
+        merged_kernel(final_kernel),
+    )
     rebuilt = rebuilt_flat.reshape(frames, channels, rows, columns)
     return (latent, rebuilt)
 

time: 130 us -> 136 us (1.046)
  the two profiles are of different devices: /device:TPU:24 before, /device:TPU:65 now
where the time goes in v1:
time: 136 us
  starting transfers between devices  74.4 us (55%)
  local copies, waits for them, and re-layouts  19.1 us (14%)
  waiting for transfers between devices  17.9 us (13%)
  Pallas kernels  17.9 us (13%)
  other arithmetic  5.31 us (4%)
    ppermute x10, starting transfers between devices, shift(): return lax.ppermute(x, ('tm', 'rows'), pairs)  43.1 us
    ppermute x10, waiting for transfers between devices, shift(): return lax.ppermute(x, ('tm', 'rows'), pairs)  17.8 us
    ppermute x6, starting transfers between devices, shift(): return lax.ppermute(x, 'rows', pairs)  17.4 us
    ppermute x5, starting transfers between devices, shift(): return lax.ppermute(x, 'tm', pairs)  13.9 us
    pallas_call x1, Pallas kernels, body(): pl.pallas_call(functools.partial(decode_kernel_body, **dims), out_shape=j...  6.59 us
    pallas_call x1, Pallas kernels, body(): pl.pallas_call(functools.partial(latent_kernel, **dims), out_shape=jax.Sh...  5.89 us
    pallas_call x1, Pallas kernels, body(): pl.pallas_call(functools.partial(gate_kernel, **dims), out_shape=jax.Shap...  5.4 us
    reshape x5, local copies, waits for them, and re-layouts, merged_kernel(): return kernel.transpose(2, 3, 0, 1, 4).reshape(3 * o, 9 * c)  4.8 us
  transfers between devices with their start and end apart: 21, of which 3 were waited for; matrix products, arithmetic and copies ran while one was open for 10% of the time, Pallas kernels for 0%

profile of v1, /device:TPU:65, one launch (start us, length us, event | category | flops | bytes accessed | tf_op | source)
XLA Modules:
  0.0 135.6 jit_solution(6318831736827055777)
XLA Ops:
  0.6 1.3 copy.35
  2.0 3.1 %collective-permute-start.1 = (bf16[2,4,96,256]{3,2,1,0:T(8,128)(2,1)S(1)}, bf16[2,4,96,256]{3,2,1,0:T(8,128)(2,1)S(1)}, u32[]{:S(2)}, u32[]{:S(2)}) collective-permute-start(bf16[2,4,96,256]{3,2,1,0:T(8,128)(2,1)S(1)} %slice.55), channel_id=1, source_target_pairs={{0,4},{4,8},{8,12},{12,16},{16,20},{20,24},{24,28},{28,32},{32,36}... | collective-permute-start | bytes 1179656 | tf_op jit(solution)/shard_map/ppermute | solution.py:19
  5.1 0.8 fusion.3
  5.9 5.8 %collective-permute-start.3 = (bf16[4,1,96,256]{3,2,1,0:T(8,128)(2,1)}, bf16[4,1,96,256]{3,2,1,0:T(8,128)(2,1)S(1)}, u32[]{:S(2)}, u32[]{:S(2)}) collective-permute-start(bf16[4,1,96,256]{3,2,1,0:T(8,128)(2,1)} %get-tuple-element.12), channel_id=1, source_target_pairs={{0,1},{1,2},{2,3},{4,5},{5,6},{6,7},{8,9},{9,10},{10,11},{12,13},{... | collective-permute-start | bytes 589832 | tf_op jit(solution)/shard_map/ppermute | solution.py:16
  11.7 1.9 %collective-permute-start.4 = (bf16[4,1,96,256]{3,2,1,0:T(8,128)(2,1)}, bf16[4,1,96,256]{3,2,1,0:T(8,128)(2,1)S(1)}, u32[]{:S(2)}, u32[]{:S(2)}) collective-permute-start(bf16[4,1,96,256]{3,2,1,0:T(8,128)(2,1)} %get-tuple-element.13), channel_id=1, source_target_pairs={{1,0},{2,1},{3,2},{5,4},{6,5},{7,6},{9,8},{10,9},{11,10},{13,12},{... | collective-permute-start | bytes 589832 | tf_op jit(solution)/shard_map/ppermute | solution.py:16
  13.6 0.7 fusion.2
  14.3 6.1 %collective-permute-start = (bf16[2,1,96,256]{3,2,1,0:T(8,128)(2,1)}, bf16[2,1,96,256]{3,2,1,0:T(8,128)(2,1)}, u32[]{:S(2)}, u32[]{:S(2)}) collective-permute-start(bf16[2,1,96,256]{3,2,1,0:T(8,128)(2,1)} %get-tuple-element.10), channel_id=1, source_target_pairs={{0,5},{1,6},{2,7},{4,9},{5,10},{6,11},{8,13},{9,14},{10,15},{12,17... | collective-permute-start | bytes 294920 | tf_op jit(solution)/shard_map/ppermute | solution.py:26
  20.4 1.9 %collective-permute-start.2 = (bf16[2,1,96,256]{3,2,1,0:T(8,128)(2,1)}, bf16[2,1,96,256]{3,2,1,0:T(8,128)(2,1)}, u32[]{:S(2)}, u32[]{:S(2)}) collective-permute-start(bf16[2,1,96,256]{3,2,1,0:T(8,128)(2,1)} %get-tuple-element.11), channel_id=1, source_target_pairs={{1,4},{2,5},{3,6},{5,8},{6,9},{7,10},{9,12},{10,13},{11,14},{13,16... | collective-permute-start | bytes 294920 | tf_op jit(solution)/shard_map/ppermute | solution.py:26
  22.3 0.5 copy.24
  22.8 1.3 reshape.19.k_ref
  24.1 0.7 copy.25.bias_ref
  24.8 0.7 copy.26.gain_ref
  25.5 0.5 copy.27
  26.0 1.3 reshape.20.k_ref
  27.3 0.0 collective-permute-done
  27.3 3.9 %collective-permute-done.2 = bf16[2,1,96,256]{3,2,1,0:T(8,128)(2,1)} collective-permute-done((bf16[2,1,96,256]{3,2,1,0:T(8,128)(2,1)}, bf16[2,1,96,256]{3,2,1,0:T(8,128)(2,1)}, u32[]{:S(2)}, u32[]{:S(2)}) %collective-permute-start.2) | collective-permute-done | bytes 98336 | tf_op jit(solution)/shard_map/ppermute | solution.py:26
  31.2 0.0 collective-permute-done.3
  31.2 0.0 collective-permute-done.4
  31.2 2.4 %maximum_maximum_fusion.x_ref = bf16[6,6,96,256]{3,2,1,0:T(8,128)(2,1)} fusion(bf16[4,1,96,256]{3,2,1,0:T(8,128)(2,1)S(1)} %collective-permute-done.4, bf16[4,4,96,256]{3,2,1,0:T(8,128)(2,1)S(1)} %bitcast.27, bf16[4,1,96,256]{3,2,1,0:T(8,128)(2,1)S(1)} %collective-permute-done.3, bf16[2,1,96,256]{3,2,1,0:T(8,128)(2,1)} %collective-permute-done.2, ...), kind=kLoop, calls=%fused_computation | loop fusion | flops 4423680 | bytes 3538944 | tf_op jit(solution)/shard_map/concatenate | solution.py:37
  33.6 5.4 %shard_map.122 = bf16[4,4,96,256]{3,2,1,0:T(8,128)(2,1)} custom-call(bf16[6,6,96,256]{3,2,1,0:T(8,128)(2,1)} %maximum_maximum_fusion.x_ref, bf16[288,864]{1,0:T(8,128)(2,1)} %reshape.19.k_ref, f32[96,1]{1,0:T(8,128)} %copy.25.bias_ref, f32[96,1]{1,0:T(8,128)} %copy.26.gain_ref), custom_call_target="tpu_custom_call" | custom-call | tf_op jit(solution)/shard_map/pallas_call | solution.py:147
  39.0 1.1 slice.60
  40.1 1.9 %collective-permute-start.6 = (bf16[2,4,96,256]{3,2,1,0:T(8,128)(2,1)S(1)}, bf16[2,4,96,256]{3,2,1,0:T(8,128)(2,1)S(1)}, u32[]{:S(2)}, u32[]{:S(2)}) collective-permute-start(bf16[2,4,96,256]{3,2,1,0:T(8,128)(2,1)S(1)} %slice.60), channel_id=1, source_target_pairs={{0,4},{4,8},{8,12},{12,16},{16,20},{20,24},{24,28},{28,32},{32,36}... | collective-permute-start | bytes 1179656 | tf_op jit(solution)/shard_map/ppermute | solution.py:19
  42.0 1.1 fusion.1
  43.1 3.5 %collective-permute-start.8 = (bf16[4,1,96,256]{3,2,1,0:T(8,128)(2,1)S(1)}, bf16[4,1,96,256]{3,2,1,0:T(8,128)(2,1)S(1)}, u32[]{:S(2)}, u32[]{:S(2)}) collective-permute-start(bf16[4,1,96,256]{3,2,1,0:T(8,128)(2,1)S(1)} %get-tuple-element.8), channel_id=1, source_target_pairs={{0,1},{1,2},{2,3},{4,5},{5,6},{6,7},{8,9},{9,10},{10,11},{12,13},{... | collective-permute-start | bytes 589832 | tf_op jit(solution)/shard_map/ppermute | solution.py:16
  46.5 1.9 %collective-permute-start.9 = (bf16[4,1,96,256]{3,2,1,0:T(8,128)(2,1)S(1)}, bf16[4,1,96,256]{3,2,1,0:T(8,128)(2,1)S(1)}, u32[]{:S(2)}, u32[]{:S(2)}) collective-permute-start(bf16[4,1,96,256]{3,2,1,0:T(8,128)(2,1)S(1)} %get-tuple-element.9), channel_id=1, source_target_pairs={{1,0},{2,1},{3,2},{5,4},{6,5},{7,6},{9,8},{10,9},{11,10},{13,12},{... | collective-permute-start | bytes 589832 | tf_op jit(solution)/shard_map/ppermute | solution.py:16
  48.5 1.0 fusion
  49.4 6.1 %collective-permute-start.5 = (bf16[2,1,96,256]{3,2,1,0:T(8,128)(2,1)S(1)}, bf16[2,1,96,256]{3,2,1,0:T(8,128)(2,1)S(1)}, u32[]{:S(2)}, u32[]{:S(2)}) collective-permute-start(bf16[2,1,96,256]{3,2,1,0:T(8,128)(2,1)S(1)} %get-tuple-element.6), channel_id=1, source_target_pairs={{0,5},{1,6},{2,7},{4,9},{5,10},{6,11},{8,13},{9,14},{10,15},{12,17... | collective-permute-start | bytes 294920 | tf_op jit(solution)/shard_map/ppermute | solution.py:26
  55.5 1.9 %collective-permute-start.7 = (bf16[2,1,96,256]{3,2,1,0:T(8,128)(2,1)S(1)}, bf16[2,1,96,256]{3,2,1,0:T(8,128)(2,1)S(1)}, u32[]{:S(2)}, u32[]{:S(2)}) collective-permute-start(bf16[2,1,96,256]{3,2,1,0:T(8,128)(2,1)S(1)} %get-tuple-element.7), channel_id=1, source_target_pairs={{1,4},{2,5},{3,6},{5,8},{6,9},{7,10},{9,12},{10,13},{11,14},{13,16... | collective-permute-start | bytes 294920 | tf_op jit(solution)/shard_map/ppermute | solution.py:26
  57.5 0.0 collective-permute-done.5
  57.5 8.5 %collective-permute-done.7 = bf16[2,1,96,256]{3,2,1,0:T(8,128)(2,1)S(1)} collective-permute-done((bf16[2,1,96,256]{3,2,1,0:T(8,128)(2,1)S(1)}, bf16[2,1,96,256]{3,2,1,0:T(8,128)(2,1)S(1)}, u32[]{:S(2)}, u32[]{:S(2)}) %collective-permute-start.7) | collective-permute-done | bytes 98336 | tf_op jit(solution)/shard_map/ppermute | solution.py:26
  66.0 0.0 collective-permute-done.8
  66.0 0.0 collective-permute-done.9
  66.0 0.0 collective-permute-done.6
  66.0 1.5 %maximum_maximum_fusion.1.x_ref = bf16[6,6,96,256]{3,2,1,0:T(8,128)(2,1)} fusion(bf16[4,1,96,256]{3,2,1,0:T(8,128)(2,1)S(1)} %collective-permute-done.9, bf16[4,4,96,256]{3,2,1,0:T(8,128)(2,1)S(1)} %copy-done.1, bf16[4,1,96,256]{3,2,1,0:T(8,128)(2,1)S(1)} %collective-permute-done.8, bf16[2,1,96,256]{3,2,1,0:T(8,128)(2,1)S(1)} %collective-permute-done.7, ...), kind=kLoop, calls=%fused_computation.1 | loop fusion | flops 4423680 | bytes 3538944 | tf_op jit(solution)/shard_map/concatenate | solution.py:37
  67.4 5.9 %shard_map.123 = bf16[4,16,256]{2,1,0:T(8,128)(2,1)} custom-call(bf16[6,6,96,256]{3,2,1,0:T(8,128)(2,1)} %maximum_maximum_fusion.1.x_ref, bf16[288,864]{1,0:T(8,128)(2,1)} %reshape.20.k_ref, bf16[4,4,96,256]{3,2,1,0:T(8,128)(2,1)} %bitcast.28, bf16[4,16,96]{2,1,0:T(8,128)(2,1)} %w_ref.1), custom_call_target="tpu_custom_call" | custom-call | tf_op jit(solution)/shard_map/pallas_call | solution.py:156
  73.3 0.8 fusion.4
  74.1 1.9 %collective-permute-start.19 = (bf16[2,16,256]{2,1,0:T(8,128)(2,1)S(1)}, bf16[2,16,256]{2,1,0:T(8,128)(2,1)S(1)}, u32[]{:S(2)}, u32[]{:S(2)}) collective-permute-start(bf16[2,16,256]{2,1,0:T(8,128)(2,1)S(1)} %get-tuple-element.14), channel_id=1, source_target_pairs={{0,1},{1,2},{2,3},{4,5},{5,6},{6,7},{8,9},{9,10},{10,11},{12,13},{... | collective-permute-start | bytes 49160 | tf_op jit(solution)/shard_map/ppermute | solution.py:16
  76.0 2.4 %collective-permute-start.20 = (bf16[2,16,256]{2,1,0:T(8,128)(2,1)S(1)}, bf16[2,16,256]{2,1,0:T(8,128)(2,1)S(1)}, u32[]{:S(2)}, u32[]{:S(2)}) collective-permute-start(bf16[2,16,256]{2,1,0:T(8,128)(2,1)S(1)} %get-tuple-element.15), channel_id=1, source_target_pairs={{1,0},{2,1},{3,2},{5,4},{6,5},{7,6},{9,8},{10,9},{11,10},{13,12},{... | collective-permute-start | bytes 49160 | tf_op jit(solution)/shard_map/ppermute | solution.py:16
  78.4 0.7 and_convert_fusion.mask_ref
  79.1 0.5 copy.29
  79.6 1.3 reshape.22.fk_ref
  80.9 0.1 copy.28
  80.9 0.1 reshape.21
  81.1 0.8 copy.30.dk_ref
  81.9 0.7 copy.31.bias_ref
  82.6 0.7 copy.32.gain_ref
  83.3 3.3 %collective-permute-start.10 = (bf16[2,16,256]{2,1,0:T(8,128)(2,1)S(1)}, bf16[2,16,256]{2,1,0:T(8,128)(2,1)S(1)}, u32[]{:S(2)}, u32[]{:S(2)}) collective-permute-start(bf16[2,16,256]{2,1,0:T(8,128)(2,1)S(1)} %get-tuple-element.14), channel_id=1, source_target_pairs={{0,13},{1,14},{2,15},{4,17},{5,18},{6,19},{8,21},{9,22},{10,23},{1... | collective-permute-start | bytes 49160 | tf_op jit(solution)/shard_map/ppermute | solution.py:26
  86.6 1.9 %collective-permute-start.12 = (bf16[2,16,256]{2,1,0:T(8,128)(2,1)S(1)}, bf16[2,16,256]{2,1,0:T(8,128)(2,1)S(1)}, u32[]{:S(2)}, u32[]{:S(2)}) collective-permute-start(bf16[2,16,256]{2,1,0:T(8,128)(2,1)S(1)} %get-tuple-element.15), channel_id=1, source_target_pairs={{1,12},{2,13},{3,14},{5,16},{6,17},{7,18},{9,20},{10,21},{11,22},{... | collective-permute-start | bytes 49160 | tf_op jit(solution)/shard_map/ppermute | solution.py:26
  88.5 3.0 %collective-permute-start.11 = (bf16[4,16,256]{2,1,0:T(8,128)(2,1)S(1)}, bf16[4,16,256]{2,1,0:T(8,128)(2,1)S(1)}, u32[]{:S(2)}, u32[]{:S(2)}) collective-permute-start(bf16[4,16,256]{2,1,0:T(8,128)(2,1)S(1)} %copy-done.5), channel_id=1, source_target_pairs={{0,12},{4,16},{8,20},{12,24},{16,28},{20,32},{24,36},{28,40},{32,4... | collective-permute-start | bytes 98312 | tf_op jit(solution)/shard_map/ppermute | solution.py:19
  91.5 0.6 copy.33
  92.1 8.0 %collective-permute-start.13 = (bf16[2,16,256]{2,1,0:T(8,128)(2,1)S(1)}, bf16[2,16,256]{2,1,0:T(8,128)(2,1)S(1)}, u32[]{:S(2)}, u32[]{:S(2)}) collective-permute-start(bf16[2,16,256]{2,1,0:T(8,128)(2,1)S(1)} %get-tuple-element.14), channel_id=1, source_target_pairs={{0,9},{1,10},{2,11},{4,13},{5,14},{6,15},{8,17},{9,18},{10,19},{12... | collective-permute-start | bytes 49160 | tf_op jit(solution)/shard_map/ppermute | solution.py:26
  100.2 1.9 %collective-permute-start.15 = (bf16[2,16,256]{2,1,0:T(8,128)(2,1)S(1)}, bf16[2,16,256]{2,1,0:T(8,128)(2,1)S(1)}, u32[]{:S(2)}, u32[]{:S(2)}) collective-permute-start(bf16[2,16,256]{2,1,0:T(8,128)(2,1)S(1)} %get-tuple-element.15), channel_id=1, source_target_pairs={{1,8},{2,9},{3,10},{5,12},{6,13},{7,14},{9,16},{10,17},{11,18},{13... | collective-permute-start | bytes 49160 | tf_op jit(solution)/shard_map/ppermute | solution.py:26
  102.1 0.0 collective-permute-done.10
  102.2 3.7 %collective-permute-start.14 = (bf16[4,16,256]{2,1,0:T(8,128)(2,1)S(1)}, bf16[4,16,256]{2,1,0:T(8,128)(2,1)S(1)}, u32[]{:S(2)}, u32[]{:S(2)}) collective-permute-start(bf16[4,16,256]{2,1,0:T(8,128)(2,1)S(1)} %copy-done.5), channel_id=1, source_target_pairs={{0,8},{4,12},{8,16},{12,20},{16,24},{20,28},{24,32},{28,36},{32,40... | collective-permute-start | bytes 98312 | tf_op jit(solution)/shard_map/ppermute | solution.py:19
  105.9 10.1 %collective-permute-start.16 = (bf16[2,16,256]{2,1,0:T(8,128)(2,1)S(1)}, bf16[2,16,256]{2,1,0:T(8,128)(2,1)S(1)}, u32[]{:S(2)}, u32[]{:S(2)}) collective-permute-start(bf16[2,16,256]{2,1,0:T(8,128)(2,1)S(1)} %get-tuple-element.14), channel_id=1, source_target_pairs={{0,5},{1,6},{2,7},{4,9},{5,10},{6,11},{8,13},{9,14},{10,15},{12,17... | collective-permute-start | bytes 49160 | tf_op jit(solution)/shard_map/ppermute | solution.py:26
  116.0 1.9 %collective-permute-start.18 = (bf16[2,16,256]{2,1,0:T(8,128)(2,1)S(1)}, bf16[2,16,256]{2,1,0:T(8,128)(2,1)S(1)}, u32[]{:S(2)}, u32[]{:S(2)}) collective-permute-start(bf16[2,16,256]{2,1,0:T(8,128)(2,1)S(1)} %get-tuple-element.15), channel_id=1, source_target_pairs={{1,4},{2,5},{3,6},{5,8},{6,9},{7,10},{9,12},{10,13},{11,14},{13,16... | collective-permute-start | bytes 49160 | tf_op jit(solution)/shard_map/ppermute | solution.py:26
  117.9 0.0 collective-permute-done.13
  118.0 2.1 %collective-permute-start.17 = (bf16[4,16,256]{2,1,0:T(8,128)(2,1)S(1)}, bf16[4,16,256]{2,1,0:T(8,128)(2,1)S(1)}, u32[]{:S(2)}, u32[]{:S(2)}) collective-permute-start(bf16[4,16,256]{2,1,0:T(8,128)(2,1)S(1)} %copy-done.5), channel_id=1, source_target_pairs={{0,4},{4,8},{8,12},{12,16},{16,20},{20,24},{24,28},{28,32},{32,36}... | collective-permute-start | bytes 98312 | tf_op jit(solution)/shard_map/ppermute | solution.py:19
  120.1 0.0 collective-permute-done.15
  120.1 0.0 collective-permute-done.14
  120.1 5.5 %collective-permute-done.18 = bf16[2,16,256]{2,1,0:T(8,128)(2,1)S(1)} collective-permute-done((bf16[2,16,256]{2,1,0:T(8,128)(2,1)S(1)}, bf16[2,16,256]{2,1,0:T(8,128)(2,1)S(1)}, u32[]{:S(2)}, u32[]{:S(2)}) %collective-permute-start.18) | collective-permute-done | bytes 16416 | tf_op jit(solution)/shard_map/ppermute | solution.py:26
  125.6 0.7 pad_maximum_fusion.lat_ref
  126.3 6.6 %shard_map.124 = bf16[4,96,1024]{2,1,0:T(8,128)(2,1)} custom-call(bf16[4,8,16,256]{3,2,1,0:T(8,128)(2,1)} %pad_maximum_fusion.lat_ref, bf16[288,144]{1,0:T(8,128)(2,1)} %copy.30.dk_ref, f32[96,1]{1,0:T(8,128)} %copy.31.bias_ref, f32[96,1]{1,0:T(8,128)} %copy.32.gain_ref, bf16[4,96,96]{2,1,0:T(8,128)(2,1)} %up_ref.1, f32[6,6]{1,0:T(8,128)} %and_convert_fusion.mask_ref, ...), custom_call_target="tpu_custom_call" | custom-call | tf_op jit(solution)/shard_map/pallas_call | solution.py:179
  132.9 2.6 %reshape.23 = bf16[4,96,4,256]{3,2,1,0:T(4,128)(2,1)} reshape(bf16[4,96,1024]{2,1,0:T(8,128)(2,1)} %shard_map.124) | data formatting | bytes 1572864 | tf_op jit(solution)/shard_map/reshape | solution.py:193
  (35 shorter events, 0.1 us)
Async XLA Ops:
  0.6 21.7 %copy-start.2 = (bf16[3,3,3,96,96]{4,3,2,1,0:T(8,128)(2,1)S(1)}, bf16[3,3,3,96,96]{4,3,2,1,0:T(8,128)(2,1)}, u32[]{:S(2)}) copy-start(bf16[3,3,3,96,96]{4,3,2,1,0:T(8,128)(2,1)} %param.12) | copy-start | bytes 1492996
  2.0 29.2 %copy-start = (bf16[4,96,4,256]{3,1,2,0:T(8,128)(2,1)}, bf16[4,96,4,256]{3,1,2,0:T(8,128)(2,1)S(1)}, u32[]{:S(2)}) copy-start(bf16[4,96,4,256]{3,1,2,0:T(8,128)(2,1)S(1)} %copy.35) | copy-start | bytes 2359300
  2.0 29.2 %collective-permute-start.1 = (bf16[2,4,96,256]{3,2,1,0:T(8,128)(2,1)S(1)}, bf16[2,4,96,256]{3,2,1,0:T(8,128)(2,1)S(1)}, u32[]{:S(2)}, u32[]{:S(2)}) collective-permute-start(bf16[2,4,96,256]{3,2,1,0:T(8,128)(2,1)S(1)} %slice.55), channel_id=1, source_target_pairs={{0,4},{4,8},{8,12},{12,16},{16,20},{20,24},{24,28},{28,32},{32,36}... | collective-permute-start | bytes 1179656 | tf_op jit(solution)/shard_map/ppermute | solution.py:19
  5.9 18.2 %copy-start.7 = (f32[96]{0:T(128)S(1)}, f32[96]{0:T(128)}, u32[]{:S(2)}) copy-start(f32[96]{0:T(128)} %param.13) | copy-start | bytes 1156
  5.9 18.9 %copy-start.8 = (f32[96]{0:T(128)S(1)}, f32[96]{0:T(128)}, u32[]{:S(2)}) copy-start(f32[96]{0:T(128)} %param.14) | copy-start | bytes 1156
  5.9 19.6 %copy-start.3 = (bf16[3,3,3,96,96]{4,3,2,1,0:T(8,128)(2,1)S(1)}, bf16[3,3,3,96,96]{4,3,2,1,0:T(8,128)(2,1)}, u32[]{:S(2)}) copy-start(bf16[3,3,3,96,96]{4,3,2,1,0:T(8,128)(2,1)} %param.15) | copy-start | bytes 1492996
  5.9 25.3 %collective-permute-start.3 = (bf16[4,1,96,256]{3,2,1,0:T(8,128)(2,1)}, bf16[4,1,96,256]{3,2,1,0:T(8,128)(2,1)S(1)}, u32[]{:S(2)}, u32[]{:S(2)}) collective-permute-start(bf16[4,1,96,256]{3,2,1,0:T(8,128)(2,1)} %get-tuple-element.12), channel_id=1, source_target_pairs={{0,1},{1,2},{2,3},{4,5},{5,6},{6,7},{8,9},{9,10},{10,11},{12,13},{... | collective-permute-start | bytes 589832 | tf_op jit(solution)/shard_map/ppermute | solution.py:16
  11.7 19.5 %collective-permute-start.4 = (bf16[4,1,96,256]{3,2,1,0:T(8,128)(2,1)}, bf16[4,1,96,256]{3,2,1,0:T(8,128)(2,1)S(1)}, u32[]{:S(2)}, u32[]{:S(2)}) collective-permute-start(bf16[4,1,96,256]{3,2,1,0:T(8,128)(2,1)} %get-tuple-element.13), channel_id=1, source_target_pairs={{1,0},{2,1},{3,2},{5,4},{6,5},{7,6},{9,8},{10,9},{11,10},{13,12},{... | collective-permute-start | bytes 589832 | tf_op jit(solution)/shard_map/ppermute | solution.py:16
  14.3 13.0 %collective-permute-start = (bf16[2,1,96,256]{3,2,1,0:T(8,128)(2,1)}, bf16[2,1,96,256]{3,2,1,0:T(8,128)(2,1)}, u32[]{:S(2)}, u32[]{:S(2)}) collective-permute-start(bf16[2,1,96,256]{3,2,1,0:T(8,128)(2,1)} %get-tuple-element.10), channel_id=1, source_target_pairs={{0,5},{1,6},{2,7},{4,9},{5,10},{6,11},{8,13},{9,14},{10,15},{12,17... | collective-permute-start | bytes 294920 | tf_op jit(solution)/shard_map/ppermute | solution.py:26
  20.4 10.8 %collective-permute-start.2 = (bf16[2,1,96,256]{3,2,1,0:T(8,128)(2,1)}, bf16[2,1,96,256]{3,2,1,0:T(8,128)(2,1)}, u32[]{:S(2)}, u32[]{:S(2)}) collective-permute-start(bf16[2,1,96,256]{3,2,1,0:T(8,128)(2,1)} %get-tuple-element.11), channel_id=1, source_target_pairs={{1,4},{2,5},{3,6},{5,8},{6,9},{7,10},{9,12},{10,13},{11,14},{13,16... | collective-permute-start | bytes 294920 | tf_op jit(solution)/shard_map/ppermute | solution.py:26
  39.0 27.0 %copy-start.1 = (bf16[4,4,96,256]{3,2,1,0:T(8,128)(2,1)S(1)}, bf16[4,4,96,256]{3,2,1,0:T(8,128)(2,1)}, u32[]{:S(2)}) copy-start(bf16[4,4,96,256]{3,2,1,0:T(8,128)(2,1)} %shard_map.122) | copy-start | bytes 2359300
  40.1 25.9 %collective-permute-start.6 = (bf16[2,4,96,256]{3,2,1,0:T(8,128)(2,1)S(1)}, bf16[2,4,96,256]{3,2,1,0:T(8,128)(2,1)S(1)}, u32[]{:S(2)}, u32[]{:S(2)}) collective-permute-start(bf16[2,4,96,256]{3,2,1,0:T(8,128)(2,1)S(1)} %slice.60), channel_id=1, source_target_pairs={{0,4},{4,8},{8,12},{12,16},{16,20},{20,24},{24,28},{28,32},{32,36}... | collective-permute-start | bytes 1179656 | tf_op jit(solution)/shard_map/ppermute | solution.py:19
  43.1 22.9 %collective-permute-start.8 = (bf16[4,1,96,256]{3,2,1,0:T(8,128)(2,1)S(1)}, bf16[4,1,96,256]{3,2,1,0:T(8,128)(2,1)S(1)}, u32[]{:S(2)}, u32[]{:S(2)}) collective-permute-start(bf16[4,1,96,256]{3,2,1,0:T(8,128)(2,1)S(1)} %get-tuple-element.8), channel_id=1, source_target_pairs={{0,1},{1,2},{2,3},{4,5},{5,6},{6,7},{8,9},{9,10},{10,11},{12,13},{... | collective-permute-start | bytes 589832 | tf_op jit(solution)/shard_map/ppermute | solution.py:16
  46.5 19.4 %collective-permute-start.9 = (bf16[4,1,96,256]{3,2,1,0:T(8,128)(2,1)S(1)}, bf16[4,1,96,256]{3,2,1,0:T(8,128)(2,1)S(1)}, u32[]{:S(2)}, u32[]{:S(2)}) collective-permute-start(bf16[4,1,96,256]{3,2,1,0:T(8,128)(2,1)S(1)} %get-tuple-element.9), channel_id=1, source_target_pairs={{1,0},{2,1},{3,2},{5,4},{6,5},{7,6},{9,8},{10,9},{11,10},{13,12},{... | collective-permute-start | bytes 589832 | tf_op jit(solution)/shard_map/ppermute | solution.py:16
  49.4 8.0 %collective-permute-start.5 = (bf16[2,1,96,256]{3,2,1,0:T(8,128)(2,1)S(1)}, bf16[2,1,96,256]{3,2,1,0:T(8,128)(2,1)S(1)}, u32[]{:S(2)}, u32[]{:S(2)}) collective-permute-start(bf16[2,1,96,256]{3,2,1,0:T(8,128)(2,1)S(1)} %get-tuple-element.6), channel_id=1, source_target_pairs={{0,5},{1,6},{2,7},{4,9},{5,10},{6,11},{8,13},{9,14},{10,15},{12,17... | collective-permute-start | bytes 294920 | tf_op jit(solution)/shard_map/ppermute | solution.py:26
  55.5 10.4 %collective-permute-start.7 = (bf16[2,1,96,256]{3,2,1,0:T(8,128)(2,1)S(1)}, bf16[2,1,96,256]{3,2,1,0:T(8,128)(2,1)S(1)}, u32[]{:S(2)}, u32[]{:S(2)}) collective-permute-start(bf16[2,1,96,256]{3,2,1,0:T(8,128)(2,1)S(1)} %get-tuple-element.7), channel_id=1, source_target_pairs={{1,4},{2,5},{3,6},{5,8},{6,9},{7,10},{9,12},{10,13},{11,14},{13,16... | collective-permute-start | bytes 294920 | tf_op jit(solution)/shard_map/ppermute | solution.py:26
  67.4 11.7 %copy-start.4 = (bf16[3,3,3,96,96]{4,3,2,1,0:T(8,128)(2,1)S(1)}, bf16[3,3,3,96,96]{4,3,2,1,0:T(8,128)(2,1)}, u32[]{:S(2)}) copy-start(bf16[3,3,3,96,96]{4,3,2,1,0:T(8,128)(2,1)} %param.21) | copy-start | bytes 1492996
  73.3 7.5 %copy-start.6 = (bf16[3,3,3,96,16]{3,4,2,1,0:T(8,128)(2,1)S(1)}, bf16[3,3,3,96,16]{3,4,2,1,0:T(8,128)(2,1)}, u32[]{:S(2)}) copy-start(bf16[3,3,3,96,16]{3,4,2,1,0:T(8,128)(2,1)} %param.17) | copy-start | bytes 248836
  74.1 18.0 %collective-permute-start.19 = (bf16[2,16,256]{2,1,0:T(8,128)(2,1)S(1)}, bf16[2,16,256]{2,1,0:T(8,128)(2,1)S(1)}, u32[]{:S(2)}, u32[]{:S(2)}) collective-permute-start(bf16[2,16,256]{2,1,0:T(8,128)(2,1)S(1)} %get-tuple-element.14), channel_id=1, source_target_pairs={{0,1},{1,2},{2,3},{4,5},{5,6},{6,7},{8,9},{9,10},{10,11},{12,13},{... | collective-permute-start | bytes 49160 | tf_op jit(solution)/shard_map/ppermute | solution.py:16
  76.0 24.2 %collective-permute-start.20 = (bf16[2,16,256]{2,1,0:T(8,128)(2,1)S(1)}, bf16[2,16,256]{2,1,0:T(8,128)(2,1)S(1)}, u32[]{:S(2)}, u32[]{:S(2)}) collective-permute-start(bf16[2,16,256]{2,1,0:T(8,128)(2,1)S(1)} %get-tuple-element.15), channel_id=1, source_target_pairs={{1,0},{2,1},{3,2},{5,4},{6,5},{7,6},{9,8},{10,9},{11,10},{13,12},{... | collective-permute-start | bytes 49160 | tf_op jit(solution)/shard_map/ppermute | solution.py:16
  79.1 2.8 %copy-start.9 = (f32[96]{0:T(128)S(1)}, f32[96]{0:T(128)}, u32[]{:S(2)}) copy-start(f32[96]{0:T(128)} %param.18) | copy-start | bytes 1156
  79.1 3.5 %copy-start.10 = (f32[96]{0:T(128)S(1)}, f32[96]{0:T(128)}, u32[]{:S(2)}) copy-start(f32[96]{0:T(128)} %param.19) | copy-start | bytes 1156
  79.1 9.4 %copy-start.5 = (bf16[4,16,256]{2,1,0:T(8,128)(2,1)S(1)}, bf16[4,16,256]{2,1,0:T(8,128)(2,1)}, u32[]{:S(2)}) copy-start(bf16[4,16,256]{2,1,0:T(8,128)(2,1)} %shard_map.123) | copy-start | bytes 98308
  83.3 18.9 %collective-permute-start.10 = (bf16[2,16,256]{2,1,0:T(8,128)(2,1)S(1)}, bf16[2,16,256]{2,1,0:T(8,128)(2,1)S(1)}, u32[]{:S(2)}, u32[]{:S(2)}) collective-permute-start(bf16[2,16,256]{2,1,0:T(8,128)(2,1)S(1)} %get-tuple-element.14), channel_id=1, source_target_pairs={{0,13},{1,14},{2,15},{4,17},{5,18},{6,19},{8,21},{9,22},{10,23},{1... | collective-permute-start | bytes 49160 | tf_op jit(solution)/shard_map/ppermute | solution.py:26
  86.6 19.3 %collective-permute-start.12 = (bf16[2,16,256]{2,1,0:T(8,128)(2,1)S(1)}, bf16[2,16,256]{2,1,0:T(8,128)(2,1)S(1)}, u32[]{:S(2)}, u32[]{:S(2)}) collective-permute-start(bf16[2,16,256]{2,1,0:T(8,128)(2,1)S(1)} %get-tuple-element.15), channel_id=1, source_target_pairs={{1,12},{2,13},{3,14},{5,16},{6,17},{7,18},{9,20},{10,21},{11,22},{... | collective-permute-start | bytes 49160 | tf_op jit(solution)/shard_map/ppermute | solution.py:26
  88.5 27.5 %collective-permute-start.11 = (bf16[4,16,256]{2,1,0:T(8,128)(2,1)S(1)}, bf16[4,16,256]{2,1,0:T(8,128)(2,1)S(1)}, u32[]{:S(2)}, u32[]{:S(2)}) collective-permute-start(bf16[4,16,256]{2,1,0:T(8,128)(2,1)S(1)} %copy-done.5), channel_id=1, source_target_pairs={{0,12},{4,16},{8,20},{12,24},{16,28},{20,32},{24,36},{28,40},{32,4... | collective-permute-start | bytes 98312 | tf_op jit(solution)/shard_map/ppermute | solution.py:19
  92.1 25.8 %collective-permute-start.13 = (bf16[2,16,256]{2,1,0:T(8,128)(2,1)S(1)}, bf16[2,16,256]{2,1,0:T(8,128)(2,1)S(1)}, u32[]{:S(2)}, u32[]{:S(2)}) collective-permute-start(bf16[2,16,256]{2,1,0:T(8,128)(2,1)S(1)} %get-tuple-element.14), channel_id=1, source_target_pairs={{0,9},{1,10},{2,11},{4,13},{5,14},{6,15},{8,17},{9,18},{10,19},{12... | collective-permute-start | bytes 49160 | tf_op jit(solution)/shard_map/ppermute | solution.py:26
  100.2 19.9 %collective-permute-start.15 = (bf16[2,16,256]{2,1,0:T(8,128)(2,1)S(1)}, bf16[2,16,256]{2,1,0:T(8,128)(2,1)S(1)}, u32[]{:S(2)}, u32[]{:S(2)}) collective-permute-start(bf16[2,16,256]{2,1,0:T(8,128)(2,1)S(1)} %get-tuple-element.15), channel_id=1, source_target_pairs={{1,8},{2,9},{3,10},{5,12},{6,13},{7,14},{9,16},{10,17},{11,18},{13... | collective-permute-start | bytes 49160 | tf_op jit(solution)/shard_map/ppermute | solution.py:26
  102.2 17.9 %collective-permute-start.14 = (bf16[4,16,256]{2,1,0:T(8,128)(2,1)S(1)}, bf16[4,16,256]{2,1,0:T(8,128)(2,1)S(1)}, u32[]{:S(2)}, u32[]{:S(2)}) collective-permute-start(bf16[4,16,256]{2,1,0:T(8,128)(2,1)S(1)} %copy-done.5), channel_id=1, source_target_pairs={{0,8},{4,12},{8,16},{12,20},{16,24},{20,28},{24,32},{28,36},{32,40... | collective-permute-start | bytes 98312 | tf_op jit(solution)/shard_map/ppermute | solution.py:19
  105.9 14.2 %collective-permute-start.16 = (bf16[2,16,256]{2,1,0:T(8,128)(2,1)S(1)}, bf16[2,16,256]{2,1,0:T(8,128)(2,1)S(1)}, u32[]{:S(2)}, u32[]{:S(2)}) collective-permute-start(bf16[2,16,256]{2,1,0:T(8,128)(2,1)S(1)} %get-tuple-element.14), channel_id=1, source_target_pairs={{0,5},{1,6},{2,7},{4,9},{5,10},{6,11},{8,13},{9,14},{10,15},{12,17... | collective-permute-start | bytes 49160 | tf_op jit(solution)/shard_map/ppermute | solution.py:26
  116.0 9.6 %collective-permute-start.18 = (bf16[2,16,256]{2,1,0:T(8,128)(2,1)S(1)}, bf16[2,16,256]{2,1,0:T(8,128)(2,1)S(1)}, u32[]{:S(2)}, u32[]{:S(2)}) collective-permute-start(bf16[2,16,256]{2,1,0:T(8,128)(2,1)S(1)} %get-tuple-element.15), channel_id=1, source_target_pairs={{1,4},{2,5},{3,6},{5,8},{6,9},{7,10},{9,12},{10,13},{11,14},{13,16... | collective-permute-start | bytes 49160 | tf_op jit(solution)/shard_map/ppermute | solution.py:26
  118.0 7.6 %collective-permute-start.17 = (bf16[4,16,256]{2,1,0:T(8,128)(2,1)S(1)}, bf16[4,16,256]{2,1,0:T(8,128)(2,1)S(1)}, u32[]{:S(2)}, u32[]{:S(2)}) collective-permute-start(bf16[4,16,256]{2,1,0:T(8,128)(2,1)S(1)} %copy-done.5), channel_id=1, source_target_pairs={{0,4},{4,8},{8,12},{12,16},{16,20},{20,24},{24,28},{28,32},{32,36}... | collective-permute-start | bytes 98312 | tf_op jit(solution)/shard_map/ppermute | solution.py:19

commit v2 on v1

--- a/solution.py
+++ b/solution.py
@@ -26,17 +26,6 @@
     return lax.ppermute(x, ("tm", "rows"), pairs)
 
 
-def haloed_rows_first(v):
-    prev = shift(v[-2:], 1, 0)
-    top = shift(v[:, -1:], 0, 1)
-    bottom = shift(v[:, :1], 0, -1)
-    top_corner = shift(v[-2:, -1:], 1, 1)
-    bottom_corner = shift(v[-2:, :1], 1, -1)
-    own = jnp.concatenate([top, v, bottom], 1)
-    before = jnp.concatenate([top_corner, prev, bottom_corner], 1)
-    return jnp.concatenate([before, own], 0)
-
-
 def merged_kernel(kernel):
     o, c = kernel.shape[3], kernel.shape[4]
     return kernel.transpose(2, 3, 0, 1, 4).reshape(3 * o, 9 * c)
@@ -61,23 +50,25 @@
     return left + acc[out_channels : 2 * out_channels] + right
 
 
-def gate_kernel(x_ref, k_ref, bias_ref, gain_ref, o_ref, *, frames, rows, columns):
+def encoder_kernel(
+    x_ref, k1_ref, bias_ref, gain_ref, mask_ref, k2_ref, w_ref, o_ref, g_ref,
+    *, frames, rows, columns
+):
+    wide = rows + 2
     bias = bias_ref[...]
     gain = gain_ref[...]
-    for t in range(frames):
-        y = tap_sum(x_ref, k_ref, t, rows, columns) + bias
+    for t in range(frames + 2):
+        y = tap_sum(x_ref, k1_ref, t, wide, columns) + bias
         scale = lax.rsqrt(jnp.mean(y * y, axis=0, keepdims=True) + 1e-06)
         z = y * scale * gain
-        g = (z / (1.0 + jnp.exp(-z))).astype(o_ref.dtype)
-        for r in range(rows):
-            o_ref[t, r] = g[:, r * columns : (r + 1) * columns]
-
-
-def latent_kernel(x_ref, k_ref, res_ref, w_ref, o_ref, *, frames, rows, columns):
+        g = z / (1.0 + jnp.exp(-z))
+        for r in range(wide):
+            piece = g[:, r * columns : (r + 1) * columns] * mask_ref[t, r]
+            g_ref[t, r] = piece.astype(g_ref.dtype)
     total = None
     for t in range(frames):
-        y = tap_sum(x_ref, k_ref, t, rows, columns)
-        res = jnp.concatenate([res_ref[t, r] for r in range(rows)], axis=1)
+        y = tap_sum(g_ref, k2_ref, t, rows, columns)
+        res = jnp.concatenate([x_ref[t + 4, r + 2] for r in range(rows)], axis=1)
         hidden = (res.astype(jnp.float32) + y).astype(jnp.bfloat16)
         part = jnp.dot(w_ref[t], hidden, preferred_element_type=jnp.float32)
         total = part if total is None else total + part
@@ -110,23 +101,6 @@
         o_ref[t] = (res.astype(jnp.float32) + y).astype(o_ref.dtype)
 
 
-def normed_silu(values, gain):
-    scale = lax.rsqrt(jnp.mean(values * values, axis=1, keepdims=True) + 1e-06)
-    return jax.nn.silu(values * scale * gain[None, :, None, None])
-
-
-def conv_valid(v, kernel):
-    out = lax.conv_general_dilated(
-        v[None],
-        kernel,
-        (1, 1, 1),
-        [(0, 0), (0, 0), (1, 1)],
-        dimension_numbers=("NDCHW", "DHWOI", "NDCHW"),
-        preferred_element_type=jnp.float32,
-    )
-    return out[0]
-
-
 def body(
     features,
     first_kernel,
@@ -144,27 +118,10 @@
     z_count = latent_weight.shape[1]
     dims = dict(frames=frames, rows=rows, columns=columns)
     own = features.transpose(0, 2, 1, 3)
-    gated = pl.pallas_call(
-        functools.partial(gate_kernel, **dims),
-        out_shape=jax.ShapeDtypeStruct((frames, rows, channels, columns), jnp.bfloat16),
-    )(
-        haloed_rows_first(own),
-        merged_kernel(first_kernel),
-        first_bias[:, None],
-        first_gain[:, None],
-    )
-    lat = pl.pallas_call(
-        functools.partial(latent_kernel, **dims),
-        out_shape=jax.ShapeDtypeStruct((rows, z_count, columns), jnp.bfloat16),
-    )(haloed_rows_first(gated), merged_kernel(second_kernel), own, latent_weight)
-    latent = lat.transpose(1, 0, 2)[None]
-    stacked = jnp.stack(
+    ext = jnp.concatenate(
         [
-            jnp.concatenate(
-                [shift(lat[-2:], dt, 1), lat if dt == 0 else shift(lat, dt, 0), shift(lat[:2], dt, -1)],
-                0,
-            )
-            for dt in (3, 2, 1, 0)
+            jnp.concatenate([shift(own[:, -2:], 1, 1), shift(own, 1, 0), shift(own[:, :2], 1, -1)], 1),
+            jnp.concatenate([shift(own[:, -2:], 0, 1), own, shift(own[:, :2], 0, -1)], 1),
         ],
         0,
     )
@@ -176,10 +133,30 @@
     inside = inside & ((frame_ids >= 2) | (lax.axis_index("tm") > 0))
     mask = inside.astype(jnp.float32)
     vmem = pl.BlockSpec(memory_space=pltpu.VMEM)
+    smem = pl.BlockSpec(memory_space=pltpu.SMEM)
+    lat = pl.pallas_call(
+        functools.partial(encoder_kernel, **dims),
+        out_shape=jax.ShapeDtypeStruct((rows, z_count, columns), jnp.bfloat16),
+        in_specs=[vmem] * 4 + [smem, vmem, vmem],
+        scratch_shapes=[pltpu.VMEM((frames + 2, rows + 2, channels, columns), jnp.bfloat16)],
+    )(
+        ext,
+        merged_kernel(first_kernel),
+        first_bias[:, None],
+        first_gain[:, None],
+        mask,
+        merged_kernel(second_kernel),
+        latent_weight,
+    )
+    latent = lat.transpose(1, 0, 2)[None]
+    lat_rows = jnp.concatenate([shift(lat[-2:], 0, 1), lat, shift(lat[:2], 0, -1)], 0)
+    stacked = jnp.stack(
+        [shift(lat_rows, 3, 0), shift(lat_rows, 2, 0), shift(lat_rows, 1, 0), lat_rows], 0
+    )
     rebuilt_flat = pl.pallas_call(
         functools.partial(decode_kernel_body, **dims),
         out_shape=jax.ShapeDtypeStruct((frames, channels, rows * columns), jnp.bfloat16),
-        in_specs=[vmem] * 5 + [pl.BlockSpec(memory_space=pltpu.SMEM), vmem],
+        in_specs=[vmem] * 5 + [smem, vmem],
         scratch_shapes=[pltpu.VMEM((frames + 2, rows + 2, channels, columns), jnp.bfloat16)],
     )(
         stacked,

time: 136 us -> 96.1 us (0.71)
  the two profiles are of different devices: /device:TPU:65 before, /device:TPU:37 now
where the time goes in v2:
time: 96.1 us; the launch traced here: 95.5 us
  starting transfers between devices  41.3 us (43%)
  Pallas kernels  18.5 us (19%)
  local copies, waits for them, and re-layouts  16.5 us (17%)
  waiting for transfers between devices  13.2 us (14%)
  other arithmetic  5.15 us (5%)
    ppermute x4, starting transfers between devices, shift(): return lax.ppermute(x, 'tm', pairs)  20 us
    ppermute x4, starting transfers between devices, shift(): return lax.ppermute(x, 'rows', pairs)  12.3 us
    pallas_call x1, Pallas kernels, body(): pl.pallas_call(functools.partial(encoder_kernel, **dims), out_shape=jax.S...  11.9 us
    ppermute x2, waiting for transfers between devices, shift(): return lax.ppermute(x, ('tm', 'rows'), pairs)  9.03 us
    ppermute x2, starting transfers between devices, shift(): return lax.ppermute(x, ('tm', 'rows'), pairs)  8.97 us
    pallas_call x1, Pallas kernels, body(): pl.pallas_call(functools.partial(decode_kernel_body, **dims), out_shape=j...  6.59 us
    reshape x5, local copies, waits for them, and re-layouts, merged_kernel(): return kernel.transpose(2, 3, 0, 1, 4).reshape(3 * o, 9 * c)  4.79 us
    ppermute x4, waiting for transfers between devices, shift(): return lax.ppermute(x, 'rows', pairs)  4.15 us
  transfers between devices with their start and end apart: 10, of which 3 were waited for; matrix products, arithmetic and copies ran while one was open for 13% of the time, Pallas kernels for 0%

profile of v2, /device:TPU:37, one launch (start us, length us, event | category | flops | bytes accessed | tf_op | source)
XLA Modules:
  0.0 95.5 jit_solution(5775359816263728127)
XLA Ops:
  0.6 0.0 copy-start
  0.6 1.3 %copy.35 = bf16[4,96,4,256]{3,1,2,0:T(8,128)(2,1)S(1)} copy(bf16[4,96,4,256]{3,2,1,0:T(4,128)(2,1)} %param.11) | data formatting | bytes 1572864 | tf_op args[0]
  2.0 2.8 %collective-permute-start.1 = (bf16[4,4,96,256]{3,2,1,0:T(8,128)(2,1)S(1)}, bf16[4,4,96,256]{3,2,1,0:T(8,128)(2,1)S(1)}, u32[]{:S(2)}, u32[]{:S(2)}) collective-permute-start(bf16[4,4,96,256]{3,2,1,0:T(8,128)(2,1)S(1)} %bitcast.21), channel_id=1, source_target_pairs={{0,4},{4,8},{8,12},{12,16},{16,20},{20,24},{24,28},{28,32},{32,36}... | collective-permute-start | bytes 2359304 | tf_op jit(solution)/shard_map/ppermute | solution.py:19
  4.8 0.9 fusion.1
  5.7 0.0 copy-start.4
  5.8 0.0 copy-start.5
  5.8 7.1 %collective-permute-start = (bf16[4,2,96,256]{3,2,1,0:T(8,128)(2,1)}, bf16[4,2,96,256]{3,2,1,0:T(8,128)(2,1)S(1)}, u32[]{:S(2)}, u32[]{:S(2)}) collective-permute-start(bf16[4,2,96,256]{3,2,1,0:T(8,128)(2,1)} %get-tuple-element.6), channel_id=1, source_target_pairs={{0,5},{1,6},{2,7},{4,9},{5,10},{6,11},{8,13},{9,14},{10,15},{12,17... | collective-permute-start | bytes 1179656 | tf_op jit(solution)/shard_map/ppermute | solution.py:26
  12.8 1.9 %collective-permute-start.2 = (bf16[4,2,96,256]{3,2,1,0:T(8,128)(2,1)}, bf16[4,2,96,256]{3,2,1,0:T(8,128)(2,1)}, u32[]{:S(2)}, u32[]{:S(2)}) collective-permute-start(bf16[4,2,96,256]{3,2,1,0:T(8,128)(2,1)} %get-tuple-element.7), channel_id=1, source_target_pairs={{1,4},{2,5},{3,6},{5,8},{6,9},{7,10},{9,12},{10,13},{11,14},{13,16... | collective-permute-start | bytes 1179656 | tf_op jit(solution)/shard_map/ppermute | solution.py:26
  14.7 6.1 %collective-permute-start.3 = (bf16[4,2,96,256]{3,2,1,0:T(8,128)(2,1)}, bf16[4,2,96,256]{3,2,1,0:T(8,128)(2,1)}, u32[]{:S(2)}, u32[]{:S(2)}) collective-permute-start(bf16[4,2,96,256]{3,2,1,0:T(8,128)(2,1)} %get-tuple-element.6), channel_id=1, source_target_pairs={{0,1},{1,2},{2,3},{4,5},{5,6},{6,7},{8,9},{9,10},{10,11},{12,13},{... | collective-permute-start | bytes 1179656 | tf_op jit(solution)/shard_map/ppermute | solution.py:16
  20.8 1.9 %collective-permute-start.4 = (bf16[4,2,96,256]{3,2,1,0:T(8,128)(2,1)}, bf16[4,2,96,256]{3,2,1,0:T(8,128)(2,1)}, u32[]{:S(2)}, u32[]{:S(2)}) collective-permute-start(bf16[4,2,96,256]{3,2,1,0:T(8,128)(2,1)} %get-tuple-element.7), channel_id=1, source_target_pairs={{1,0},{2,1},{3,2},{5,4},{6,5},{7,6},{9,8},{10,9},{11,10},{13,12},{... | collective-permute-start | bytes 1179656 | tf_op jit(solution)/shard_map/ppermute | solution.py:16
  22.8 0.0 copy-done
  22.8 0.5 copy.24
  23.2 1.3 %reshape.19.k1_ref = bf16[288,864]{1,0:T(8,128)(2,1)} reshape(bf16[3,96,3,3,96]{4,3,2,1,0:T(4,128)(2,1)S(1)} %copy.24) | data formatting | bytes 995328 | tf_op jit(solution)/shard_map/reshape | solution.py:31
  24.5 1.5 %copy.25 = bf16[3,96,3,3,96]{4,3,2,1,0:T(4,128)(2,1)S(1)} copy(bf16[3,96,3,3,96]{4,1,0,3,2:T(8,128)(2,1)} %bitcast.25) | data formatting | bytes 995328 | tf_op jit(solution)/shard_map/transpose | solution.py:31
  26.1 1.3 %reshape.20.k2_ref = bf16[288,864]{1,0:T(8,128)(2,1)} reshape(bf16[3,96,3,3,96]{4,3,2,1,0:T(4,128)(2,1)S(1)} %copy.25) | data formatting | bytes 995328 | tf_op jit(solution)/shard_map/reshape | solution.py:31
  27.4 0.0 copy-done.4
  27.4 0.7 copy.26.bias_ref
  28.1 0.0 copy-done.5
  28.1 0.7 copy.27.gain_ref
  28.8 0.7 and_convert_fusion.mask_ref
  29.5 3.6 %collective-permute-done = bf16[4,2,96,256]{3,2,1,0:T(8,128)(2,1)S(1)} collective-permute-done((bf16[4,2,96,256]{3,2,1,0:T(8,128)(2,1)}, bf16[4,2,96,256]{3,2,1,0:T(8,128)(2,1)S(1)}, u32[]{:S(2)}, u32[]{:S(2)}) %collective-permute-start) | collective-permute-done | bytes 393248 | tf_op jit(solution)/shard_map/ppermute | solution.py:26
  33.1 5.4 %collective-permute-done.2 = bf16[4,2,96,256]{3,2,1,0:T(8,128)(2,1)} collective-permute-done((bf16[4,2,96,256]{3,2,1,0:T(8,128)(2,1)}, bf16[4,2,96,256]{3,2,1,0:T(8,128)(2,1)}, u32[]{:S(2)}, u32[]{:S(2)}) %collective-permute-start.2) | collective-permute-done | bytes 393248 | tf_op jit(solution)/shard_map/ppermute | solution.py:26
  38.5 0.0 collective-permute-done.3
  38.5 0.0 collective-permute-done.4
  38.5 0.0 collective-permute-done.1
  38.5 3.0 %maximum_maximum_fusion.x_ref = bf16[8,8,96,256]{3,2,1,0:T(8,128)(2,1)} fusion(bf16[4,2,96,256]{3,2,1,0:T(8,128)(2,1)} %collective-permute-done.4, bf16[4,4,96,256]{3,2,1,0:T(8,128)(2,1)S(1)} %bitcast.23, bf16[4,2,96,256]{3,2,1,0:T(8,128)(2,1)} %collective-permute-done.3, bf16[4,2,96,256]{3,2,1,0:T(8,128)(2,1)} %collective-permute-done.2, ...), kind=kLoop, calls=%fused_computation | loop fusion | flops 7864320 | bytes 6291456 | tf_op jit(solution)/shard_map/concatenate | solution.py:121
  41.5 0.0 copy-start.1
  41.5 0.0 copy-start.3
  41.5 0.0 copy-start.6
  41.5 0.0 copy-start.7
  41.5 11.9 %shard_map.122 = bf16[4,16,256]{2,1,0:T(8,128)(2,1)} custom-call(bf16[8,8,96,256]{3,2,1,0:T(8,128)(2,1)} %maximum_maximum_fusion.x_ref, bf16[288,864]{1,0:T(8,128)(2,1)} %reshape.19.k1_ref, f32[96,1]{1,0:T(8,128)} %copy.26.bias_ref, f32[96,1]{1,0:T(8,128)} %copy.27.gain_ref, f32[6,6]{1,0:T(8,128)} %and_convert_fusion.mask_ref, ...), custom_call_target="tpu_custom_call" | custom-call | tf_op jit(solution)/shard_map/pallas_call | solution.py:137
  53.4 0.0 copy-start.2
  53.5 0.8 fusion.2
  54.2 1.9 %collective-permute-start.5 = (bf16[2,16,256]{2,1,0:T(8,128)(2,1)S(1)}, bf16[2,16,256]{2,1,0:T(8,128)(2,1)S(1)}, u32[]{:S(2)}, u32[]{:S(2)}) collective-permute-start(bf16[2,16,256]{2,1,0:T(8,128)(2,1)S(1)} %get-tuple-element.10), channel_id=1, source_target_pairs={{0,1},{1,2},{2,3},{4,5},{5,6},{6,7},{8,9},{9,10},{10,11},{12,13},{... | collective-permute-start | bytes 49160 | tf_op jit(solution)/shard_map/ppermute | solution.py:16
  56.2 2.4 %collective-permute-start.6 = (bf16[2,16,256]{2,1,0:T(8,128)(2,1)S(1)}, bf16[2,16,256]{2,1,0:T(8,128)(2,1)S(1)}, u32[]{:S(2)}, u32[]{:S(2)}) collective-permute-start(bf16[2,16,256]{2,1,0:T(8,128)(2,1)S(1)} %get-tuple-element.11), channel_id=1, source_target_pairs={{1,0},{2,1},{3,2},{5,4},{6,5},{7,6},{9,8},{10,9},{11,10},{13,12},{... | collective-permute-start | bytes 49160 | tf_op jit(solution)/shard_map/ppermute | solution.py:16
  58.6 0.0 collective-permute-done.5
  58.6 4.1 %collective-permute-done.6 = bf16[2,16,256]{2,1,0:T(8,128)(2,1)S(1)} collective-permute-done((bf16[2,16,256]{2,1,0:T(8,128)(2,1)S(1)}, bf16[2,16,256]{2,1,0:T(8,128)(2,1)S(1)}, u32[]{:S(2)}, u32[]{:S(2)}) %collective-permute-start.6) | collective-permute-done | bytes 16416 | tf_op jit(solution)/shard_map/ppermute | solution.py:16
  62.7 0.8 pad_maximum_fusion.1
  63.5 3.5 %collective-permute-start.7 = (bf16[8,16,256]{2,1,0:T(8,128)(2,1)S(1)}, bf16[8,16,256]{2,1,0:T(8,128)(2,1)S(1)}, u32[]{:S(2)}, u32[]{:S(2)}) collective-permute-start(bf16[8,16,256]{2,1,0:T(8,128)(2,1)S(1)} %get-tuple-element.8), channel_id=1, source_target_pairs={{0,12},{4,16},{8,20},{12,24},{16,28},{20,32},{24,36},{28,40},{32,4... | collective-permute-start | bytes 196616 | tf_op jit(solution)/shard_map/ppermute | solution.py:19
  67.0 8.4 %collective-permute-start.8 = (bf16[8,16,256]{2,1,0:T(8,128)(2,1)S(1)}, bf16[8,16,256]{2,1,0:T(8,128)(2,1)S(1)}, u32[]{:S(2)}, u32[]{:S(2)}) collective-permute-start(bf16[8,16,256]{2,1,0:T(8,128)(2,1)S(1)} %get-tuple-element.8), channel_id=1, source_target_pairs={{0,8},{4,12},{8,16},{12,20},{16,24},{20,28},{24,32},{28,36},{32,40... | collective-permute-start | bytes 196616 | tf_op jit(solution)/shard_map/ppermute | solution.py:19
  75.4 5.2 %collective-permute-start.9 = (bf16[8,16,256]{2,1,0:T(8,128)(2,1)S(1)}, bf16[8,16,256]{2,1,0:T(8,128)(2,1)S(1)}, u32[]{:S(2)}, u32[]{:S(2)}) collective-permute-start(bf16[8,16,256]{2,1,0:T(8,128)(2,1)S(1)} %get-tuple-element.8), channel_id=1, source_target_pairs={{0,4},{4,8},{8,12},{12,16},{16,20},{20,24},{24,28},{28,32},{32,36}... | collective-permute-start | bytes 196616 | tf_op jit(solution)/shard_map/ppermute | solution.py:19
  80.7 0.0 copy-done.1
  80.7 0.5 copy.29
  81.2 1.3 %reshape.22.fk_ref = bf16[288,864]{1,0:T(8,128)(2,1)} reshape(bf16[3,96,3,3,96]{4,3,2,1,0:T(4,128)(2,1)S(1)} %copy.29) | data formatting | bytes 995328 | tf_op jit(solution)/shard_map/reshape | solution.py:31
  82.5 0.0 copy-done.3
  82.5 0.1 copy.28
  82.5 0.1 reshape.21
  82.7 0.8 copy.30.dk_ref
  83.5 0.0 copy-done.6
  83.5 0.7 copy.31.bias_ref
  84.2 0.0 copy-done.7
  84.2 0.7 copy.32.gain_ref
  84.9 0.0 copy-done.2
  84.9 0.6 copy.33
  85.5 0.0 collective-permute-done.7
  85.5 0.0 collective-permute-done.8
  85.5 0.0 collective-permute-done.9
  85.5 0.7 pad_maximum_fusion.lat_ref
  86.3 6.6 %shard_map.123 = bf16[4,96,1024]{2,1,0:T(8,128)(2,1)} custom-call(bf16[4,8,16,256]{3,2,1,0:T(8,128)(2,1)} %pad_maximum_fusion.lat_ref, bf16[288,144]{1,0:T(8,128)(2,1)} %copy.30.dk_ref, f32[96,1]{1,0:T(8,128)} %copy.31.bias_ref, f32[96,1]{1,0:T(8,128)} %copy.32.gain_ref, bf16[4,96,96]{2,1,0:T(8,128)(2,1)} %up_ref.1, f32[6,6]{1,0:T(8,128)} %and_convert_fusion.mask_ref, ...), custom_call_target="tpu_custom_call" | custom-call | tf_op jit(solution)/shard_map/pallas_call | solution.py:156
  92.9 2.6 %reshape.23 = bf16[4,96,4,256]{3,2,1,0:T(4,128)(2,1)} reshape(bf16[4,96,1024]{2,1,0:T(8,128)(2,1)} %shard_map.123) | data formatting | bytes 1572864 | tf_op jit(solution)/shard_map/reshape | solution.py:170
  (1 shorter events, 0.0 us)
Async XLA Ops:
  0.6 22.1 %copy-start = (bf16[3,3,3,96,96]{4,3,2,1,0:T(8,128)(2,1)S(1)}, bf16[3,3,3,96,96]{4,3,2,1,0:T(8,128)(2,1)}, u32[]{:S(2)}) copy-start(bf16[3,3,3,96,96]{4,3,2,1,0:T(8,128)(2,1)} %param.12) | copy-start | bytes 1492996
  2.0 36.5 %collective-permute-start.1 = (bf16[4,4,96,256]{3,2,1,0:T(8,128)(2,1)S(1)}, bf16[4,4,96,256]{3,2,1,0:T(8,128)(2,1)S(1)}, u32[]{:S(2)}, u32[]{:S(2)}) collective-permute-start(bf16[4,4,96,256]{3,2,1,0:T(8,128)(2,1)S(1)} %bitcast.21), channel_id=1, source_target_pairs={{0,4},{4,8},{8,12},{12,16},{16,20},{20,24},{24,28},{28,32},{32,36}... | collective-permute-start | bytes 2359304 | tf_op jit(solution)/shard_map/ppermute | solution.py:19
  5.7 21.6 %copy-start.4 = (f32[96]{0:T(128)S(1)}, f32[96]{0:T(128)}, u32[]{:S(2)}) copy-start(f32[96]{0:T(128)} %param.13) | copy-start | bytes 1156
  5.8 22.3 %copy-start.5 = (f32[96]{0:T(128)S(1)}, f32[96]{0:T(128)}, u32[]{:S(2)}) copy-start(f32[96]{0:T(128)} %param.14) | copy-start | bytes 1156
  5.8 27.3 %collective-permute-start = (bf16[4,2,96,256]{3,2,1,0:T(8,128)(2,1)}, bf16[4,2,96,256]{3,2,1,0:T(8,128)(2,1)S(1)}, u32[]{:S(2)}, u32[]{:S(2)}) collective-permute-start(bf16[4,2,96,256]{3,2,1,0:T(8,128)(2,1)} %get-tuple-element.6), channel_id=1, source_target_pairs={{0,5},{1,6},{2,7},{4,9},{5,10},{6,11},{8,13},{9,14},{10,15},{12,17... | collective-permute-start | bytes 1179656 | tf_op jit(solution)/shard_map/ppermute | solution.py:26
  12.8 25.7 %collective-permute-start.2 = (bf16[4,2,96,256]{3,2,1,0:T(8,128)(2,1)}, bf16[4,2,96,256]{3,2,1,0:T(8,128)(2,1)}, u32[]{:S(2)}, u32[]{:S(2)}) collective-permute-start(bf16[4,2,96,256]{3,2,1,0:T(8,128)(2,1)} %get-tuple-element.7), channel_id=1, source_target_pairs={{1,4},{2,5},{3,6},{5,8},{6,9},{7,10},{9,12},{10,13},{11,14},{13,16... | collective-permute-start | bytes 1179656 | tf_op jit(solution)/shard_map/ppermute | solution.py:26
  14.7 23.8 %collective-permute-start.3 = (bf16[4,2,96,256]{3,2,1,0:T(8,128)(2,1)}, bf16[4,2,96,256]{3,2,1,0:T(8,128)(2,1)}, u32[]{:S(2)}, u32[]{:S(2)}) collective-permute-start(bf16[4,2,96,256]{3,2,1,0:T(8,128)(2,1)} %get-tuple-element.6), channel_id=1, source_target_pairs={{0,1},{1,2},{2,3},{4,5},{5,6},{6,7},{8,9},{9,10},{10,11},{12,13},{... | collective-permute-start | bytes 1179656 | tf_op jit(solution)/shard_map/ppermute | solution.py:16
  20.8 17.7 %collective-permute-start.4 = (bf16[4,2,96,256]{3,2,1,0:T(8,128)(2,1)}, bf16[4,2,96,256]{3,2,1,0:T(8,128)(2,1)}, u32[]{:S(2)}, u32[]{:S(2)}) collective-permute-start(bf16[4,2,96,256]{3,2,1,0:T(8,128)(2,1)} %get-tuple-element.7), channel_id=1, source_target_pairs={{1,0},{2,1},{3,2},{5,4},{6,5},{7,6},{9,8},{10,9},{11,10},{13,12},{... | collective-permute-start | bytes 1179656 | tf_op jit(solution)/shard_map/ppermute | solution.py:16
  41.5 39.2 %copy-start.1 = (bf16[3,3,3,96,96]{4,3,2,1,0:T(8,128)(2,1)S(1)}, bf16[3,3,3,96,96]{4,3,2,1,0:T(8,128)(2,1)}, u32[]{:S(2)}) copy-start(bf16[3,3,3,96,96]{4,3,2,1,0:T(8,128)(2,1)} %param.21) | copy-start | bytes 1492996
  41.5 41.0 %copy-start.3 = (bf16[3,3,3,96,16]{3,4,2,1,0:T(8,128)(2,1)S(1)}, bf16[3,3,3,96,16]{3,4,2,1,0:T(8,128)(2,1)}, u32[]{:S(2)}) copy-start(bf16[3,3,3,96,16]{3,4,2,1,0:T(8,128)(2,1)} %param.17) | copy-start | bytes 248836
  41.5 42.0 %copy-start.6 = (f32[96]{0:T(128)S(1)}, f32[96]{0:T(128)}, u32[]{:S(2)}) copy-start(f32[96]{0:T(128)} %param.18) | copy-start | bytes 1156
  41.5 42.7 %copy-start.7 = (f32[96]{0:T(128)S(1)}, f32[96]{0:T(128)}, u32[]{:S(2)}) copy-start(f32[96]{0:T(128)} %param.19) | copy-start | bytes 1156
  53.4 31.4 %copy-start.2 = (bf16[4,16,256]{2,1,0:T(8,128)(2,1)S(1)}, bf16[4,16,256]{2,1,0:T(8,128)(2,1)}, u32[]{:S(2)}) copy-start(bf16[4,16,256]{2,1,0:T(8,128)(2,1)} %shard_map.122) | copy-start | bytes 98308
  54.2 4.3 %collective-permute-start.5 = (bf16[2,16,256]{2,1,0:T(8,128)(2,1)S(1)}, bf16[2,16,256]{2,1,0:T(8,128)(2,1)S(1)}, u32[]{:S(2)}, u32[]{:S(2)}) collective-permute-start(bf16[2,16,256]{2,1,0:T(8,128)(2,1)S(1)} %get-tuple-element.10), channel_id=1, source_target_pairs={{0,1},{1,2},{2,3},{4,5},{5,6},{6,7},{8,9},{9,10},{10,11},{12,13},{... | collective-permute-start | bytes 49160 | tf_op jit(solution)/shard_map/ppermute | solution.py:16
  56.2 6.6 %collective-permute-start.6 = (bf16[2,16,256]{2,1,0:T(8,128)(2,1)S(1)}, bf16[2,16,256]{2,1,0:T(8,128)(2,1)S(1)}, u32[]{:S(2)}, u32[]{:S(2)}) collective-permute-start(bf16[2,16,256]{2,1,0:T(8,128)(2,1)S(1)} %get-tuple-element.11), channel_id=1, source_target_pairs={{1,0},{2,1},{3,2},{5,4},{6,5},{7,6},{9,8},{10,9},{11,10},{13,12},{... | collective-permute-start | bytes 49160 | tf_op jit(solution)/shard_map/ppermute | solution.py:16
  63.5 22.0 %collective-permute-start.7 = (bf16[8,16,256]{2,1,0:T(8,128)(2,1)S(1)}, bf16[8,16,256]{2,1,0:T(8,128)(2,1)S(1)}, u32[]{:S(2)}, u32[]{:S(2)}) collective-permute-start(bf16[8,16,256]{2,1,0:T(8,128)(2,1)S(1)} %get-tuple-element.8), channel_id=1, source_target_pairs={{0,12},{4,16},{8,20},{12,24},{16,28},{20,32},{24,36},{28,40},{32,4... | collective-permute-start | bytes 196616 | tf_op jit(solution)/shard_map/ppermute | solution.py:19
  67.0 18.5 %collective-permute-start.8 = (bf16[8,16,256]{2,1,0:T(8,128)(2,1)S(1)}, bf16[8,16,256]{2,1,0:T(8,128)(2,1)S(1)}, u32[]{:S(2)}, u32[]{:S(2)}) collective-permute-start(bf16[8,16,256]{2,1,0:T(8,128)(2,1)S(1)} %get-tuple-element.8), channel_id=1, source_target_pairs={{0,8},{4,12},{8,16},{12,20},{16,24},{20,28},{24,32},{28,36},{32,40... | collective-permute-start | bytes 196616 | tf_op jit(solution)/shard_map/ppermute | solution.py:19
  75.4 10.1 %collective-permute-start.9 = (bf16[8,16,256]{2,1,0:T(8,128)(2,1)S(1)}, bf16[8,16,256]{2,1,0:T(8,128)(2,1)S(1)}, u32[]{:S(2)}, u32[]{:S(2)}) collective-permute-start(bf16[8,16,256]{2,1,0:T(8,128)(2,1)S(1)} %get-tuple-element.8), channel_id=1, source_target_pairs={{0,4},{4,8},{8,12},{12,16},{16,20},{20,24},{24,28},{28,32},{32,36}... | collective-permute-start | bytes 196616 | tf_op jit(solution)/shard_map/ppermute | solution.py:19

commit v3 on v2

--- a/solution.py
+++ b/solution.py
@@ -31,13 +31,32 @@
     return kernel.transpose(2, 3, 0, 1, 4).reshape(3 * o, 9 * c)
 
 
-def tap_sum(x_ref, k_ref, t, rows, columns):
+def frame_rows(get, t, r0, rows):
+    return jnp.concatenate([get(t, r0 + r) for r in range(rows)], axis=1)
+
+
+def from_ref(x_ref):
+    return lambda t, r: x_ref[t, r]
+
+
+def tiled(parts, frames_each, rows_top, rows_mid):
+    def get(t, r):
+        block = parts[t // frames_each]
+        f = t % frames_each
+        if r < rows_top:
+            return block[0][f, :, r, :]
+        if r < rows_top + rows_mid:
+            return block[1][f, :, r - rows_top, :]
+        return block[2][f, :, r - rows_top - rows_mid, :]
+
+    return get
+
+
+def tap_sum(get, k_ref, t, rows, columns):
     pieces = []
     for a in range(3):
         for b in range(3):
-            pieces.append(
-                jnp.concatenate([x_ref[t + a, r + b] for r in range(rows)], axis=1)
-            )
+            pieces.append(frame_rows(get, t + a, b, rows))
     stacked = jnp.concatenate(pieces, axis=0)
     acc = jnp.dot(k_ref[...], stacked, preferred_element_type=jnp.float32)
     out_channels = acc.shape[0] // 3
@@ -51,14 +70,16 @@
 
 
 def encoder_kernel(
-    x_ref, k1_ref, bias_ref, gain_ref, mask_ref, k2_ref, w_ref, o_ref, g_ref,
+    tc_ref, pv_ref, bc_ref, tp_ref, own_ref, bt_ref,
+    k1_ref, bias_ref, gain_ref, mask_ref, k2_ref, w_ref, o_ref, g_ref,
     *, frames, rows, columns
 ):
     wide = rows + 2
     bias = bias_ref[...]
     gain = gain_ref[...]
+    x = tiled([(tc_ref, pv_ref, bc_ref), (tp_ref, own_ref, bt_ref)], frames, 2, rows)
     for t in range(frames + 2):
-        y = tap_sum(x_ref, k1_ref, t, wide, columns) + bias
+        y = tap_sum(x, k1_ref, t, wide, columns) + bias
         scale = lax.rsqrt(jnp.mean(y * y, axis=0, keepdims=True) + 1e-06)
         z = y * scale * gain
         g = z / (1.0 + jnp.exp(-z))
@@ -67,24 +88,26 @@
             g_ref[t, r] = piece.astype(g_ref.dtype)
     total = None
     for t in range(frames):
-        y = tap_sum(g_ref, k2_ref, t, rows, columns)
-        res = jnp.concatenate([x_ref[t + 4, r + 2] for r in range(rows)], axis=1)
+        y = tap_sum(from_ref(g_ref), k2_ref, t, rows, columns)
+        res = frame_rows(x, t + frames, 2, rows)
         hidden = (res.astype(jnp.float32) + y).astype(jnp.bfloat16)
         part = jnp.dot(w_ref[t], hidden, preferred_element_type=jnp.float32)
         total = part if total is None else total + part
     for r in range(rows):
-        o_ref[r] = total[:, r * columns : (r + 1) * columns].astype(o_ref.dtype)
+        o_ref[0, :, r, :] = total[:, r * columns : (r + 1) * columns].astype(o_ref.dtype)
 
 
 def decode_kernel_body(
-    lat_ref, dk_ref, bias_ref, gain_ref, up_ref, mask_ref, fk_ref, o_ref, ext_ref,
+    l3_ref, l2_ref, l1_ref, l0_ref, dk_ref, bias_ref, gain_ref, up_ref, mask_ref, fk_ref, o_ref, ext_ref,
     *, frames, rows, columns
 ):
     wide = rows + 2
     bias = bias_ref[...]
     gain = gain_ref[...]
+    lat_refs = (l3_ref, l2_ref, l1_ref, l0_ref)
+    lat = lambda t, r: lat_refs[t][0, :, r, :]
     for f in range(2):
-        y = tap_sum(lat_ref, dk_ref, f, wide, columns) + bias
+        y = tap_sum(lat, dk_ref, f, wide, columns) + bias
         scale = lax.rsqrt(jnp.mean(y * y, axis=0, keepdims=True) + 1e-06)
         z = y * scale * gain
         act = (z / (1.0 + jnp.exp(-z))).astype(jnp.bfloat16)
@@ -96,9 +119,11 @@
                 piece = up[:, r * columns : (r + 1) * columns] * mask_ref[slot, r]
                 ext_ref[slot, r] = piece.astype(ext_ref.dtype)
     for t in range(frames):
-        y = tap_sum(ext_ref, fk_ref, t, rows, columns)
-        res = jnp.concatenate([ext_ref[t + 2, r + 1] for r in range(rows)], axis=1)
-        o_ref[t] = (res.astype(jnp.float32) + y).astype(o_ref.dtype)
+        y = tap_sum(from_ref(ext_ref), fk_ref, t, rows, columns)
+        res = frame_rows(from_ref(ext_ref), t + 2, 1, rows)
+        out = (res.astype(jnp.float32) + y).astype(o_ref.dtype)
+        for r in range(rows):
+            o_ref[t, :, r, :] = out[:, r * columns : (r + 1) * columns]
 
 
 def body(
@@ -117,14 +142,16 @@
     frames, channels, rows, columns = features.shape
     z_count = latent_weight.shape[1]
     dims = dict(frames=frames, rows=rows, columns=columns)
-    own = features.transpose(0, 2, 1, 3)
-    ext = jnp.concatenate(
-        [
-            jnp.concatenate([shift(own[:, -2:], 1, 1), shift(own, 1, 0), shift(own[:, :2], 1, -1)], 1),
-            jnp.concatenate([shift(own[:, -2:], 0, 1), own, shift(own[:, :2], 0, -1)], 1),
-        ],
-        0,
-    )
+    top = features[:, :, -2:]
+    bottom = features[:, :, :2]
+    pieces = [
+        shift(top, 1, 1),
+        shift(features, 1, 0),
+        shift(bottom, 1, -1),
+        shift(top, 0, 1),
+        features,
+        shift(bottom, 0, -1),
+    ]
     band = lax.axis_index("rows")
     bands = lax.axis_size("rows")
     row_ids = lax.broadcasted_iota(jnp.int32, (frames + 2, rows + 2), 1)
@@ -134,13 +161,13 @@
     mask = inside.astype(jnp.float32)
     vmem = pl.BlockSpec(memory_space=pltpu.VMEM)
     smem = pl.BlockSpec(memory_space=pltpu.SMEM)
-    lat = pl.pallas_call(
+    latent = pl.pallas_call(
         functools.partial(encoder_kernel, **dims),
-        out_shape=jax.ShapeDtypeStruct((rows, z_count, columns), jnp.bfloat16),
-        in_specs=[vmem] * 4 + [smem, vmem, vmem],
+        out_shape=jax.ShapeDtypeStruct((1, z_count, rows, columns), jnp.bfloat16),
+        in_specs=[vmem] * 9 + [smem, vmem, vmem],
         scratch_shapes=[pltpu.VMEM((frames + 2, rows + 2, channels, columns), jnp.bfloat16)],
     )(
-        ext,
+        *pieces,
         merged_kernel(first_kernel),
         first_bias[:, None],
         first_gain[:, None],
@@ -148,18 +175,17 @@
         merged_kernel(second_kernel),
         latent_weight,
     )
-    latent = lat.transpose(1, 0, 2)[None]
-    lat_rows = jnp.concatenate([shift(lat[-2:], 0, 1), lat, shift(lat[:2], 0, -1)], 0)
-    stacked = jnp.stack(
-        [shift(lat_rows, 3, 0), shift(lat_rows, 2, 0), shift(lat_rows, 1, 0), lat_rows], 0
-    )
-    rebuilt_flat = pl.pallas_call(
+    lat_rows = jnp.concatenate(
+        [shift(latent[:, :, -2:], 0, 1), latent, shift(latent[:, :, :2], 0, -1)], 2
+    )
+    lat_frames = [shift(lat_rows, 3, 0), shift(lat_rows, 2, 0), shift(lat_rows, 1, 0), lat_rows]
+    rebuilt = pl.pallas_call(
         functools.partial(decode_kernel_body, **dims),
-        out_shape=jax.ShapeDtypeStruct((frames, channels, rows * columns), jnp.bfloat16),
-        in_specs=[vmem] * 5 + [smem, vmem],
+        out_shape=jax.ShapeDtypeStruct((frames, channels, rows, columns), jnp.bfloat16),
+        in_specs=[vmem] * 8 + [smem, vmem],
         scratch_shapes=[pltpu.VMEM((frames + 2, rows + 2, channels, columns), jnp.bfloat16)],
     )(
-        stacked,
+        *lat_frames,
         merged_kernel(decode_kernel),
         decode_bias[:, None],
         decode_gain[:, None],
@@ -167,7 +193,6 @@
         mask,
         merged_kernel(final_kernel),
     )
-    rebuilt = rebuilt_flat.reshape(frames, channels, rows, columns)
     return (latent, rebuilt)
 
 

time: 96.1 us -> 109 us (1.13)
  the two profiles are of different devices: /device:TPU:37 before, /device:TPU:5 now
where the time goes in v3:
time: 109 us
  starting transfers between devices  41.1 us (38%)
  Pallas kernels  36.3 us (33%)
  local copies, waits for them, and re-layouts  18.7 us (17%)
  waiting for transfers between devices  11.1 us (10%)
    pallas_call x1, Pallas kernels, body(): pl.pallas_call(functools.partial(encoder_kernel, **dims), out_shape=jax.S...  28.4 us
    ppermute x4, starting transfers between devices, shift(): return lax.ppermute(x, 'tm', pairs)  20 us
    ppermute x4, starting transfers between devices, shift(): return lax.ppermute(x, 'rows', pairs)  12.3 us
    ppermute x2, starting transfers between devices, shift(): return lax.ppermute(x, ('tm', 'rows'), pairs)  8.84 us
    pallas_call x1, Pallas kernels, body(): pl.pallas_call(functools.partial(decode_kernel_body, **dims), out_shape=j...  7.94 us
    ppermute x2, waiting for transfers between devices, shift(): return lax.ppermute(x, ('tm', 'rows'), pairs)  6.94 us
    unnamed x34, local copies, waits for them, and re-layouts  5.65 us
    reshape x5, local copies, waits for them, and re-layouts, merged_kernel(): return kernel.transpose(2, 3, 0, 1, 4).reshape(3 * o, 9 * c)  4.81 us
  transfers between devices with their start and end apart: 10, of which 3 were waited for; matrix products, arithmetic and copies ran while one was open for 12% of the time, Pallas kernels for 0%

profile of v3, /device:TPU:5, one launch (start us, length us, event | category | flops | bytes accessed | tf_op | source)
XLA Modules:
  0.0 108.8 jit_solution(8453453969013533275)
XLA Ops:
  0.6 0.0 copy-start.1
  0.6 3.0 %collective-permute-start.1 = (bf16[4,96,4,256]{3,2,1,0:T(4,128)(2,1)}, bf16[4,96,4,256]{3,2,1,0:T(4,128)(2,1)S(1)}, u32[]{:S(2)}, u32[]{:S(2)}) collective-permute-start(bf16[4,96,4,256]{3,2,1,0:T(4,128)(2,1)} %own_ref.1), channel_id=1, source_target_pairs={{0,4},{4,8},{8,12},{12,16},{16,20},{20,24},{24,28},{28,32},{32,36}... | collective-permute-start | bytes 2359304 | tf_op jit(solution)/shard_map/ppermute | solution.py:19
  3.6 3.0 %fusion = (bf16[4,96,2,256]{3,2,1,0:T(2,128)(2,1)}, bf16[4,96,2,256]{3,2,1,0:T(2,128)(2,1)}) fusion(bf16[4,96,4,256]{3,2,1,0:T(4,128)(2,1)} %own_ref.1), kind=kLoop, calls=%fused_computation.4 | loop fusion | bytes 1572864 | tf_op jit(solution)/shard_map/slice | solution.py:146
  6.6 6.9 %collective-permute-start = (bf16[4,96,2,256]{3,2,1,0:T(2,128)(2,1)}, bf16[4,96,2,256]{3,2,1,0:T(2,128)(2,1)S(1)}, u32[]{:S(2)}, u32[]{:S(2)}) collective-permute-start(bf16[4,96,2,256]{3,2,1,0:T(2,128)(2,1)} %get-tuple-element.3), channel_id=1, source_target_pairs={{0,5},{1,6},{2,7},{4,9},{5,10},{6,11},{8,13},{9,14},{10,15},{12,17... | collective-permute-start | bytes 1179656 | tf_op jit(solution)/shard_map/ppermute | solution.py:26
  13.5 1.9 %collective-permute-start.2 = (bf16[4,96,2,256]{3,2,1,0:T(2,128)(2,1)}, bf16[4,96,2,256]{3,2,1,0:T(2,128)(2,1)S(1)}, u32[]{:S(2)}, u32[]{:S(2)}) collective-permute-start(bf16[4,96,2,256]{3,2,1,0:T(2,128)(2,1)} %get-tuple-element.2), channel_id=1, source_target_pairs={{1,4},{2,5},{3,6},{5,8},{6,9},{7,10},{9,12},{10,13},{11,14},{13,16... | collective-permute-start | bytes 1179656 | tf_op jit(solution)/shard_map/ppermute | solution.py:26
  15.5 6.1 %collective-permute-start.3 = (bf16[4,96,2,256]{3,2,1,0:T(2,128)(2,1)}, bf16[4,96,2,256]{3,2,1,0:T(2,128)(2,1)S(1)}, u32[]{:S(2)}, u32[]{:S(2)}) collective-permute-start(bf16[4,96,2,256]{3,2,1,0:T(2,128)(2,1)} %get-tuple-element.3), channel_id=1, source_target_pairs={{0,1},{1,2},{2,3},{4,5},{5,6},{6,7},{8,9},{9,10},{10,11},{12,13},{... | collective-permute-start | bytes 1179656 | tf_op jit(solution)/shard_map/ppermute | solution.py:16
  21.5 1.9 %collective-permute-start.4 = (bf16[4,96,2,256]{3,2,1,0:T(2,128)(2,1)}, bf16[4,96,2,256]{3,2,1,0:T(2,128)(2,1)}, u32[]{:S(2)}, u32[]{:S(2)}) collective-permute-start(bf16[4,96,2,256]{3,2,1,0:T(2,128)(2,1)} %get-tuple-element.2), channel_id=1, source_target_pairs={{1,0},{2,1},{3,2},{5,4},{6,5},{7,6},{9,8},{10,9},{11,10},{13,12},{... | collective-permute-start | bytes 1179656 | tf_op jit(solution)/shard_map/ppermute | solution.py:16
  23.5 0.0 copy-done.1
  23.5 0.5 copy.21
  24.0 0.0 copy-start.2
  24.0 1.3 %reshape.16.k1_ref = bf16[288,864]{1,0:T(8,128)(2,1)} reshape(bf16[3,96,3,3,96]{4,3,2,1,0:T(4,128)(2,1)S(1)} %copy.21) | data formatting | bytes 995328 | tf_op jit(solution)/shard_map/reshape | solution.py:31
  25.3 0.0 copy-done.2
  25.3 0.5 copy.22
  25.7 1.3 %reshape.17.k2_ref = bf16[288,864]{1,0:T(8,128)(2,1)} reshape(bf16[3,96,3,3,96]{4,3,2,1,0:T(4,128)(2,1)S(1)} %copy.22) | data formatting | bytes 995328 | tf_op jit(solution)/shard_map/reshape | solution.py:31
  27.0 0.0 copy-start.13
  27.0 0.7 copy-done.13
  27.7 0.7 copy.23.bias_ref
  28.4 0.0 copy-start.14
  28.4 0.7 copy-done.14
  29.1 0.7 copy.24.gain_ref
  29.8 0.7 and_convert_fusion.mask_ref
  30.5 0.0 copy-start.3
  30.5 1.5 %collective-permute-done.tc_ref = bf16[4,96,2,256]{3,2,1,0:T(2,128)(2,1)S(1)} collective-permute-done((bf16[4,96,2,256]{3,2,1,0:T(2,128)(2,1)}, bf16[4,96,2,256]{3,2,1,0:T(2,128)(2,1)S(1)}, u32[]{:S(2)}, u32[]{:S(2)}) %collective-permute-start) | collective-permute-done | bytes 393248 | tf_op jit(solution)/shard_map/ppermute | solution.py:26
  32.0 5.4 %collective-permute-done.2.bc_ref = bf16[4,96,2,256]{3,2,1,0:T(2,128)(2,1)S(1)} collective-permute-done((bf16[4,96,2,256]{3,2,1,0:T(2,128)(2,1)}, bf16[4,96,2,256]{3,2,1,0:T(2,128)(2,1)S(1)}, u32[]{:S(2)}, u32[]{:S(2)}) %collective-permute-start.2) | collective-permute-done | bytes 393248 | tf_op jit(solution)/shard_map/ppermute | solution.py:26
  37.4 0.0 collective-permute-done.3.tp_ref
  37.4 0.0 collective-permute-done.4.bt_ref
  37.4 0.0 collective-permute-done.1.pv_ref
  37.4 0.0 copy-done.4
  37.4 0.7 copy-done.5
  38.2 0.2 copy-done.6
  38.3 0.9 copy-done
  39.2 28.4 %shard_map.122 = bf16[1,16,4,256]{3,2,1,0:T(4,128)(2,1)} custom-call(bf16[4,96,2,256]{3,2,1,0:T(2,128)(2,1)} %copy-done.4, bf16[4,96,4,256]{3,2,1,0:T(4,128)(2,1)} %copy-done, bf16[4,96,2,256]{3,2,1,0:T(2,128)(2,1)} %copy-done.5, bf16[4,96,2,256]{3,2,1,0:T(2,128)(2,1)} %copy-done.6, bf16[4,96,4,256]{3,2,1,0:T(4,128)(2,1)} %own_ref.1, ...), custom_call_target="tpu_custom_call" | custom-call | tf_op jit(solution)/shard_map/pallas_call | solution.py:164
  67.6 0.9 fusion.1
  68.5 1.9 %collective-permute-start.5 = (bf16[1,16,2,256]{3,2,1,0:T(2,128)(2,1)S(1)}, bf16[1,16,2,256]{3,2,1,0:T(2,128)(2,1)S(1)}, u32[]{:S(2)}, u32[]{:S(2)}) collective-permute-start(bf16[1,16,2,256]{3,2,1,0:T(2,128)(2,1)S(1)} %get-tuple-element.4), channel_id=1, source_target_pairs={{0,1},{1,2},{2,3},{4,5},{5,6},{6,7},{8,9},{9,10},{10,11},{12,13},{... | collective-permute-start | bytes 49160 | tf_op jit(solution)/shard_map/ppermute | solution.py:16
  70.4 2.4 %collective-permute-start.6 = (bf16[1,16,2,256]{3,2,1,0:T(2,128)(2,1)S(1)}, bf16[1,16,2,256]{3,2,1,0:T(2,128)(2,1)S(1)}, u32[]{:S(2)}, u32[]{:S(2)}) collective-permute-start(bf16[1,16,2,256]{3,2,1,0:T(2,128)(2,1)S(1)} %get-tuple-element.5), channel_id=1, source_target_pairs={{1,0},{2,1},{3,2},{5,4},{6,5},{7,6},{9,8},{10,9},{11,10},{13,12},{... | collective-permute-start | bytes 49160 | tf_op jit(solution)/shard_map/ppermute | solution.py:16
  72.8 0.0 collective-permute-done.5
  72.9 4.1 %collective-permute-done.6 = bf16[1,16,2,256]{3,2,1,0:T(2,128)(2,1)S(1)} collective-permute-done((bf16[1,16,2,256]{3,2,1,0:T(2,128)(2,1)S(1)}, bf16[1,16,2,256]{3,2,1,0:T(2,128)(2,1)S(1)}, u32[]{:S(2)}, u32[]{:S(2)}) %collective-permute-start.6) | collective-permute-done | bytes 16416 | tf_op jit(solution)/shard_map/ppermute | solution.py:16
  77.0 0.0 copy-done.7
  77.0 0.1 pad_maximum_fusion.l0_ref
  77.1 0.0 copy-start.8
  77.1 3.5 %collective-permute-start.7 = (bf16[1,16,8,256]{3,2,1,0:T(8,128)(2,1)S(1)}, bf16[1,16,8,256]{3,2,1,0:T(8,128)(2,1)S(1)}, u32[]{:S(2)}, u32[]{:S(2)}) collective-permute-start(bf16[1,16,8,256]{3,2,1,0:T(8,128)(2,1)S(1)} %pad_maximum_fusion.l0_ref), channel_id=1, source_target_pairs={{0,12},{4,16},{8,20},{12,24},{16,28},{20,32},{24,36},{28,40},{32,4... | collective-permute-start | bytes 196616 | tf_op jit(solution)/shard_map/ppermute | solution.py:19
  80.6 8.8 %collective-permute-start.8 = (bf16[1,16,8,256]{3,2,1,0:T(8,128)(2,1)S(1)}, bf16[1,16,8,256]{3,2,1,0:T(8,128)(2,1)S(1)}, u32[]{:S(2)}, u32[]{:S(2)}) collective-permute-start(bf16[1,16,8,256]{3,2,1,0:T(8,128)(2,1)S(1)} %pad_maximum_fusion.l0_ref), channel_id=1, source_target_pairs={{0,8},{4,12},{8,16},{12,20},{16,24},{20,28},{24,32},{28,36},{32,40... | collective-permute-start | bytes 196616 | tf_op jit(solution)/shard_map/ppermute | solution.py:19
  89.4 4.7 %collective-permute-start.9 = (bf16[1,16,8,256]{3,2,1,0:T(8,128)(2,1)S(1)}, bf16[1,16,8,256]{3,2,1,0:T(8,128)(2,1)S(1)}, u32[]{:S(2)}, u32[]{:S(2)}) collective-permute-start(bf16[1,16,8,256]{3,2,1,0:T(8,128)(2,1)S(1)} %pad_maximum_fusion.l0_ref), channel_id=1, source_target_pairs={{0,4},{4,8},{8,12},{12,16},{16,20},{20,24},{24,28},{28,32},{32,36}... | collective-permute-start | bytes 196616 | tf_op jit(solution)/shard_map/ppermute | solution.py:19
  94.1 0.0 copy-done.3
  94.1 0.5 copy.26
  94.6 0.0 copy-done.8
  94.6 0.0 copy-start.9
  94.6 1.3 %reshape.19.fk_ref = bf16[288,864]{1,0:T(8,128)(2,1)} reshape(bf16[3,96,3,3,96]{4,3,2,1,0:T(4,128)(2,1)S(1)} %copy.26) | data formatting | bytes 995328 | tf_op jit(solution)/shard_map/reshape | solution.py:31
  95.9 0.0 copy-done.9
  95.9 0.1 copy.25
  96.0 0.1 reshape.18
  96.1 0.8 copy.27.dk_ref
  96.9 0.7 copy-done.15
  97.5 0.7 copy.28.bias_ref
  98.2 0.7 copy-done.16
  98.9 0.7 copy.29.gain_ref
  99.6 0.0 collective-permute-done.7.l3_ref
  99.6 0.0 collective-permute-done.8.l2_ref
  99.6 0.0 copy-start.11
  99.6 0.0 collective-permute-done.9.l1_ref
  99.7 0.6 copy-done.10
  100.2 0.0 copy-done.11
  100.3 0.6 copy-done.12
  100.9 7.9 %shard_map.123 = bf16[4,96,4,256]{3,2,1,0:T(4,128)(2,1)} custom-call(bf16[1,16,8,256]{3,2,1,0:T(8,128)(2,1)} %copy-done.10, bf16[1,16,8,256]{3,2,1,0:T(8,128)(2,1)} %copy-done.11, bf16[1,16,8,256]{3,2,1,0:T(8,128)(2,1)} %copy-done.12, bf16[1,16,8,256]{3,2,1,0:T(8,128)(2,1)} %copy-done.8, bf16[288,144]{1,0:T(8,128)(2,1)} %copy.27.dk_ref, ...), custom_call_target="tpu_custom_call" | custom-call | tf_op jit(solution)/shard_map/pallas_call | solution.py:182
  (10 shorter events, 0.0 us)
Async XLA Ops:
  0.6 22.9 %copy-start.1 = (bf16[3,3,3,96,96]{4,3,2,1,0:T(8,128)(2,1)S(1)}, bf16[3,3,3,96,96]{4,3,2,1,0:T(8,128)(2,1)}, u32[]{:S(2)}) copy-start(bf16[3,3,3,96,96]{4,3,2,1,0:T(8,128)(2,1)} %param.12) | copy-start | bytes 1492996
  0.6 36.8 %collective-permute-start.1 = (bf16[4,96,4,256]{3,2,1,0:T(4,128)(2,1)}, bf16[4,96,4,256]{3,2,1,0:T(4,128)(2,1)S(1)}, u32[]{:S(2)}, u32[]{:S(2)}) collective-permute-start(bf16[4,96,4,256]{3,2,1,0:T(4,128)(2,1)} %own_ref.1), channel_id=1, source_target_pairs={{0,4},{4,8},{8,12},{12,16},{16,20},{20,24},{24,28},{28,32},{32,36}... | collective-permute-start | bytes 2359304 | tf_op jit(solution)/shard_map/ppermute | solution.py:19
  6.6 25.4 %collective-permute-start = (bf16[4,96,2,256]{3,2,1,0:T(2,128)(2,1)}, bf16[4,96,2,256]{3,2,1,0:T(2,128)(2,1)S(1)}, u32[]{:S(2)}, u32[]{:S(2)}) collective-permute-start(bf16[4,96,2,256]{3,2,1,0:T(2,128)(2,1)} %get-tuple-element.3), channel_id=1, source_target_pairs={{0,5},{1,6},{2,7},{4,9},{5,10},{6,11},{8,13},{9,14},{10,15},{12,17... | collective-permute-start | bytes 1179656 | tf_op jit(solution)/shard_map/ppermute | solution.py:26
  13.5 23.9 %collective-permute-start.2 = (bf16[4,96,2,256]{3,2,1,0:T(2,128)(2,1)}, bf16[4,96,2,256]{3,2,1,0:T(2,128)(2,1)S(1)}, u32[]{:S(2)}, u32[]{:S(2)}) collective-permute-start(bf16[4,96,2,256]{3,2,1,0:T(2,128)(2,1)} %get-tuple-element.2), channel_id=1, source_target_pairs={{1,4},{2,5},{3,6},{5,8},{6,9},{7,10},{9,12},{10,13},{11,14},{13,16... | collective-permute-start | bytes 1179656 | tf_op jit(solution)/shard_map/ppermute | solution.py:26
  15.5 22.0 %collective-permute-start.3 = (bf16[4,96,2,256]{3,2,1,0:T(2,128)(2,1)}, bf16[4,96,2,256]{3,2,1,0:T(2,128)(2,1)S(1)}, u32[]{:S(2)}, u32[]{:S(2)}) collective-permute-start(bf16[4,96,2,256]{3,2,1,0:T(2,128)(2,1)} %get-tuple-element.3), channel_id=1, source_target_pairs={{0,1},{1,2},{2,3},{4,5},{5,6},{6,7},{8,9},{9,10},{10,11},{12,13},{... | collective-permute-start | bytes 1179656 | tf_op jit(solution)/shard_map/ppermute | solution.py:16
  21.5 15.9 %collective-permute-start.4 = (bf16[4,96,2,256]{3,2,1,0:T(2,128)(2,1)}, bf16[4,96,2,256]{3,2,1,0:T(2,128)(2,1)}, u32[]{:S(2)}, u32[]{:S(2)}) collective-permute-start(bf16[4,96,2,256]{3,2,1,0:T(2,128)(2,1)} %get-tuple-element.2), channel_id=1, source_target_pairs={{1,0},{2,1},{3,2},{5,4},{6,5},{7,6},{9,8},{10,9},{11,10},{13,12},{... | collective-permute-start | bytes 1179656 | tf_op jit(solution)/shard_map/ppermute | solution.py:16
  24.0 1.3 %copy-start.2 = (bf16[3,3,3,96,96]{4,3,2,1,0:T(8,128)(2,1)S(1)}, bf16[3,3,3,96,96]{4,3,2,1,0:T(8,128)(2,1)}, u32[]{:S(2)}) copy-start(bf16[3,3,3,96,96]{4,3,2,1,0:T(8,128)(2,1)} %param.15) | copy-start | bytes 1492996
  27.0 0.7 copy-start.13
  28.4 0.7 copy-start.14
  30.5 63.6 %copy-start.3 = (bf16[3,3,3,96,96]{4,3,2,1,0:T(8,128)(2,1)S(1)}, bf16[3,3,3,96,96]{4,3,2,1,0:T(8,128)(2,1)}, u32[]{:S(2)}) copy-start(bf16[3,3,3,96,96]{4,3,2,1,0:T(8,128)(2,1)} %param.21) | copy-start | bytes 1492996
  32.0 5.4 %copy-start.4 = (bf16[4,96,2,256]{3,2,1,0:T(2,128)(2,1)}, bf16[4,96,2,256]{3,2,1,0:T(2,128)(2,1)S(1)}, u32[]{:S(2)}) copy-start(bf16[4,96,2,256]{3,2,1,0:T(2,128)(2,1)S(1)} %collective-permute-done.tc_ref) | copy-start | bytes 1179652
  37.4 0.8 copy-start.5
  37.4 0.9 copy-start.6
  38.3 0.9 copy-start
  67.6 9.4 %copy-start.7 = (bf16[1,16,4,256]{3,2,1,0:T(4,128)(2,1)S(1)}, bf16[1,16,4,256]{3,2,1,0:T(4,128)(2,1)}, u32[]{:S(2)}) copy-start(bf16[1,16,4,256]{3,2,1,0:T(4,128)(2,1)} %shard_map.122) | copy-start | bytes 98308
  68.5 4.3 %collective-permute-start.5 = (bf16[1,16,2,256]{3,2,1,0:T(2,128)(2,1)S(1)}, bf16[1,16,2,256]{3,2,1,0:T(2,128)(2,1)S(1)}, u32[]{:S(2)}, u32[]{:S(2)}) collective-permute-start(bf16[1,16,2,256]{3,2,1,0:T(2,128)(2,1)S(1)} %get-tuple-element.4), channel_id=1, source_target_pairs={{0,1},{1,2},{2,3},{4,5},{5,6},{6,7},{8,9},{9,10},{10,11},{12,13},{... | collective-permute-start | bytes 49160 | tf_op jit(solution)/shard_map/ppermute | solution.py:16
  70.4 6.6 %collective-permute-start.6 = (bf16[1,16,2,256]{3,2,1,0:T(2,128)(2,1)S(1)}, bf16[1,16,2,256]{3,2,1,0:T(2,128)(2,1)S(1)}, u32[]{:S(2)}, u32[]{:S(2)}) collective-permute-start(bf16[1,16,2,256]{3,2,1,0:T(2,128)(2,1)S(1)} %get-tuple-element.5), channel_id=1, source_target_pairs={{1,0},{2,1},{3,2},{5,4},{6,5},{7,6},{9,8},{10,9},{11,10},{13,12},{... | collective-permute-start | bytes 49160 | tf_op jit(solution)/shard_map/ppermute | solution.py:16
  77.1 17.5 %copy-start.8 = (bf16[1,16,8,256]{3,2,1,0:T(8,128)(2,1)}, bf16[1,16,8,256]{3,2,1,0:T(8,128)(2,1)S(1)}, u32[]{:S(2)}) copy-start(bf16[1,16,8,256]{3,2,1,0:T(8,128)(2,1)S(1)} %pad_maximum_fusion.l0_ref) | copy-start | bytes 196612
  77.1 22.5 %collective-permute-start.7 = (bf16[1,16,8,256]{3,2,1,0:T(8,128)(2,1)S(1)}, bf16[1,16,8,256]{3,2,1,0:T(8,128)(2,1)S(1)}, u32[]{:S(2)}, u32[]{:S(2)}) collective-permute-start(bf16[1,16,8,256]{3,2,1,0:T(8,128)(2,1)S(1)} %pad_maximum_fusion.l0_ref), channel_id=1, source_target_pairs={{0,12},{4,16},{8,20},{12,24},{16,28},{20,32},{24,36},{28,40},{32,4... | collective-permute-start | bytes 196616 | tf_op jit(solution)/shard_map/ppermute | solution.py:19
  80.6 19.0 %collective-permute-start.8 = (bf16[1,16,8,256]{3,2,1,0:T(8,128)(2,1)S(1)}, bf16[1,16,8,256]{3,2,1,0:T(8,128)(2,1)S(1)}, u32[]{:S(2)}, u32[]{:S(2)}) collective-permute-start(bf16[1,16,8,256]{3,2,1,0:T(8,128)(2,1)S(1)} %pad_maximum_fusion.l0_ref), channel_id=1, source_target_pairs={{0,8},{4,12},{8,16},{12,20},{16,24},{20,28},{24,32},{28,36},{32,40... | collective-permute-start | bytes 196616 | tf_op jit(solution)/shard_map/ppermute | solution.py:19
  89.4 10.2 %collective-permute-start.9 = (bf16[1,16,8,256]{3,2,1,0:T(8,128)(2,1)S(1)}, bf16[1,16,8,256]{3,2,1,0:T(8,128)(2,1)S(1)}, u32[]{:S(2)}, u32[]{:S(2)}) collective-permute-start(bf16[1,16,8,256]{3,2,1,0:T(8,128)(2,1)S(1)} %pad_maximum_fusion.l0_ref), channel_id=1, source_target_pairs={{0,4},{4,8},{8,12},{12,16},{16,20},{20,24},{24,28},{28,32},{32,36}... | collective-permute-start | bytes 196616 | tf_op jit(solution)/shard_map/ppermute | solution.py:19
  94.6 1.3 %copy-start.9 = (bf16[3,3,3,96,16]{3,4,2,1,0:T(8,128)(2,1)S(1)}, bf16[3,3,3,96,16]{3,4,2,1,0:T(8,128)(2,1)}, u32[]{:S(2)}) copy-start(bf16[3,3,3,96,16]{3,4,2,1,0:T(8,128)(2,1)} %param.17) | copy-start | bytes 248836
  96.9 0.7 copy-start.15
  98.2 0.7 copy-start.16
  99.6 0.6 copy-start.10
  99.6 0.6 copy-start.11
  100.3 0.6 copy-start.12

commit v4 on v3

--- a/solution.py
+++ b/solution.py
@@ -44,10 +44,10 @@
         block = parts[t // frames_each]
         f = t % frames_each
         if r < rows_top:
-            return block[0][f, :, r, :]
+            return block[0][f, r]
         if r < rows_top + rows_mid:
-            return block[1][f, :, r - rows_top, :]
-        return block[2][f, :, r - rows_top - rows_mid, :]
+            return block[1][f, r - rows_top]
+        return block[2][f, r - rows_top - rows_mid]
 
     return get
 
@@ -142,14 +142,15 @@
     frames, channels, rows, columns = features.shape
     z_count = latent_weight.shape[1]
     dims = dict(frames=frames, rows=rows, columns=columns)
-    top = features[:, :, -2:]
-    bottom = features[:, :, :2]
+    own = features.transpose(0, 2, 1, 3)
+    top = own[:, -2:]
+    bottom = own[:, :2]
     pieces = [
         shift(top, 1, 1),
-        shift(features, 1, 0),
+        shift(own, 1, 0),
         shift(bottom, 1, -1),
         shift(top, 0, 1),
-        features,
+        own,
         shift(bottom, 0, -1),
     ]
     band = lax.axis_index("rows")

time: 109 us -> 93.3 us (0.86)
  the two profiles are of different devices: /device:TPU:5 before, /device:TPU:37 now
where the time goes in v4:
time: 93.3 us; the launch traced here: 92.8 us
  starting transfers between devices  41.3 us (44%)
  Pallas kernels  19.8 us (21%)
  local copies, waits for them, and re-layouts  17 us (18%)
  waiting for transfers between devices  13 us (14%)
    ppermute x4, starting transfers between devices, shift(): return lax.ppermute(x, 'tm', pairs)  20.1 us
    ppermute x4, starting transfers between devices, shift(): return lax.ppermute(x, 'rows', pairs)  12.3 us
    pallas_call x1, Pallas kernels, body(): pl.pallas_call(functools.partial(encoder_kernel, **dims), out_shape=jax.S...  11.9 us
    ppermute x2, waiting for transfers between devices, shift(): return lax.ppermute(x, ('tm', 'rows'), pairs)  8.89 us
    ppermute x2, starting transfers between devices, shift(): return lax.ppermute(x, ('tm', 'rows'), pairs)  8.84 us
    pallas_call x1, Pallas kernels, body(): pl.pallas_call(functools.partial(decode_kernel_body, **dims), out_shape=j...  7.93 us
    unnamed x33, local copies, waits for them, and re-layouts  6.03 us
    reshape x5, local copies, waits for them, and re-layouts, merged_kernel(): return kernel.transpose(2, 3, 0, 1, 4).reshape(3 * o, 9 * c)  4.81 us
  transfers between devices with their start and end apart: 10, of which 3 were waited for; matrix products, arithmetic and copies ran while one was open for 12% of the time, Pallas kernels for 0%

profile of v4, /device:TPU:37, one launch (start us, length us, event | category | flops | bytes accessed | tf_op | source)
XLA Modules:
  0.0 92.8 jit_solution(17957140214504261721)
XLA Ops:
  0.6 1.3 %copy.33 = bf16[4,96,4,256]{3,1,2,0:T(8,128)(2,1)S(1)} copy(bf16[4,96,4,256]{3,2,1,0:T(4,128)(2,1)} %param.11) | data formatting | bytes 1572864 | tf_op args[0]
  1.9 0.0 copy-start
  1.9 0.0 copy-start.2
  1.9 3.0 %collective-permute-start.1 = (bf16[4,4,96,256]{3,2,1,0:T(8,128)(2,1)S(1)}, bf16[4,4,96,256]{3,2,1,0:T(8,128)(2,1)S(1)}, u32[]{:S(2)}, u32[]{:S(2)}) collective-permute-start(bf16[4,4,96,256]{3,2,1,0:T(8,128)(2,1)S(1)} %bitcast.13), channel_id=1, source_target_pairs={{0,4},{4,8},{8,12},{12,16},{16,20},{20,24},{24,28},{28,32},{32,36}... | collective-permute-start | bytes 2359304 | tf_op jit(solution)/shard_map/ppermute | solution.py:19
  4.9 1.0 %fusion = (bf16[4,2,96,256]{3,2,1,0:T(8,128)(2,1)}, bf16[4,2,96,256]{3,2,1,0:T(8,128)(2,1)}) fusion(bf16[4,4,96,256]{3,2,1,0:T(8,128)(2,1)S(1)} %bitcast.14), kind=kLoop, calls=%fused_computation.5 | loop fusion | bytes 1572864 | tf_op jit(solution)/shard_map/slice | solution.py:147
  5.8 0.0 copy-done
  5.8 6.9 %collective-permute-start = (bf16[4,2,96,256]{3,2,1,0:T(8,128)(2,1)}, bf16[4,2,96,256]{3,2,1,0:T(8,128)(2,1)S(1)}, u32[]{:S(2)}, u32[]{:S(2)}) collective-permute-start(bf16[4,2,96,256]{3,2,1,0:T(8,128)(2,1)} %get-tuple-element.3), channel_id=1, source_target_pairs={{0,5},{1,6},{2,7},{4,9},{5,10},{6,11},{8,13},{9,14},{10,15},{12,17... | collective-permute-start | bytes 1179656 | tf_op jit(solution)/shard_map/ppermute | solution.py:26
  12.8 1.9 %collective-permute-start.2 = (bf16[4,2,96,256]{3,2,1,0:T(8,128)(2,1)}, bf16[4,2,96,256]{3,2,1,0:T(8,128)(2,1)}, u32[]{:S(2)}, u32[]{:S(2)}) collective-permute-start(bf16[4,2,96,256]{3,2,1,0:T(8,128)(2,1)} %get-tuple-element.2), channel_id=1, source_target_pairs={{1,4},{2,5},{3,6},{5,8},{6,9},{7,10},{9,12},{10,13},{11,14},{13,16... | collective-permute-start | bytes 1179656 | tf_op jit(solution)/shard_map/ppermute | solution.py:26
  14.7 6.1 %collective-permute-start.3 = (bf16[4,2,96,256]{3,2,1,0:T(8,128)(2,1)}, bf16[4,2,96,256]{3,2,1,0:T(8,128)(2,1)}, u32[]{:S(2)}, u32[]{:S(2)}) collective-permute-start(bf16[4,2,96,256]{3,2,1,0:T(8,128)(2,1)} %get-tuple-element.3), channel_id=1, source_target_pairs={{0,1},{1,2},{2,3},{4,5},{5,6},{6,7},{8,9},{9,10},{10,11},{12,13},{... | collective-permute-start | bytes 1179656 | tf_op jit(solution)/shard_map/ppermute | solution.py:16
  20.8 1.9 %collective-permute-start.4 = (bf16[4,2,96,256]{3,2,1,0:T(8,128)(2,1)}, bf16[4,2,96,256]{3,2,1,0:T(8,128)(2,1)}, u32[]{:S(2)}, u32[]{:S(2)}) collective-permute-start(bf16[4,2,96,256]{3,2,1,0:T(8,128)(2,1)} %get-tuple-element.2), channel_id=1, source_target_pairs={{1,0},{2,1},{3,2},{5,4},{6,5},{7,6},{9,8},{10,9},{11,10},{13,12},{... | collective-permute-start | bytes 1179656 | tf_op jit(solution)/shard_map/ppermute | solution.py:16
  22.7 0.0 copy-done.2
  22.7 0.5 copy.23
  23.2 0.0 copy-start.3
  23.2 1.3 %reshape.16.k1_ref = bf16[288,864]{1,0:T(8,128)(2,1)} reshape(bf16[3,96,3,3,96]{4,3,2,1,0:T(4,128)(2,1)S(1)} %copy.23) | data formatting | bytes 995328 | tf_op jit(solution)/shard_map/reshape | solution.py:31
  24.5 0.0 copy-done.3
  24.5 0.5 copy.24
  25.0 1.3 %reshape.17.k2_ref = bf16[288,864]{1,0:T(8,128)(2,1)} reshape(bf16[3,96,3,3,96]{4,3,2,1,0:T(4,128)(2,1)S(1)} %copy.24) | data formatting | bytes 995328 | tf_op jit(solution)/shard_map/reshape | solution.py:31
  26.3 0.0 copy-start.12
  26.3 0.7 copy-done.12
  26.9 0.7 copy.25.bias_ref
  27.6 0.7 copy-done.13
  28.3 0.7 copy.26.gain_ref
  29.0 0.7 and_convert_fusion.mask_ref
  29.7 3.5 %collective-permute-done.tc_ref = bf16[4,2,96,256]{3,2,1,0:T(8,128)(2,1)S(1)} collective-permute-done((bf16[4,2,96,256]{3,2,1,0:T(8,128)(2,1)}, bf16[4,2,96,256]{3,2,1,0:T(8,128)(2,1)S(1)}, u32[]{:S(2)}, u32[]{:S(2)}) %collective-permute-start) | collective-permute-done | bytes 393248 | tf_op jit(solution)/shard_map/ppermute | solution.py:26
  33.2 5.4 %collective-permute-done.2.bc_ref = bf16[4,2,96,256]{3,2,1,0:T(8,128)(2,1)} collective-permute-done((bf16[4,2,96,256]{3,2,1,0:T(8,128)(2,1)}, bf16[4,2,96,256]{3,2,1,0:T(8,128)(2,1)}, u32[]{:S(2)}, u32[]{:S(2)}) %collective-permute-start.2) | collective-permute-done | bytes 393248 | tf_op jit(solution)/shard_map/ppermute | solution.py:26
  38.6 0.0 collective-permute-done.3.tp_ref
  38.6 0.0 collective-permute-done.4.bt_ref
  38.6 0.0 collective-permute-done.1.pv_ref
  38.6 0.0 copy-done.5
  38.6 0.0 copy-start.1
  38.6 0.9 copy-done.1
  39.5 11.9 %shard_map.122 = bf16[1,16,4,256]{3,2,1,0:T(4,128)(2,1)} custom-call(bf16[4,2,96,256]{3,2,1,0:T(8,128)(2,1)} %copy-done.5, bf16[4,4,96,256]{3,2,1,0:T(8,128)(2,1)} %copy-done.1, bf16[4,2,96,256]{3,2,1,0:T(8,128)(2,1)} %collective-permute-done.2.bc_ref, bf16[4,2,96,256]{3,2,1,0:T(8,128)(2,1)} %collective-permute-done.3.tp_ref, ...), custom_call_target="tpu_custom_call" | custom-call | tf_op jit(solution)/shard_map/pallas_call | solution.py:165
  51.4 0.9 fusion.1
  52.3 1.9 %collective-permute-start.5 = (bf16[1,16,2,256]{3,2,1,0:T(2,128)(2,1)S(1)}, bf16[1,16,2,256]{3,2,1,0:T(2,128)(2,1)S(1)}, u32[]{:S(2)}, u32[]{:S(2)}) collective-permute-start(bf16[1,16,2,256]{3,2,1,0:T(2,128)(2,1)S(1)} %get-tuple-element.4), channel_id=1, source_target_pairs={{0,1},{1,2},{2,3},{4,5},{5,6},{6,7},{8,9},{9,10},{10,11},{12,13},{... | collective-permute-start | bytes 49160 | tf_op jit(solution)/shard_map/ppermute | solution.py:16
  54.2 2.4 %collective-permute-start.6 = (bf16[1,16,2,256]{3,2,1,0:T(2,128)(2,1)S(1)}, bf16[1,16,2,256]{3,2,1,0:T(2,128)(2,1)S(1)}, u32[]{:S(2)}, u32[]{:S(2)}) collective-permute-start(bf16[1,16,2,256]{3,2,1,0:T(2,128)(2,1)S(1)} %get-tuple-element.5), channel_id=1, source_target_pairs={{1,0},{2,1},{3,2},{5,4},{6,5},{7,6},{9,8},{10,9},{11,10},{13,12},{... | collective-permute-start | bytes 49160 | tf_op jit(solution)/shard_map/ppermute | solution.py:16
  56.6 0.0 collective-permute-done.5
  56.6 4.1 %collective-permute-done.6 = bf16[1,16,2,256]{3,2,1,0:T(2,128)(2,1)S(1)} collective-permute-done((bf16[1,16,2,256]{3,2,1,0:T(2,128)(2,1)S(1)}, bf16[1,16,2,256]{3,2,1,0:T(2,128)(2,1)S(1)}, u32[]{:S(2)}, u32[]{:S(2)}) %collective-permute-start.6) | collective-permute-done | bytes 16416 | tf_op jit(solution)/shard_map/ppermute | solution.py:16
  60.8 0.0 copy-done.6
  60.8 0.1 pad_maximum_fusion.l0_ref
  60.8 0.0 copy-start.7
  60.8 3.5 %collective-permute-start.7 = (bf16[1,16,8,256]{3,2,1,0:T(8,128)(2,1)S(1)}, bf16[1,16,8,256]{3,2,1,0:T(8,128)(2,1)S(1)}, u32[]{:S(2)}, u32[]{:S(2)}) collective-permute-start(bf16[1,16,8,256]{3,2,1,0:T(8,128)(2,1)S(1)} %pad_maximum_fusion.l0_ref), channel_id=1, source_target_pairs={{0,12},{4,16},{8,20},{12,24},{16,28},{20,32},{24,36},{28,40},{32,4... | collective-permute-start | bytes 196616 | tf_op jit(solution)/shard_map/ppermute | solution.py:19
  64.3 8.4 %collective-permute-start.8 = (bf16[1,16,8,256]{3,2,1,0:T(8,128)(2,1)S(1)}, bf16[1,16,8,256]{3,2,1,0:T(8,128)(2,1)S(1)}, u32[]{:S(2)}, u32[]{:S(2)}) collective-permute-start(bf16[1,16,8,256]{3,2,1,0:T(8,128)(2,1)S(1)} %pad_maximum_fusion.l0_ref), channel_id=1, source_target_pairs={{0,8},{4,12},{8,16},{12,20},{16,24},{20,28},{24,32},{28,36},{32,40... | collective-permute-start | bytes 196616 | tf_op jit(solution)/shard_map/ppermute | solution.py:19
  72.8 5.3 %collective-permute-start.9 = (bf16[1,16,8,256]{3,2,1,0:T(8,128)(2,1)S(1)}, bf16[1,16,8,256]{3,2,1,0:T(8,128)(2,1)S(1)}, u32[]{:S(2)}, u32[]{:S(2)}) collective-permute-start(bf16[1,16,8,256]{3,2,1,0:T(8,128)(2,1)S(1)} %pad_maximum_fusion.l0_ref), channel_id=1, source_target_pairs={{0,4},{4,8},{8,12},{12,16},{16,20},{20,24},{24,28},{28,32},{32,36}... | collective-permute-start | bytes 196616 | tf_op jit(solution)/shard_map/ppermute | solution.py:19
  78.0 0.0 copy-done.4
  78.0 0.5 copy.28
  78.5 0.0 copy-done.7
  78.5 0.0 copy-start.8
  78.5 1.3 %reshape.19.fk_ref = bf16[288,864]{1,0:T(8,128)(2,1)} reshape(bf16[3,96,3,3,96]{4,3,2,1,0:T(4,128)(2,1)S(1)} %copy.28) | data formatting | bytes 995328 | tf_op jit(solution)/shard_map/reshape | solution.py:31
  79.8 0.0 copy-done.8
  79.8 0.1 copy.27
  79.9 0.1 reshape.18
  80.0 0.8 copy.29.dk_ref
  80.8 0.7 copy-done.14
  81.5 0.7 copy.30.bias_ref
  82.2 0.7 copy-done.15
  82.8 0.7 copy.31.gain_ref
  83.6 0.0 collective-permute-done.7.l3_ref
  83.6 0.0 collective-permute-done.8.l2_ref
  83.6 0.0 copy-start.10
  83.6 0.0 collective-permute-done.9.l1_ref
  83.6 0.6 copy-done.9
  84.2 0.0 copy-done.10
  84.2 0.6 copy-done.11
  84.8 7.9 %shard_map.123 = bf16[4,96,4,256]{3,2,1,0:T(4,128)(2,1)} custom-call(bf16[1,16,8,256]{3,2,1,0:T(8,128)(2,1)} %copy-done.9, bf16[1,16,8,256]{3,2,1,0:T(8,128)(2,1)} %copy-done.10, bf16[1,16,8,256]{3,2,1,0:T(8,128)(2,1)} %copy-done.11, bf16[1,16,8,256]{3,2,1,0:T(8,128)(2,1)} %copy-done.7, bf16[288,144]{1,0:T(8,128)(2,1)} %copy.29.dk_ref, ...), custom_call_target="tpu_custom_call" | custom-call | tf_op jit(solution)/shard_map/pallas_call | solution.py:183
  (9 shorter events, 0.0 us)
Async XLA Ops:
  1.9 3.9 %copy-start = (bf16[4,96,4,256]{3,1,2,0:T(8,128)(2,1)}, bf16[4,96,4,256]{3,1,2,0:T(8,128)(2,1)S(1)}, u32[]{:S(2)}) copy-start(bf16[4,96,4,256]{3,1,2,0:T(8,128)(2,1)S(1)} %copy.33) | copy-start | bytes 2359300
  1.9 20.8 %copy-start.2 = (bf16[3,3,3,96,96]{4,3,2,1,0:T(8,128)(2,1)S(1)}, bf16[3,3,3,96,96]{4,3,2,1,0:T(8,128)(2,1)}, u32[]{:S(2)}) copy-start(bf16[3,3,3,96,96]{4,3,2,1,0:T(8,128)(2,1)} %param.12) | copy-start | bytes 1492996
  1.9 36.7 %collective-permute-start.1 = (bf16[4,4,96,256]{3,2,1,0:T(8,128)(2,1)S(1)}, bf16[4,4,96,256]{3,2,1,0:T(8,128)(2,1)S(1)}, u32[]{:S(2)}, u32[]{:S(2)}) collective-permute-start(bf16[4,4,96,256]{3,2,1,0:T(8,128)(2,1)S(1)} %bitcast.13), channel_id=1, source_target_pairs={{0,4},{4,8},{8,12},{12,16},{16,20},{20,24},{24,28},{28,32},{32,36}... | collective-permute-start | bytes 2359304 | tf_op jit(solution)/shard_map/ppermute | solution.py:19
  5.8 27.3 %collective-permute-start = (bf16[4,2,96,256]{3,2,1,0:T(8,128)(2,1)}, bf16[4,2,96,256]{3,2,1,0:T(8,128)(2,1)S(1)}, u32[]{:S(2)}, u32[]{:S(2)}) collective-permute-start(bf16[4,2,96,256]{3,2,1,0:T(8,128)(2,1)} %get-tuple-element.3), channel_id=1, source_target_pairs={{0,5},{1,6},{2,7},{4,9},{5,10},{6,11},{8,13},{9,14},{10,15},{12,17... | collective-permute-start | bytes 1179656 | tf_op jit(solution)/shard_map/ppermute | solution.py:26
  12.8 25.8 %collective-permute-start.2 = (bf16[4,2,96,256]{3,2,1,0:T(8,128)(2,1)}, bf16[4,2,96,256]{3,2,1,0:T(8,128)(2,1)}, u32[]{:S(2)}, u32[]{:S(2)}) collective-permute-start(bf16[4,2,96,256]{3,2,1,0:T(8,128)(2,1)} %get-tuple-element.2), channel_id=1, source_target_pairs={{1,4},{2,5},{3,6},{5,8},{6,9},{7,10},{9,12},{10,13},{11,14},{13,16... | collective-permute-start | bytes 1179656 | tf_op jit(solution)/shard_map/ppermute | solution.py:26
  14.7 23.9 %collective-permute-start.3 = (bf16[4,2,96,256]{3,2,1,0:T(8,128)(2,1)}, bf16[4,2,96,256]{3,2,1,0:T(8,128)(2,1)}, u32[]{:S(2)}, u32[]{:S(2)}) collective-permute-start(bf16[4,2,96,256]{3,2,1,0:T(8,128)(2,1)} %get-tuple-element.3), channel_id=1, source_target_pairs={{0,1},{1,2},{2,3},{4,5},{5,6},{6,7},{8,9},{9,10},{10,11},{12,13},{... | collective-permute-start | bytes 1179656 | tf_op jit(solution)/shard_map/ppermute | solution.py:16
  20.8 17.8 %collective-permute-start.4 = (bf16[4,2,96,256]{3,2,1,0:T(8,128)(2,1)}, bf16[4,2,96,256]{3,2,1,0:T(8,128)(2,1)}, u32[]{:S(2)}, u32[]{:S(2)}) collective-permute-start(bf16[4,2,96,256]{3,2,1,0:T(8,128)(2,1)} %get-tuple-element.2), channel_id=1, source_target_pairs={{1,0},{2,1},{3,2},{5,4},{6,5},{7,6},{9,8},{10,9},{11,10},{13,12},{... | collective-permute-start | bytes 1179656 | tf_op jit(solution)/shard_map/ppermute | solution.py:16
  23.2 1.3 %copy-start.3 = (bf16[3,3,3,96,96]{4,3,2,1,0:T(8,128)(2,1)S(1)}, bf16[3,3,3,96,96]{4,3,2,1,0:T(8,128)(2,1)}, u32[]{:S(2)}) copy-start(bf16[3,3,3,96,96]{4,3,2,1,0:T(8,128)(2,1)} %param.15) | copy-start | bytes 1492996
  26.3 0.7 copy-start.12
  27.6 0.7 copy-start.13
  29.7 48.4 %copy-start.4 = (bf16[3,3,3,96,96]{4,3,2,1,0:T(8,128)(2,1)S(1)}, bf16[3,3,3,96,96]{4,3,2,1,0:T(8,128)(2,1)}, u32[]{:S(2)}) copy-start(bf16[3,3,3,96,96]{4,3,2,1,0:T(8,128)(2,1)} %param.21) | copy-start | bytes 1492996
  33.2 5.4 %copy-start.5 = (bf16[4,2,96,256]{3,2,1,0:T(8,128)(2,1)}, bf16[4,2,96,256]{3,2,1,0:T(8,128)(2,1)S(1)}, u32[]{:S(2)}) copy-start(bf16[4,2,96,256]{3,2,1,0:T(8,128)(2,1)S(1)} %collective-permute-done.tc_ref) | copy-start | bytes 1179652
  38.6 0.9 copy-start.1
  51.4 9.4 %copy-start.6 = (bf16[1,16,4,256]{3,2,1,0:T(4,128)(2,1)S(1)}, bf16[1,16,4,256]{3,2,1,0:T(4,128)(2,1)}, u32[]{:S(2)}) copy-start(bf16[1,16,4,256]{3,2,1,0:T(4,128)(2,1)} %shard_map.122) | copy-start | bytes 98308
  52.3 4.3 %collective-permute-start.5 = (bf16[1,16,2,256]{3,2,1,0:T(2,128)(2,1)S(1)}, bf16[1,16,2,256]{3,2,1,0:T(2,128)(2,1)S(1)}, u32[]{:S(2)}, u32[]{:S(2)}) collective-permute-start(bf16[1,16,2,256]{3,2,1,0:T(2,128)(2,1)S(1)} %get-tuple-element.4), channel_id=1, source_target_pairs={{0,1},{1,2},{2,3},{4,5},{5,6},{6,7},{8,9},{9,10},{10,11},{12,13},{... | collective-permute-start | bytes 49160 | tf_op jit(solution)/shard_map/ppermute | solution.py:16
  54.2 6.6 %collective-permute-start.6 = (bf16[1,16,2,256]{3,2,1,0:T(2,128)(2,1)S(1)}, bf16[1,16,2,256]{3,2,1,0:T(2,128)(2,1)S(1)}, u32[]{:S(2)}, u32[]{:S(2)}) collective-permute-start(bf16[1,16,2,256]{3,2,1,0:T(2,128)(2,1)S(1)} %get-tuple-element.5), channel_id=1, source_target_pairs={{1,0},{2,1},{3,2},{5,4},{6,5},{7,6},{9,8},{10,9},{11,10},{13,12},{... | collective-permute-start | bytes 49160 | tf_op jit(solution)/shard_map/ppermute | solution.py:16
  60.8 17.7 %copy-start.7 = (bf16[1,16,8,256]{3,2,1,0:T(8,128)(2,1)}, bf16[1,16,8,256]{3,2,1,0:T(8,128)(2,1)S(1)}, u32[]{:S(2)}) copy-start(bf16[1,16,8,256]{3,2,1,0:T(8,128)(2,1)S(1)} %pad_maximum_fusion.l0_ref) | copy-start | bytes 196612
  60.8 22.7 %collective-permute-start.7 = (bf16[1,16,8,256]{3,2,1,0:T(8,128)(2,1)S(1)}, bf16[1,16,8,256]{3,2,1,0:T(8,128)(2,1)S(1)}, u32[]{:S(2)}, u32[]{:S(2)}) collective-permute-start(bf16[1,16,8,256]{3,2,1,0:T(8,128)(2,1)S(1)} %pad_maximum_fusion.l0_ref), channel_id=1, source_target_pairs={{0,12},{4,16},{8,20},{12,24},{16,28},{20,32},{24,36},{28,40},{32,4... | collective-permute-start | bytes 196616 | tf_op jit(solution)/shard_map/ppermute | solution.py:19
  64.3 19.2 %collective-permute-start.8 = (bf16[1,16,8,256]{3,2,1,0:T(8,128)(2,1)S(1)}, bf16[1,16,8,256]{3,2,1,0:T(8,128)(2,1)S(1)}, u32[]{:S(2)}, u32[]{:S(2)}) collective-permute-start(bf16[1,16,8,256]{3,2,1,0:T(8,128)(2,1)S(1)} %pad_maximum_fusion.l0_ref), channel_id=1, source_target_pairs={{0,8},{4,12},{8,16},{12,20},{16,24},{20,28},{24,32},{28,36},{32,40... | collective-permute-start | bytes 196616 | tf_op jit(solution)/shard_map/ppermute | solution.py:19
  72.8 10.8 %collective-permute-start.9 = (bf16[1,16,8,256]{3,2,1,0:T(8,128)(2,1)S(1)}, bf16[1,16,8,256]{3,2,1,0:T(8,128)(2,1)S(1)}, u32[]{:S(2)}, u32[]{:S(2)}) collective-permute-start(bf16[1,16,8,256]{3,2,1,0:T(8,128)(2,1)S(1)} %pad_maximum_fusion.l0_ref), channel_id=1, source_target_pairs={{0,4},{4,8},{8,12},{12,16},{16,20},{20,24},{24,28},{28,32},{32,36}... | collective-permute-start | bytes 196616 | tf_op jit(solution)/shard_map/ppermute | solution.py:19
  78.5 1.3 %copy-start.8 = (bf16[3,3,3,96,16]{3,4,2,1,0:T(8,128)(2,1)S(1)}, bf16[3,3,3,96,16]{3,4,2,1,0:T(8,128)(2,1)}, u32[]{:S(2)}) copy-start(bf16[3,3,3,96,16]{3,4,2,1,0:T(8,128)(2,1)} %param.17) | copy-start | bytes 248836
  80.8 0.7 copy-start.14
  82.2 0.7 copy-start.15
  83.6 0.6 copy-start.9
  83.6 0.6 copy-start.10
  84.2 0.6 copy-start.11

commit v5 on v4

--- a/solution.py
+++ b/solution.py
@@ -145,10 +145,11 @@
     own = features.transpose(0, 2, 1, 3)
     top = own[:, -2:]
     bottom = own[:, :2]
+    previous = shift(own, 1, 0)
     pieces = [
-        shift(top, 1, 1),
-        shift(own, 1, 0),
-        shift(bottom, 1, -1),
+        shift(previous[:, -2:], 0, 1),
+        previous,
+        shift(previous[:, :2], 0, -1),
         shift(top, 0, 1),
         own,
         shift(bottom, 0, -1),

time: 93.3 us -> 92.4 us (level)
  the two profiles are of different devices: /device:TPU:37 before, /device:TPU:5 now
where the time goes in v5:
time: 92.4 us; the launch traced here: 91.9 us
  starting transfers between devices  37.8 us (41%)
  Pallas kernels  19.8 us (21%)
  local copies, waits for them, and re-layouts  17.3 us (19%)
  waiting for transfers between devices  15.4 us (17%)
    ppermute x6, starting transfers between devices, shift(): return lax.ppermute(x, 'rows', pairs)  21.9 us
    ppermute x4, starting transfers between devices, shift(): return lax.ppermute(x, 'tm', pairs)  15.8 us
    pallas_call x1, Pallas kernels, body(): pl.pallas_call(functools.partial(encoder_kernel, **dims), out_shape=jax.S...  11.9 us
    ppermute x4, waiting for transfers between devices, shift(): return lax.ppermute(x, 'tm', pairs)  8.79 us
    pallas_call x1, Pallas kernels, body(): pl.pallas_call(functools.partial(decode_kernel_body, **dims), out_shape=j...  7.93 us
    ppermute x6, waiting for transfers between devices, shift(): return lax.ppermute(x, 'rows', pairs)  6.6 us
    unnamed x37, local copies, waits for them, and re-layouts  5.29 us
    reshape x5, local copies, waits for them, and re-layouts, merged_kernel(): return kernel.transpose(2, 3, 0, 1, 4).reshape(3 * o, 9 * c)  4.83 us
  transfers between devices with their start and end apart: 10, of which 3 were waited for; matrix products, arithmetic and copies ran while one was open for 13% of the time, Pallas kernels for 0%

profile of v5, /device:TPU:5, one launch (start us, length us, event | category | flops | bytes accessed | tf_op | source)
XLA Modules:
  0.0 91.9 jit_solution(586305587366254757)
XLA Ops:
  0.6 1.3 %copy.33 = bf16[4,96,4,256]{3,1,2,0:T(8,128)(2,1)S(1)} copy(bf16[4,96,4,256]{3,2,1,0:T(4,128)(2,1)} %param.11) | data formatting | bytes 1572864 | tf_op args[0]
  1.9 0.0 copy-start
  1.9 2.8 %collective-permute-start = (bf16[4,4,96,256]{3,2,1,0:T(8,128)(2,1)S(1)}, bf16[4,4,96,256]{3,2,1,0:T(8,128)(2,1)S(1)}, u32[]{:S(2)}, u32[]{:S(2)}) collective-permute-start(bf16[4,4,96,256]{3,2,1,0:T(8,128)(2,1)S(1)} %bitcast.13), channel_id=1, source_target_pairs={{0,4},{4,8},{8,12},{12,16},{16,20},{20,24},{24,28},{28,32},{32,36}... | collective-permute-start | bytes 2359304 | tf_op jit(solution)/shard_map/ppermute | solution.py:19
  4.7 1.0 %fusion = (bf16[4,2,96,256]{3,2,1,0:T(8,128)(2,1)}, bf16[4,2,96,256]{3,2,1,0:T(8,128)(2,1)}) fusion(bf16[4,4,96,256]{3,2,1,0:T(8,128)(2,1)S(1)} %bitcast.14), kind=kLoop, calls=%fused_computation.5 | loop fusion | bytes 1572864 | tf_op jit(solution)/shard_map/slice | solution.py:147
  5.7 0.0 copy-done
  5.7 5.7 %collective-permute-start.3 = (bf16[4,2,96,256]{3,2,1,0:T(8,128)(2,1)}, bf16[4,2,96,256]{3,2,1,0:T(8,128)(2,1)S(1)}, u32[]{:S(2)}, u32[]{:S(2)}) collective-permute-start(bf16[4,2,96,256]{3,2,1,0:T(8,128)(2,1)} %get-tuple-element.3), channel_id=1, source_target_pairs={{0,1},{1,2},{2,3},{4,5},{5,6},{6,7},{8,9},{9,10},{10,11},{12,13},{... | collective-permute-start | bytes 1179656 | tf_op jit(solution)/shard_map/ppermute | solution.py:16
  11.4 0.0 copy-start.2
  11.4 2.1 %collective-permute-start.4 = (bf16[4,2,96,256]{3,2,1,0:T(8,128)(2,1)}, bf16[4,2,96,256]{3,2,1,0:T(8,128)(2,1)S(1)}, u32[]{:S(2)}, u32[]{:S(2)}) collective-permute-start(bf16[4,2,96,256]{3,2,1,0:T(8,128)(2,1)} %get-tuple-element.2), channel_id=1, source_target_pairs={{1,0},{2,1},{3,2},{5,4},{6,5},{7,6},{9,8},{10,9},{11,10},{13,12},{... | collective-permute-start | bytes 1179656 | tf_op jit(solution)/shard_map/ppermute | solution.py:16
  13.4 8.8 %collective-permute-done.pv_ref = bf16[4,4,96,256]{3,2,1,0:T(8,128)(2,1)S(1)} collective-permute-done((bf16[4,4,96,256]{3,2,1,0:T(8,128)(2,1)S(1)}, bf16[4,4,96,256]{3,2,1,0:T(8,128)(2,1)S(1)}, u32[]{:S(2)}, u32[]{:S(2)}) %collective-permute-start) | collective-permute-done | bytes 786464 | tf_op jit(solution)/shard_map/ppermute | solution.py:19
  22.2 1.0 %fusion.1 = (bf16[4,2,96,256]{3,2,1,0:T(8,128)(2,1)}, bf16[4,2,96,256]{3,2,1,0:T(8,128)(2,1)}) fusion(bf16[4,4,96,256]{3,2,1,0:T(8,128)(2,1)S(1)} %collective-permute-done.pv_ref), kind=kLoop, calls=%fused_computation.6 | loop fusion | bytes 1572864 | tf_op jit(solution)/shard_map/slice | solution.py:152
  23.2 0.1 copy-done.1
  23.3 6.2 %collective-permute-start.1 = (bf16[4,2,96,256]{3,2,1,0:T(8,128)(2,1)}, bf16[4,2,96,256]{3,2,1,0:T(8,128)(2,1)S(1)}, u32[]{:S(2)}, u32[]{:S(2)}) collective-permute-start(bf16[4,2,96,256]{3,2,1,0:T(8,128)(2,1)} %get-tuple-element.5), channel_id=1, source_target_pairs={{0,1},{1,2},{2,3},{4,5},{5,6},{6,7},{8,9},{9,10},{10,11},{12,13},{... | collective-permute-start | bytes 1179656 | tf_op jit(solution)/shard_map/ppermute | solution.py:16
  29.6 1.9 %collective-permute-start.2 = (bf16[4,2,96,256]{3,2,1,0:T(8,128)(2,1)}, bf16[4,2,96,256]{3,2,1,0:T(8,128)(2,1)}, u32[]{:S(2)}, u32[]{:S(2)}) collective-permute-start(bf16[4,2,96,256]{3,2,1,0:T(8,128)(2,1)} %get-tuple-element.4), channel_id=1, source_target_pairs={{1,0},{2,1},{3,2},{5,4},{6,5},{7,6},{9,8},{10,9},{11,10},{13,12},{... | collective-permute-start | bytes 1179656 | tf_op jit(solution)/shard_map/ppermute | solution.py:16
  31.5 0.0 copy-done.2
  31.5 0.5 copy.23
  32.0 0.0 copy-start.3
  32.0 1.3 %reshape.16.k1_ref = bf16[288,864]{1,0:T(8,128)(2,1)} reshape(bf16[3,96,3,3,96]{4,3,2,1,0:T(4,128)(2,1)S(1)} %copy.23) | data formatting | bytes 995328 | tf_op jit(solution)/shard_map/reshape | solution.py:31
  33.3 0.0 copy-done.3
  33.3 0.5 copy.24
  33.8 1.3 %reshape.17.k2_ref = bf16[288,864]{1,0:T(8,128)(2,1)} reshape(bf16[3,96,3,3,96]{4,3,2,1,0:T(4,128)(2,1)S(1)} %copy.24) | data formatting | bytes 995328 | tf_op jit(solution)/shard_map/reshape | solution.py:31
  35.1 0.7 copy-done.14
  35.7 0.7 copy.25.bias_ref
  36.5 0.7 copy-done.15
  37.1 0.7 copy.26.gain_ref
  37.8 0.7 and_convert_fusion.mask_ref
  38.5 0.0 collective-permute-done.3.tp_ref
  38.5 0.0 collective-permute-done.4.bt_ref
  38.5 0.0 copy-start.6
  38.5 0.0 collective-permute-done.1.tc_ref
  38.5 0.0 copy-start.7
  38.5 2.0 %collective-permute-done.2.bc_ref = bf16[4,2,96,256]{3,2,1,0:T(8,128)(2,1)} collective-permute-done((bf16[4,2,96,256]{3,2,1,0:T(8,128)(2,1)}, bf16[4,2,96,256]{3,2,1,0:T(8,128)(2,1)}, u32[]{:S(2)}, u32[]{:S(2)}) %collective-permute-start.2) | collective-permute-done | bytes 393248 | tf_op jit(solution)/shard_map/ppermute | solution.py:16
  40.5 0.0 copy-done.5
  40.5 0.0 copy-done.6
  40.5 0.0 copy-done.7
  40.5 11.9 %shard_map.122 = bf16[1,16,4,256]{3,2,1,0:T(4,128)(2,1)} custom-call(bf16[4,2,96,256]{3,2,1,0:T(8,128)(2,1)} %copy-done.7, bf16[4,4,96,256]{3,2,1,0:T(8,128)(2,1)} %copy-done.1, bf16[4,2,96,256]{3,2,1,0:T(8,128)(2,1)} %collective-permute-done.2.bc_ref, bf16[4,2,96,256]{3,2,1,0:T(8,128)(2,1)} %copy-done.5, bf16[4,4,96,256]{3,2,1,0:T(8,128)(2,1)} %bitcast.15, ...), custom_call_target="tpu_custom_call" | custom-call | tf_op jit(solution)/shard_map/pallas_call | solution.py:166
  52.4 0.9 fusion.2
  53.3 4.1 %collective-permute-start.5 = (bf16[1,16,2,256]{3,2,1,0:T(2,128)(2,1)S(1)}, bf16[1,16,2,256]{3,2,1,0:T(2,128)(2,1)S(1)}, u32[]{:S(2)}, u32[]{:S(2)}) collective-permute-start(bf16[1,16,2,256]{3,2,1,0:T(2,128)(2,1)S(1)} %get-tuple-element.6), channel_id=1, source_target_pairs={{0,1},{1,2},{2,3},{4,5},{5,6},{6,7},{8,9},{9,10},{10,11},{12,13},{... | collective-permute-start | bytes 49160 | tf_op jit(solution)/shard_map/ppermute | solution.py:16
  57.4 1.9 %collective-permute-start.6 = (bf16[1,16,2,256]{3,2,1,0:T(2,128)(2,1)S(1)}, bf16[1,16,2,256]{3,2,1,0:T(2,128)(2,1)S(1)}, u32[]{:S(2)}, u32[]{:S(2)}) collective-permute-start(bf16[1,16,2,256]{3,2,1,0:T(2,128)(2,1)S(1)} %get-tuple-element.7), channel_id=1, source_target_pairs={{1,0},{2,1},{3,2},{5,4},{6,5},{7,6},{9,8},{10,9},{11,10},{13,12},{... | collective-permute-start | bytes 49160 | tf_op jit(solution)/shard_map/ppermute | solution.py:16
  59.4 0.0 collective-permute-done.5
  59.4 4.6 %collective-permute-done.6 = bf16[1,16,2,256]{3,2,1,0:T(2,128)(2,1)S(1)} collective-permute-done((bf16[1,16,2,256]{3,2,1,0:T(2,128)(2,1)S(1)}, bf16[1,16,2,256]{3,2,1,0:T(2,128)(2,1)S(1)}, u32[]{:S(2)}, u32[]{:S(2)}) %collective-permute-start.6) | collective-permute-done | bytes 16416 | tf_op jit(solution)/shard_map/ppermute | solution.py:16
  64.0 0.1 pad_maximum_fusion.l0_ref
  64.1 0.0 copy-start.9
  64.1 3.5 %collective-permute-start.7 = (bf16[1,16,8,256]{3,2,1,0:T(8,128)(2,1)S(1)}, bf16[1,16,8,256]{3,2,1,0:T(8,128)(2,1)S(1)}, u32[]{:S(2)}, u32[]{:S(2)}) collective-permute-start(bf16[1,16,8,256]{3,2,1,0:T(8,128)(2,1)S(1)} %pad_maximum_fusion.l0_ref), channel_id=1, source_target_pairs={{0,12},{4,16},{8,20},{12,24},{16,28},{20,32},{24,36},{28,40},{32,4... | collective-permute-start | bytes 196616 | tf_op jit(solution)/shard_map/ppermute | solution.py:19
  67.6 4.4 %collective-permute-start.8 = (bf16[1,16,8,256]{3,2,1,0:T(8,128)(2,1)S(1)}, bf16[1,16,8,256]{3,2,1,0:T(8,128)(2,1)S(1)}, u32[]{:S(2)}, u32[]{:S(2)}) collective-permute-start(bf16[1,16,8,256]{3,2,1,0:T(8,128)(2,1)S(1)} %pad_maximum_fusion.l0_ref), channel_id=1, source_target_pairs={{0,8},{4,12},{8,16},{12,20},{16,24},{20,28},{24,32},{28,36},{32,40... | collective-permute-start | bytes 196616 | tf_op jit(solution)/shard_map/ppermute | solution.py:19
  72.0 5.1 %collective-permute-start.9 = (bf16[1,16,8,256]{3,2,1,0:T(8,128)(2,1)S(1)}, bf16[1,16,8,256]{3,2,1,0:T(8,128)(2,1)S(1)}, u32[]{:S(2)}, u32[]{:S(2)}) collective-permute-start(bf16[1,16,8,256]{3,2,1,0:T(8,128)(2,1)S(1)} %pad_maximum_fusion.l0_ref), channel_id=1, source_target_pairs={{0,4},{4,8},{8,12},{12,16},{16,20},{20,24},{24,28},{28,32},{32,36}... | collective-permute-start | bytes 196616 | tf_op jit(solution)/shard_map/ppermute | solution.py:19
  77.1 0.0 copy-done.4
  77.1 0.5 copy.28
  77.6 0.0 copy-done.9
  77.6 0.0 copy-start.10
  77.6 1.3 %reshape.19.fk_ref = bf16[288,864]{1,0:T(8,128)(2,1)} reshape(bf16[3,96,3,3,96]{4,3,2,1,0:T(4,128)(2,1)S(1)} %copy.28) | data formatting | bytes 995328 | tf_op jit(solution)/shard_map/reshape | solution.py:31
  78.9 0.1 copy.27
  79.0 0.1 reshape.18
  79.1 0.8 copy.29.dk_ref
  79.9 0.7 copy-done.16
  80.6 0.7 copy.30.bias_ref
  81.3 0.7 copy-done.17
  82.0 0.7 copy.31.gain_ref
  82.7 0.0 collective-permute-done.7.l3_ref
  82.7 0.0 collective-permute-done.8.l2_ref
  82.7 0.0 collective-permute-done.9.l1_ref
  82.7 0.6 copy-done.11
  83.3 0.0 copy-done.12
  83.3 0.6 copy-done.13
  84.0 7.9 %shard_map.123 = bf16[4,96,4,256]{3,2,1,0:T(4,128)(2,1)} custom-call(bf16[1,16,8,256]{3,2,1,0:T(8,128)(2,1)} %copy-done.11, bf16[1,16,8,256]{3,2,1,0:T(8,128)(2,1)} %copy-done.12, bf16[1,16,8,256]{3,2,1,0:T(8,128)(2,1)} %copy-done.13, bf16[1,16,8,256]{3,2,1,0:T(8,128)(2,1)} %copy-done.9, bf16[288,144]{1,0:T(8,128)(2,1)} %copy.29.dk_ref, ...), custom_call_target="tpu_custom_call" | custom-call | tf_op jit(solution)/shard_map/pallas_call | solution.py:184
  (14 shorter events, 0.0 us)
Async XLA Ops:
  1.9 3.8 %copy-start = (bf16[4,96,4,256]{3,1,2,0:T(8,128)(2,1)}, bf16[4,96,4,256]{3,1,2,0:T(8,128)(2,1)S(1)}, u32[]{:S(2)}) copy-start(bf16[4,96,4,256]{3,1,2,0:T(8,128)(2,1)S(1)} %copy.33) | copy-start | bytes 2359300
  1.9 20.3 %collective-permute-start = (bf16[4,4,96,256]{3,2,1,0:T(8,128)(2,1)S(1)}, bf16[4,4,96,256]{3,2,1,0:T(8,128)(2,1)S(1)}, u32[]{:S(2)}, u32[]{:S(2)}) collective-permute-start(bf16[4,4,96,256]{3,2,1,0:T(8,128)(2,1)S(1)} %bitcast.13), channel_id=1, source_target_pairs={{0,4},{4,8},{8,12},{12,16},{16,20},{20,24},{24,28},{28,32},{32,36}... | collective-permute-start | bytes 2359304 | tf_op jit(solution)/shard_map/ppermute | solution.py:19
  5.7 32.8 %collective-permute-start.3 = (bf16[4,2,96,256]{3,2,1,0:T(8,128)(2,1)}, bf16[4,2,96,256]{3,2,1,0:T(8,128)(2,1)S(1)}, u32[]{:S(2)}, u32[]{:S(2)}) collective-permute-start(bf16[4,2,96,256]{3,2,1,0:T(8,128)(2,1)} %get-tuple-element.3), channel_id=1, source_target_pairs={{0,1},{1,2},{2,3},{4,5},{5,6},{6,7},{8,9},{9,10},{10,11},{12,13},{... | collective-permute-start | bytes 1179656 | tf_op jit(solution)/shard_map/ppermute | solution.py:16
  11.4 20.2 %copy-start.2 = (bf16[3,3,3,96,96]{4,3,2,1,0:T(8,128)(2,1)S(1)}, bf16[3,3,3,96,96]{4,3,2,1,0:T(8,128)(2,1)}, u32[]{:S(2)}) copy-start(bf16[3,3,3,96,96]{4,3,2,1,0:T(8,128)(2,1)} %param.12) | copy-start | bytes 1492996
  11.4 27.1 %collective-permute-start.4 = (bf16[4,2,96,256]{3,2,1,0:T(8,128)(2,1)}, bf16[4,2,96,256]{3,2,1,0:T(8,128)(2,1)S(1)}, u32[]{:S(2)}, u32[]{:S(2)}) collective-permute-start(bf16[4,2,96,256]{3,2,1,0:T(8,128)(2,1)} %get-tuple-element.2), channel_id=1, source_target_pairs={{1,0},{2,1},{3,2},{5,4},{6,5},{7,6},{9,8},{10,9},{11,10},{13,12},{... | collective-permute-start | bytes 1179656 | tf_op jit(solution)/shard_map/ppermute | solution.py:16
  22.2 1.1 %copy-start.1 = (bf16[4,4,96,256]{3,2,1,0:T(8,128)(2,1)}, bf16[4,4,96,256]{3,2,1,0:T(8,128)(2,1)S(1)}, u32[]{:S(2)}) copy-start(bf16[4,4,96,256]{3,2,1,0:T(8,128)(2,1)S(1)} %collective-permute-done.pv_ref) | copy-start | bytes 2359300
  23.3 15.2 %collective-permute-start.1 = (bf16[4,2,96,256]{3,2,1,0:T(8,128)(2,1)}, bf16[4,2,96,256]{3,2,1,0:T(8,128)(2,1)S(1)}, u32[]{:S(2)}, u32[]{:S(2)}) collective-permute-start(bf16[4,2,96,256]{3,2,1,0:T(8,128)(2,1)} %get-tuple-element.5), channel_id=1, source_target_pairs={{0,1},{1,2},{2,3},{4,5},{5,6},{6,7},{8,9},{9,10},{10,11},{12,13},{... | collective-permute-start | bytes 1179656 | tf_op jit(solution)/shard_map/ppermute | solution.py:16
  29.6 10.9 %collective-permute-start.2 = (bf16[4,2,96,256]{3,2,1,0:T(8,128)(2,1)}, bf16[4,2,96,256]{3,2,1,0:T(8,128)(2,1)}, u32[]{:S(2)}, u32[]{:S(2)}) collective-permute-start(bf16[4,2,96,256]{3,2,1,0:T(8,128)(2,1)} %get-tuple-element.4), channel_id=1, source_target_pairs={{1,0},{2,1},{3,2},{5,4},{6,5},{7,6},{9,8},{10,9},{11,10},{13,12},{... | collective-permute-start | bytes 1179656 | tf_op jit(solution)/shard_map/ppermute | solution.py:16
  32.0 1.3 %copy-start.3 = (bf16[3,3,3,96,96]{4,3,2,1,0:T(8,128)(2,1)S(1)}, bf16[3,3,3,96,96]{4,3,2,1,0:T(8,128)(2,1)}, u32[]{:S(2)}) copy-start(bf16[3,3,3,96,96]{4,3,2,1,0:T(8,128)(2,1)} %param.15) | copy-start | bytes 1492996
  35.1 0.7 copy-start.14
  36.5 0.7 copy-start.15
  38.5 38.6 %copy-start.4 = (bf16[3,3,3,96,96]{4,3,2,1,0:T(8,128)(2,1)S(1)}, bf16[3,3,3,96,96]{4,3,2,1,0:T(8,128)(2,1)}, u32[]{:S(2)}) copy-start(bf16[3,3,3,96,96]{4,3,2,1,0:T(8,128)(2,1)} %param.21) | copy-start | bytes 1492996
  38.5 2.0 %copy-start.5 = (bf16[4,2,96,256]{3,2,1,0:T(8,128)(2,1)}, bf16[4,2,96,256]{3,2,1,0:T(8,128)(2,1)S(1)}, u32[]{:S(2)}) copy-start(bf16[4,2,96,256]{3,2,1,0:T(8,128)(2,1)S(1)} %collective-permute-done.3.tp_ref) | copy-start | bytes 1179652
  38.5 2.0 %copy-start.6 = (bf16[4,2,96,256]{3,2,1,0:T(8,128)(2,1)}, bf16[4,2,96,256]{3,2,1,0:T(8,128)(2,1)S(1)}, u32[]{:S(2)}) copy-start(bf16[4,2,96,256]{3,2,1,0:T(8,128)(2,1)S(1)} %collective-permute-done.4.bt_ref) | copy-start | bytes 1179652
  38.5 2.0 %copy-start.7 = (bf16[4,2,96,256]{3,2,1,0:T(8,128)(2,1)}, bf16[4,2,96,256]{3,2,1,0:T(8,128)(2,1)S(1)}, u32[]{:S(2)}) copy-start(bf16[4,2,96,256]{3,2,1,0:T(8,128)(2,1)S(1)} %collective-permute-done.1.tc_ref) | copy-start | bytes 1179652
  52.4 11.6 %copy-start.8 = (bf16[1,16,4,256]{3,2,1,0:T(4,128)(2,1)S(1)}, bf16[1,16,4,256]{3,2,1,0:T(4,128)(2,1)}, u32[]{:S(2)}) copy-start(bf16[1,16,4,256]{3,2,1,0:T(4,128)(2,1)} %shard_map.122) | copy-start | bytes 98308
  53.3 6.1 %collective-permute-start.5 = (bf16[1,16,2,256]{3,2,1,0:T(2,128)(2,1)S(1)}, bf16[1,16,2,256]{3,2,1,0:T(2,128)(2,1)S(1)}, u32[]{:S(2)}, u32[]{:S(2)}) collective-permute-start(bf16[1,16,2,256]{3,2,1,0:T(2,128)(2,1)S(1)} %get-tuple-element.6), channel_id=1, source_target_pairs={{0,1},{1,2},{2,3},{4,5},{5,6},{6,7},{8,9},{9,10},{10,11},{12,13},{... | collective-permute-start | bytes 49160 | tf_op jit(solution)/shard_map/ppermute | solution.py:16
  57.4 6.6 %collective-permute-start.6 = (bf16[1,16,2,256]{3,2,1,0:T(2,128)(2,1)S(1)}, bf16[1,16,2,256]{3,2,1,0:T(2,128)(2,1)S(1)}, u32[]{:S(2)}, u32[]{:S(2)}) collective-permute-start(bf16[1,16,2,256]{3,2,1,0:T(2,128)(2,1)S(1)} %get-tuple-element.7), channel_id=1, source_target_pairs={{1,0},{2,1},{3,2},{5,4},{6,5},{7,6},{9,8},{10,9},{11,10},{13,12},{... | collective-permute-start | bytes 49160 | tf_op jit(solution)/shard_map/ppermute | solution.py:16
  64.1 13.5 %copy-start.9 = (bf16[1,16,8,256]{3,2,1,0:T(8,128)(2,1)}, bf16[1,16,8,256]{3,2,1,0:T(8,128)(2,1)S(1)}, u32[]{:S(2)}) copy-start(bf16[1,16,8,256]{3,2,1,0:T(8,128)(2,1)S(1)} %pad_maximum_fusion.l0_ref) | copy-start | bytes 196612
  64.1 18.6 %collective-permute-start.7 = (bf16[1,16,8,256]{3,2,1,0:T(8,128)(2,1)S(1)}, bf16[1,16,8,256]{3,2,1,0:T(8,128)(2,1)S(1)}, u32[]{:S(2)}, u32[]{:S(2)}) collective-permute-start(bf16[1,16,8,256]{3,2,1,0:T(8,128)(2,1)S(1)} %pad_maximum_fusion.l0_ref), channel_id=1, source_target_pairs={{0,12},{4,16},{8,20},{12,24},{16,28},{20,32},{24,36},{28,40},{32,4... | collective-permute-start | bytes 196616 | tf_op jit(solution)/shard_map/ppermute | solution.py:19
  67.6 15.1 %collective-permute-start.8 = (bf16[1,16,8,256]{3,2,1,0:T(8,128)(2,1)S(1)}, bf16[1,16,8,256]{3,2,1,0:T(8,128)(2,1)S(1)}, u32[]{:S(2)}, u32[]{:S(2)}) collective-permute-start(bf16[1,16,8,256]{3,2,1,0:T(8,128)(2,1)S(1)} %pad_maximum_fusion.l0_ref), channel_id=1, source_target_pairs={{0,8},{4,12},{8,16},{12,20},{16,24},{20,28},{24,32},{28,36},{32,40... | collective-permute-start | bytes 196616 | tf_op jit(solution)/shard_map/ppermute | solution.py:19
  72.0 10.7 %collective-permute-start.9 = (bf16[1,16,8,256]{3,2,1,0:T(8,128)(2,1)S(1)}, bf16[1,16,8,256]{3,2,1,0:T(8,128)(2,1)S(1)}, u32[]{:S(2)}, u32[]{:S(2)}) collective-permute-start(bf16[1,16,8,256]{3,2,1,0:T(8,128)(2,1)S(1)} %pad_maximum_fusion.l0_ref), channel_id=1, source_target_pairs={{0,4},{4,8},{8,12},{12,16},{16,20},{20,24},{24,28},{28,32},{32,36}... | collective-permute-start | bytes 196616 | tf_op jit(solution)/shard_map/ppermute | solution.py:19
  77.6 1.3 %copy-start.10 = (bf16[3,3,3,96,16]{3,4,2,1,0:T(8,128)(2,1)S(1)}, bf16[3,3,3,96,16]{3,4,2,1,0:T(8,128)(2,1)}, u32[]{:S(2)}) copy-start(bf16[3,3,3,96,16]{3,4,2,1,0:T(8,128)(2,1)} %param.17) | copy-start | bytes 248836
  79.9 0.7 copy-start.16
  81.3 0.7 copy-start.17
  82.7 0.6 copy-start.11
  82.7 0.7 copy-start.12
  83.3 0.6 copy-start.13

commit v6 on v5

--- a/solution.py
+++ b/solution.py
@@ -71,12 +71,12 @@
 
 def encoder_kernel(
     tc_ref, pv_ref, bc_ref, tp_ref, own_ref, bt_ref,
-    k1_ref, bias_ref, gain_ref, mask_ref, k2_ref, w_ref, o_ref, g_ref,
+    k1_ref, vec_ref, mask_ref, k2_ref, w_ref, o_ref, g_ref,
     *, frames, rows, columns
 ):
     wide = rows + 2
-    bias = bias_ref[...]
-    gain = gain_ref[...]
+    bias = vec_ref[:, 0:1]
+    gain = vec_ref[:, 1:2]
     x = tiled([(tc_ref, pv_ref, bc_ref), (tp_ref, own_ref, bt_ref)], frames, 2, rows)
     for t in range(frames + 2):
         y = tap_sum(x, k1_ref, t, wide, columns) + bias
@@ -98,12 +98,12 @@
 
 
 def decode_kernel_body(
-    l3_ref, l2_ref, l1_ref, l0_ref, dk_ref, bias_ref, gain_ref, up_ref, mask_ref, fk_ref, o_ref, ext_ref,
+    l3_ref, l2_ref, l1_ref, l0_ref, dk_ref, vec_ref, up_ref, mask_ref, fk_ref, o_ref, ext_ref,
     *, frames, rows, columns
 ):
     wide = rows + 2
-    bias = bias_ref[...]
-    gain = gain_ref[...]
+    bias = vec_ref[:, 2:3]
+    gain = vec_ref[:, 3:4]
     lat_refs = (l3_ref, l2_ref, l1_ref, l0_ref)
     lat = lambda t, r: lat_refs[t][0, :, r, :]
     for f in range(2):
@@ -146,35 +146,45 @@
     top = own[:, -2:]
     bottom = own[:, :2]
     previous = shift(own, 1, 0)
-    pieces = [
-        shift(previous[:, -2:], 0, 1),
-        previous,
-        shift(previous[:, :2], 0, -1),
-        shift(top, 0, 1),
-        own,
-        shift(bottom, 0, -1),
-    ]
     band = lax.axis_index("rows")
     bands = lax.axis_size("rows")
     row_ids = lax.broadcasted_iota(jnp.int32, (frames + 2, rows + 2), 1)
     frame_ids = lax.broadcasted_iota(jnp.int32, (frames + 2, rows + 2), 0)
     inside = ((row_ids > 0) | (band > 0)) & ((row_ids < rows + 1) | (band < bands - 1))
     inside = inside & ((frame_ids >= 2) | (lax.axis_index("tm") > 0))
-    mask = inside.astype(jnp.float32)
+    params = (
+        merged_kernel(first_kernel),
+        merged_kernel(second_kernel),
+        merged_kernel(decode_kernel),
+        merged_kernel(final_kernel),
+        jnp.stack([first_bias, first_gain, decode_bias, decode_gain], 1),
+        inside.astype(jnp.float32),
+    )
+    prev_top, prev_bottom, *params = lax.optimization_barrier(
+        (previous[:, -2:], previous[:, :2], *params)
+    )
+    k1, k2, dk, fk, vec, mask = params
+    pieces = [
+        shift(prev_top, 0, 1),
+        previous,
+        shift(prev_bottom, 0, -1),
+        shift(top, 0, 1),
+        own,
+        shift(bottom, 0, -1),
+    ]
     vmem = pl.BlockSpec(memory_space=pltpu.VMEM)
     smem = pl.BlockSpec(memory_space=pltpu.SMEM)
     latent = pl.pallas_call(
         functools.partial(encoder_kernel, **dims),
         out_shape=jax.ShapeDtypeStruct((1, z_count, rows, columns), jnp.bfloat16),
-        in_specs=[vmem] * 9 + [smem, vmem, vmem],
+        in_specs=[vmem] * 8 + [smem, vmem, vmem],
         scratch_shapes=[pltpu.VMEM((frames + 2, rows + 2, channels, columns), jnp.bfloat16)],
     )(
         *pieces,
-        merged_kernel(first_kernel),
-        first_bias[:, None],
-        first_gain[:, None],
+        k1,
+        vec,
         mask,
-        merged_kernel(second_kernel),
+        k2,
         latent_weight,
     )
     lat_rows = jnp.concatenate(
@@ -184,16 +194,15 @@
     rebuilt = pl.pallas_call(
         functools.partial(decode_kernel_body, **dims),
         out_shape=jax.ShapeDtypeStruct((frames, channels, rows, columns), jnp.bfloat16),
-        in_specs=[vmem] * 8 + [smem, vmem],
+        in_specs=[vmem] * 7 + [smem, vmem],
         scratch_shapes=[pltpu.VMEM((frames + 2, rows + 2, channels, columns), jnp.bfloat16)],
     )(
         *lat_frames,
-        merged_kernel(decode_kernel),
-        decode_bias[:, None],
-        decode_gain[:, None],
+        dk,
+        vec,
         upsample_weight,
         mask,
-        merged_kernel(final_kernel),
+        fk,
     )
     return (latent, rebuilt)
 

time: 92.4 us -> 90.1 us (0.975)
  the two profiles are of different devices: /device:TPU:5 before, /device:TPU:24 now
where the time goes in v6:
time: 90.1 us; the launch traced here: 89.6 us
  starting transfers between devices  31.8 us (35%)
  waiting for transfers between devices  23.4 us (26%)
  Pallas kernels  19.7 us (22%)
  local copies, waits for them, and re-layouts  13 us (14%)
    ppermute x6, starting transfers between devices, shift(): return lax.ppermute(x, 'rows', pairs)  21.4 us
    ppermute x4, waiting for transfers between devices, shift(): return lax.ppermute(x, 'tm', pairs)  14.2 us
    pallas_call x1, Pallas kernels, body(): pl.pallas_call(functools.partial(encoder_kernel, **dims), out_shape=jax.S...  11.9 us
    ppermute x4, starting transfers between devices, shift(): return lax.ppermute(x, 'tm', pairs)  10.5 us
    ppermute x6, waiting for transfers between devices, shift(): return lax.ppermute(x, 'rows', pairs)  9.18 us
    pallas_call x1, Pallas kernels, body(): pl.pallas_call(functools.partial(decode_kernel_body, **dims), out_shape=j...  7.88 us
    unnamed x35, local copies, waits for them, and re-layouts  4.14 us
    reshape x4, local copies, waits for them, and re-layouts, merged_kernel(): return kernel.transpose(2, 3, 0, 1, 4).reshape(3 * o, 9 * c)  4.06 us
  transfers between devices with their start and end apart: 10, of which 7 were waited for; matrix products, arithmetic and copies ran while one was open for 10% of the time, Pallas kernels for 0%

profile of v6, /device:TPU:24, one launch (start us, length us, event | category | flops | bytes accessed | tf_op | source)
XLA Modules:
  0.0 89.6 jit_solution(3868322294925590357)
XLA Ops:
  0.6 1.3 %copy.41 = bf16[4,96,4,256]{3,1,2,0:T(8,128)(2,1)S(1)} copy(bf16[4,96,4,256]{3,2,1,0:T(4,128)(2,1)} %param.11) | data formatting | bytes 1572864 | tf_op args[0]
  1.9 0.0 copy-start
  1.9 0.0 copy-start.2
  1.9 3.5 %collective-permute-start = (bf16[4,4,96,256]{3,2,1,0:T(8,128)(2,1)S(1)}, bf16[4,4,96,256]{3,2,1,0:T(8,128)(2,1)S(1)}, u32[]{:S(2)}, u32[]{:S(2)}) collective-permute-start(bf16[4,4,96,256]{3,2,1,0:T(8,128)(2,1)S(1)} %bitcast.13), channel_id=1, source_target_pairs={{0,4},{4,8},{8,12},{12,16},{16,20},{20,24},{24,28},{28,32},{32,36}... | collective-permute-start | bytes 2359304 | tf_op jit(solution)/shard_map/ppermute | solution.py:19
  5.5 1.0 %fusion = (bf16[4,2,96,256]{3,2,1,0:T(8,128)(2,1)}, bf16[4,2,96,256]{3,2,1,0:T(8,128)(2,1)}) fusion(bf16[4,4,96,256]{3,2,1,0:T(8,128)(2,1)S(1)} %bitcast.14), kind=kLoop, calls=%fused_computation.6 | loop fusion | bytes 1572864 | tf_op jit(solution)/shard_map/slice | solution.py:147
  6.4 0.0 copy-done
  6.4 1.9 %collective-permute-start.3 = (bf16[4,2,96,256]{3,2,1,0:T(8,128)(2,1)}, bf16[4,2,96,256]{3,2,1,0:T(8,128)(2,1)}, u32[]{:S(2)}, u32[]{:S(2)}) collective-permute-start(bf16[4,2,96,256]{3,2,1,0:T(8,128)(2,1)} %get-tuple-element.19), channel_id=1, source_target_pairs={{0,1},{1,2},{2,3},{4,5},{5,6},{6,7},{8,9},{9,10},{10,11},{12,13},{... | collective-permute-start | bytes 1179656 | tf_op jit(solution)/shard_map/ppermute | solution.py:16
  8.3 5.1 %collective-permute-start.4 = (bf16[4,2,96,256]{3,2,1,0:T(8,128)(2,1)}, bf16[4,2,96,256]{3,2,1,0:T(8,128)(2,1)}, u32[]{:S(2)}, u32[]{:S(2)}) collective-permute-start(bf16[4,2,96,256]{3,2,1,0:T(8,128)(2,1)} %get-tuple-element.18), channel_id=1, source_target_pairs={{1,0},{2,1},{3,2},{5,4},{6,5},{7,6},{9,8},{10,9},{11,10},{13,12},{... | collective-permute-start | bytes 1179656 | tf_op jit(solution)/shard_map/ppermute | solution.py:16
  13.5 0.0 copy-done.2
  13.5 0.5 copy.33
  14.0 0.0 copy-start.3
  14.0 1.3 %reshape.16.k1_ref = bf16[288,864]{1,0:T(8,128)(2,1)} reshape(bf16[3,96,3,3,96]{4,3,2,1,0:T(4,128)(2,1)S(1)} %copy.33) | data formatting | bytes 995328 | tf_op jit(solution)/shard_map/reshape | solution.py:31
  15.3 0.0 copy-done.3
  15.3 0.5 copy.34
  15.8 0.0 copy-start.9
  15.8 0.0 copy-start.4
  15.8 1.3 %reshape.17.k2_ref = bf16[288,864]{1,0:T(8,128)(2,1)} reshape(bf16[3,96,3,3,96]{4,3,2,1,0:T(4,128)(2,1)S(1)} %copy.34) | data formatting | bytes 995328 | tf_op jit(solution)/shard_map/reshape | solution.py:31
  17.1 0.0 copy-done.9
  17.1 0.1 copy.35
  17.1 0.1 reshape.18
  17.3 0.0 copy-done.4
  17.3 0.5 copy.36
  17.8 0.0 copy-start.16
  17.8 1.3 %reshape.19.fk_ref = bf16[288,864]{1,0:T(8,128)(2,1)} reshape(bf16[3,96,3,3,96]{4,3,2,1,0:T(4,128)(2,1)S(1)} %copy.36) | data formatting | bytes 995328 | tf_op jit(solution)/shard_map/reshape | solution.py:31
  19.1 0.0 copy-start.13
  19.1 0.0 copy-start.14
  19.1 0.0 copy-start.15
  19.1 0.0 copy-done.16
  19.1 0.6 copy-done.13
  19.8 0.0 copy-done.14
  19.8 0.0 copy-done.15
  19.8 0.7 and_convert_fusion.mask_ref
  20.5 7.5 %collective-permute-done.pv_ref = bf16[4,4,96,256]{3,2,1,0:T(8,128)(2,1)S(1)} collective-permute-done((bf16[4,4,96,256]{3,2,1,0:T(8,128)(2,1)S(1)}, bf16[4,4,96,256]{3,2,1,0:T(8,128)(2,1)S(1)}, u32[]{:S(2)}, u32[]{:S(2)}) %collective-permute-start) | collective-permute-done | bytes 786464 | tf_op jit(solution)/shard_map/ppermute | solution.py:19
  28.0 0.1 fusion.1
  28.1 0.8 copy-done.1
  28.9 1.9 %collective-permute-start.1 = (bf16[4,2,96,256]{3,2,1,0:T(8,128)(2,1)S(1)}, bf16[4,2,96,256]{3,2,1,0:T(8,128)(2,1)S(1)}, u32[]{:S(2)}, u32[]{:S(2)}) collective-permute-start(bf16[4,2,96,256]{3,2,1,0:T(8,128)(2,1)S(1)} %get-tuple-element.10), channel_id=1, source_target_pairs={{0,1},{1,2},{2,3},{4,5},{5,6},{6,7},{8,9},{9,10},{10,11},{12,13},{... | collective-permute-start | bytes 1179656 | tf_op jit(solution)/shard_map/ppermute | solution.py:16
  30.8 5.1 %collective-permute-start.2 = (bf16[4,2,96,256]{3,2,1,0:T(8,128)(2,1)S(1)}, bf16[4,2,96,256]{3,2,1,0:T(8,128)(2,1)S(1)}, u32[]{:S(2)}, u32[]{:S(2)}) collective-permute-start(bf16[4,2,96,256]{3,2,1,0:T(8,128)(2,1)S(1)} %get-tuple-element.11), channel_id=1, source_target_pairs={{1,0},{2,1},{3,2},{5,4},{6,5},{7,6},{9,8},{10,9},{11,10},{13,12},{... | collective-permute-start | bytes 1179656 | tf_op jit(solution)/shard_map/ppermute | solution.py:16
  35.9 0.7 copy.37.vec_ref
  36.7 0.0 collective-permute-done.3.tp_ref
  36.7 0.0 collective-permute-done.4.bt_ref
  36.7 2.8 %collective-permute-done.1.tc_ref = bf16[4,2,96,256]{3,2,1,0:T(8,128)(2,1)S(1)} collective-permute-done((bf16[4,2,96,256]{3,2,1,0:T(8,128)(2,1)S(1)}, bf16[4,2,96,256]{3,2,1,0:T(8,128)(2,1)S(1)}, u32[]{:S(2)}, u32[]{:S(2)}) %collective-permute-start.1) | collective-permute-done | bytes 393248 | tf_op jit(solution)/shard_map/ppermute | solution.py:16
  39.5 1.8 %collective-permute-done.2.bc_ref = bf16[4,2,96,256]{3,2,1,0:T(8,128)(2,1)S(1)} collective-permute-done((bf16[4,2,96,256]{3,2,1,0:T(8,128)(2,1)S(1)}, bf16[4,2,96,256]{3,2,1,0:T(8,128)(2,1)S(1)}, u32[]{:S(2)}, u32[]{:S(2)}) %collective-permute-start.2) | collective-permute-done | bytes 393248 | tf_op jit(solution)/shard_map/ppermute | solution.py:16
  41.2 0.0 copy-done.5
  41.2 0.7 copy-done.6
  42.0 11.9 %shard_map.122 = bf16[1,16,4,256]{3,2,1,0:T(4,128)(2,1)} custom-call(bf16[4,2,96,256]{3,2,1,0:T(8,128)(2,1)} %copy-done.5, bf16[4,4,96,256]{3,2,1,0:T(8,128)(2,1)} %copy-done.1, bf16[4,2,96,256]{3,2,1,0:T(8,128)(2,1)} %copy-done.6, bf16[4,2,96,256]{3,2,1,0:T(8,128)(2,1)} %collective-permute-done.3.tp_ref, bf16[4,4,96,256]{3,2,1,0:T(8,128)(2,1)} %bitcast.15, ...), custom_call_target="tpu_custom_call" | custom-call | tf_op jit(solution)/shard_map/pallas_call | solution.py:177
  53.8 0.9 %fusion.2 = (bf16[1,16,2,256]{3,2,1,0:T(2,128)(2,1)S(1)}, bf16[1,16,2,256]{3,2,1,0:T(2,128)(2,1)S(1)}) fusion(bf16[1,16,4,256]{3,2,1,0:T(4,128)(2,1)} %shard_map.122), kind=kLoop, calls=%fused_computation.8 | loop fusion | bytes 65536 | tf_op jit(solution)/shard_map/slice | solution.py:191
  54.7 5.3 %collective-permute-start.6 = (bf16[1,16,2,256]{3,2,1,0:T(2,128)(2,1)S(1)}, bf16[1,16,2,256]{3,2,1,0:T(2,128)(2,1)S(1)}, u32[]{:S(2)}, u32[]{:S(2)}) collective-permute-start(bf16[1,16,2,256]{3,2,1,0:T(2,128)(2,1)S(1)} %get-tuple-element.23), channel_id=1, source_target_pairs={{1,0},{2,1},{3,2},{5,4},{6,5},{7,6},{9,8},{10,9},{11,10},{13,12},{... | collective-permute-start | bytes 49160 | tf_op jit(solution)/shard_map/ppermute | solution.py:16
  60.1 1.9 %collective-permute-start.5 = (bf16[1,16,2,256]{3,2,1,0:T(2,128)(2,1)S(1)}, bf16[1,16,2,256]{3,2,1,0:T(2,128)(2,1)S(1)}, u32[]{:S(2)}, u32[]{:S(2)}) collective-permute-start(bf16[1,16,2,256]{3,2,1,0:T(2,128)(2,1)S(1)} %get-tuple-element.22), channel_id=1, source_target_pairs={{0,1},{1,2},{2,3},{4,5},{5,6},{6,7},{8,9},{9,10},{10,11},{12,13},{... | collective-permute-start | bytes 49160 | tf_op jit(solution)/shard_map/ppermute | solution.py:16
  62.0 0.0 collective-permute-done.6
  62.0 4.6 %collective-permute-done.5 = bf16[1,16,2,256]{3,2,1,0:T(2,128)(2,1)S(1)} collective-permute-done((bf16[1,16,2,256]{3,2,1,0:T(2,128)(2,1)S(1)}, bf16[1,16,2,256]{3,2,1,0:T(2,128)(2,1)S(1)}, u32[]{:S(2)}, u32[]{:S(2)}) %collective-permute-start.5) | collective-permute-done | bytes 16416 | tf_op jit(solution)/shard_map/ppermute | solution.py:16
  66.6 0.0 copy-done.7
  66.6 0.1 pad_maximum_fusion.l0_ref
  66.7 0.0 copy-start.8
  66.7 1.9 %collective-permute-start.7 = (bf16[1,16,8,256]{3,2,1,0:T(8,128)(2,1)S(1)}, bf16[1,16,8,256]{3,2,1,0:T(8,128)(2,1)S(1)}, u32[]{:S(2)}, u32[]{:S(2)}) collective-permute-start(bf16[1,16,8,256]{3,2,1,0:T(8,128)(2,1)S(1)} %pad_maximum_fusion.l0_ref), channel_id=1, source_target_pairs={{0,12},{4,16},{8,20},{12,24},{16,28},{20,32},{24,36},{28,40},{32,4... | collective-permute-start | bytes 196616 | tf_op jit(solution)/shard_map/ppermute | solution.py:19
  68.6 2.0 %collective-permute-start.8 = (bf16[1,16,8,256]{3,2,1,0:T(8,128)(2,1)S(1)}, bf16[1,16,8,256]{3,2,1,0:T(8,128)(2,1)S(1)}, u32[]{:S(2)}, u32[]{:S(2)}) collective-permute-start(bf16[1,16,8,256]{3,2,1,0:T(8,128)(2,1)S(1)} %pad_maximum_fusion.l0_ref), channel_id=1, source_target_pairs={{0,8},{4,12},{8,16},{12,20},{16,24},{20,28},{24,32},{28,36},{32,40... | collective-permute-start | bytes 196616 | tf_op jit(solution)/shard_map/ppermute | solution.py:19
  70.7 3.0 %collective-permute-start.9 = (bf16[1,16,8,256]{3,2,1,0:T(8,128)(2,1)S(1)}, bf16[1,16,8,256]{3,2,1,0:T(8,128)(2,1)S(1)}, u32[]{:S(2)}, u32[]{:S(2)}) collective-permute-start(bf16[1,16,8,256]{3,2,1,0:T(8,128)(2,1)S(1)} %pad_maximum_fusion.l0_ref), channel_id=1, source_target_pairs={{0,4},{4,8},{8,12},{12,16},{16,20},{20,24},{24,28},{28,32},{32,36}... | collective-permute-start | bytes 196616 | tf_op jit(solution)/shard_map/ppermute | solution.py:19
  73.6 0.8 copy.38.dk_ref
  74.4 0.0 copy-done.8
  74.4 1.5 %collective-permute-done.7.l3_ref = bf16[1,16,8,256]{3,2,1,0:T(8,128)(2,1)S(1)} collective-permute-done((bf16[1,16,8,256]{3,2,1,0:T(8,128)(2,1)S(1)}, bf16[1,16,8,256]{3,2,1,0:T(8,128)(2,1)S(1)}, u32[]{:S(2)}, u32[]{:S(2)}) %collective-permute-start.7) | collective-permute-done | bytes 65568 | tf_op jit(solution)/shard_map/ppermute | solution.py:19
  75.9 3.4 %collective-permute-done.8.l2_ref = bf16[1,16,8,256]{3,2,1,0:T(8,128)(2,1)S(1)} collective-permute-done((bf16[1,16,8,256]{3,2,1,0:T(8,128)(2,1)S(1)}, bf16[1,16,8,256]{3,2,1,0:T(8,128)(2,1)S(1)}, u32[]{:S(2)}, u32[]{:S(2)}) %collective-permute-start.8) | collective-permute-done | bytes 65568 | tf_op jit(solution)/shard_map/ppermute | solution.py:19
  79.3 1.8 %collective-permute-done.9.l1_ref = bf16[1,16,8,256]{3,2,1,0:T(8,128)(2,1)S(1)} collective-permute-done((bf16[1,16,8,256]{3,2,1,0:T(8,128)(2,1)S(1)}, bf16[1,16,8,256]{3,2,1,0:T(8,128)(2,1)S(1)}, u32[]{:S(2)}, u32[]{:S(2)}) %collective-permute-start.9) | collective-permute-done | bytes 65568 | tf_op jit(solution)/shard_map/ppermute | solution.py:19
  81.1 0.0 copy-done.10
  81.1 0.6 copy-done.12
  81.7 7.9 %shard_map.123 = bf16[4,96,4,256]{3,2,1,0:T(4,128)(2,1)} custom-call(bf16[1,16,8,256]{3,2,1,0:T(8,128)(2,1)} %copy-done.10, bf16[1,16,8,256]{3,2,1,0:T(8,128)(2,1)} %copy-done.11, bf16[1,16,8,256]{3,2,1,0:T(8,128)(2,1)} %copy-done.12, bf16[1,16,8,256]{3,2,1,0:T(8,128)(2,1)} %copy-done.8, bf16[288,144]{1,0:T(8,128)(2,1)} %copy.38.dk_ref, ...), custom_call_target="tpu_custom_call" | custom-call | tf_op jit(solution)/shard_map/pallas_call | solution.py:194
  (10 shorter events, 0.0 us)
Async XLA Ops:
  1.9 4.5 %copy-start = (bf16[4,96,4,256]{3,1,2,0:T(8,128)(2,1)}, bf16[4,96,4,256]{3,1,2,0:T(8,128)(2,1)S(1)}, u32[]{:S(2)}) copy-start(bf16[4,96,4,256]{3,1,2,0:T(8,128)(2,1)S(1)} %copy.41) | copy-start | bytes 2359300
  1.9 11.6 %copy-start.2 = (bf16[3,3,3,96,96]{4,3,2,1,0:T(8,128)(2,1)S(1)}, bf16[3,3,3,96,96]{4,3,2,1,0:T(8,128)(2,1)}, u32[]{:S(2)}) copy-start(bf16[3,3,3,96,96]{4,3,2,1,0:T(8,128)(2,1)} %param.12) | copy-start | bytes 1492996
  1.9 26.1 %collective-permute-start = (bf16[4,4,96,256]{3,2,1,0:T(8,128)(2,1)S(1)}, bf16[4,4,96,256]{3,2,1,0:T(8,128)(2,1)S(1)}, u32[]{:S(2)}, u32[]{:S(2)}) collective-permute-start(bf16[4,4,96,256]{3,2,1,0:T(8,128)(2,1)S(1)} %bitcast.13), channel_id=1, source_target_pairs={{0,4},{4,8},{8,12},{12,16},{16,20},{20,24},{24,28},{28,32},{32,36}... | collective-permute-start | bytes 2359304 | tf_op jit(solution)/shard_map/ppermute | solution.py:19
  6.4 30.3 %collective-permute-start.3 = (bf16[4,2,96,256]{3,2,1,0:T(8,128)(2,1)}, bf16[4,2,96,256]{3,2,1,0:T(8,128)(2,1)}, u32[]{:S(2)}, u32[]{:S(2)}) collective-permute-start(bf16[4,2,96,256]{3,2,1,0:T(8,128)(2,1)} %get-tuple-element.19), channel_id=1, source_target_pairs={{0,1},{1,2},{2,3},{4,5},{5,6},{6,7},{8,9},{9,10},{10,11},{12,13},{... | collective-permute-start | bytes 1179656 | tf_op jit(solution)/shard_map/ppermute | solution.py:16
  8.3 28.3 %collective-permute-start.4 = (bf16[4,2,96,256]{3,2,1,0:T(8,128)(2,1)}, bf16[4,2,96,256]{3,2,1,0:T(8,128)(2,1)}, u32[]{:S(2)}, u32[]{:S(2)}) collective-permute-start(bf16[4,2,96,256]{3,2,1,0:T(8,128)(2,1)} %get-tuple-element.18), channel_id=1, source_target_pairs={{1,0},{2,1},{3,2},{5,4},{6,5},{7,6},{9,8},{10,9},{11,10},{13,12},{... | collective-permute-start | bytes 1179656 | tf_op jit(solution)/shard_map/ppermute | solution.py:16
  14.0 1.3 %copy-start.3 = (bf16[3,3,3,96,96]{4,3,2,1,0:T(8,128)(2,1)S(1)}, bf16[3,3,3,96,96]{4,3,2,1,0:T(8,128)(2,1)}, u32[]{:S(2)}) copy-start(bf16[3,3,3,96,96]{4,3,2,1,0:T(8,128)(2,1)} %param.15) | copy-start | bytes 1492996
  15.8 1.3 %copy-start.9 = (bf16[3,3,3,96,16]{3,4,2,1,0:T(8,128)(2,1)S(1)}, bf16[3,3,3,96,16]{3,4,2,1,0:T(8,128)(2,1)}, u32[]{:S(2)}) copy-start(bf16[3,3,3,96,16]{3,4,2,1,0:T(8,128)(2,1)} %param.17) | copy-start | bytes 248836
  15.8 1.5 %copy-start.4 = (bf16[3,3,3,96,96]{4,3,2,1,0:T(8,128)(2,1)S(1)}, bf16[3,3,3,96,96]{4,3,2,1,0:T(8,128)(2,1)}, u32[]{:S(2)}) copy-start(bf16[3,3,3,96,96]{4,3,2,1,0:T(8,128)(2,1)} %param.21) | copy-start | bytes 1492996
  17.8 1.4 %copy-start.16 = (f32[96]{0:T(128)S(1)}, f32[96]{0:T(128)}, u32[]{:S(2)}) copy-start(f32[96]{0:T(128)} %param.13) | copy-start | bytes 1156
  19.1 0.7 copy-start.13
  19.1 0.7 copy-start.14
  19.1 0.7 copy-start.15
  28.0 0.9 copy-start.1
  28.9 10.6 %collective-permute-start.1 = (bf16[4,2,96,256]{3,2,1,0:T(8,128)(2,1)S(1)}, bf16[4,2,96,256]{3,2,1,0:T(8,128)(2,1)S(1)}, u32[]{:S(2)}, u32[]{:S(2)}) collective-permute-start(bf16[4,2,96,256]{3,2,1,0:T(8,128)(2,1)S(1)} %get-tuple-element.10), channel_id=1, source_target_pairs={{0,1},{1,2},{2,3},{4,5},{5,6},{6,7},{8,9},{9,10},{10,11},{12,13},{... | collective-permute-start | bytes 1179656 | tf_op jit(solution)/shard_map/ppermute | solution.py:16
  30.8 10.4 %collective-permute-start.2 = (bf16[4,2,96,256]{3,2,1,0:T(8,128)(2,1)S(1)}, bf16[4,2,96,256]{3,2,1,0:T(8,128)(2,1)S(1)}, u32[]{:S(2)}, u32[]{:S(2)}) collective-permute-start(bf16[4,2,96,256]{3,2,1,0:T(8,128)(2,1)S(1)} %get-tuple-element.11), channel_id=1, source_target_pairs={{1,0},{2,1},{3,2},{5,4},{6,5},{7,6},{9,8},{10,9},{11,10},{13,12},{... | collective-permute-start | bytes 1179656 | tf_op jit(solution)/shard_map/ppermute | solution.py:16
  39.5 1.8 %copy-start.5 = (bf16[4,2,96,256]{3,2,1,0:T(8,128)(2,1)}, bf16[4,2,96,256]{3,2,1,0:T(8,128)(2,1)S(1)}, u32[]{:S(2)}) copy-start(bf16[4,2,96,256]{3,2,1,0:T(8,128)(2,1)S(1)} %collective-permute-done.1.tc_ref) | copy-start | bytes 1179652
  41.2 0.7 copy-start.6
  53.8 12.8 %copy-start.7 = (bf16[1,16,4,256]{3,2,1,0:T(4,128)(2,1)S(1)}, bf16[1,16,4,256]{3,2,1,0:T(4,128)(2,1)}, u32[]{:S(2)}) copy-start(bf16[1,16,4,256]{3,2,1,0:T(4,128)(2,1)} %shard_map.122) | copy-start | bytes 98308
  54.7 7.3 %collective-permute-start.6 = (bf16[1,16,2,256]{3,2,1,0:T(2,128)(2,1)S(1)}, bf16[1,16,2,256]{3,2,1,0:T(2,128)(2,1)S(1)}, u32[]{:S(2)}, u32[]{:S(2)}) collective-permute-start(bf16[1,16,2,256]{3,2,1,0:T(2,128)(2,1)S(1)} %get-tuple-element.23), channel_id=1, source_target_pairs={{1,0},{2,1},{3,2},{5,4},{6,5},{7,6},{9,8},{10,9},{11,10},{13,12},{... | collective-permute-start | bytes 49160 | tf_op jit(solution)/shard_map/ppermute | solution.py:16
  60.1 6.6 %collective-permute-start.5 = (bf16[1,16,2,256]{3,2,1,0:T(2,128)(2,1)S(1)}, bf16[1,16,2,256]{3,2,1,0:T(2,128)(2,1)S(1)}, u32[]{:S(2)}, u32[]{:S(2)}) collective-permute-start(bf16[1,16,2,256]{3,2,1,0:T(2,128)(2,1)S(1)} %get-tuple-element.22), channel_id=1, source_target_pairs={{0,1},{1,2},{2,3},{4,5},{5,6},{6,7},{8,9},{9,10},{10,11},{12,13},{... | collective-permute-start | bytes 49160 | tf_op jit(solution)/shard_map/ppermute | solution.py:16
  66.7 7.7 %copy-start.8 = (bf16[1,16,8,256]{3,2,1,0:T(8,128)(2,1)}, bf16[1,16,8,256]{3,2,1,0:T(8,128)(2,1)S(1)}, u32[]{:S(2)}) copy-start(bf16[1,16,8,256]{3,2,1,0:T(8,128)(2,1)S(1)} %pad_maximum_fusion.l0_ref) | copy-start | bytes 196612
  66.7 9.2 %collective-permute-start.7 = (bf16[1,16,8,256]{3,2,1,0:T(8,128)(2,1)S(1)}, bf16[1,16,8,256]{3,2,1,0:T(8,128)(2,1)S(1)}, u32[]{:S(2)}, u32[]{:S(2)}) collective-permute-start(bf16[1,16,8,256]{3,2,1,0:T(8,128)(2,1)S(1)} %pad_maximum_fusion.l0_ref), channel_id=1, source_target_pairs={{0,12},{4,16},{8,20},{12,24},{16,28},{20,32},{24,36},{28,40},{32,4... | collective-permute-start | bytes 196616 | tf_op jit(solution)/shard_map/ppermute | solution.py:19
  68.6 10.7 %collective-permute-start.8 = (bf16[1,16,8,256]{3,2,1,0:T(8,128)(2,1)S(1)}, bf16[1,16,8,256]{3,2,1,0:T(8,128)(2,1)S(1)}, u32[]{:S(2)}, u32[]{:S(2)}) collective-permute-start(bf16[1,16,8,256]{3,2,1,0:T(8,128)(2,1)S(1)} %pad_maximum_fusion.l0_ref), channel_id=1, source_target_pairs={{0,8},{4,12},{8,16},{12,20},{16,24},{20,28},{24,32},{28,36},{32,40... | collective-permute-start | bytes 196616 | tf_op jit(solution)/shard_map/ppermute | solution.py:19
  70.7 10.4 %collective-permute-start.9 = (bf16[1,16,8,256]{3,2,1,0:T(8,128)(2,1)S(1)}, bf16[1,16,8,256]{3,2,1,0:T(8,128)(2,1)S(1)}, u32[]{:S(2)}, u32[]{:S(2)}) collective-permute-start(bf16[1,16,8,256]{3,2,1,0:T(8,128)(2,1)S(1)} %pad_maximum_fusion.l0_ref), channel_id=1, source_target_pairs={{0,4},{4,8},{8,12},{12,16},{16,20},{20,24},{24,28},{28,32},{32,36}... | collective-permute-start | bytes 196616 | tf_op jit(solution)/shard_map/ppermute | solution.py:19
  75.9 5.1 %copy-start.10 = (bf16[1,16,8,256]{3,2,1,0:T(8,128)(2,1)}, bf16[1,16,8,256]{3,2,1,0:T(8,128)(2,1)S(1)}, u32[]{:S(2)}) copy-start(bf16[1,16,8,256]{3,2,1,0:T(8,128)(2,1)S(1)} %collective-permute-done.7.l3_ref) | copy-start | bytes 196612
  79.3 1.8 %copy-start.11 = (bf16[1,16,8,256]{3,2,1,0:T(8,128)(2,1)}, bf16[1,16,8,256]{3,2,1,0:T(8,128)(2,1)S(1)}, u32[]{:S(2)}) copy-start(bf16[1,16,8,256]{3,2,1,0:T(8,128)(2,1)S(1)} %collective-permute-done.8.l2_ref) | copy-start | bytes 196612
  81.1 0.6 copy-start.12

commit v7 on v6

--- a/solution.py
+++ b/solution.py
@@ -190,7 +190,9 @@
     lat_rows = jnp.concatenate(
         [shift(latent[:, :, -2:], 0, 1), latent, shift(latent[:, :, :2], 0, -1)], 2
     )
-    lat_frames = [shift(lat_rows, 3, 0), shift(lat_rows, 2, 0), shift(lat_rows, 1, 0), lat_rows]
+    lat_1 = shift(lat_rows, 1, 0)
+    lat_32 = shift(jnp.concatenate([lat_1, lat_rows], 0), 2, 0)
+    lat_frames = [lat_32[:1], lat_32[1:], lat_1, lat_rows]
     rebuilt = pl.pallas_call(
         functools.partial(decode_kernel_body, **dims),
         out_shape=jax.ShapeDtypeStruct((frames, channels, rows, columns), jnp.bfloat16),

time: 90.1 us -> 98.1 us (1.089)
  waiting for transfers between devices: 23.4 us -> 33.7 us
  starting transfers between devices: 31.8 us -> 28.9 us
    ppermute x4 -> x3, waiting for transfers between devices: 14.2 us -> 24.5 us  [shift(): return lax.ppermute(x, 'tm', pairs)]
    ppermute x4 -> x3, starting transfers between devices: 10.5 us -> 7.54 us  [shift(): return lax.ppermute(x, 'tm', pairs)]
    unnamed x35 -> x31, local copies, waits for them, and re-layouts: 4.14 us -> 4.06 us
  transfers between devices with their start and end apart: 10 -> 9, of which waited for: 7 -> 6; matrix products, arithmetic and copies ran while one was open for 10% -> 9% of each run, Pallas kernels for 0% -> 0%
where the time goes in v7:
time: 98.1 us; the launch traced here: 97.6 us
  waiting for transfers between devices  33.7 us (34%)
  starting transfers between devices  28.9 us (29%)
  Pallas kernels  19.7 us (20%)
  local copies, waits for them, and re-layouts  13.6 us (14%)
    ppermute x3, waiting for transfers between devices, shift(): return lax.ppermute(x, 'tm', pairs)  24.5 us
    ppermute x6, starting transfers between devices, shift(): return lax.ppermute(x, 'rows', pairs)  21.4 us
    pallas_call x1, Pallas kernels, body(): pl.pallas_call(functools.partial(encoder_kernel, **dims), out_shape=jax.S...  11.9 us
    ppermute x6, waiting for transfers between devices, shift(): return lax.ppermute(x, 'rows', pairs)  9.18 us
    pallas_call x1, Pallas kernels, body(): pl.pallas_call(functools.partial(decode_kernel_body, **dims), out_shape=j...  7.89 us
    ppermute x3, starting transfers between devices, shift(): return lax.ppermute(x, 'tm', pairs)  7.54 us
    unnamed x31, local copies, waits for them, and re-layouts  4.06 us
    reshape x4, local copies, waits for them, and re-layouts, merged_kernel(): return kernel.transpose(2, 3, 0, 1, 4).reshape(3 * o, 9 * c)  4.04 us
  transfers between devices with their start and end apart: 9, of which 6 were waited for; matrix products, arithmetic and copies ran while one was open for 9% of the time, Pallas kernels for 0%

profile of v7, /device:TPU:24, one launch (start us, length us, event | category | flops | bytes accessed | tf_op | source)
XLA Modules:
  0.0 97.6 jit_solution(139281071233617229)
XLA Ops:
  0.6 1.3 %copy.41 = bf16[4,96,4,256]{3,1,2,0:T(8,128)(2,1)S(1)} copy(bf16[4,96,4,256]{3,2,1,0:T(4,128)(2,1)} %param.11) | data formatting | bytes 1572864 | tf_op args[0]
  1.9 0.0 copy-start
  1.9 0.0 copy-start.2
  1.9 3.5 %collective-permute-start = (bf16[4,4,96,256]{3,2,1,0:T(8,128)(2,1)S(1)}, bf16[4,4,96,256]{3,2,1,0:T(8,128)(2,1)S(1)}, u32[]{:S(2)}, u32[]{:S(2)}) collective-permute-start(bf16[4,4,96,256]{3,2,1,0:T(8,128)(2,1)S(1)} %bitcast.13), channel_id=1, source_target_pairs={{0,4},{4,8},{8,12},{12,16},{16,20},{20,24},{24,28},{28,32},{32,36}... | collective-permute-start | bytes 2359304 | tf_op jit(solution)/shard_map/ppermute | solution.py:19
  5.5 1.0 fusion
  6.4 0.0 copy-done
  6.4 1.9 %collective-permute-start.3 = (bf16[4,2,96,256]{3,2,1,0:T(8,128)(2,1)}, bf16[4,2,96,256]{3,2,1,0:T(8,128)(2,1)}, u32[]{:S(2)}, u32[]{:S(2)}) collective-permute-start(bf16[4,2,96,256]{3,2,1,0:T(8,128)(2,1)} %get-tuple-element.19), channel_id=1, source_target_pairs={{0,1},{1,2},{2,3},{4,5},{5,6},{6,7},{8,9},{9,10},{10,11},{12,13},{... | collective-permute-start | bytes 1179656 | tf_op jit(solution)/shard_map/ppermute | solution.py:16
  8.3 5.1 %collective-permute-start.4 = (bf16[4,2,96,256]{3,2,1,0:T(8,128)(2,1)}, bf16[4,2,96,256]{3,2,1,0:T(8,128)(2,1)}, u32[]{:S(2)}, u32[]{:S(2)}) collective-permute-start(bf16[4,2,96,256]{3,2,1,0:T(8,128)(2,1)} %get-tuple-element.18), channel_id=1, source_target_pairs={{1,0},{2,1},{3,2},{5,4},{6,5},{7,6},{9,8},{10,9},{11,10},{13,12},{... | collective-permute-start | bytes 1179656 | tf_op jit(solution)/shard_map/ppermute | solution.py:16
  13.5 0.0 copy-done.2
  13.5 0.5 copy.33
  14.0 0.0 copy-start.3
  14.0 1.3 %reshape.16.k1_ref = bf16[288,864]{1,0:T(8,128)(2,1)} reshape(bf16[3,96,3,3,96]{4,3,2,1,0:T(4,128)(2,1)S(1)} %copy.33) | data formatting | bytes 995328 | tf_op jit(solution)/shard_map/reshape | solution.py:31
  15.3 0.0 copy-done.3
  15.3 0.5 copy.34
  15.7 0.0 copy-start.10
  15.8 0.0 copy-start.4
  15.8 1.3 %reshape.17.k2_ref = bf16[288,864]{1,0:T(8,128)(2,1)} reshape(bf16[3,96,3,3,96]{4,3,2,1,0:T(4,128)(2,1)S(1)} %copy.34) | data formatting | bytes 995328 | tf_op jit(solution)/shard_map/reshape | solution.py:31
  17.1 0.0 copy-done.10
  17.1 0.1 copy.35
  17.1 0.1 reshape.18
  17.3 0.0 copy-done.4
  17.3 0.5 copy.36
  17.8 0.0 copy-start.14
  17.8 1.3 %reshape.19.fk_ref = bf16[288,864]{1,0:T(8,128)(2,1)} reshape(bf16[3,96,3,3,96]{4,3,2,1,0:T(4,128)(2,1)S(1)} %copy.36) | data formatting | bytes 995328 | tf_op jit(solution)/shard_map/reshape | solution.py:31
  19.1 0.0 copy-start.11
  19.1 0.0 copy-start.12
  19.1 0.0 copy-start.13
  19.1 0.0 copy-done.14
  19.1 0.6 copy-done.11
  19.7 0.0 copy-done.12
  19.8 0.0 copy-done.13
  19.8 0.7 and_convert_fusion.mask_ref
  20.4 7.6 %collective-permute-done.pv_ref = bf16[4,4,96,256]{3,2,1,0:T(8,128)(2,1)S(1)} collective-permute-done((bf16[4,4,96,256]{3,2,1,0:T(8,128)(2,1)S(1)}, bf16[4,4,96,256]{3,2,1,0:T(8,128)(2,1)S(1)}, u32[]{:S(2)}, u32[]{:S(2)}) %collective-permute-start) | collective-permute-done | bytes 786464 | tf_op jit(solution)/shard_map/ppermute | solution.py:19
  28.0 0.0 copy-start.1
  28.0 0.1 fusion.1
  28.1 0.8 copy-done.1
  28.9 1.9 %collective-permute-start.1 = (bf16[4,2,96,256]{3,2,1,0:T(8,128)(2,1)S(1)}, bf16[4,2,96,256]{3,2,1,0:T(8,128)(2,1)S(1)}, u32[]{:S(2)}, u32[]{:S(2)}) collective-permute-start(bf16[4,2,96,256]{3,2,1,0:T(8,128)(2,1)S(1)} %get-tuple-element.10), channel_id=1, source_target_pairs={{0,1},{1,2},{2,3},{4,5},{5,6},{6,7},{8,9},{9,10},{10,11},{12,13},{... | collective-permute-start | bytes 1179656 | tf_op jit(solution)/shard_map/ppermute | solution.py:16
  30.8 5.1 %collective-permute-start.2 = (bf16[4,2,96,256]{3,2,1,0:T(8,128)(2,1)S(1)}, bf16[4,2,96,256]{3,2,1,0:T(8,128)(2,1)S(1)}, u32[]{:S(2)}, u32[]{:S(2)}) collective-permute-start(bf16[4,2,96,256]{3,2,1,0:T(8,128)(2,1)S(1)} %get-tuple-element.11), channel_id=1, source_target_pairs={{1,0},{2,1},{3,2},{5,4},{6,5},{7,6},{9,8},{10,9},{11,10},{13,12},{... | collective-permute-start | bytes 1179656 | tf_op jit(solution)/shard_map/ppermute | solution.py:16
  35.9 0.7 copy.37.vec_ref
  36.7 0.0 collective-permute-done.3.tp_ref
  36.7 0.0 collective-permute-done.4.bt_ref
  36.7 2.8 %collective-permute-done.1.tc_ref = bf16[4,2,96,256]{3,2,1,0:T(8,128)(2,1)S(1)} collective-permute-done((bf16[4,2,96,256]{3,2,1,0:T(8,128)(2,1)S(1)}, bf16[4,2,96,256]{3,2,1,0:T(8,128)(2,1)S(1)}, u32[]{:S(2)}, u32[]{:S(2)}) %collective-permute-start.1) | collective-permute-done | bytes 393248 | tf_op jit(solution)/shard_map/ppermute | solution.py:16
  39.5 1.8 %collective-permute-done.2.bc_ref = bf16[4,2,96,256]{3,2,1,0:T(8,128)(2,1)S(1)} collective-permute-done((bf16[4,2,96,256]{3,2,1,0:T(8,128)(2,1)S(1)}, bf16[4,2,96,256]{3,2,1,0:T(8,128)(2,1)S(1)}, u32[]{:S(2)}, u32[]{:S(2)}) %collective-permute-start.2) | collective-permute-done | bytes 393248 | tf_op jit(solution)/shard_map/ppermute | solution.py:16
  41.2 0.0 copy-done.6
  41.2 0.7 copy-done.7
  42.0 11.9 %shard_map.122 = bf16[1,16,4,256]{3,2,1,0:T(4,128)(2,1)} custom-call(bf16[4,2,96,256]{3,2,1,0:T(8,128)(2,1)} %copy-done.6, bf16[4,4,96,256]{3,2,1,0:T(8,128)(2,1)} %copy-done.1, bf16[4,2,96,256]{3,2,1,0:T(8,128)(2,1)} %copy-done.7, bf16[4,2,96,256]{3,2,1,0:T(8,128)(2,1)} %collective-permute-done.3.tp_ref, bf16[4,4,96,256]{3,2,1,0:T(8,128)(2,1)} %bitcast.15, ...), custom_call_target="tpu_custom_call" | custom-call | tf_op jit(solution)/shard_map/pallas_call | solution.py:177
  53.8 0.9 fusion.3
  54.7 5.3 %collective-permute-start.6 = (bf16[1,16,2,256]{3,2,1,0:T(2,128)(2,1)S(1)}, bf16[1,16,2,256]{3,2,1,0:T(2,128)(2,1)S(1)}, u32[]{:S(2)}, u32[]{:S(2)}) collective-permute-start(bf16[1,16,2,256]{3,2,1,0:T(2,128)(2,1)S(1)} %get-tuple-element.25), channel_id=1, source_target_pairs={{1,0},{2,1},{3,2},{5,4},{6,5},{7,6},{9,8},{10,9},{11,10},{13,12},{... | collective-permute-start | bytes 49160 | tf_op jit(solution)/shard_map/ppermute | solution.py:16
  60.1 1.9 %collective-permute-start.5 = (bf16[1,16,2,256]{3,2,1,0:T(2,128)(2,1)S(1)}, bf16[1,16,2,256]{3,2,1,0:T(2,128)(2,1)S(1)}, u32[]{:S(2)}, u32[]{:S(2)}) collective-permute-start(bf16[1,16,2,256]{3,2,1,0:T(2,128)(2,1)S(1)} %get-tuple-element.24), channel_id=1, source_target_pairs={{0,1},{1,2},{2,3},{4,5},{5,6},{6,7},{8,9},{9,10},{10,11},{12,13},{... | collective-permute-start | bytes 49160 | tf_op jit(solution)/shard_map/ppermute | solution.py:16
  62.0 0.0 collective-permute-done.6
  62.0 4.6 %collective-permute-done.5 = bf16[1,16,2,256]{3,2,1,0:T(2,128)(2,1)S(1)} collective-permute-done((bf16[1,16,2,256]{3,2,1,0:T(2,128)(2,1)S(1)}, bf16[1,16,2,256]{3,2,1,0:T(2,128)(2,1)S(1)}, u32[]{:S(2)}, u32[]{:S(2)}) %collective-permute-start.5) | collective-permute-done | bytes 16416 | tf_op jit(solution)/shard_map/ppermute | solution.py:16
  66.6 0.0 copy-done.5
  66.6 0.1 pad_maximum_fusion.l0_ref
  66.7 0.0 copy-start.8
  66.7 1.9 %collective-permute-start.7 = (bf16[1,16,8,256]{3,2,1,0:T(8,128)(2,1)S(1)}, bf16[1,16,8,256]{3,2,1,0:T(8,128)(2,1)S(1)}, u32[]{:S(2)}, u32[]{:S(2)}) collective-permute-start(bf16[1,16,8,256]{3,2,1,0:T(8,128)(2,1)S(1)} %pad_maximum_fusion.l0_ref), channel_id=1, source_target_pairs={{0,4},{4,8},{8,12},{12,16},{16,20},{20,24},{24,28},{28,32},{32,36}... | collective-permute-start | bytes 196616 | tf_op jit(solution)/shard_map/ppermute | solution.py:19
  68.6 8.4 %collective-permute-done.7.l1_ref = bf16[1,16,8,256]{3,2,1,0:T(8,128)(2,1)S(1)} collective-permute-done((bf16[1,16,8,256]{3,2,1,0:T(8,128)(2,1)S(1)}, bf16[1,16,8,256]{3,2,1,0:T(8,128)(2,1)S(1)}, u32[]{:S(2)}, u32[]{:S(2)}) %collective-permute-start.7) | collective-permute-done | bytes 65568 | tf_op jit(solution)/shard_map/ppermute | solution.py:19
  77.1 0.1 maximum_maximum_fusion
  77.1 0.0 copy-done.8
  77.1 0.5 copy-done.9
  77.7 2.1 %collective-permute-start.8 = (bf16[2,16,8,256]{3,2,1,0:T(8,128)(2,1)S(1)}, bf16[2,16,8,256]{3,2,1,0:T(8,128)(2,1)S(1)}, u32[]{:S(2)}, u32[]{:S(2)}) collective-permute-start(bf16[2,16,8,256]{3,2,1,0:T(8,128)(2,1)S(1)} %maximum_maximum_fusion), channel_id=1, source_target_pairs={{0,8},{4,12},{8,16},{12,20},{16,24},{20,28},{24,32},{28,36},{32,40... | collective-permute-start | bytes 393224 | tf_op jit(solution)/shard_map/ppermute | solution.py:19
  79.8 0.8 copy.38.dk_ref
  80.6 8.5 %collective-permute-done.8 = bf16[2,16,8,256]{3,2,1,0:T(8,128)(2,1)S(1)} collective-permute-done((bf16[2,16,8,256]{3,2,1,0:T(8,128)(2,1)S(1)}, bf16[2,16,8,256]{3,2,1,0:T(8,128)(2,1)S(1)}, u32[]{:S(2)}, u32[]{:S(2)}) %collective-permute-start.8) | collective-permute-done | bytes 131104 | tf_op jit(solution)/shard_map/ppermute | solution.py:19
  89.0 0.7 fusion.2
  89.7 7.9 %shard_map.123 = bf16[4,96,4,256]{3,2,1,0:T(4,128)(2,1)} custom-call(bf16[1,16,8,256]{3,2,1,0:T(8,128)(2,1)} %get-tuple-element.23.l3_ref, bf16[1,16,8,256]{3,2,1,0:T(8,128)(2,1)} %get-tuple-element.22.l2_ref, bf16[1,16,8,256]{3,2,1,0:T(8,128)(2,1)} %copy-done.9, bf16[1,16,8,256]{3,2,1,0:T(8,128)(2,1)} %copy-done.8, bf16[288,144]{1,0:T(8,128)(2,1)} %copy.38.dk_ref, ...), custom_call_target="tpu_custom_call" | custom-call | tf_op jit(solution)/shard_map/pallas_call | solution.py:196
  (6 shorter events, 0.0 us)
Async XLA Ops:
  1.9 4.5 %copy-start = (bf16[4,96,4,256]{3,1,2,0:T(8,128)(2,1)}, bf16[4,96,4,256]{3,1,2,0:T(8,128)(2,1)S(1)}, u32[]{:S(2)}) copy-start(bf16[4,96,4,256]{3,1,2,0:T(8,128)(2,1)S(1)} %copy.41) | copy-start | bytes 2359300
  1.9 11.6 %copy-start.2 = (bf16[3,3,3,96,96]{4,3,2,1,0:T(8,128)(2,1)S(1)}, bf16[3,3,3,96,96]{4,3,2,1,0:T(8,128)(2,1)}, u32[]{:S(2)}) copy-start(bf16[3,3,3,96,96]{4,3,2,1,0:T(8,128)(2,1)} %param.12) | copy-start | bytes 1492996
  1.9 26.1 %collective-permute-start = (bf16[4,4,96,256]{3,2,1,0:T(8,128)(2,1)S(1)}, bf16[4,4,96,256]{3,2,1,0:T(8,128)(2,1)S(1)}, u32[]{:S(2)}, u32[]{:S(2)}) collective-permute-start(bf16[4,4,96,256]{3,2,1,0:T(8,128)(2,1)S(1)} %bitcast.13), channel_id=1, source_target_pairs={{0,4},{4,8},{8,12},{12,16},{16,20},{20,24},{24,28},{28,32},{32,36}... | collective-permute-start | bytes 2359304 | tf_op jit(solution)/shard_map/ppermute | solution.py:19
  6.4 30.3 %collective-permute-start.3 = (bf16[4,2,96,256]{3,2,1,0:T(8,128)(2,1)}, bf16[4,2,96,256]{3,2,1,0:T(8,128)(2,1)}, u32[]{:S(2)}, u32[]{:S(2)}) collective-permute-start(bf16[4,2,96,256]{3,2,1,0:T(8,128)(2,1)} %get-tuple-element.19), channel_id=1, source_target_pairs={{0,1},{1,2},{2,3},{4,5},{5,6},{6,7},{8,9},{9,10},{10,11},{12,13},{... | collective-permute-start | bytes 1179656 | tf_op jit(solution)/shard_map/ppermute | solution.py:16
  8.3 28.3 %collective-permute-start.4 = (bf16[4,2,96,256]{3,2,1,0:T(8,128)(2,1)}, bf16[4,2,96,256]{3,2,1,0:T(8,128)(2,1)}, u32[]{:S(2)}, u32[]{:S(2)}) collective-permute-start(bf16[4,2,96,256]{3,2,1,0:T(8,128)(2,1)} %get-tuple-element.18), channel_id=1, source_target_pairs={{1,0},{2,1},{3,2},{5,4},{6,5},{7,6},{9,8},{10,9},{11,10},{13,12},{... | collective-permute-start | bytes 1179656 | tf_op jit(solution)/shard_map/ppermute | solution.py:16
  14.0 1.3 %copy-start.3 = (bf16[3,3,3,96,96]{4,3,2,1,0:T(8,128)(2,1)S(1)}, bf16[3,3,3,96,96]{4,3,2,1,0:T(8,128)(2,1)}, u32[]{:S(2)}) copy-start(bf16[3,3,3,96,96]{4,3,2,1,0:T(8,128)(2,1)} %param.15) | copy-start | bytes 1492996
  15.7 1.3 %copy-start.10 = (bf16[3,3,3,96,16]{3,4,2,1,0:T(8,128)(2,1)S(1)}, bf16[3,3,3,96,16]{3,4,2,1,0:T(8,128)(2,1)}, u32[]{:S(2)}) copy-start(bf16[3,3,3,96,16]{3,4,2,1,0:T(8,128)(2,1)} %param.17) | copy-start | bytes 248836
  15.8 1.5 %copy-start.4 = (bf16[3,3,3,96,96]{4,3,2,1,0:T(8,128)(2,1)S(1)}, bf16[3,3,3,96,96]{4,3,2,1,0:T(8,128)(2,1)}, u32[]{:S(2)}) copy-start(bf16[3,3,3,96,96]{4,3,2,1,0:T(8,128)(2,1)} %param.21) | copy-start | bytes 1492996
  17.8 1.4 %copy-start.14 = (f32[96]{0:T(128)S(1)}, f32[96]{0:T(128)}, u32[]{:S(2)}) copy-start(f32[96]{0:T(128)} %param.13) | copy-start | bytes 1156
  19.1 0.7 copy-start.11
  19.1 0.7 copy-start.12
  19.1 0.7 copy-start.13
  28.0 0.9 copy-start.1
  28.9 10.6 %collective-permute-start.1 = (bf16[4,2,96,256]{3,2,1,0:T(8,128)(2,1)S(1)}, bf16[4,2,96,256]{3,2,1,0:T(8,128)(2,1)S(1)}, u32[]{:S(2)}, u32[]{:S(2)}) collective-permute-start(bf16[4,2,96,256]{3,2,1,0:T(8,128)(2,1)S(1)} %get-tuple-element.10), channel_id=1, source_target_pairs={{0,1},{1,2},{2,3},{4,5},{5,6},{6,7},{8,9},{9,10},{10,11},{12,13},{... | collective-permute-start | bytes 1179656 | tf_op jit(solution)/shard_map/ppermute | solution.py:16
  30.8 10.4 %collective-permute-start.2 = (bf16[4,2,96,256]{3,2,1,0:T(8,128)(2,1)S(1)}, bf16[4,2,96,256]{3,2,1,0:T(8,128)(2,1)S(1)}, u32[]{:S(2)}, u32[]{:S(2)}) collective-permute-start(bf16[4,2,96,256]{3,2,1,0:T(8,128)(2,1)S(1)} %get-tuple-element.11), channel_id=1, source_target_pairs={{1,0},{2,1},{3,2},{5,4},{6,5},{7,6},{9,8},{10,9},{11,10},{13,12},{... | collective-permute-start | bytes 1179656 | tf_op jit(solution)/shard_map/ppermute | solution.py:16
  39.5 1.8 %copy-start.6 = (bf16[4,2,96,256]{3,2,1,0:T(8,128)(2,1)}, bf16[4,2,96,256]{3,2,1,0:T(8,128)(2,1)S(1)}, u32[]{:S(2)}) copy-start(bf16[4,2,96,256]{3,2,1,0:T(8,128)(2,1)S(1)} %collective-permute-done.1.tc_ref) | copy-start | bytes 1179652
  41.2 0.7 copy-start.7
  53.8 12.8 %copy-start.5 = (bf16[1,16,4,256]{3,2,1,0:T(4,128)(2,1)S(1)}, bf16[1,16,4,256]{3,2,1,0:T(4,128)(2,1)}, u32[]{:S(2)}) copy-start(bf16[1,16,4,256]{3,2,1,0:T(4,128)(2,1)} %shard_map.122) | copy-start | bytes 98308
  54.7 7.3 %collective-permute-start.6 = (bf16[1,16,2,256]{3,2,1,0:T(2,128)(2,1)S(1)}, bf16[1,16,2,256]{3,2,1,0:T(2,128)(2,1)S(1)}, u32[]{:S(2)}, u32[]{:S(2)}) collective-permute-start(bf16[1,16,2,256]{3,2,1,0:T(2,128)(2,1)S(1)} %get-tuple-element.25), channel_id=1, source_target_pairs={{1,0},{2,1},{3,2},{5,4},{6,5},{7,6},{9,8},{10,9},{11,10},{13,12},{... | collective-permute-start | bytes 49160 | tf_op jit(solution)/shard_map/ppermute | solution.py:16
  60.1 6.6 %collective-permute-start.5 = (bf16[1,16,2,256]{3,2,1,0:T(2,128)(2,1)S(1)}, bf16[1,16,2,256]{3,2,1,0:T(2,128)(2,1)S(1)}, u32[]{:S(2)}, u32[]{:S(2)}) collective-permute-start(bf16[1,16,2,256]{3,2,1,0:T(2,128)(2,1)S(1)} %get-tuple-element.24), channel_id=1, source_target_pairs={{0,1},{1,2},{2,3},{4,5},{5,6},{6,7},{8,9},{9,10},{10,11},{12,13},{... | collective-permute-start | bytes 49160 | tf_op jit(solution)/shard_map/ppermute | solution.py:16
  66.7 10.5 %copy-start.8 = (bf16[1,16,8,256]{3,2,1,0:T(8,128)(2,1)}, bf16[1,16,8,256]{3,2,1,0:T(8,128)(2,1)S(1)}, u32[]{:S(2)}) copy-start(bf16[1,16,8,256]{3,2,1,0:T(8,128)(2,1)S(1)} %pad_maximum_fusion.l0_ref) | copy-start | bytes 196612
  66.7 10.4 %collective-permute-start.7 = (bf16[1,16,8,256]{3,2,1,0:T(8,128)(2,1)S(1)}, bf16[1,16,8,256]{3,2,1,0:T(8,128)(2,1)S(1)}, u32[]{:S(2)}, u32[]{:S(2)}) collective-permute-start(bf16[1,16,8,256]{3,2,1,0:T(8,128)(2,1)S(1)} %pad_maximum_fusion.l0_ref), channel_id=1, source_target_pairs={{0,4},{4,8},{8,12},{12,16},{16,20},{20,24},{24,28},{28,32},{32,36}... | collective-permute-start | bytes 196616 | tf_op jit(solution)/shard_map/ppermute | solution.py:19
  77.1 0.6 copy-start.9
  77.7 11.4 %collective-permute-start.8 = (bf16[2,16,8,256]{3,2,1,0:T(8,128)(2,1)S(1)}, bf16[2,16,8,256]{3,2,1,0:T(8,128)(2,1)S(1)}, u32[]{:S(2)}, u32[]{:S(2)}) collective-permute-start(bf16[2,16,8,256]{3,2,1,0:T(8,128)(2,1)S(1)} %maximum_maximum_fusion), channel_id=1, source_target_pairs={{0,8},{4,12},{8,16},{12,20},{16,24},{20,28},{24,32},{28,36},{32,40... | collective-permute-start | bytes 393224 | tf_op jit(solution)/shard_map/ppermute | solution.py:19

commit v8 on v6

--- a/solution.py
+++ b/solution.py
@@ -71,7 +71,7 @@
 
 def encoder_kernel(
     tc_ref, pv_ref, bc_ref, tp_ref, own_ref, bt_ref,
-    k1_ref, vec_ref, mask_ref, k2_ref, w_ref, o_ref, g_ref,
+    k1_ref, vec_ref, mask_ref, k2_ref, w_ref, o_ref, top_ref, bottom_ref, g_ref,
     *, frames, rows, columns
 ):
     wide = rows + 2
@@ -94,7 +94,12 @@
         part = jnp.dot(w_ref[t], hidden, preferred_element_type=jnp.float32)
         total = part if total is None else total + part
     for r in range(rows):
-        o_ref[0, :, r, :] = total[:, r * columns : (r + 1) * columns].astype(o_ref.dtype)
+        piece = total[:, r * columns : (r + 1) * columns].astype(o_ref.dtype)
+        o_ref[0, :, r, :] = piece
+        if r < 2:
+            bottom_ref[0, :, r, :] = piece
+        if r >= rows - 2:
+            top_ref[0, :, r - rows + 2, :] = piece
 
 
 def decode_kernel_body(
@@ -174,9 +179,13 @@
     ]
     vmem = pl.BlockSpec(memory_space=pltpu.VMEM)
     smem = pl.BlockSpec(memory_space=pltpu.SMEM)
-    latent = pl.pallas_call(
+    latent, lat_top, lat_bottom = pl.pallas_call(
         functools.partial(encoder_kernel, **dims),
-        out_shape=jax.ShapeDtypeStruct((1, z_count, rows, columns), jnp.bfloat16),
+        out_shape=(
+            jax.ShapeDtypeStruct((1, z_count, rows, columns), jnp.bfloat16),
+            jax.ShapeDtypeStruct((1, z_count, 2, columns), jnp.bfloat16),
+            jax.ShapeDtypeStruct((1, z_count, 2, columns), jnp.bfloat16),
+        ),
         in_specs=[vmem] * 8 + [smem, vmem, vmem],
         scratch_shapes=[pltpu.VMEM((frames + 2, rows + 2, channels, columns), jnp.bfloat16)],
     )(
@@ -188,7 +197,7 @@
         latent_weight,
     )
     lat_rows = jnp.concatenate(
-        [shift(latent[:, :, -2:], 0, 1), latent, shift(latent[:, :, :2], 0, -1)], 2
+        [shift(lat_top, 0, 1), latent, shift(lat_bottom, 0, -1)], 2
     )
     lat_frames = [shift(lat_rows, 3, 0), shift(lat_rows, 2, 0), shift(lat_rows, 1, 0), lat_rows]
     rebuilt = pl.pallas_call(

time: 90.1 us -> 90.2 us (level)
    unnamed x35 -> x33, local copies, waits for them, and re-layouts: 4.14 us -> 4.14 us
where the time goes in v8:
time: 90.2 us; the launch traced here: 89.6 us
  starting transfers between devices  31.8 us (35%)
  waiting for transfers between devices  23.6 us (26%)
  Pallas kernels  19.8 us (22%)
  local copies, waits for them, and re-layouts  12.1 us (13%)
  other arithmetic  1.5 us (2%)
    ppermute x6, starting transfers between devices, shift(): return lax.ppermute(x, 'rows', pairs)  21.3 us
    ppermute x4, waiting for transfers between devices, shift(): return lax.ppermute(x, 'tm', pairs)  14.2 us
    pallas_call x1, Pallas kernels, body(): pl.pallas_call(functools.partial(encoder_kernel, **dims), out_shape=(jax....  11.9 us
    ppermute x4, starting transfers between devices, shift(): return lax.ppermute(x, 'tm', pairs)  10.5 us
    ppermute x6, waiting for transfers between devices, shift(): return lax.ppermute(x, 'rows', pairs)  9.39 us
    pallas_call x1, Pallas kernels, body(): pl.pallas_call(functools.partial(decode_kernel_body, **dims), out_shape=j...  7.89 us
    unnamed x33, local copies, waits for them, and re-layouts  4.14 us
    reshape x4, local copies, waits for them, and re-layouts, merged_kernel(): return kernel.transpose(2, 3, 0, 1, 4).reshape(3 * o, 9 * c)  4.04 us
  transfers between devices with their start and end apart: 10, of which 7 were waited for; matrix products, arithmetic and copies ran while one was open for 10% of the time, Pallas kernels for 0%

profile of v8, /device:TPU:24, one launch (start us, length us, event | category | flops | bytes accessed | tf_op | source)
XLA Modules:
  0.0 89.6 jit_solution(8644314688076030180)
XLA Ops:
  0.6 1.3 %copy.41 = bf16[4,96,4,256]{3,1,2,0:T(8,128)(2,1)S(1)} copy(bf16[4,96,4,256]{3,2,1,0:T(4,128)(2,1)} %param.11) | data formatting | bytes 1572864 | tf_op args[0]
  1.9 0.0 copy-start
  1.9 0.0 copy-start.2
  1.9 3.5 %collective-permute-start = (bf16[4,4,96,256]{3,2,1,0:T(8,128)(2,1)S(1)}, bf16[4,4,96,256]{3,2,1,0:T(8,128)(2,1)S(1)}, u32[]{:S(2)}, u32[]{:S(2)}) collective-permute-start(bf16[4,4,96,256]{3,2,1,0:T(8,128)(2,1)S(1)} %bitcast.13), channel_id=1, source_target_pairs={{0,4},{4,8},{8,12},{12,16},{16,20},{20,24},{24,28},{28,32},{32,36}... | collective-permute-start | bytes 2359304 | tf_op jit(solution)/shard_map/ppermute | solution.py:19
  5.5 1.0 %fusion = (bf16[4,2,96,256]{3,2,1,0:T(8,128)(2,1)}, bf16[4,2,96,256]{3,2,1,0:T(8,128)(2,1)}) fusion(bf16[4,4,96,256]{3,2,1,0:T(8,128)(2,1)S(1)} %bitcast.14), kind=kLoop, calls=%fused_computation.6 | loop fusion | bytes 1572864 | tf_op jit(solution)/shard_map/slice | solution.py:152
  6.4 0.0 copy-done
  6.4 1.9 %collective-permute-start.3 = (bf16[4,2,96,256]{3,2,1,0:T(8,128)(2,1)}, bf16[4,2,96,256]{3,2,1,0:T(8,128)(2,1)}, u32[]{:S(2)}, u32[]{:S(2)}) collective-permute-start(bf16[4,2,96,256]{3,2,1,0:T(8,128)(2,1)} %get-tuple-element.25), channel_id=1, source_target_pairs={{0,1},{1,2},{2,3},{4,5},{5,6},{6,7},{8,9},{9,10},{10,11},{12,13},{... | collective-permute-start | bytes 1179656 | tf_op jit(solution)/shard_map/ppermute | solution.py:16
  8.3 5.1 %collective-permute-start.4 = (bf16[4,2,96,256]{3,2,1,0:T(8,128)(2,1)}, bf16[4,2,96,256]{3,2,1,0:T(8,128)(2,1)}, u32[]{:S(2)}, u32[]{:S(2)}) collective-permute-start(bf16[4,2,96,256]{3,2,1,0:T(8,128)(2,1)} %get-tuple-element.24), channel_id=1, source_target_pairs={{1,0},{2,1},{3,2},{5,4},{6,5},{7,6},{9,8},{10,9},{11,10},{13,12},{... | collective-permute-start | bytes 1179656 | tf_op jit(solution)/shard_map/ppermute | solution.py:16
  13.5 0.0 copy-done.2
  13.5 0.5 copy.33
  14.0 0.0 copy-start.3
  14.0 1.3 %reshape.16.k1_ref = bf16[288,864]{1,0:T(8,128)(2,1)} reshape(bf16[3,96,3,3,96]{4,3,2,1,0:T(4,128)(2,1)S(1)} %copy.33) | data formatting | bytes 995328 | tf_op jit(solution)/shard_map/reshape | solution.py:31
  15.3 0.0 copy-done.3
  15.3 0.5 copy.34
  15.8 0.0 copy-start.8
  15.8 0.0 copy-start.4
  15.8 1.3 %reshape.17.k2_ref = bf16[288,864]{1,0:T(8,128)(2,1)} reshape(bf16[3,96,3,3,96]{4,3,2,1,0:T(4,128)(2,1)S(1)} %copy.34) | data formatting | bytes 995328 | tf_op jit(solution)/shard_map/reshape | solution.py:31
  17.1 0.0 copy-done.8
  17.1 0.1 copy.35
  17.1 0.1 reshape.18
  17.3 0.0 copy-done.4
  17.3 0.5 copy.36
  17.8 0.0 copy-start.15
  17.8 1.3 %reshape.19.fk_ref = bf16[288,864]{1,0:T(8,128)(2,1)} reshape(bf16[3,96,3,3,96]{4,3,2,1,0:T(4,128)(2,1)S(1)} %copy.36) | data formatting | bytes 995328 | tf_op jit(solution)/shard_map/reshape | solution.py:31
  19.1 0.0 copy-start.12
  19.1 0.0 copy-start.13
  19.1 0.0 copy-start.14
  19.1 0.0 copy-done.15
  19.1 0.6 copy-done.12
  19.7 0.0 copy-done.13
  19.8 0.0 copy-done.14
  19.8 0.7 and_convert_fusion.mask_ref
  20.4 7.6 %collective-permute-done.pv_ref = bf16[4,4,96,256]{3,2,1,0:T(8,128)(2,1)S(1)} collective-permute-done((bf16[4,4,96,256]{3,2,1,0:T(8,128)(2,1)S(1)}, bf16[4,4,96,256]{3,2,1,0:T(8,128)(2,1)S(1)}, u32[]{:S(2)}, u32[]{:S(2)}) %collective-permute-start) | collective-permute-done | bytes 786464 | tf_op jit(solution)/shard_map/ppermute | solution.py:19
  28.0 0.0 copy-start.1
  28.0 0.1 fusion.1
  28.1 0.8 copy-done.1
  28.9 1.9 %collective-permute-start.1 = (bf16[4,2,96,256]{3,2,1,0:T(8,128)(2,1)S(1)}, bf16[4,2,96,256]{3,2,1,0:T(8,128)(2,1)S(1)}, u32[]{:S(2)}, u32[]{:S(2)}) collective-permute-start(bf16[4,2,96,256]{3,2,1,0:T(8,128)(2,1)S(1)} %get-tuple-element.13), channel_id=1, source_target_pairs={{0,1},{1,2},{2,3},{4,5},{5,6},{6,7},{8,9},{9,10},{10,11},{12,13},{... | collective-permute-start | bytes 1179656 | tf_op jit(solution)/shard_map/ppermute | solution.py:16
  30.8 5.1 %collective-permute-start.2 = (bf16[4,2,96,256]{3,2,1,0:T(8,128)(2,1)S(1)}, bf16[4,2,96,256]{3,2,1,0:T(8,128)(2,1)S(1)}, u32[]{:S(2)}, u32[]{:S(2)}) collective-permute-start(bf16[4,2,96,256]{3,2,1,0:T(8,128)(2,1)S(1)} %get-tuple-element.14), channel_id=1, source_target_pairs={{1,0},{2,1},{3,2},{5,4},{6,5},{7,6},{9,8},{10,9},{11,10},{13,12},{... | collective-permute-start | bytes 1179656 | tf_op jit(solution)/shard_map/ppermute | solution.py:16
  35.9 0.7 copy.37.vec_ref
  36.7 0.0 collective-permute-done.3.tp_ref
  36.7 0.0 collective-permute-done.4.bt_ref
  36.7 2.8 %collective-permute-done.1.tc_ref = bf16[4,2,96,256]{3,2,1,0:T(8,128)(2,1)S(1)} collective-permute-done((bf16[4,2,96,256]{3,2,1,0:T(8,128)(2,1)S(1)}, bf16[4,2,96,256]{3,2,1,0:T(8,128)(2,1)S(1)}, u32[]{:S(2)}, u32[]{:S(2)}) %collective-permute-start.1) | collective-permute-done | bytes 393248 | tf_op jit(solution)/shard_map/ppermute | solution.py:16
  39.5 1.8 %collective-permute-done.2.bc_ref = bf16[4,2,96,256]{3,2,1,0:T(8,128)(2,1)S(1)} collective-permute-done((bf16[4,2,96,256]{3,2,1,0:T(8,128)(2,1)S(1)}, bf16[4,2,96,256]{3,2,1,0:T(8,128)(2,1)S(1)}, u32[]{:S(2)}, u32[]{:S(2)}) %collective-permute-start.2) | collective-permute-done | bytes 393248 | tf_op jit(solution)/shard_map/ppermute | solution.py:16
  41.2 0.0 copy-done.5
  41.2 0.7 copy-done.6
  42.0 11.9 %shard_map.122 = (bf16[1,16,4,256]{3,2,1,0:T(4,128)(2,1)}, bf16[1,16,2,256]{3,2,1,0:T(2,128)(2,1)}, bf16[1,16,2,256]{3,2,1,0:T(2,128)(2,1)}) custom-call(bf16[4,2,96,256]{3,2,1,0:T(8,128)(2,1)} %copy-done.5, bf16[4,4,96,256]{3,2,1,0:T(8,128)(2,1)} %copy-done.1, bf16[4,2,96,256]{3,2,1,0:T(8,128)(2,1)} %copy-done.6, ...), custom_call_target="tpu_custom_call" | custom-call | tf_op jit(solution)/shard_map/pallas_call | solution.py:182
  53.8 5.3 %collective-permute-start.6 = (bf16[1,16,2,256]{3,2,1,0:T(2,128)(2,1)}, bf16[1,16,2,256]{3,2,1,0:T(2,128)(2,1)S(1)}, u32[]{:S(2)}, u32[]{:S(2)}) collective-permute-start(bf16[1,16,2,256]{3,2,1,0:T(2,128)(2,1)} %get-tuple-element.21), channel_id=1, source_target_pairs={{1,0},{2,1},{3,2},{5,4},{6,5},{7,6},{9,8},{10,9},{11,10},{13,12},{... | collective-permute-start | bytes 49160 | tf_op jit(solution)/shard_map/ppermute | solution.py:16
  59.1 1.9 %collective-permute-start.5 = (bf16[1,16,2,256]{3,2,1,0:T(2,128)(2,1)}, bf16[1,16,2,256]{3,2,1,0:T(2,128)(2,1)S(1)}, u32[]{:S(2)}, u32[]{:S(2)}) collective-permute-start(bf16[1,16,2,256]{3,2,1,0:T(2,128)(2,1)} %get-tuple-element.20), channel_id=1, source_target_pairs={{0,1},{1,2},{2,3},{4,5},{5,6},{6,7},{8,9},{9,10},{10,11},{12,13},{... | collective-permute-start | bytes 49160 | tf_op jit(solution)/shard_map/ppermute | solution.py:16
  61.1 0.0 collective-permute-done.6
  61.1 4.8 %collective-permute-done.5 = bf16[1,16,2,256]{3,2,1,0:T(2,128)(2,1)S(1)} collective-permute-done((bf16[1,16,2,256]{3,2,1,0:T(2,128)(2,1)}, bf16[1,16,2,256]{3,2,1,0:T(2,128)(2,1)S(1)}, u32[]{:S(2)}, u32[]{:S(2)}) %collective-permute-start.5) | collective-permute-done | bytes 16416 | tf_op jit(solution)/shard_map/ppermute | solution.py:16
  65.9 0.8 pad_maximum_fusion.l0_ref
  66.7 0.0 copy-start.7
  66.7 1.9 %collective-permute-start.7 = (bf16[1,16,8,256]{3,2,1,0:T(8,128)(2,1)S(1)}, bf16[1,16,8,256]{3,2,1,0:T(8,128)(2,1)S(1)}, u32[]{:S(2)}, u32[]{:S(2)}) collective-permute-start(bf16[1,16,8,256]{3,2,1,0:T(8,128)(2,1)S(1)} %pad_maximum_fusion.l0_ref), channel_id=1, source_target_pairs={{0,12},{4,16},{8,20},{12,24},{16,28},{20,32},{24,36},{28,40},{32,4... | collective-permute-start | bytes 196616 | tf_op jit(solution)/shard_map/ppermute | solution.py:19
  68.7 2.0 %collective-permute-start.8 = (bf16[1,16,8,256]{3,2,1,0:T(8,128)(2,1)S(1)}, bf16[1,16,8,256]{3,2,1,0:T(8,128)(2,1)S(1)}, u32[]{:S(2)}, u32[]{:S(2)}) collective-permute-start(bf16[1,16,8,256]{3,2,1,0:T(8,128)(2,1)S(1)} %pad_maximum_fusion.l0_ref), channel_id=1, source_target_pairs={{0,8},{4,12},{8,16},{12,20},{16,24},{20,28},{24,32},{28,36},{32,40... | collective-permute-start | bytes 196616 | tf_op jit(solution)/shard_map/ppermute | solution.py:19
  70.7 3.0 %collective-permute-start.9 = (bf16[1,16,8,256]{3,2,1,0:T(8,128)(2,1)S(1)}, bf16[1,16,8,256]{3,2,1,0:T(8,128)(2,1)S(1)}, u32[]{:S(2)}, u32[]{:S(2)}) collective-permute-start(bf16[1,16,8,256]{3,2,1,0:T(8,128)(2,1)S(1)} %pad_maximum_fusion.l0_ref), channel_id=1, source_target_pairs={{0,4},{4,8},{8,12},{12,16},{16,20},{20,24},{24,28},{28,32},{32,36}... | collective-permute-start | bytes 196616 | tf_op jit(solution)/shard_map/ppermute | solution.py:19
  73.7 0.8 copy.38.dk_ref
  74.5 0.0 copy-done.7
  74.5 1.5 %collective-permute-done.7.l3_ref = bf16[1,16,8,256]{3,2,1,0:T(8,128)(2,1)S(1)} collective-permute-done((bf16[1,16,8,256]{3,2,1,0:T(8,128)(2,1)S(1)}, bf16[1,16,8,256]{3,2,1,0:T(8,128)(2,1)S(1)}, u32[]{:S(2)}, u32[]{:S(2)}) %collective-permute-start.7) | collective-permute-done | bytes 65568 | tf_op jit(solution)/shard_map/ppermute | solution.py:19
  76.0 3.4 %collective-permute-done.8.l2_ref = bf16[1,16,8,256]{3,2,1,0:T(8,128)(2,1)S(1)} collective-permute-done((bf16[1,16,8,256]{3,2,1,0:T(8,128)(2,1)S(1)}, bf16[1,16,8,256]{3,2,1,0:T(8,128)(2,1)S(1)}, u32[]{:S(2)}, u32[]{:S(2)}) %collective-permute-start.8) | collective-permute-done | bytes 65568 | tf_op jit(solution)/shard_map/ppermute | solution.py:19
  79.4 1.8 %collective-permute-done.9.l1_ref = bf16[1,16,8,256]{3,2,1,0:T(8,128)(2,1)S(1)} collective-permute-done((bf16[1,16,8,256]{3,2,1,0:T(8,128)(2,1)S(1)}, bf16[1,16,8,256]{3,2,1,0:T(8,128)(2,1)S(1)}, u32[]{:S(2)}, u32[]{:S(2)}) %collective-permute-start.9) | collective-permute-done | bytes 65568 | tf_op jit(solution)/shard_map/ppermute | solution.py:19
  81.1 0.0 copy-done.9
  81.1 0.0 copy-done.10
  81.1 0.6 copy-done.11
  81.7 7.9 %shard_map.123 = bf16[4,96,4,256]{3,2,1,0:T(4,128)(2,1)} custom-call(bf16[1,16,8,256]{3,2,1,0:T(8,128)(2,1)} %copy-done.9, bf16[1,16,8,256]{3,2,1,0:T(8,128)(2,1)} %copy-done.10, bf16[1,16,8,256]{3,2,1,0:T(8,128)(2,1)} %copy-done.11, bf16[1,16,8,256]{3,2,1,0:T(8,128)(2,1)} %copy-done.7, bf16[288,144]{1,0:T(8,128)(2,1)} %copy.38.dk_ref, ...), custom_call_target="tpu_custom_call" | custom-call | tf_op jit(solution)/shard_map/pallas_call | solution.py:203
  (7 shorter events, 0.0 us)
Async XLA Ops:
  1.9 4.5 %copy-start = (bf16[4,96,4,256]{3,1,2,0:T(8,128)(2,1)}, bf16[4,96,4,256]{3,1,2,0:T(8,128)(2,1)S(1)}, u32[]{:S(2)}) copy-start(bf16[4,96,4,256]{3,1,2,0:T(8,128)(2,1)S(1)} %copy.41) | copy-start | bytes 2359300
  1.9 11.6 %copy-start.2 = (bf16[3,3,3,96,96]{4,3,2,1,0:T(8,128)(2,1)S(1)}, bf16[3,3,3,96,96]{4,3,2,1,0:T(8,128)(2,1)}, u32[]{:S(2)}) copy-start(bf16[3,3,3,96,96]{4,3,2,1,0:T(8,128)(2,1)} %param.12) | copy-start | bytes 1492996
  1.9 26.1 %collective-permute-start = (bf16[4,4,96,256]{3,2,1,0:T(8,128)(2,1)S(1)}, bf16[4,4,96,256]{3,2,1,0:T(8,128)(2,1)S(1)}, u32[]{:S(2)}, u32[]{:S(2)}) collective-permute-start(bf16[4,4,96,256]{3,2,1,0:T(8,128)(2,1)S(1)} %bitcast.13), channel_id=1, source_target_pairs={{0,4},{4,8},{8,12},{12,16},{16,20},{20,24},{24,28},{28,32},{32,36}... | collective-permute-start | bytes 2359304 | tf_op jit(solution)/shard_map/ppermute | solution.py:19
  6.4 30.3 %collective-permute-start.3 = (bf16[4,2,96,256]{3,2,1,0:T(8,128)(2,1)}, bf16[4,2,96,256]{3,2,1,0:T(8,128)(2,1)}, u32[]{:S(2)}, u32[]{:S(2)}) collective-permute-start(bf16[4,2,96,256]{3,2,1,0:T(8,128)(2,1)} %get-tuple-element.25), channel_id=1, source_target_pairs={{0,1},{1,2},{2,3},{4,5},{5,6},{6,7},{8,9},{9,10},{10,11},{12,13},{... | collective-permute-start | bytes 1179656 | tf_op jit(solution)/shard_map/ppermute | solution.py:16
  8.3 28.3 %collective-permute-start.4 = (bf16[4,2,96,256]{3,2,1,0:T(8,128)(2,1)}, bf16[4,2,96,256]{3,2,1,0:T(8,128)(2,1)}, u32[]{:S(2)}, u32[]{:S(2)}) collective-permute-start(bf16[4,2,96,256]{3,2,1,0:T(8,128)(2,1)} %get-tuple-element.24), channel_id=1, source_target_pairs={{1,0},{2,1},{3,2},{5,4},{6,5},{7,6},{9,8},{10,9},{11,10},{13,12},{... | collective-permute-start | bytes 1179656 | tf_op jit(solution)/shard_map/ppermute | solution.py:16
  14.0 1.3 %copy-start.3 = (bf16[3,3,3,96,96]{4,3,2,1,0:T(8,128)(2,1)S(1)}, bf16[3,3,3,96,96]{4,3,2,1,0:T(8,128)(2,1)}, u32[]{:S(2)}) copy-start(bf16[3,3,3,96,96]{4,3,2,1,0:T(8,128)(2,1)} %param.15) | copy-start | bytes 1492996
  15.8 1.3 %copy-start.8 = (bf16[3,3,3,96,16]{3,4,2,1,0:T(8,128)(2,1)S(1)}, bf16[3,3,3,96,16]{3,4,2,1,0:T(8,128)(2,1)}, u32[]{:S(2)}) copy-start(bf16[3,3,3,96,16]{3,4,2,1,0:T(8,128)(2,1)} %param.17) | copy-start | bytes 248836
  15.8 1.5 %copy-start.4 = (bf16[3,3,3,96,96]{4,3,2,1,0:T(8,128)(2,1)S(1)}, bf16[3,3,3,96,96]{4,3,2,1,0:T(8,128)(2,1)}, u32[]{:S(2)}) copy-start(bf16[3,3,3,96,96]{4,3,2,1,0:T(8,128)(2,1)} %param.21) | copy-start | bytes 1492996
  17.8 1.4 %copy-start.15 = (f32[96]{0:T(128)S(1)}, f32[96]{0:T(128)}, u32[]{:S(2)}) copy-start(f32[96]{0:T(128)} %param.13) | copy-start | bytes 1156
  19.1 0.7 copy-start.12
  19.1 0.7 copy-start.13
  19.1 0.7 copy-start.14
  28.0 0.9 copy-start.1
  28.9 10.6 %collective-permute-start.1 = (bf16[4,2,96,256]{3,2,1,0:T(8,128)(2,1)S(1)}, bf16[4,2,96,256]{3,2,1,0:T(8,128)(2,1)S(1)}, u32[]{:S(2)}, u32[]{:S(2)}) collective-permute-start(bf16[4,2,96,256]{3,2,1,0:T(8,128)(2,1)S(1)} %get-tuple-element.13), channel_id=1, source_target_pairs={{0,1},{1,2},{2,3},{4,5},{5,6},{6,7},{8,9},{9,10},{10,11},{12,13},{... | collective-permute-start | bytes 1179656 | tf_op jit(solution)/shard_map/ppermute | solution.py:16
  30.8 10.4 %collective-permute-start.2 = (bf16[4,2,96,256]{3,2,1,0:T(8,128)(2,1)S(1)}, bf16[4,2,96,256]{3,2,1,0:T(8,128)(2,1)S(1)}, u32[]{:S(2)}, u32[]{:S(2)}) collective-permute-start(bf16[4,2,96,256]{3,2,1,0:T(8,128)(2,1)S(1)} %get-tuple-element.14), channel_id=1, source_target_pairs={{1,0},{2,1},{3,2},{5,4},{6,5},{7,6},{9,8},{10,9},{11,10},{13,12},{... | collective-permute-start | bytes 1179656 | tf_op jit(solution)/shard_map/ppermute | solution.py:16
  39.5 1.8 %copy-start.5 = (bf16[4,2,96,256]{3,2,1,0:T(8,128)(2,1)}, bf16[4,2,96,256]{3,2,1,0:T(8,128)(2,1)S(1)}, u32[]{:S(2)}) copy-start(bf16[4,2,96,256]{3,2,1,0:T(8,128)(2,1)S(1)} %collective-permute-done.1.tc_ref) | copy-start | bytes 1179652
  41.2 0.7 copy-start.6
  53.8 7.2 %collective-permute-start.6 = (bf16[1,16,2,256]{3,2,1,0:T(2,128)(2,1)}, bf16[1,16,2,256]{3,2,1,0:T(2,128)(2,1)S(1)}, u32[]{:S(2)}, u32[]{:S(2)}) collective-permute-start(bf16[1,16,2,256]{3,2,1,0:T(2,128)(2,1)} %get-tuple-element.21), channel_id=1, source_target_pairs={{1,0},{2,1},{3,2},{5,4},{6,5},{7,6},{9,8},{10,9},{11,10},{13,12},{... | collective-permute-start | bytes 49160 | tf_op jit(solution)/shard_map/ppermute | solution.py:16
  59.1 6.8 %collective-permute-start.5 = (bf16[1,16,2,256]{3,2,1,0:T(2,128)(2,1)}, bf16[1,16,2,256]{3,2,1,0:T(2,128)(2,1)S(1)}, u32[]{:S(2)}, u32[]{:S(2)}) collective-permute-start(bf16[1,16,2,256]{3,2,1,0:T(2,128)(2,1)} %get-tuple-element.20), channel_id=1, source_target_pairs={{0,1},{1,2},{2,3},{4,5},{5,6},{6,7},{8,9},{9,10},{10,11},{12,13},{... | collective-permute-start | bytes 49160 | tf_op jit(solution)/shard_map/ppermute | solution.py:16
  66.7 7.7 %copy-start.7 = (bf16[1,16,8,256]{3,2,1,0:T(8,128)(2,1)}, bf16[1,16,8,256]{3,2,1,0:T(8,128)(2,1)S(1)}, u32[]{:S(2)}) copy-start(bf16[1,16,8,256]{3,2,1,0:T(8,128)(2,1)S(1)} %pad_maximum_fusion.l0_ref) | copy-start | bytes 196612
  66.7 9.2 %collective-permute-start.7 = (bf16[1,16,8,256]{3,2,1,0:T(8,128)(2,1)S(1)}, bf16[1,16,8,256]{3,2,1,0:T(8,128)(2,1)S(1)}, u32[]{:S(2)}, u32[]{:S(2)}) collective-permute-start(bf16[1,16,8,256]{3,2,1,0:T(8,128)(2,1)S(1)} %pad_maximum_fusion.l0_ref), channel_id=1, source_target_pairs={{0,12},{4,16},{8,20},{12,24},{16,28},{20,32},{24,36},{28,40},{32,4... | collective-permute-start | bytes 196616 | tf_op jit(solution)/shard_map/ppermute | solution.py:19
  68.7 10.7 %collective-permute-start.8 = (bf16[1,16,8,256]{3,2,1,0:T(8,128)(2,1)S(1)}, bf16[1,16,8,256]{3,2,1,0:T(8,128)(2,1)S(1)}, u32[]{:S(2)}, u32[]{:S(2)}) collective-permute-start(bf16[1,16,8,256]{3,2,1,0:T(8,128)(2,1)S(1)} %pad_maximum_fusion.l0_ref), channel_id=1, source_target_pairs={{0,8},{4,12},{8,16},{12,20},{16,24},{20,28},{24,32},{28,36},{32,40... | collective-permute-start | bytes 196616 | tf_op jit(solution)/shard_map/ppermute | solution.py:19
  70.7 10.4 %collective-permute-start.9 = (bf16[1,16,8,256]{3,2,1,0:T(8,128)(2,1)S(1)}, bf16[1,16,8,256]{3,2,1,0:T(8,128)(2,1)S(1)}, u32[]{:S(2)}, u32[]{:S(2)}) collective-permute-start(bf16[1,16,8,256]{3,2,1,0:T(8,128)(2,1)S(1)} %pad_maximum_fusion.l0_ref), channel_id=1, source_target_pairs={{0,4},{4,8},{8,12},{12,16},{16,20},{20,24},{24,28},{28,32},{32,36}... | collective-permute-start | bytes 196616 | tf_op jit(solution)/shard_map/ppermute | solution.py:19
  76.0 5.1 %copy-start.9 = (bf16[1,16,8,256]{3,2,1,0:T(8,128)(2,1)}, bf16[1,16,8,256]{3,2,1,0:T(8,128)(2,1)S(1)}, u32[]{:S(2)}) copy-start(bf16[1,16,8,256]{3,2,1,0:T(8,128)(2,1)S(1)} %collective-permute-done.7.l3_ref) | copy-start | bytes 196612
  79.3 1.8 %copy-start.10 = (bf16[1,16,8,256]{3,2,1,0:T(8,128)(2,1)}, bf16[1,16,8,256]{3,2,1,0:T(8,128)(2,1)S(1)}, u32[]{:S(2)}) copy-start(bf16[1,16,8,256]{3,2,1,0:T(8,128)(2,1)S(1)} %collective-permute-done.8.l2_ref) | copy-start | bytes 196612
  81.1 0.6 copy-start.11

commit v9 on v8

--- a/solution.py
+++ b/solution.py
@@ -69,6 +69,10 @@
     return left + acc[out_channels : 2 * out_channels] + right
 
 
+def at_row(get, r):
+    return lambda t, rr: get(t, rr + r)
+
+
 def encoder_kernel(
     tc_ref, pv_ref, bc_ref, tp_ref, own_ref, bt_ref,
     k1_ref, vec_ref, mask_ref, k2_ref, w_ref, o_ref, top_ref, bottom_ref, g_ref,
@@ -79,22 +83,22 @@
     gain = vec_ref[:, 1:2]
     x = tiled([(tc_ref, pv_ref, bc_ref), (tp_ref, own_ref, bt_ref)], frames, 2, rows)
     for t in range(frames + 2):
-        y = tap_sum(x, k1_ref, t, wide, columns) + bias
-        scale = lax.rsqrt(jnp.mean(y * y, axis=0, keepdims=True) + 1e-06)
-        z = y * scale * gain
-        g = z / (1.0 + jnp.exp(-z))
         for r in range(wide):
-            piece = g[:, r * columns : (r + 1) * columns] * mask_ref[t, r]
-            g_ref[t, r] = piece.astype(g_ref.dtype)
-    total = None
+            y = tap_sum(at_row(x, r), k1_ref, t, 1, columns) + bias
+            scale = lax.rsqrt(jnp.mean(y * y, axis=0, keepdims=True) + 1e-06)
+            z = y * scale * gain
+            g = z / (1.0 + jnp.exp(-z))
+            g_ref[t, r] = (g * mask_ref[t, r]).astype(g_ref.dtype)
+    totals = [None] * rows
     for t in range(frames):
-        y = tap_sum(from_ref(g_ref), k2_ref, t, rows, columns)
-        res = frame_rows(x, t + frames, 2, rows)
-        hidden = (res.astype(jnp.float32) + y).astype(jnp.bfloat16)
-        part = jnp.dot(w_ref[t], hidden, preferred_element_type=jnp.float32)
-        total = part if total is None else total + part
+        for r in range(rows):
+            y = tap_sum(at_row(from_ref(g_ref), r), k2_ref, t, 1, columns)
+            res = x(t + frames, r + 2)
+            hidden = (res.astype(jnp.float32) + y).astype(jnp.bfloat16)
+            part = jnp.dot(w_ref[t], hidden, preferred_element_type=jnp.float32)
+            totals[r] = part if totals[r] is None else totals[r] + part
     for r in range(rows):
-        piece = total[:, r * columns : (r + 1) * columns].astype(o_ref.dtype)
+        piece = totals[r].astype(o_ref.dtype)
         o_ref[0, :, r, :] = piece
         if r < 2:
             bottom_ref[0, :, r, :] = piece
@@ -124,11 +128,10 @@
                 piece = up[:, r * columns : (r + 1) * columns] * mask_ref[slot, r]
                 ext_ref[slot, r] = piece.astype(ext_ref.dtype)
     for t in range(frames):
-        y = tap_sum(from_ref(ext_ref), fk_ref, t, rows, columns)
-        res = frame_rows(from_ref(ext_ref), t + 2, 1, rows)
-        out = (res.astype(jnp.float32) + y).astype(o_ref.dtype)
         for r in range(rows):
-            o_ref[t, :, r, :] = out[:, r * columns : (r + 1) * columns]
+            y = tap_sum(at_row(from_ref(ext_ref), r), fk_ref, t, 1, columns)
+            res = ext_ref[t + 2, r + 1]
+            o_ref[t, :, r, :] = (res.astype(jnp.float32) + y).astype(o_ref.dtype)
 
 
 def body(

time: 90.2 us -> 92.6 us (1.027)
  Pallas kernels: 19.8 us -> 22.2 us
    pallas_call x1, Pallas kernels: 11.9 us -> 14.6 us  [body(): pl.pallas_call(functools.partial(encoder_kernel, **dims), out_shape=(jax....]
  transfers between devices with their start and end apart: 10 -> 10, of which waited for: 7 -> 7; matrix products, arithmetic and copies ran while one was open for 10% -> 9% of each run, Pallas kernels for 0% -> 0%
where the time goes in v9:
time: 92.6 us; the launch traced here: 92.1 us
  starting transfers between devices  32 us (35%)
  waiting for transfers between devices  23.3 us (25%)
  Pallas kernels  22.2 us (24%)
  local copies, waits for them, and re-layouts  12.1 us (13%)
  other arithmetic  1.5 us (2%)
    ppermute x6, starting transfers between devices, shift(): return lax.ppermute(x, 'rows', pairs)  21.5 us
    pallas_call x1, Pallas kernels, body(): pl.pallas_call(functools.partial(encoder_kernel, **dims), out_shape=(jax....  14.6 us
    ppermute x4, waiting for transfers between devices, shift(): return lax.ppermute(x, 'tm', pairs)  14.1 us
    ppermute x4, starting transfers between devices, shift(): return lax.ppermute(x, 'tm', pairs)  10.5 us
    ppermute x6, waiting for transfers between devices, shift(): return lax.ppermute(x, 'rows', pairs)  9.21 us
    pallas_call x1, Pallas kernels, body(): pl.pallas_call(functools.partial(decode_kernel_body, **dims), out_shape=j...  7.62 us
    unnamed x33, local copies, waits for them, and re-layouts  4.14 us
    reshape x4, local copies, waits for them, and re-layouts, merged_kernel(): return kernel.transpose(2, 3, 0, 1, 4).reshape(3 * o, 9 * c)  4.04 us
  transfers between devices with their start and end apart: 10, of which 7 were waited for; matrix products, arithmetic and copies ran while one was open for 9% of the time, Pallas kernels for 0%

profile of v9, /device:TPU:24, one launch (start us, length us, event | category | flops | bytes accessed | tf_op | source)
XLA Modules:
  0.0 92.1 jit_solution(9146030715513350562)
XLA Ops:
  0.6 1.3 %copy.41 = bf16[4,96,4,256]{3,1,2,0:T(8,128)(2,1)S(1)} copy(bf16[4,96,4,256]{3,2,1,0:T(4,128)(2,1)} %param.11) | data formatting | bytes 1572864 | tf_op args[0]
  1.9 0.0 copy-start
  1.9 0.0 copy-start.2
  1.9 3.5 %collective-permute-start = (bf16[4,4,96,256]{3,2,1,0:T(8,128)(2,1)S(1)}, bf16[4,4,96,256]{3,2,1,0:T(8,128)(2,1)S(1)}, u32[]{:S(2)}, u32[]{:S(2)}) collective-permute-start(bf16[4,4,96,256]{3,2,1,0:T(8,128)(2,1)S(1)} %bitcast.13), channel_id=1, source_target_pairs={{0,4},{4,8},{8,12},{12,16},{16,20},{20,24},{24,28},{28,32},{32,36}... | collective-permute-start | bytes 2359304 | tf_op jit(solution)/shard_map/ppermute | solution.py:19
  5.5 1.0 %fusion = (bf16[4,2,96,256]{3,2,1,0:T(8,128)(2,1)}, bf16[4,2,96,256]{3,2,1,0:T(8,128)(2,1)}) fusion(bf16[4,4,96,256]{3,2,1,0:T(8,128)(2,1)S(1)} %bitcast.14), kind=kLoop, calls=%fused_computation.6 | loop fusion | bytes 1572864 | tf_op jit(solution)/shard_map/slice | solution.py:155
  6.4 0.0 copy-done
  6.4 1.9 %collective-permute-start.3 = (bf16[4,2,96,256]{3,2,1,0:T(8,128)(2,1)}, bf16[4,2,96,256]{3,2,1,0:T(8,128)(2,1)}, u32[]{:S(2)}, u32[]{:S(2)}) collective-permute-start(bf16[4,2,96,256]{3,2,1,0:T(8,128)(2,1)} %get-tuple-element.25), channel_id=1, source_target_pairs={{0,1},{1,2},{2,3},{4,5},{5,6},{6,7},{8,9},{9,10},{10,11},{12,13},{... | collective-permute-start | bytes 1179656 | tf_op jit(solution)/shard_map/ppermute | solution.py:16
  8.3 5.1 %collective-permute-start.4 = (bf16[4,2,96,256]{3,2,1,0:T(8,128)(2,1)}, bf16[4,2,96,256]{3,2,1,0:T(8,128)(2,1)}, u32[]{:S(2)}, u32[]{:S(2)}) collective-permute-start(bf16[4,2,96,256]{3,2,1,0:T(8,128)(2,1)} %get-tuple-element.24), channel_id=1, source_target_pairs={{1,0},{2,1},{3,2},{5,4},{6,5},{7,6},{9,8},{10,9},{11,10},{13,12},{... | collective-permute-start | bytes 1179656 | tf_op jit(solution)/shard_map/ppermute | solution.py:16
  13.5 0.0 copy-done.2
  13.5 0.5 copy.33
  14.0 0.0 copy-start.3
  14.0 1.3 %reshape.16.k1_ref = bf16[288,864]{1,0:T(8,128)(2,1)} reshape(bf16[3,96,3,3,96]{4,3,2,1,0:T(4,128)(2,1)S(1)} %copy.33) | data formatting | bytes 995328 | tf_op jit(solution)/shard_map/reshape | solution.py:31
  15.3 0.0 copy-done.3
  15.3 0.5 copy.34
  15.8 0.0 copy-start.8
  15.8 0.0 copy-start.4
  15.8 1.3 %reshape.17.k2_ref = bf16[288,864]{1,0:T(8,128)(2,1)} reshape(bf16[3,96,3,3,96]{4,3,2,1,0:T(4,128)(2,1)S(1)} %copy.34) | data formatting | bytes 995328 | tf_op jit(solution)/shard_map/reshape | solution.py:31
  17.1 0.0 copy-done.8
  17.1 0.1 copy.35
  17.1 0.1 reshape.18
  17.3 0.0 copy-done.4
  17.3 0.5 copy.36
  17.8 0.0 copy-start.15
  17.8 1.3 %reshape.19.fk_ref = bf16[288,864]{1,0:T(8,128)(2,1)} reshape(bf16[3,96,3,3,96]{4,3,2,1,0:T(4,128)(2,1)S(1)} %copy.36) | data formatting | bytes 995328 | tf_op jit(solution)/shard_map/reshape | solution.py:31
  19.1 0.0 copy-start.12
  19.1 0.0 copy-start.13
  19.1 0.0 copy-start.14
  19.1 0.0 copy-done.15
  19.1 0.6 copy-done.12
  19.7 0.0 copy-done.13
  19.8 0.0 copy-done.14
  19.8 0.7 and_convert_fusion.mask_ref
  20.4 7.6 %collective-permute-done.pv_ref = bf16[4,4,96,256]{3,2,1,0:T(8,128)(2,1)S(1)} collective-permute-done((bf16[4,4,96,256]{3,2,1,0:T(8,128)(2,1)S(1)}, bf16[4,4,96,256]{3,2,1,0:T(8,128)(2,1)S(1)}, u32[]{:S(2)}, u32[]{:S(2)}) %collective-permute-start) | collective-permute-done | bytes 786464 | tf_op jit(solution)/shard_map/ppermute | solution.py:19
  28.0 0.0 copy-start.1
  28.0 0.1 fusion.1
  28.1 0.8 copy-done.1
  28.9 1.9 %collective-permute-start.1 = (bf16[4,2,96,256]{3,2,1,0:T(8,128)(2,1)S(1)}, bf16[4,2,96,256]{3,2,1,0:T(8,128)(2,1)S(1)}, u32[]{:S(2)}, u32[]{:S(2)}) collective-permute-start(bf16[4,2,96,256]{3,2,1,0:T(8,128)(2,1)S(1)} %get-tuple-element.13), channel_id=1, source_target_pairs={{0,1},{1,2},{2,3},{4,5},{5,6},{6,7},{8,9},{9,10},{10,11},{12,13},{... | collective-permute-start | bytes 1179656 | tf_op jit(solution)/shard_map/ppermute | solution.py:16
  30.8 5.3 %collective-permute-start.2 = (bf16[4,2,96,256]{3,2,1,0:T(8,128)(2,1)S(1)}, bf16[4,2,96,256]{3,2,1,0:T(8,128)(2,1)S(1)}, u32[]{:S(2)}, u32[]{:S(2)}) collective-permute-start(bf16[4,2,96,256]{3,2,1,0:T(8,128)(2,1)S(1)} %get-tuple-element.14), channel_id=1, source_target_pairs={{1,0},{2,1},{3,2},{5,4},{6,5},{7,6},{9,8},{10,9},{11,10},{13,12},{... | collective-permute-start | bytes 1179656 | tf_op jit(solution)/shard_map/ppermute | solution.py:16
  36.1 0.7 copy.37.vec_ref
  36.8 0.0 collective-permute-done.3.tp_ref
  36.8 0.0 collective-permute-done.4.bt_ref
  36.8 2.6 %collective-permute-done.1.tc_ref = bf16[4,2,96,256]{3,2,1,0:T(8,128)(2,1)S(1)} collective-permute-done((bf16[4,2,96,256]{3,2,1,0:T(8,128)(2,1)S(1)}, bf16[4,2,96,256]{3,2,1,0:T(8,128)(2,1)S(1)}, u32[]{:S(2)}, u32[]{:S(2)}) %collective-permute-start.1) | collective-permute-done | bytes 393248 | tf_op jit(solution)/shard_map/ppermute | solution.py:16
  39.5 1.8 %collective-permute-done.2.bc_ref = bf16[4,2,96,256]{3,2,1,0:T(8,128)(2,1)S(1)} collective-permute-done((bf16[4,2,96,256]{3,2,1,0:T(8,128)(2,1)S(1)}, bf16[4,2,96,256]{3,2,1,0:T(8,128)(2,1)S(1)}, u32[]{:S(2)}, u32[]{:S(2)}) %collective-permute-start.2) | collective-permute-done | bytes 393248 | tf_op jit(solution)/shard_map/ppermute | solution.py:16
  41.2 0.0 copy-done.5
  41.2 0.7 copy-done.6
  42.0 14.6 %shard_map.122 = (bf16[1,16,4,256]{3,2,1,0:T(4,128)(2,1)}, bf16[1,16,2,256]{3,2,1,0:T(2,128)(2,1)}, bf16[1,16,2,256]{3,2,1,0:T(2,128)(2,1)}) custom-call(bf16[4,2,96,256]{3,2,1,0:T(8,128)(2,1)} %copy-done.5, bf16[4,4,96,256]{3,2,1,0:T(8,128)(2,1)} %copy-done.1, bf16[4,2,96,256]{3,2,1,0:T(8,128)(2,1)} %copy-done.6, ...), custom_call_target="tpu_custom_call" | custom-call | tf_op jit(solution)/shard_map/pallas_call | solution.py:185
  56.5 5.3 %collective-permute-start.6 = (bf16[1,16,2,256]{3,2,1,0:T(2,128)(2,1)}, bf16[1,16,2,256]{3,2,1,0:T(2,128)(2,1)S(1)}, u32[]{:S(2)}, u32[]{:S(2)}) collective-permute-start(bf16[1,16,2,256]{3,2,1,0:T(2,128)(2,1)} %get-tuple-element.21), channel_id=1, source_target_pairs={{1,0},{2,1},{3,2},{5,4},{6,5},{7,6},{9,8},{10,9},{11,10},{13,12},{... | collective-permute-start | bytes 49160 | tf_op jit(solution)/shard_map/ppermute | solution.py:16
  61.8 1.9 %collective-permute-start.5 = (bf16[1,16,2,256]{3,2,1,0:T(2,128)(2,1)}, bf16[1,16,2,256]{3,2,1,0:T(2,128)(2,1)S(1)}, u32[]{:S(2)}, u32[]{:S(2)}) collective-permute-start(bf16[1,16,2,256]{3,2,1,0:T(2,128)(2,1)} %get-tuple-element.20), channel_id=1, source_target_pairs={{0,1},{1,2},{2,3},{4,5},{5,6},{6,7},{8,9},{9,10},{10,11},{12,13},{... | collective-permute-start | bytes 49160 | tf_op jit(solution)/shard_map/ppermute | solution.py:16
  63.8 0.0 collective-permute-done.6
  63.8 4.8 %collective-permute-done.5 = bf16[1,16,2,256]{3,2,1,0:T(2,128)(2,1)S(1)} collective-permute-done((bf16[1,16,2,256]{3,2,1,0:T(2,128)(2,1)}, bf16[1,16,2,256]{3,2,1,0:T(2,128)(2,1)S(1)}, u32[]{:S(2)}, u32[]{:S(2)}) %collective-permute-start.5) | collective-permute-done | bytes 16416 | tf_op jit(solution)/shard_map/ppermute | solution.py:16
  68.6 0.8 pad_maximum_fusion.l0_ref
  69.4 0.0 copy-start.7
  69.4 1.9 %collective-permute-start.7 = (bf16[1,16,8,256]{3,2,1,0:T(8,128)(2,1)S(1)}, bf16[1,16,8,256]{3,2,1,0:T(8,128)(2,1)S(1)}, u32[]{:S(2)}, u32[]{:S(2)}) collective-permute-start(bf16[1,16,8,256]{3,2,1,0:T(8,128)(2,1)S(1)} %pad_maximum_fusion.l0_ref), channel_id=1, source_target_pairs={{0,12},{4,16},{8,20},{12,24},{16,28},{20,32},{24,36},{28,40},{32,4... | collective-permute-start | bytes 196616 | tf_op jit(solution)/shard_map/ppermute | solution.py:19
  71.4 2.0 %collective-permute-start.8 = (bf16[1,16,8,256]{3,2,1,0:T(8,128)(2,1)S(1)}, bf16[1,16,8,256]{3,2,1,0:T(8,128)(2,1)S(1)}, u32[]{:S(2)}, u32[]{:S(2)}) collective-permute-start(bf16[1,16,8,256]{3,2,1,0:T(8,128)(2,1)S(1)} %pad_maximum_fusion.l0_ref), channel_id=1, source_target_pairs={{0,8},{4,12},{8,16},{12,20},{16,24},{20,28},{24,32},{28,36},{32,40... | collective-permute-start | bytes 196616 | tf_op jit(solution)/shard_map/ppermute | solution.py:19
  73.4 3.0 %collective-permute-start.9 = (bf16[1,16,8,256]{3,2,1,0:T(8,128)(2,1)S(1)}, bf16[1,16,8,256]{3,2,1,0:T(8,128)(2,1)S(1)}, u32[]{:S(2)}, u32[]{:S(2)}) collective-permute-start(bf16[1,16,8,256]{3,2,1,0:T(8,128)(2,1)S(1)} %pad_maximum_fusion.l0_ref), channel_id=1, source_target_pairs={{0,4},{4,8},{8,12},{12,16},{16,20},{20,24},{24,28},{28,32},{32,36}... | collective-permute-start | bytes 196616 | tf_op jit(solution)/shard_map/ppermute | solution.py:19
  76.4 0.8 copy.38.dk_ref
  77.2 0.0 copy-done.7
  77.2 1.5 %collective-permute-done.7.l3_ref = bf16[1,16,8,256]{3,2,1,0:T(8,128)(2,1)S(1)} collective-permute-done((bf16[1,16,8,256]{3,2,1,0:T(8,128)(2,1)S(1)}, bf16[1,16,8,256]{3,2,1,0:T(8,128)(2,1)S(1)}, u32[]{:S(2)}, u32[]{:S(2)}) %collective-permute-start.7) | collective-permute-done | bytes 65568 | tf_op jit(solution)/shard_map/ppermute | solution.py:19
  78.7 3.4 %collective-permute-done.8.l2_ref = bf16[1,16,8,256]{3,2,1,0:T(8,128)(2,1)S(1)} collective-permute-done((bf16[1,16,8,256]{3,2,1,0:T(8,128)(2,1)S(1)}, bf16[1,16,8,256]{3,2,1,0:T(8,128)(2,1)S(1)}, u32[]{:S(2)}, u32[]{:S(2)}) %collective-permute-start.8) | collective-permute-done | bytes 65568 | tf_op jit(solution)/shard_map/ppermute | solution.py:19
  82.0 1.8 %collective-permute-done.9.l1_ref = bf16[1,16,8,256]{3,2,1,0:T(8,128)(2,1)S(1)} collective-permute-done((bf16[1,16,8,256]{3,2,1,0:T(8,128)(2,1)S(1)}, bf16[1,16,8,256]{3,2,1,0:T(8,128)(2,1)S(1)}, u32[]{:S(2)}, u32[]{:S(2)}) %collective-permute-start.9) | collective-permute-done | bytes 65568 | tf_op jit(solution)/shard_map/ppermute | solution.py:19
  83.8 0.0 copy-done.9
  83.8 0.0 copy-done.10
  83.8 0.6 copy-done.11
  84.4 7.6 %shard_map.123 = bf16[4,96,4,256]{3,2,1,0:T(4,128)(2,1)} custom-call(bf16[1,16,8,256]{3,2,1,0:T(8,128)(2,1)} %copy-done.9, bf16[1,16,8,256]{3,2,1,0:T(8,128)(2,1)} %copy-done.10, bf16[1,16,8,256]{3,2,1,0:T(8,128)(2,1)} %copy-done.11, bf16[1,16,8,256]{3,2,1,0:T(8,128)(2,1)} %copy-done.7, bf16[288,144]{1,0:T(8,128)(2,1)} %copy.38.dk_ref, ...), custom_call_target="tpu_custom_call" | custom-call | tf_op jit(solution)/shard_map/pallas_call | solution.py:206
  (7 shorter events, 0.0 us)
Async XLA Ops:
  1.9 4.5 %copy-start = (bf16[4,96,4,256]{3,1,2,0:T(8,128)(2,1)}, bf16[4,96,4,256]{3,1,2,0:T(8,128)(2,1)S(1)}, u32[]{:S(2)}) copy-start(bf16[4,96,4,256]{3,1,2,0:T(8,128)(2,1)S(1)} %copy.41) | copy-start | bytes 2359300
  1.9 11.6 %copy-start.2 = (bf16[3,3,3,96,96]{4,3,2,1,0:T(8,128)(2,1)S(1)}, bf16[3,3,3,96,96]{4,3,2,1,0:T(8,128)(2,1)}, u32[]{:S(2)}) copy-start(bf16[3,3,3,96,96]{4,3,2,1,0:T(8,128)(2,1)} %param.12) | copy-start | bytes 1492996
  1.9 26.1 %collective-permute-start = (bf16[4,4,96,256]{3,2,1,0:T(8,128)(2,1)S(1)}, bf16[4,4,96,256]{3,2,1,0:T(8,128)(2,1)S(1)}, u32[]{:S(2)}, u32[]{:S(2)}) collective-permute-start(bf16[4,4,96,256]{3,2,1,0:T(8,128)(2,1)S(1)} %bitcast.13), channel_id=1, source_target_pairs={{0,4},{4,8},{8,12},{12,16},{16,20},{20,24},{24,28},{28,32},{32,36}... | collective-permute-start | bytes 2359304 | tf_op jit(solution)/shard_map/ppermute | solution.py:19
  6.4 30.4 %collective-permute-start.3 = (bf16[4,2,96,256]{3,2,1,0:T(8,128)(2,1)}, bf16[4,2,96,256]{3,2,1,0:T(8,128)(2,1)}, u32[]{:S(2)}, u32[]{:S(2)}) collective-permute-start(bf16[4,2,96,256]{3,2,1,0:T(8,128)(2,1)} %get-tuple-element.25), channel_id=1, source_target_pairs={{0,1},{1,2},{2,3},{4,5},{5,6},{6,7},{8,9},{9,10},{10,11},{12,13},{... | collective-permute-start | bytes 1179656 | tf_op jit(solution)/shard_map/ppermute | solution.py:16
  8.3 28.5 %collective-permute-start.4 = (bf16[4,2,96,256]{3,2,1,0:T(8,128)(2,1)}, bf16[4,2,96,256]{3,2,1,0:T(8,128)(2,1)}, u32[]{:S(2)}, u32[]{:S(2)}) collective-permute-start(bf16[4,2,96,256]{3,2,1,0:T(8,128)(2,1)} %get-tuple-element.24), channel_id=1, source_target_pairs={{1,0},{2,1},{3,2},{5,4},{6,5},{7,6},{9,8},{10,9},{11,10},{13,12},{... | collective-permute-start | bytes 1179656 | tf_op jit(solution)/shard_map/ppermute | solution.py:16
  14.0 1.3 %copy-start.3 = (bf16[3,3,3,96,96]{4,3,2,1,0:T(8,128)(2,1)S(1)}, bf16[3,3,3,96,96]{4,3,2,1,0:T(8,128)(2,1)}, u32[]{:S(2)}) copy-start(bf16[3,3,3,96,96]{4,3,2,1,0:T(8,128)(2,1)} %param.15) | copy-start | bytes 1492996
  15.8 1.3 %copy-start.8 = (bf16[3,3,3,96,16]{3,4,2,1,0:T(8,128)(2,1)S(1)}, bf16[3,3,3,96,16]{3,4,2,1,0:T(8,128)(2,1)}, u32[]{:S(2)}) copy-start(bf16[3,3,3,96,16]{3,4,2,1,0:T(8,128)(2,1)} %param.17) | copy-start | bytes 248836
  15.8 1.5 %copy-start.4 = (bf16[3,3,3,96,96]{4,3,2,1,0:T(8,128)(2,1)S(1)}, bf16[3,3,3,96,96]{4,3,2,1,0:T(8,128)(2,1)}, u32[]{:S(2)}) copy-start(bf16[3,3,3,96,96]{4,3,2,1,0:T(8,128)(2,1)} %param.21) | copy-start | bytes 1492996
  17.8 1.4 %copy-start.15 = (f32[96]{0:T(128)S(1)}, f32[96]{0:T(128)}, u32[]{:S(2)}) copy-start(f32[96]{0:T(128)} %param.13) | copy-start | bytes 1156
  19.1 0.7 copy-start.12
  19.1 0.7 copy-start.13
  19.1 0.7 copy-start.14
  28.0 0.9 copy-start.1
  28.9 10.6 %collective-permute-start.1 = (bf16[4,2,96,256]{3,2,1,0:T(8,128)(2,1)S(1)}, bf16[4,2,96,256]{3,2,1,0:T(8,128)(2,1)S(1)}, u32[]{:S(2)}, u32[]{:S(2)}) collective-permute-start(bf16[4,2,96,256]{3,2,1,0:T(8,128)(2,1)S(1)} %get-tuple-element.13), channel_id=1, source_target_pairs={{0,1},{1,2},{2,3},{4,5},{5,6},{6,7},{8,9},{9,10},{10,11},{12,13},{... | collective-permute-start | bytes 1179656 | tf_op jit(solution)/shard_map/ppermute | solution.py:16
  30.8 10.4 %collective-permute-start.2 = (bf16[4,2,96,256]{3,2,1,0:T(8,128)(2,1)S(1)}, bf16[4,2,96,256]{3,2,1,0:T(8,128)(2,1)S(1)}, u32[]{:S(2)}, u32[]{:S(2)}) collective-permute-start(bf16[4,2,96,256]{3,2,1,0:T(8,128)(2,1)S(1)} %get-tuple-element.14), channel_id=1, source_target_pairs={{1,0},{2,1},{3,2},{5,4},{6,5},{7,6},{9,8},{10,9},{11,10},{13,12},{... | collective-permute-start | bytes 1179656 | tf_op jit(solution)/shard_map/ppermute | solution.py:16
  39.5 1.8 %copy-start.5 = (bf16[4,2,96,256]{3,2,1,0:T(8,128)(2,1)}, bf16[4,2,96,256]{3,2,1,0:T(8,128)(2,1)S(1)}, u32[]{:S(2)}) copy-start(bf16[4,2,96,256]{3,2,1,0:T(8,128)(2,1)S(1)} %collective-permute-done.1.tc_ref) | copy-start | bytes 1179652
  41.2 0.7 copy-start.6
  56.5 7.2 %collective-permute-start.6 = (bf16[1,16,2,256]{3,2,1,0:T(2,128)(2,1)}, bf16[1,16,2,256]{3,2,1,0:T(2,128)(2,1)S(1)}, u32[]{:S(2)}, u32[]{:S(2)}) collective-permute-start(bf16[1,16,2,256]{3,2,1,0:T(2,128)(2,1)} %get-tuple-element.21), channel_id=1, source_target_pairs={{1,0},{2,1},{3,2},{5,4},{6,5},{7,6},{9,8},{10,9},{11,10},{13,12},{... | collective-permute-start | bytes 49160 | tf_op jit(solution)/shard_map/ppermute | solution.py:16
  61.8 6.8 %collective-permute-start.5 = (bf16[1,16,2,256]{3,2,1,0:T(2,128)(2,1)}, bf16[1,16,2,256]{3,2,1,0:T(2,128)(2,1)S(1)}, u32[]{:S(2)}, u32[]{:S(2)}) collective-permute-start(bf16[1,16,2,256]{3,2,1,0:T(2,128)(2,1)} %get-tuple-element.20), channel_id=1, source_target_pairs={{0,1},{1,2},{2,3},{4,5},{5,6},{6,7},{8,9},{9,10},{10,11},{12,13},{... | collective-permute-start | bytes 49160 | tf_op jit(solution)/shard_map/ppermute | solution.py:16
  69.4 7.8 %copy-start.7 = (bf16[1,16,8,256]{3,2,1,0:T(8,128)(2,1)}, bf16[1,16,8,256]{3,2,1,0:T(8,128)(2,1)S(1)}, u32[]{:S(2)}) copy-start(bf16[1,16,8,256]{3,2,1,0:T(8,128)(2,1)S(1)} %pad_maximum_fusion.l0_ref) | copy-start | bytes 196612
  69.4 9.2 %collective-permute-start.7 = (bf16[1,16,8,256]{3,2,1,0:T(8,128)(2,1)S(1)}, bf16[1,16,8,256]{3,2,1,0:T(8,128)(2,1)S(1)}, u32[]{:S(2)}, u32[]{:S(2)}) collective-permute-start(bf16[1,16,8,256]{3,2,1,0:T(8,128)(2,1)S(1)} %pad_maximum_fusion.l0_ref), channel_id=1, source_target_pairs={{0,12},{4,16},{8,20},{12,24},{16,28},{20,32},{24,36},{28,40},{32,4... | collective-permute-start | bytes 196616 | tf_op jit(solution)/shard_map/ppermute | solution.py:19
  71.4 10.7 %collective-permute-start.8 = (bf16[1,16,8,256]{3,2,1,0:T(8,128)(2,1)S(1)}, bf16[1,16,8,256]{3,2,1,0:T(8,128)(2,1)S(1)}, u32[]{:S(2)}, u32[]{:S(2)}) collective-permute-start(bf16[1,16,8,256]{3,2,1,0:T(8,128)(2,1)S(1)} %pad_maximum_fusion.l0_ref), channel_id=1, source_target_pairs={{0,8},{4,12},{8,16},{12,20},{16,24},{20,28},{24,32},{28,36},{32,40... | collective-permute-start | bytes 196616 | tf_op jit(solution)/shard_map/ppermute | solution.py:19
  73.4 10.4 %collective-permute-start.9 = (bf16[1,16,8,256]{3,2,1,0:T(8,128)(2,1)S(1)}, bf16[1,16,8,256]{3,2,1,0:T(8,128)(2,1)S(1)}, u32[]{:S(2)}, u32[]{:S(2)}) collective-permute-start(bf16[1,16,8,256]{3,2,1,0:T(8,128)(2,1)S(1)} %pad_maximum_fusion.l0_ref), channel_id=1, source_target_pairs={{0,4},{4,8},{8,12},{12,16},{16,20},{20,24},{24,28},{28,32},{32,36}... | collective-permute-start | bytes 196616 | tf_op jit(solution)/shard_map/ppermute | solution.py:19
  78.7 5.1 %copy-start.9 = (bf16[1,16,8,256]{3,2,1,0:T(8,128)(2,1)}, bf16[1,16,8,256]{3,2,1,0:T(8,128)(2,1)S(1)}, u32[]{:S(2)}) copy-start(bf16[1,16,8,256]{3,2,1,0:T(8,128)(2,1)S(1)} %collective-permute-done.7.l3_ref) | copy-start | bytes 196612
  82.0 1.8 %copy-start.10 = (bf16[1,16,8,256]{3,2,1,0:T(8,128)(2,1)}, bf16[1,16,8,256]{3,2,1,0:T(8,128)(2,1)S(1)}, u32[]{:S(2)}) copy-start(bf16[1,16,8,256]{3,2,1,0:T(8,128)(2,1)S(1)} %collective-permute-done.8.l2_ref) | copy-start | bytes 196612
  83.8 0.6 copy-start.11

commit v10 on v8

--- a/solution.py
+++ b/solution.py
@@ -52,15 +52,17 @@
     return get
 
 
-def tap_sum(get, k_ref, t, rows, columns):
+def tap_sum(get, k_ref, t, rows, columns, count=1):
     pieces = []
     for a in range(3):
         for b in range(3):
-            pieces.append(frame_rows(get, t + a, b, rows))
+            pieces.append(
+                jnp.concatenate([frame_rows(get, t + i + a, b, rows) for i in range(count)], axis=1)
+            )
     stacked = jnp.concatenate(pieces, axis=0)
     acc = jnp.dot(k_ref[...], stacked, preferred_element_type=jnp.float32)
     out_channels = acc.shape[0] // 3
-    width = rows * columns
+    width = count * rows * columns
     lane = lax.broadcasted_iota(jnp.int32, (out_channels, width), 1) % columns
     left = pltpu.roll(acc[:out_channels], 1, 1)
     right = pltpu.roll(acc[2 * out_channels :], width - 1, 1)
@@ -78,21 +80,26 @@
     bias = vec_ref[:, 0:1]
     gain = vec_ref[:, 1:2]
     x = tiled([(tc_ref, pv_ref, bc_ref), (tp_ref, own_ref, bt_ref)], frames, 2, rows)
-    for t in range(frames + 2):
-        y = tap_sum(x, k1_ref, t, wide, columns) + bias
+    span = wide * columns
+    for t in range(0, frames + 2, 2):
+        y = tap_sum(x, k1_ref, t, wide, columns, 2) + bias
         scale = lax.rsqrt(jnp.mean(y * y, axis=0, keepdims=True) + 1e-06)
         z = y * scale * gain
         g = z / (1.0 + jnp.exp(-z))
-        for r in range(wide):
-            piece = g[:, r * columns : (r + 1) * columns] * mask_ref[t, r]
-            g_ref[t, r] = piece.astype(g_ref.dtype)
+        for i in range(2):
+            for r in range(wide):
+                lo = i * span + r * columns
+                piece = g[:, lo : lo + columns] * mask_ref[t + i, r]
+                g_ref[t + i, r] = piece.astype(g_ref.dtype)
     total = None
-    for t in range(frames):
-        y = tap_sum(from_ref(g_ref), k2_ref, t, rows, columns)
-        res = frame_rows(x, t + frames, 2, rows)
-        hidden = (res.astype(jnp.float32) + y).astype(jnp.bfloat16)
-        part = jnp.dot(w_ref[t], hidden, preferred_element_type=jnp.float32)
-        total = part if total is None else total + part
+    width = rows * columns
+    for t in range(0, frames, 2):
+        y = tap_sum(from_ref(g_ref), k2_ref, t, rows, columns, 2)
+        for i in range(2):
+            res = frame_rows(x, t + i + frames, 2, rows)
+            hidden = (res.astype(jnp.float32) + y[:, i * width : (i + 1) * width]).astype(jnp.bfloat16)
+            part = jnp.dot(w_ref[t + i], hidden, preferred_element_type=jnp.float32)
+            total = part if total is None else total + part
     for r in range(rows):
         piece = total[:, r * columns : (r + 1) * columns].astype(o_ref.dtype)
         o_ref[0, :, r, :] = piece

time: 90.2 us -> 89.8 us (level)
  no operation moved by 1% of the time
where the time goes in v10:
time: 89.8 us; the launch traced here: 89.3 us
  starting transfers between devices  31.8 us (35%)
  waiting for transfers between devices  23.6 us (26%)
  Pallas kernels  19.4 us (22%)
  local copies, waits for them, and re-layouts  12.1 us (13%)
  other arithmetic  1.5 us (2%)
    ppermute x6, starting transfers between devices, shift(): return lax.ppermute(x, 'rows', pairs)  21.3 us
    ppermute x4, waiting for transfers between devices, shift(): return lax.ppermute(x, 'tm', pairs)  14.2 us
    pallas_call x1, Pallas kernels, body(): pl.pallas_call(functools.partial(encoder_kernel, **dims), out_shape=(jax....  11.6 us
    ppermute x4, starting transfers between devices, shift(): return lax.ppermute(x, 'tm', pairs)  10.5 us
    ppermute x6, waiting for transfers between devices, shift(): return lax.ppermute(x, 'rows', pairs)  9.39 us
    pallas_call x1, Pallas kernels, body(): pl.pallas_call(functools.partial(decode_kernel_body, **dims), out_shape=j...  7.88 us
    unnamed x33, local copies, waits for them, and re-layouts  4.14 us
    reshape x4, local copies, waits for them, and re-layouts, merged_kernel(): return kernel.transpose(2, 3, 0, 1, 4).reshape(3 * o, 9 * c)  4.04 us
  transfers between devices with their start and end apart: 10, of which 7 were waited for; matrix products, arithmetic and copies ran while one was open for 10% of the time, Pallas kernels for 0%

profile of v10, /device:TPU:24, one launch (start us, length us, event | category | flops | bytes accessed | tf_op | source)
XLA Modules:
  0.0 89.3 jit_solution(12895311904337118229)
XLA Ops:
  0.6 1.3 %copy.41 = bf16[4,96,4,256]{3,1,2,0:T(8,128)(2,1)S(1)} copy(bf16[4,96,4,256]{3,2,1,0:T(4,128)(2,1)} %param.11) | data formatting | bytes 1572864 | tf_op args[0]
  1.9 0.0 copy-start
  1.9 0.0 copy-start.2
  1.9 3.5 %collective-permute-start = (bf16[4,4,96,256]{3,2,1,0:T(8,128)(2,1)S(1)}, bf16[4,4,96,256]{3,2,1,0:T(8,128)(2,1)S(1)}, u32[]{:S(2)}, u32[]{:S(2)}) collective-permute-start(bf16[4,4,96,256]{3,2,1,0:T(8,128)(2,1)S(1)} %bitcast.13), channel_id=1, source_target_pairs={{0,4},{4,8},{8,12},{12,16},{16,20},{20,24},{24,28},{28,32},{32,36}... | collective-permute-start | bytes 2359304 | tf_op jit(solution)/shard_map/ppermute | solution.py:19
  5.5 1.0 %fusion = (bf16[4,2,96,256]{3,2,1,0:T(8,128)(2,1)}, bf16[4,2,96,256]{3,2,1,0:T(8,128)(2,1)}) fusion(bf16[4,4,96,256]{3,2,1,0:T(8,128)(2,1)S(1)} %bitcast.14), kind=kLoop, calls=%fused_computation.6 | loop fusion | bytes 1572864 | tf_op jit(solution)/shard_map/slice | solution.py:159
  6.4 0.0 copy-done
  6.4 1.9 %collective-permute-start.3 = (bf16[4,2,96,256]{3,2,1,0:T(8,128)(2,1)}, bf16[4,2,96,256]{3,2,1,0:T(8,128)(2,1)}, u32[]{:S(2)}, u32[]{:S(2)}) collective-permute-start(bf16[4,2,96,256]{3,2,1,0:T(8,128)(2,1)} %get-tuple-element.25), channel_id=1, source_target_pairs={{0,1},{1,2},{2,3},{4,5},{5,6},{6,7},{8,9},{9,10},{10,11},{12,13},{... | collective-permute-start | bytes 1179656 | tf_op jit(solution)/shard_map/ppermute | solution.py:16
  8.3 5.1 %collective-permute-start.4 = (bf16[4,2,96,256]{3,2,1,0:T(8,128)(2,1)}, bf16[4,2,96,256]{3,2,1,0:T(8,128)(2,1)}, u32[]{:S(2)}, u32[]{:S(2)}) collective-permute-start(bf16[4,2,96,256]{3,2,1,0:T(8,128)(2,1)} %get-tuple-element.24), channel_id=1, source_target_pairs={{1,0},{2,1},{3,2},{5,4},{6,5},{7,6},{9,8},{10,9},{11,10},{13,12},{... | collective-permute-start | bytes 1179656 | tf_op jit(solution)/shard_map/ppermute | solution.py:16
  13.5 0.0 copy-done.2
  13.5 0.5 copy.33
  14.0 0.0 copy-start.3
  14.0 1.3 %reshape.16.k1_ref = bf16[288,864]{1,0:T(8,128)(2,1)} reshape(bf16[3,96,3,3,96]{4,3,2,1,0:T(4,128)(2,1)S(1)} %copy.33) | data formatting | bytes 995328 | tf_op jit(solution)/shard_map/reshape | solution.py:31
  15.3 0.0 copy-done.3
  15.3 0.5 copy.34
  15.8 0.0 copy-start.8
  15.8 0.0 copy-start.4
  15.8 1.3 %reshape.17.k2_ref = bf16[288,864]{1,0:T(8,128)(2,1)} reshape(bf16[3,96,3,3,96]{4,3,2,1,0:T(4,128)(2,1)S(1)} %copy.34) | data formatting | bytes 995328 | tf_op jit(solution)/shard_map/reshape | solution.py:31
  17.1 0.0 copy-done.8
  17.1 0.1 copy.35
  17.1 0.1 reshape.18
  17.3 0.0 copy-done.4
  17.3 0.5 copy.36
  17.8 0.0 copy-start.15
  17.8 1.3 %reshape.19.fk_ref = bf16[288,864]{1,0:T(8,128)(2,1)} reshape(bf16[3,96,3,3,96]{4,3,2,1,0:T(4,128)(2,1)S(1)} %copy.36) | data formatting | bytes 995328 | tf_op jit(solution)/shard_map/reshape | solution.py:31
  19.1 0.0 copy-start.12
  19.1 0.0 copy-start.13
  19.1 0.0 copy-start.14
  19.1 0.0 copy-done.15
  19.1 0.6 copy-done.12
  19.7 0.0 copy-done.13
  19.8 0.0 copy-done.14
  19.8 0.7 and_convert_fusion.mask_ref
  20.4 7.6 %collective-permute-done.pv_ref = bf16[4,4,96,256]{3,2,1,0:T(8,128)(2,1)S(1)} collective-permute-done((bf16[4,4,96,256]{3,2,1,0:T(8,128)(2,1)S(1)}, bf16[4,4,96,256]{3,2,1,0:T(8,128)(2,1)S(1)}, u32[]{:S(2)}, u32[]{:S(2)}) %collective-permute-start) | collective-permute-done | bytes 786464 | tf_op jit(solution)/shard_map/ppermute | solution.py:19
  28.0 0.0 copy-start.1
  28.0 0.1 fusion.1
  28.1 0.8 copy-done.1
  28.9 1.9 %collective-permute-start.1 = (bf16[4,2,96,256]{3,2,1,0:T(8,128)(2,1)S(1)}, bf16[4,2,96,256]{3,2,1,0:T(8,128)(2,1)S(1)}, u32[]{:S(2)}, u32[]{:S(2)}) collective-permute-start(bf16[4,2,96,256]{3,2,1,0:T(8,128)(2,1)S(1)} %get-tuple-element.13), channel_id=1, source_target_pairs={{0,1},{1,2},{2,3},{4,5},{5,6},{6,7},{8,9},{9,10},{10,11},{12,13},{... | collective-permute-start | bytes 1179656 | tf_op jit(solution)/shard_map/ppermute | solution.py:16
  30.8 5.1 %collective-permute-start.2 = (bf16[4,2,96,256]{3,2,1,0:T(8,128)(2,1)S(1)}, bf16[4,2,96,256]{3,2,1,0:T(8,128)(2,1)S(1)}, u32[]{:S(2)}, u32[]{:S(2)}) collective-permute-start(bf16[4,2,96,256]{3,2,1,0:T(8,128)(2,1)S(1)} %get-tuple-element.14), channel_id=1, source_target_pairs={{1,0},{2,1},{3,2},{5,4},{6,5},{7,6},{9,8},{10,9},{11,10},{13,12},{... | collective-permute-start | bytes 1179656 | tf_op jit(solution)/shard_map/ppermute | solution.py:16
  35.9 0.7 copy.37.vec_ref
  36.7 0.0 collective-permute-done.3.tp_ref
  36.7 0.0 collective-permute-done.4.bt_ref
  36.7 2.8 %collective-permute-done.1.tc_ref = bf16[4,2,96,256]{3,2,1,0:T(8,128)(2,1)S(1)} collective-permute-done((bf16[4,2,96,256]{3,2,1,0:T(8,128)(2,1)S(1)}, bf16[4,2,96,256]{3,2,1,0:T(8,128)(2,1)S(1)}, u32[]{:S(2)}, u32[]{:S(2)}) %collective-permute-start.1) | collective-permute-done | bytes 393248 | tf_op jit(solution)/shard_map/ppermute | solution.py:16
  39.5 1.8 %collective-permute-done.2.bc_ref = bf16[4,2,96,256]{3,2,1,0:T(8,128)(2,1)S(1)} collective-permute-done((bf16[4,2,96,256]{3,2,1,0:T(8,128)(2,1)S(1)}, bf16[4,2,96,256]{3,2,1,0:T(8,128)(2,1)S(1)}, u32[]{:S(2)}, u32[]{:S(2)}) %collective-permute-start.2) | collective-permute-done | bytes 393248 | tf_op jit(solution)/shard_map/ppermute | solution.py:16
  41.2 0.0 copy-done.5
  41.2 0.7 copy-done.6
  42.0 11.6 %shard_map.122 = (bf16[1,16,4,256]{3,2,1,0:T(4,128)(2,1)}, bf16[1,16,2,256]{3,2,1,0:T(2,128)(2,1)}, bf16[1,16,2,256]{3,2,1,0:T(2,128)(2,1)}) custom-call(bf16[4,2,96,256]{3,2,1,0:T(8,128)(2,1)} %copy-done.5, bf16[4,4,96,256]{3,2,1,0:T(8,128)(2,1)} %copy-done.1, bf16[4,2,96,256]{3,2,1,0:T(8,128)(2,1)} %copy-done.6, ...), custom_call_target="tpu_custom_call" | custom-call | tf_op jit(solution)/shard_map/pallas_call | solution.py:189
  53.5 5.3 %collective-permute-start.6 = (bf16[1,16,2,256]{3,2,1,0:T(2,128)(2,1)}, bf16[1,16,2,256]{3,2,1,0:T(2,128)(2,1)S(1)}, u32[]{:S(2)}, u32[]{:S(2)}) collective-permute-start(bf16[1,16,2,256]{3,2,1,0:T(2,128)(2,1)} %get-tuple-element.21), channel_id=1, source_target_pairs={{1,0},{2,1},{3,2},{5,4},{6,5},{7,6},{9,8},{10,9},{11,10},{13,12},{... | collective-permute-start | bytes 49160 | tf_op jit(solution)/shard_map/ppermute | solution.py:16
  58.8 1.9 %collective-permute-start.5 = (bf16[1,16,2,256]{3,2,1,0:T(2,128)(2,1)}, bf16[1,16,2,256]{3,2,1,0:T(2,128)(2,1)S(1)}, u32[]{:S(2)}, u32[]{:S(2)}) collective-permute-start(bf16[1,16,2,256]{3,2,1,0:T(2,128)(2,1)} %get-tuple-element.20), channel_id=1, source_target_pairs={{0,1},{1,2},{2,3},{4,5},{5,6},{6,7},{8,9},{9,10},{10,11},{12,13},{... | collective-permute-start | bytes 49160 | tf_op jit(solution)/shard_map/ppermute | solution.py:16
  60.8 0.0 collective-permute-done.6
  60.8 4.8 %collective-permute-done.5 = bf16[1,16,2,256]{3,2,1,0:T(2,128)(2,1)S(1)} collective-permute-done((bf16[1,16,2,256]{3,2,1,0:T(2,128)(2,1)}, bf16[1,16,2,256]{3,2,1,0:T(2,128)(2,1)S(1)}, u32[]{:S(2)}, u32[]{:S(2)}) %collective-permute-start.5) | collective-permute-done | bytes 16416 | tf_op jit(solution)/shard_map/ppermute | solution.py:16
  65.6 0.8 pad_maximum_fusion.l0_ref
  66.4 0.0 copy-start.7
  66.4 1.9 %collective-permute-start.7 = (bf16[1,16,8,256]{3,2,1,0:T(8,128)(2,1)S(1)}, bf16[1,16,8,256]{3,2,1,0:T(8,128)(2,1)S(1)}, u32[]{:S(2)}, u32[]{:S(2)}) collective-permute-start(bf16[1,16,8,256]{3,2,1,0:T(8,128)(2,1)S(1)} %pad_maximum_fusion.l0_ref), channel_id=1, source_target_pairs={{0,12},{4,16},{8,20},{12,24},{16,28},{20,32},{24,36},{28,40},{32,4... | collective-permute-start | bytes 196616 | tf_op jit(solution)/shard_map/ppermute | solution.py:19
  68.4 2.0 %collective-permute-start.8 = (bf16[1,16,8,256]{3,2,1,0:T(8,128)(2,1)S(1)}, bf16[1,16,8,256]{3,2,1,0:T(8,128)(2,1)S(1)}, u32[]{:S(2)}, u32[]{:S(2)}) collective-permute-start(bf16[1,16,8,256]{3,2,1,0:T(8,128)(2,1)S(1)} %pad_maximum_fusion.l0_ref), channel_id=1, source_target_pairs={{0,8},{4,12},{8,16},{12,20},{16,24},{20,28},{24,32},{28,36},{32,40... | collective-permute-start | bytes 196616 | tf_op jit(solution)/shard_map/ppermute | solution.py:19
  70.4 3.0 %collective-permute-start.9 = (bf16[1,16,8,256]{3,2,1,0:T(8,128)(2,1)S(1)}, bf16[1,16,8,256]{3,2,1,0:T(8,128)(2,1)S(1)}, u32[]{:S(2)}, u32[]{:S(2)}) collective-permute-start(bf16[1,16,8,256]{3,2,1,0:T(8,128)(2,1)S(1)} %pad_maximum_fusion.l0_ref), channel_id=1, source_target_pairs={{0,4},{4,8},{8,12},{12,16},{16,20},{20,24},{24,28},{28,32},{32,36}... | collective-permute-start | bytes 196616 | tf_op jit(solution)/shard_map/ppermute | solution.py:19
  73.4 0.8 copy.38.dk_ref
  74.2 0.0 copy-done.7
  74.2 1.5 %collective-permute-done.7.l3_ref = bf16[1,16,8,256]{3,2,1,0:T(8,128)(2,1)S(1)} collective-permute-done((bf16[1,16,8,256]{3,2,1,0:T(8,128)(2,1)S(1)}, bf16[1,16,8,256]{3,2,1,0:T(8,128)(2,1)S(1)}, u32[]{:S(2)}, u32[]{:S(2)}) %collective-permute-start.7) | collective-permute-done | bytes 65568 | tf_op jit(solution)/shard_map/ppermute | solution.py:19
  75.7 3.4 %collective-permute-done.8.l2_ref = bf16[1,16,8,256]{3,2,1,0:T(8,128)(2,1)S(1)} collective-permute-done((bf16[1,16,8,256]{3,2,1,0:T(8,128)(2,1)S(1)}, bf16[1,16,8,256]{3,2,1,0:T(8,128)(2,1)S(1)}, u32[]{:S(2)}, u32[]{:S(2)}) %collective-permute-start.8) | collective-permute-done | bytes 65568 | tf_op jit(solution)/shard_map/ppermute | solution.py:19
  79.0 1.8 %collective-permute-done.9.l1_ref = bf16[1,16,8,256]{3,2,1,0:T(8,128)(2,1)S(1)} collective-permute-done((bf16[1,16,8,256]{3,2,1,0:T(8,128)(2,1)S(1)}, bf16[1,16,8,256]{3,2,1,0:T(8,128)(2,1)S(1)}, u32[]{:S(2)}, u32[]{:S(2)}) %collective-permute-start.9) | collective-permute-done | bytes 65568 | tf_op jit(solution)/shard_map/ppermute | solution.py:19
  80.8 0.0 copy-done.9
  80.8 0.0 copy-done.10
  80.8 0.6 copy-done.11
  81.4 7.9 %shard_map.123 = bf16[4,96,4,256]{3,2,1,0:T(4,128)(2,1)} custom-call(bf16[1,16,8,256]{3,2,1,0:T(8,128)(2,1)} %copy-done.9, bf16[1,16,8,256]{3,2,1,0:T(8,128)(2,1)} %copy-done.10, bf16[1,16,8,256]{3,2,1,0:T(8,128)(2,1)} %copy-done.11, bf16[1,16,8,256]{3,2,1,0:T(8,128)(2,1)} %copy-done.7, bf16[288,144]{1,0:T(8,128)(2,1)} %copy.38.dk_ref, ...), custom_call_target="tpu_custom_call" | custom-call | tf_op jit(solution)/shard_map/pallas_call | solution.py:210
  (7 shorter events, 0.0 us)
Async XLA Ops:
  1.9 4.5 %copy-start = (bf16[4,96,4,256]{3,1,2,0:T(8,128)(2,1)}, bf16[4,96,4,256]{3,1,2,0:T(8,128)(2,1)S(1)}, u32[]{:S(2)}) copy-start(bf16[4,96,4,256]{3,1,2,0:T(8,128)(2,1)S(1)} %copy.41) | copy-start | bytes 2359300
  1.9 11.6 %copy-start.2 = (bf16[3,3,3,96,96]{4,3,2,1,0:T(8,128)(2,1)S(1)}, bf16[3,3,3,96,96]{4,3,2,1,0:T(8,128)(2,1)}, u32[]{:S(2)}) copy-start(bf16[3,3,3,96,96]{4,3,2,1,0:T(8,128)(2,1)} %param.12) | copy-start | bytes 1492996
  1.9 26.1 %collective-permute-start = (bf16[4,4,96,256]{3,2,1,0:T(8,128)(2,1)S(1)}, bf16[4,4,96,256]{3,2,1,0:T(8,128)(2,1)S(1)}, u32[]{:S(2)}, u32[]{:S(2)}) collective-permute-start(bf16[4,4,96,256]{3,2,1,0:T(8,128)(2,1)S(1)} %bitcast.13), channel_id=1, source_target_pairs={{0,4},{4,8},{8,12},{12,16},{16,20},{20,24},{24,28},{28,32},{32,36}... | collective-permute-start | bytes 2359304 | tf_op jit(solution)/shard_map/ppermute | solution.py:19
  6.4 30.3 %collective-permute-start.3 = (bf16[4,2,96,256]{3,2,1,0:T(8,128)(2,1)}, bf16[4,2,96,256]{3,2,1,0:T(8,128)(2,1)}, u32[]{:S(2)}, u32[]{:S(2)}) collective-permute-start(bf16[4,2,96,256]{3,2,1,0:T(8,128)(2,1)} %get-tuple-element.25), channel_id=1, source_target_pairs={{0,1},{1,2},{2,3},{4,5},{5,6},{6,7},{8,9},{9,10},{10,11},{12,13},{... | collective-permute-start | bytes 1179656 | tf_op jit(solution)/shard_map/ppermute | solution.py:16
  8.3 28.3 %collective-permute-start.4 = (bf16[4,2,96,256]{3,2,1,0:T(8,128)(2,1)}, bf16[4,2,96,256]{3,2,1,0:T(8,128)(2,1)}, u32[]{:S(2)}, u32[]{:S(2)}) collective-permute-start(bf16[4,2,96,256]{3,2,1,0:T(8,128)(2,1)} %get-tuple-element.24), channel_id=1, source_target_pairs={{1,0},{2,1},{3,2},{5,4},{6,5},{7,6},{9,8},{10,9},{11,10},{13,12},{... | collective-permute-start | bytes 1179656 | tf_op jit(solution)/shard_map/ppermute | solution.py:16
  14.0 1.3 %copy-start.3 = (bf16[3,3,3,96,96]{4,3,2,1,0:T(8,128)(2,1)S(1)}, bf16[3,3,3,96,96]{4,3,2,1,0:T(8,128)(2,1)}, u32[]{:S(2)}) copy-start(bf16[3,3,3,96,96]{4,3,2,1,0:T(8,128)(2,1)} %param.15) | copy-start | bytes 1492996
  15.8 1.3 %copy-start.8 = (bf16[3,3,3,96,16]{3,4,2,1,0:T(8,128)(2,1)S(1)}, bf16[3,3,3,96,16]{3,4,2,1,0:T(8,128)(2,1)}, u32[]{:S(2)}) copy-start(bf16[3,3,3,96,16]{3,4,2,1,0:T(8,128)(2,1)} %param.17) | copy-start | bytes 248836
  15.8 1.5 %copy-start.4 = (bf16[3,3,3,96,96]{4,3,2,1,0:T(8,128)(2,1)S(1)}, bf16[3,3,3,96,96]{4,3,2,1,0:T(8,128)(2,1)}, u32[]{:S(2)}) copy-start(bf16[3,3,3,96,96]{4,3,2,1,0:T(8,128)(2,1)} %param.21) | copy-start | bytes 1492996
  17.8 1.4 %copy-start.15 = (f32[96]{0:T(128)S(1)}, f32[96]{0:T(128)}, u32[]{:S(2)}) copy-start(f32[96]{0:T(128)} %param.13) | copy-start | bytes 1156
  19.1 0.7 copy-start.12
  19.1 0.7 copy-start.13
  19.1 0.7 copy-start.14
  28.0 0.9 copy-start.1
  28.9 10.6 %collective-permute-start.1 = (bf16[4,2,96,256]{3,2,1,0:T(8,128)(2,1)S(1)}, bf16[4,2,96,256]{3,2,1,0:T(8,128)(2,1)S(1)}, u32[]{:S(2)}, u32[]{:S(2)}) collective-permute-start(bf16[4,2,96,256]{3,2,1,0:T(8,128)(2,1)S(1)} %get-tuple-element.13), channel_id=1, source_target_pairs={{0,1},{1,2},{2,3},{4,5},{5,6},{6,7},{8,9},{9,10},{10,11},{12,13},{... | collective-permute-start | bytes 1179656 | tf_op jit(solution)/shard_map/ppermute | solution.py:16
  30.8 10.4 %collective-permute-start.2 = (bf16[4,2,96,256]{3,2,1,0:T(8,128)(2,1)S(1)}, bf16[4,2,96,256]{3,2,1,0:T(8,128)(2,1)S(1)}, u32[]{:S(2)}, u32[]{:S(2)}) collective-permute-start(bf16[4,2,96,256]{3,2,1,0:T(8,128)(2,1)S(1)} %get-tuple-element.14), channel_id=1, source_target_pairs={{1,0},{2,1},{3,2},{5,4},{6,5},{7,6},{9,8},{10,9},{11,10},{13,12},{... | collective-permute-start | bytes 1179656 | tf_op jit(solution)/shard_map/ppermute | solution.py:16
  39.5 1.8 %copy-start.5 = (bf16[4,2,96,256]{3,2,1,0:T(8,128)(2,1)}, bf16[4,2,96,256]{3,2,1,0:T(8,128)(2,1)S(1)}, u32[]{:S(2)}) copy-start(bf16[4,2,96,256]{3,2,1,0:T(8,128)(2,1)S(1)} %collective-permute-done.1.tc_ref) | copy-start | bytes 1179652
  41.2 0.7 copy-start.6
  53.5 7.2 %collective-permute-start.6 = (bf16[1,16,2,256]{3,2,1,0:T(2,128)(2,1)}, bf16[1,16,2,256]{3,2,1,0:T(2,128)(2,1)S(1)}, u32[]{:S(2)}, u32[]{:S(2)}) collective-permute-start(bf16[1,16,2,256]{3,2,1,0:T(2,128)(2,1)} %get-tuple-element.21), channel_id=1, source_target_pairs={{1,0},{2,1},{3,2},{5,4},{6,5},{7,6},{9,8},{10,9},{11,10},{13,12},{... | collective-permute-start | bytes 49160 | tf_op jit(solution)/shard_map/ppermute | solution.py:16
  58.8 6.8 %collective-permute-start.5 = (bf16[1,16,2,256]{3,2,1,0:T(2,128)(2,1)}, bf16[1,16,2,256]{3,2,1,0:T(2,128)(2,1)S(1)}, u32[]{:S(2)}, u32[]{:S(2)}) collective-permute-start(bf16[1,16,2,256]{3,2,1,0:T(2,128)(2,1)} %get-tuple-element.20), channel_id=1, source_target_pairs={{0,1},{1,2},{2,3},{4,5},{5,6},{6,7},{8,9},{9,10},{10,11},{12,13},{... | collective-permute-start | bytes 49160 | tf_op jit(solution)/shard_map/ppermute | solution.py:16
  66.4 7.7 %copy-start.7 = (bf16[1,16,8,256]{3,2,1,0:T(8,128)(2,1)}, bf16[1,16,8,256]{3,2,1,0:T(8,128)(2,1)S(1)}, u32[]{:S(2)}) copy-start(bf16[1,16,8,256]{3,2,1,0:T(8,128)(2,1)S(1)} %pad_maximum_fusion.l0_ref) | copy-start | bytes 196612
  66.4 9.2 %collective-permute-start.7 = (bf16[1,16,8,256]{3,2,1,0:T(8,128)(2,1)S(1)}, bf16[1,16,8,256]{3,2,1,0:T(8,128)(2,1)S(1)}, u32[]{:S(2)}, u32[]{:S(2)}) collective-permute-start(bf16[1,16,8,256]{3,2,1,0:T(8,128)(2,1)S(1)} %pad_maximum_fusion.l0_ref), channel_id=1, source_target_pairs={{0,12},{4,16},{8,20},{12,24},{16,28},{20,32},{24,36},{28,40},{32,4... | collective-permute-start | bytes 196616 | tf_op jit(solution)/shard_map/ppermute | solution.py:19
  68.4 10.7 %collective-permute-start.8 = (bf16[1,16,8,256]{3,2,1,0:T(8,128)(2,1)S(1)}, bf16[1,16,8,256]{3,2,1,0:T(8,128)(2,1)S(1)}, u32[]{:S(2)}, u32[]{:S(2)}) collective-permute-start(bf16[1,16,8,256]{3,2,1,0:T(8,128)(2,1)S(1)} %pad_maximum_fusion.l0_ref), channel_id=1, source_target_pairs={{0,8},{4,12},{8,16},{12,20},{16,24},{20,28},{24,32},{28,36},{32,40... | collective-permute-start | bytes 196616 | tf_op jit(solution)/shard_map/ppermute | solution.py:19
  70.4 10.4 %collective-permute-start.9 = (bf16[1,16,8,256]{3,2,1,0:T(8,128)(2,1)S(1)}, bf16[1,16,8,256]{3,2,1,0:T(8,128)(2,1)S(1)}, u32[]{:S(2)}, u32[]{:S(2)}) collective-permute-start(bf16[1,16,8,256]{3,2,1,0:T(8,128)(2,1)S(1)} %pad_maximum_fusion.l0_ref), channel_id=1, source_target_pairs={{0,4},{4,8},{8,12},{12,16},{16,20},{20,24},{24,28},{28,32},{32,36}... | collective-permute-start | bytes 196616 | tf_op jit(solution)/shard_map/ppermute | solution.py:19
  75.7 5.1 %copy-start.9 = (bf16[1,16,8,256]{3,2,1,0:T(8,128)(2,1)}, bf16[1,16,8,256]{3,2,1,0:T(8,128)(2,1)S(1)}, u32[]{:S(2)}) copy-start(bf16[1,16,8,256]{3,2,1,0:T(8,128)(2,1)S(1)} %collective-permute-done.7.l3_ref) | copy-start | bytes 196612
  79.0 1.8 %copy-start.10 = (bf16[1,16,8,256]{3,2,1,0:T(8,128)(2,1)}, bf16[1,16,8,256]{3,2,1,0:T(8,128)(2,1)S(1)}, u32[]{:S(2)}) copy-start(bf16[1,16,8,256]{3,2,1,0:T(8,128)(2,1)S(1)} %collective-permute-done.8.l2_ref) | copy-start | bytes 196612
  80.8 0.6 copy-start.11

commit v11 on v10

--- a/solution.py
+++ b/solution.py
@@ -71,8 +71,25 @@
     return left + acc[out_channels : 2 * out_channels] + right
 
 
+def late_gate_kernel(
+    tp_ref, own_ref, bt_ref, k1_ref, vec_ref, mask_ref, o_ref, *, frames, rows, columns
+):
+    wide = rows + 2
+    span = wide * columns
+    x = tiled([(tp_ref, own_ref, bt_ref)], frames, 2, rows)
+    y = tap_sum(x, k1_ref, frames - 4, wide, columns, 2) + vec_ref[:, 0:1]
+    scale = lax.rsqrt(jnp.mean(y * y, axis=0, keepdims=True) + 1e-06)
+    z = y * scale * vec_ref[:, 1:2]
+    g = z / (1.0 + jnp.exp(-z))
+    for i in range(2):
+        for r in range(wide):
+            lo = i * span + r * columns
+            piece = g[:, lo : lo + columns] * mask_ref[frames + i, r]
+            o_ref[i, r] = piece.astype(o_ref.dtype)
+
+
 def encoder_kernel(
-    tc_ref, pv_ref, bc_ref, tp_ref, own_ref, bt_ref,
+    tc_ref, pv_ref, bc_ref, tp_ref, own_ref, bt_ref, late_ref,
     k1_ref, vec_ref, mask_ref, k2_ref, w_ref, o_ref, top_ref, bottom_ref, g_ref,
     *, frames, rows, columns
 ):
@@ -81,7 +98,7 @@
     gain = vec_ref[:, 1:2]
     x = tiled([(tc_ref, pv_ref, bc_ref), (tp_ref, own_ref, bt_ref)], frames, 2, rows)
     span = wide * columns
-    for t in range(0, frames + 2, 2):
+    for t in range(0, frames, 2):
         y = tap_sum(x, k1_ref, t, wide, columns, 2) + bias
         scale = lax.rsqrt(jnp.mean(y * y, axis=0, keepdims=True) + 1e-06)
         z = y * scale * gain
@@ -91,10 +108,11 @@
                 lo = i * span + r * columns
                 piece = g[:, lo : lo + columns] * mask_ref[t + i, r]
                 g_ref[t + i, r] = piece.astype(g_ref.dtype)
+    gated = lambda t, r: g_ref[t, r] if t < frames else late_ref[t - frames, r]
     total = None
     width = rows * columns
     for t in range(0, frames, 2):
-        y = tap_sum(from_ref(g_ref), k2_ref, t, rows, columns, 2)
+        y = tap_sum(gated, k2_ref, t, rows, columns, 2)
         for i in range(2):
             res = frame_rows(x, t + i + frames, 2, rows)
             hidden = (res.astype(jnp.float32) + y[:, i * width : (i + 1) * width]).astype(jnp.bfloat16)
@@ -186,6 +204,11 @@
     ]
     vmem = pl.BlockSpec(memory_space=pltpu.VMEM)
     smem = pl.BlockSpec(memory_space=pltpu.SMEM)
+    late = pl.pallas_call(
+        functools.partial(late_gate_kernel, **dims),
+        out_shape=jax.ShapeDtypeStruct((2, rows + 2, channels, columns), jnp.bfloat16),
+        in_specs=[vmem] * 5 + [smem],
+    )(pieces[3], own, pieces[5], k1, vec, mask)
     latent, lat_top, lat_bottom = pl.pallas_call(
         functools.partial(encoder_kernel, **dims),
         out_shape=(
@@ -193,10 +216,11 @@
             jax.ShapeDtypeStruct((1, z_count, 2, columns), jnp.bfloat16),
             jax.ShapeDtypeStruct((1, z_count, 2, columns), jnp.bfloat16),
         ),
-        in_specs=[vmem] * 8 + [smem, vmem, vmem],
-        scratch_shapes=[pltpu.VMEM((frames + 2, rows + 2, channels, columns), jnp.bfloat16)],
+        in_specs=[vmem] * 9 + [smem, vmem, vmem],
+        scratch_shapes=[pltpu.VMEM((frames, rows + 2, channels, columns), jnp.bfloat16)],
     )(
         *pieces,
+        late,
         k1,
         vec,
         mask,

time: 89.8 us -> 88.6 us (0.987)
  waiting for transfers between devices: 23.6 us -> 17 us
  local copies, waits for them, and re-layouts: 12.1 us -> 16.6 us
  Pallas kernels: 19.4 us -> 22.9 us
  starting transfers between devices: 31.8 us -> 29.1 us
    pallas_call x0 -> x1, Pallas kernels: none -> 5.03 us  [body(): pl.pallas_call(functools.partial(late_gate_kernel, **dims), out_shape=jax...]
    ppermute x6, waiting for transfers between devices: 9.39 us -> 4.85 us  [shift(): return lax.ppermute(x, 'rows', pairs)]
    ppermute x6, starting transfers between devices: 21.3 us -> 18.6 us  [shift(): return lax.ppermute(x, 'rows', pairs)]
    unnamed x33, local copies, waits for them, and re-layouts: 4.14 us -> 6.37 us
    transpose x4, local copies, waits for them, and re-layouts: 1.43 us -> 3.61 us  [merged_kernel(): return kernel.transpose(2, 3, 0, 1, 4).reshape(3 * o, 9 * c)]
    ppermute x4, waiting for transfers between devices: 14.2 us -> 12.2 us  [shift(): return lax.ppermute(x, 'tm', pairs)]
    pallas_call x1, Pallas kernels: 11.6 us -> 10 us  [body(): pl.pallas_call(functools.partial(encoder_kernel, **dims), out_shape=(jax....]
  transfers between devices with their start and end apart: 10 -> 10, of which waited for: 7 -> 5; matrix products, arithmetic and copies ran while one was open for 10% -> 12% of each run, Pallas kernels for 0% -> 6%
where the time goes in v11:
time: 88.6 us; the launch traced here: 88 us
  starting transfers between devices  29.1 us (33%)
  Pallas kernels  22.9 us (26%)
  waiting for transfers between devices  17 us (19%)
  local copies, waits for them, and re-layouts  16.6 us (19%)
  other arithmetic  1.5 us (2%)
    ppermute x6, starting transfers between devices, shift(): return lax.ppermute(x, 'rows', pairs)  18.6 us
    ppermute x4, waiting for transfers between devices, shift(): return lax.ppermute(x, 'tm', pairs)  12.2 us
    ppermute x4, starting transfers between devices, shift(): return lax.ppermute(x, 'tm', pairs)  10.5 us
    pallas_call x1, Pallas kernels, body(): pl.pallas_call(functools.partial(encoder_kernel, **dims), out_shape=(jax....  10 us
    pallas_call x1, Pallas kernels, body(): pl.pallas_call(functools.partial(decode_kernel_body, **dims), out_shape=j...  7.88 us
    unnamed x33, local copies, waits for them, and re-layouts  6.37 us
    pallas_call x1, Pallas kernels, body(): pl.pallas_call(functools.partial(late_gate_kernel, **dims), out_shape=jax...  5.03 us
    ppermute x6, waiting for transfers between devices, shift(): return lax.ppermute(x, 'rows', pairs)  4.85 us
  transfers between devices with their start and end apart: 10, of which 5 were waited for; matrix products, arithmetic and copies ran while one was open for 12% of the time, Pallas kernels for 6%

profile of v11, /device:TPU:24, one launch (start us, length us, event | category | flops | bytes accessed | tf_op | source)
XLA Modules:
  0.0 88.0 jit_solution(360557703265649779)
XLA Ops:
  0.6 1.3 %copy.42 = bf16[4,96,4,256]{3,1,2,0:T(8,128)(2,1)S(1)} copy(bf16[4,96,4,256]{3,2,1,0:T(4,128)(2,1)} %param.11) | data formatting | bytes 1572864 | tf_op args[0]
  1.9 0.0 copy-start
  1.9 0.0 copy-start.4
  1.9 3.5 %collective-permute-start = (bf16[4,4,96,256]{3,2,1,0:T(8,128)(2,1)S(1)}, bf16[4,4,96,256]{3,2,1,0:T(8,128)(2,1)S(1)}, u32[]{:S(2)}, u32[]{:S(2)}) collective-permute-start(bf16[4,4,96,256]{3,2,1,0:T(8,128)(2,1)S(1)} %bitcast.13), channel_id=1, source_target_pairs={{0,4},{4,8},{8,12},{12,16},{16,20},{20,24},{24,28},{28,32},{32,36}... | collective-permute-start | bytes 2359304 | tf_op jit(solution)/shard_map/ppermute | solution.py:19
  5.5 1.0 %fusion = (bf16[4,2,96,256]{3,2,1,0:T(8,128)(2,1)}, bf16[4,2,96,256]{3,2,1,0:T(8,128)(2,1)}) fusion(bf16[4,4,96,256]{3,2,1,0:T(8,128)(2,1)S(1)} %bitcast.14), kind=kLoop, calls=%fused_computation.6 | loop fusion | bytes 1572864 | tf_op jit(solution)/shard_map/slice | solution.py:177
  6.4 0.0 copy-done
  6.4 1.9 %collective-permute-start.3 = (bf16[4,2,96,256]{3,2,1,0:T(8,128)(2,1)}, bf16[4,2,96,256]{3,2,1,0:T(8,128)(2,1)S(1)}, u32[]{:S(2)}, u32[]{:S(2)}) collective-permute-start(bf16[4,2,96,256]{3,2,1,0:T(8,128)(2,1)} %get-tuple-element.25), channel_id=1, source_target_pairs={{0,1},{1,2},{2,3},{4,5},{5,6},{6,7},{8,9},{9,10},{10,11},{12,13},{... | collective-permute-start | bytes 1179656 | tf_op jit(solution)/shard_map/ppermute | solution.py:16
  8.3 5.1 %collective-permute-start.4 = (bf16[4,2,96,256]{3,2,1,0:T(8,128)(2,1)}, bf16[4,2,96,256]{3,2,1,0:T(8,128)(2,1)S(1)}, u32[]{:S(2)}, u32[]{:S(2)}) collective-permute-start(bf16[4,2,96,256]{3,2,1,0:T(8,128)(2,1)} %get-tuple-element.24), channel_id=1, source_target_pairs={{1,0},{2,1},{3,2},{5,4},{6,5},{7,6},{9,8},{10,9},{11,10},{13,12},{... | collective-permute-start | bytes 1179656 | tf_op jit(solution)/shard_map/ppermute | solution.py:16
  13.5 0.0 copy-done.4
  13.5 0.5 copy.33
  14.0 1.3 %reshape.16.k1_ref = bf16[288,864]{1,0:T(8,128)(2,1)} reshape(bf16[3,96,3,3,96]{4,3,2,1,0:T(4,128)(2,1)S(1)} %copy.33) | data formatting | bytes 995328 | tf_op jit(solution)/shard_map/reshape | solution.py:31
  15.3 1.5 %copy.34 = bf16[3,96,3,3,96]{4,3,2,1,0:T(4,128)(2,1)S(1)} copy(bf16[3,96,3,3,96]{4,1,0,3,2:T(8,128)(2,1)} %bitcast.18) | data formatting | bytes 995328 | tf_op jit(solution)/shard_map/transpose | solution.py:31
  16.8 0.0 copy-start.8
  16.8 1.3 %reshape.17.k2_ref = bf16[288,864]{1,0:T(8,128)(2,1)} reshape(bf16[3,96,3,3,96]{4,3,2,1,0:T(4,128)(2,1)S(1)} %copy.34) | data formatting | bytes 995328 | tf_op jit(solution)/shard_map/reshape | solution.py:31
  18.1 0.0 copy-done.8
  18.1 0.1 copy.35
  18.2 0.1 reshape.18
  18.3 1.6 %copy.36 = bf16[3,96,3,3,96]{4,3,2,1,0:T(4,128)(2,1)S(1)} copy(bf16[3,96,3,3,96]{4,1,0,3,2:T(8,128)(2,1)} %bitcast.19) | data formatting | bytes 995328 | tf_op jit(solution)/shard_map/transpose | solution.py:31
  19.9 0.0 copy-start.15
  19.9 1.3 %reshape.19.fk_ref = bf16[288,864]{1,0:T(8,128)(2,1)} reshape(bf16[3,96,3,3,96]{4,3,2,1,0:T(4,128)(2,1)S(1)} %copy.36) | data formatting | bytes 995328 | tf_op jit(solution)/shard_map/reshape | solution.py:31
  21.2 0.0 copy-start.12
  21.3 0.0 copy-start.13
  21.3 0.0 copy-start.14
  21.3 0.0 copy-done.15
  21.3 0.6 copy-done.12
  21.9 0.0 copy-done.13
  21.9 0.0 copy-done.14
  21.9 0.7 and_convert_fusion.mask_ref
  22.6 5.4 %collective-permute-done.pv_ref = bf16[4,4,96,256]{3,2,1,0:T(8,128)(2,1)S(1)} collective-permute-done((bf16[4,4,96,256]{3,2,1,0:T(8,128)(2,1)S(1)}, bf16[4,4,96,256]{3,2,1,0:T(8,128)(2,1)S(1)}, u32[]{:S(2)}, u32[]{:S(2)}) %collective-permute-start) | collective-permute-done | bytes 786464 | tf_op jit(solution)/shard_map/ppermute | solution.py:19
  28.0 0.0 copy-start.1
  28.0 0.1 fusion.1
  28.1 0.8 copy-done.1
  28.9 1.9 %collective-permute-start.1 = (bf16[4,2,96,256]{3,2,1,0:T(8,128)(2,1)S(1)}, bf16[4,2,96,256]{3,2,1,0:T(8,128)(2,1)S(1)}, u32[]{:S(2)}, u32[]{:S(2)}) collective-permute-start(bf16[4,2,96,256]{3,2,1,0:T(8,128)(2,1)S(1)} %get-tuple-element.13), channel_id=1, source_target_pairs={{0,1},{1,2},{2,3},{4,5},{5,6},{6,7},{8,9},{9,10},{10,11},{12,13},{... | collective-permute-start | bytes 1179656 | tf_op jit(solution)/shard_map/ppermute | solution.py:16
  30.8 5.1 %collective-permute-start.2 = (bf16[4,2,96,256]{3,2,1,0:T(8,128)(2,1)S(1)}, bf16[4,2,96,256]{3,2,1,0:T(8,128)(2,1)S(1)}, u32[]{:S(2)}, u32[]{:S(2)}) collective-permute-start(bf16[4,2,96,256]{3,2,1,0:T(8,128)(2,1)S(1)} %get-tuple-element.14), channel_id=1, source_target_pairs={{1,0},{2,1},{3,2},{5,4},{6,5},{7,6},{9,8},{10,9},{11,10},{13,12},{... | collective-permute-start | bytes 1179656 | tf_op jit(solution)/shard_map/ppermute | solution.py:16
  35.9 0.7 copy.37.vec_ref
  36.7 0.0 collective-permute-done.3.tp_ref
  36.7 0.0 collective-permute-done.4.bt_ref
  36.7 0.7 copy-done.2
  37.4 0.0 copy-start.3
  37.4 0.7 copy-done.3
  38.2 5.0 %shard_map.122.late_ref = bf16[2,6,96,256]{3,2,1,0:T(8,128)(2,1)} custom-call(bf16[4,2,96,256]{3,2,1,0:T(8,128)(2,1)} %copy-done.2, bf16[4,4,96,256]{3,2,1,0:T(8,128)(2,1)} %bitcast.15, bf16[4,2,96,256]{3,2,1,0:T(8,128)(2,1)} %copy-done.3, bf16[288,864]{1,0:T(8,128)(2,1)} %reshape.16.k1_ref, f32[96,4]{1,0:T(8,128)} %copy.37.vec_ref, ...), custom_call_target="tpu_custom_call" | custom-call | tf_op jit(solution)/shard_map/pallas_call | solution.py:207
  43.2 0.0 collective-permute-done.1.tc_ref
  43.2 0.0 collective-permute-done.2.bc_ref
  43.2 0.7 copy-done.5
  44.0 0.7 copy-done.6
  44.7 10.0 %shard_map.123 = (bf16[1,16,4,256]{3,2,1,0:T(4,128)(2,1)}, bf16[1,16,2,256]{3,2,1,0:T(2,128)(2,1)}, bf16[1,16,2,256]{3,2,1,0:T(2,128)(2,1)}) custom-call(bf16[4,2,96,256]{3,2,1,0:T(8,128)(2,1)} %copy-done.5, bf16[4,4,96,256]{3,2,1,0:T(8,128)(2,1)} %copy-done.1, bf16[4,2,96,256]{3,2,1,0:T(8,128)(2,1)} %copy-done.6, bf16[4,2,96,256]{3,2,1,0:T(8,128)(2,1)} %copy-done.2, ...), custom_call_target="tpu_custom_call" | custom-call | tf_op jit(solution)/shard_map/pallas_call | solution.py:212
  54.7 2.6 %collective-permute-start.6 = (bf16[1,16,2,256]{3,2,1,0:T(2,128)(2,1)}, bf16[1,16,2,256]{3,2,1,0:T(2,128)(2,1)S(1)}, u32[]{:S(2)}, u32[]{:S(2)}) collective-permute-start(bf16[1,16,2,256]{3,2,1,0:T(2,128)(2,1)} %get-tuple-element.21), channel_id=1, source_target_pairs={{1,0},{2,1},{3,2},{5,4},{6,5},{7,6},{9,8},{10,9},{11,10},{13,12},{... | collective-permute-start | bytes 49160 | tf_op jit(solution)/shard_map/ppermute | solution.py:16
  57.3 1.9 %collective-permute-start.5 = (bf16[1,16,2,256]{3,2,1,0:T(2,128)(2,1)}, bf16[1,16,2,256]{3,2,1,0:T(2,128)(2,1)S(1)}, u32[]{:S(2)}, u32[]{:S(2)}) collective-permute-start(bf16[1,16,2,256]{3,2,1,0:T(2,128)(2,1)} %get-tuple-element.20), channel_id=1, source_target_pairs={{0,1},{1,2},{2,3},{4,5},{5,6},{6,7},{8,9},{9,10},{10,11},{12,13},{... | collective-permute-start | bytes 49160 | tf_op jit(solution)/shard_map/ppermute | solution.py:16
  59.2 0.0 collective-permute-done.6
  59.2 4.8 %collective-permute-done.5 = bf16[1,16,2,256]{3,2,1,0:T(2,128)(2,1)S(1)} collective-permute-done((bf16[1,16,2,256]{3,2,1,0:T(2,128)(2,1)}, bf16[1,16,2,256]{3,2,1,0:T(2,128)(2,1)S(1)}, u32[]{:S(2)}, u32[]{:S(2)}) %collective-permute-start.5) | collective-permute-done | bytes 16416 | tf_op jit(solution)/shard_map/ppermute | solution.py:16
  64.1 0.8 pad_maximum_fusion.l0_ref
  64.9 0.0 copy-start.7
  64.9 2.1 %collective-permute-start.7 = (bf16[1,16,8,256]{3,2,1,0:T(8,128)(2,1)S(1)}, bf16[1,16,8,256]{3,2,1,0:T(8,128)(2,1)S(1)}, u32[]{:S(2)}, u32[]{:S(2)}) collective-permute-start(bf16[1,16,8,256]{3,2,1,0:T(8,128)(2,1)S(1)} %pad_maximum_fusion.l0_ref), channel_id=1, source_target_pairs={{0,12},{4,16},{8,20},{12,24},{16,28},{20,32},{24,36},{28,40},{32,4... | collective-permute-start | bytes 196616 | tf_op jit(solution)/shard_map/ppermute | solution.py:19
  67.0 2.0 %collective-permute-start.8 = (bf16[1,16,8,256]{3,2,1,0:T(8,128)(2,1)S(1)}, bf16[1,16,8,256]{3,2,1,0:T(8,128)(2,1)S(1)}, u32[]{:S(2)}, u32[]{:S(2)}) collective-permute-start(bf16[1,16,8,256]{3,2,1,0:T(8,128)(2,1)S(1)} %pad_maximum_fusion.l0_ref), channel_id=1, source_target_pairs={{0,8},{4,12},{8,16},{12,20},{16,24},{20,28},{24,32},{28,36},{32,40... | collective-permute-start | bytes 196616 | tf_op jit(solution)/shard_map/ppermute | solution.py:19
  69.1 2.8 %collective-permute-start.9 = (bf16[1,16,8,256]{3,2,1,0:T(8,128)(2,1)S(1)}, bf16[1,16,8,256]{3,2,1,0:T(8,128)(2,1)S(1)}, u32[]{:S(2)}, u32[]{:S(2)}) collective-permute-start(bf16[1,16,8,256]{3,2,1,0:T(8,128)(2,1)S(1)} %pad_maximum_fusion.l0_ref), channel_id=1, source_target_pairs={{0,4},{4,8},{8,12},{12,16},{16,20},{20,24},{24,28},{28,32},{32,36}... | collective-permute-start | bytes 196616 | tf_op jit(solution)/shard_map/ppermute | solution.py:19
  71.9 0.8 copy.39.dk_ref
  72.6 0.0 copy-done.7
  72.6 1.4 %collective-permute-done.7.l3_ref = bf16[1,16,8,256]{3,2,1,0:T(8,128)(2,1)S(1)} collective-permute-done((bf16[1,16,8,256]{3,2,1,0:T(8,128)(2,1)S(1)}, bf16[1,16,8,256]{3,2,1,0:T(8,128)(2,1)S(1)}, u32[]{:S(2)}, u32[]{:S(2)}) %collective-permute-start.7) | collective-permute-done | bytes 65568 | tf_op jit(solution)/shard_map/ppermute | solution.py:19
  74.1 3.6 %collective-permute-done.8.l2_ref = bf16[1,16,8,256]{3,2,1,0:T(8,128)(2,1)S(1)} collective-permute-done((bf16[1,16,8,256]{3,2,1,0:T(8,128)(2,1)S(1)}, bf16[1,16,8,256]{3,2,1,0:T(8,128)(2,1)S(1)}, u32[]{:S(2)}, u32[]{:S(2)}) %collective-permute-start.8) | collective-permute-done | bytes 65568 | tf_op jit(solution)/shard_map/ppermute | solution.py:19
  77.7 1.8 %collective-permute-done.9.l1_ref = bf16[1,16,8,256]{3,2,1,0:T(8,128)(2,1)S(1)} collective-permute-done((bf16[1,16,8,256]{3,2,1,0:T(8,128)(2,1)S(1)}, bf16[1,16,8,256]{3,2,1,0:T(8,128)(2,1)S(1)}, u32[]{:S(2)}, u32[]{:S(2)}) %collective-permute-start.9) | collective-permute-done | bytes 65568 | tf_op jit(solution)/shard_map/ppermute | solution.py:19
  79.5 0.0 copy-done.9
  79.5 0.0 copy-done.10
  79.5 0.6 copy-done.11
  80.1 7.9 %shard_map.124 = bf16[4,96,4,256]{3,2,1,0:T(4,128)(2,1)} custom-call(bf16[1,16,8,256]{3,2,1,0:T(8,128)(2,1)} %copy-done.9, bf16[1,16,8,256]{3,2,1,0:T(8,128)(2,1)} %copy-done.10, bf16[1,16,8,256]{3,2,1,0:T(8,128)(2,1)} %copy-done.11, bf16[1,16,8,256]{3,2,1,0:T(8,128)(2,1)} %copy-done.7, bf16[288,144]{1,0:T(8,128)(2,1)} %copy.39.dk_ref, ...), custom_call_target="tpu_custom_call" | custom-call | tf_op jit(solution)/shard_map/pallas_call | solution.py:234
  (8 shorter events, 0.0 us)
Async XLA Ops:
  1.9 4.5 %copy-start = (bf16[4,96,4,256]{3,1,2,0:T(8,128)(2,1)}, bf16[4,96,4,256]{3,1,2,0:T(8,128)(2,1)S(1)}, u32[]{:S(2)}) copy-start(bf16[4,96,4,256]{3,1,2,0:T(8,128)(2,1)S(1)} %copy.42) | copy-start | bytes 2359300
  1.9 11.6 %copy-start.4 = (bf16[3,3,3,96,96]{4,3,2,1,0:T(8,128)(2,1)S(1)}, bf16[3,3,3,96,96]{4,3,2,1,0:T(8,128)(2,1)}, u32[]{:S(2)}) copy-start(bf16[3,3,3,96,96]{4,3,2,1,0:T(8,128)(2,1)} %param.12) | copy-start | bytes 1492996
  1.9 26.1 %collective-permute-start = (bf16[4,4,96,256]{3,2,1,0:T(8,128)(2,1)S(1)}, bf16[4,4,96,256]{3,2,1,0:T(8,128)(2,1)S(1)}, u32[]{:S(2)}, u32[]{:S(2)}) collective-permute-start(bf16[4,4,96,256]{3,2,1,0:T(8,128)(2,1)S(1)} %bitcast.13), channel_id=1, source_target_pairs={{0,4},{4,8},{8,12},{12,16},{16,20},{20,24},{24,28},{28,32},{32,36}... | collective-permute-start | bytes 2359304 | tf_op jit(solution)/shard_map/ppermute | solution.py:19
  6.4 30.3 %collective-permute-start.3 = (bf16[4,2,96,256]{3,2,1,0:T(8,128)(2,1)}, bf16[4,2,96,256]{3,2,1,0:T(8,128)(2,1)S(1)}, u32[]{:S(2)}, u32[]{:S(2)}) collective-permute-start(bf16[4,2,96,256]{3,2,1,0:T(8,128)(2,1)} %get-tuple-element.25), channel_id=1, source_target_pairs={{0,1},{1,2},{2,3},{4,5},{5,6},{6,7},{8,9},{9,10},{10,11},{12,13},{... | collective-permute-start | bytes 1179656 | tf_op jit(solution)/shard_map/ppermute | solution.py:16
  8.3 28.3 %collective-permute-start.4 = (bf16[4,2,96,256]{3,2,1,0:T(8,128)(2,1)}, bf16[4,2,96,256]{3,2,1,0:T(8,128)(2,1)S(1)}, u32[]{:S(2)}, u32[]{:S(2)}) collective-permute-start(bf16[4,2,96,256]{3,2,1,0:T(8,128)(2,1)} %get-tuple-element.24), channel_id=1, source_target_pairs={{1,0},{2,1},{3,2},{5,4},{6,5},{7,6},{9,8},{10,9},{11,10},{13,12},{... | collective-permute-start | bytes 1179656 | tf_op jit(solution)/shard_map/ppermute | solution.py:16
  16.8 1.3 %copy-start.8 = (bf16[3,3,3,96,16]{3,4,2,1,0:T(8,128)(2,1)S(1)}, bf16[3,3,3,96,16]{3,4,2,1,0:T(8,128)(2,1)}, u32[]{:S(2)}) copy-start(bf16[3,3,3,96,16]{3,4,2,1,0:T(8,128)(2,1)} %param.17) | copy-start | bytes 248836
  19.9 1.4 %copy-start.15 = (f32[96]{0:T(128)S(1)}, f32[96]{0:T(128)}, u32[]{:S(2)}) copy-start(f32[96]{0:T(128)} %param.13) | copy-start | bytes 1156
  21.2 0.7 copy-start.12
  21.3 0.7 copy-start.13
  21.3 0.7 copy-start.14
  28.0 0.9 copy-start.1
  28.9 14.3 %collective-permute-start.1 = (bf16[4,2,96,256]{3,2,1,0:T(8,128)(2,1)S(1)}, bf16[4,2,96,256]{3,2,1,0:T(8,128)(2,1)S(1)}, u32[]{:S(2)}, u32[]{:S(2)}) collective-permute-start(bf16[4,2,96,256]{3,2,1,0:T(8,128)(2,1)S(1)} %get-tuple-element.13), channel_id=1, source_target_pairs={{0,1},{1,2},{2,3},{4,5},{5,6},{6,7},{8,9},{9,10},{10,11},{12,13},{... | collective-permute-start | bytes 1179656 | tf_op jit(solution)/shard_map/ppermute | solution.py:16
  30.8 12.4 %collective-permute-start.2 = (bf16[4,2,96,256]{3,2,1,0:T(8,128)(2,1)S(1)}, bf16[4,2,96,256]{3,2,1,0:T(8,128)(2,1)S(1)}, u32[]{:S(2)}, u32[]{:S(2)}) collective-permute-start(bf16[4,2,96,256]{3,2,1,0:T(8,128)(2,1)S(1)} %get-tuple-element.14), channel_id=1, source_target_pairs={{1,0},{2,1},{3,2},{5,4},{6,5},{7,6},{9,8},{10,9},{11,10},{13,12},{... | collective-permute-start | bytes 1179656 | tf_op jit(solution)/shard_map/ppermute | solution.py:16
  36.7 0.8 copy-start.2
  37.4 0.7 copy-start.3
  43.2 0.8 copy-start.5
  44.0 0.7 copy-start.6
  54.7 4.5 %collective-permute-start.6 = (bf16[1,16,2,256]{3,2,1,0:T(2,128)(2,1)}, bf16[1,16,2,256]{3,2,1,0:T(2,128)(2,1)S(1)}, u32[]{:S(2)}, u32[]{:S(2)}) collective-permute-start(bf16[1,16,2,256]{3,2,1,0:T(2,128)(2,1)} %get-tuple-element.21), channel_id=1, source_target_pairs={{1,0},{2,1},{3,2},{5,4},{6,5},{7,6},{9,8},{10,9},{11,10},{13,12},{... | collective-permute-start | bytes 49160 | tf_op jit(solution)/shard_map/ppermute | solution.py:16
  57.3 6.8 %collective-permute-start.5 = (bf16[1,16,2,256]{3,2,1,0:T(2,128)(2,1)}, bf16[1,16,2,256]{3,2,1,0:T(2,128)(2,1)S(1)}, u32[]{:S(2)}, u32[]{:S(2)}) collective-permute-start(bf16[1,16,2,256]{3,2,1,0:T(2,128)(2,1)} %get-tuple-element.20), channel_id=1, source_target_pairs={{0,1},{1,2},{2,3},{4,5},{5,6},{6,7},{8,9},{9,10},{10,11},{12,13},{... | collective-permute-start | bytes 49160 | tf_op jit(solution)/shard_map/ppermute | solution.py:16
  64.9 7.8 %copy-start.7 = (bf16[1,16,8,256]{3,2,1,0:T(8,128)(2,1)}, bf16[1,16,8,256]{3,2,1,0:T(8,128)(2,1)S(1)}, u32[]{:S(2)}) copy-start(bf16[1,16,8,256]{3,2,1,0:T(8,128)(2,1)S(1)} %pad_maximum_fusion.l0_ref) | copy-start | bytes 196612
  64.9 9.2 %collective-permute-start.7 = (bf16[1,16,8,256]{3,2,1,0:T(8,128)(2,1)S(1)}, bf16[1,16,8,256]{3,2,1,0:T(8,128)(2,1)S(1)}, u32[]{:S(2)}, u32[]{:S(2)}) collective-permute-start(bf16[1,16,8,256]{3,2,1,0:T(8,128)(2,1)S(1)} %pad_maximum_fusion.l0_ref), channel_id=1, source_target_pairs={{0,12},{4,16},{8,20},{12,24},{16,28},{20,32},{24,36},{28,40},{32,4... | collective-permute-start | bytes 196616 | tf_op jit(solution)/shard_map/ppermute | solution.py:19
  67.0 10.7 %collective-permute-start.8 = (bf16[1,16,8,256]{3,2,1,0:T(8,128)(2,1)S(1)}, bf16[1,16,8,256]{3,2,1,0:T(8,128)(2,1)S(1)}, u32[]{:S(2)}, u32[]{:S(2)}) collective-permute-start(bf16[1,16,8,256]{3,2,1,0:T(8,128)(2,1)S(1)} %pad_maximum_fusion.l0_ref), channel_id=1, source_target_pairs={{0,8},{4,12},{8,16},{12,20},{16,24},{20,28},{24,32},{28,36},{32,40... | collective-permute-start | bytes 196616 | tf_op jit(solution)/shard_map/ppermute | solution.py:19
  69.1 10.4 %collective-permute-start.9 = (bf16[1,16,8,256]{3,2,1,0:T(8,128)(2,1)S(1)}, bf16[1,16,8,256]{3,2,1,0:T(8,128)(2,1)S(1)}, u32[]{:S(2)}, u32[]{:S(2)}) collective-permute-start(bf16[1,16,8,256]{3,2,1,0:T(8,128)(2,1)S(1)} %pad_maximum_fusion.l0_ref), channel_id=1, source_target_pairs={{0,4},{4,8},{8,12},{12,16},{16,20},{20,24},{24,28},{28,32},{32,36}... | collective-permute-start | bytes 196616 | tf_op jit(solution)/shard_map/ppermute | solution.py:19
  74.1 5.4 %copy-start.9 = (bf16[1,16,8,256]{3,2,1,0:T(8,128)(2,1)}, bf16[1,16,8,256]{3,2,1,0:T(8,128)(2,1)S(1)}, u32[]{:S(2)}) copy-start(bf16[1,16,8,256]{3,2,1,0:T(8,128)(2,1)S(1)} %collective-permute-done.7.l3_ref) | copy-start | bytes 196612
  77.7 1.8 %copy-start.10 = (bf16[1,16,8,256]{3,2,1,0:T(8,128)(2,1)}, bf16[1,16,8,256]{3,2,1,0:T(8,128)(2,1)S(1)}, u32[]{:S(2)}) copy-start(bf16[1,16,8,256]{3,2,1,0:T(8,128)(2,1)S(1)} %collective-permute-done.8.l2_ref) | copy-start | bytes 196612
  79.5 0.6 copy-start.11

commit v12 on v11

--- a/solution.py
+++ b/solution.py
@@ -71,44 +71,64 @@
     return left + acc[out_channels : 2 * out_channels] + right
 
 
-def late_gate_kernel(
-    tp_ref, own_ref, bt_ref, k1_ref, vec_ref, mask_ref, o_ref, *, frames, rows, columns
-):
-    wide = rows + 2
-    span = wide * columns
-    x = tiled([(tp_ref, own_ref, bt_ref)], frames, 2, rows)
-    y = tap_sum(x, k1_ref, frames - 4, wide, columns, 2) + vec_ref[:, 0:1]
+def at_row(get, r):
+    return lambda t, rr: get(t, rr + r)
+
+
+def gate_block(x, k1_ref, vec_ref, mask_ref, t, r0, count, columns, store):
+    span = count * columns
+    y = tap_sum(at_row(x, r0), k1_ref, t, count, columns, 2) + vec_ref[:, 0:1]
     scale = lax.rsqrt(jnp.mean(y * y, axis=0, keepdims=True) + 1e-06)
     z = y * scale * vec_ref[:, 1:2]
     g = z / (1.0 + jnp.exp(-z))
     for i in range(2):
-        for r in range(wide):
+        for r in range(count):
             lo = i * span + r * columns
-            piece = g[:, lo : lo + columns] * mask_ref[frames + i, r]
-            o_ref[i, r] = piece.astype(o_ref.dtype)
+            store(i, r, g[:, lo : lo + columns])
+
+
+def late_gate_kernel(
+    tp_ref, own_ref, bt_ref, k1_ref, vec_ref, mask_ref, o_ref, *, frames, rows, columns
+):
+    x = tiled([(tp_ref, own_ref, bt_ref)], frames, 2, rows)
+
+    def store(i, r, piece):
+        o_ref[i, r] = (piece * mask_ref[frames + i, r]).astype(o_ref.dtype)
+
+    gate_block(x, k1_ref, vec_ref, mask_ref, frames - 4, 0, rows + 2, columns, store)
+
+
+def inner_gate_kernel(pv_ref, own_ref, k1_ref, vec_ref, mask_ref, o_ref, *, frames, rows, columns):
+    x = tiled([(None, pv_ref, None), (None, own_ref, None)], frames, 2, rows)
+    for t in range(0, frames, 2):
+
+        def store(i, r, piece, t=t):
+            o_ref[t + i, r] = (piece * mask_ref[t + i, r + 2]).astype(o_ref.dtype)
+
+        gate_block(x, k1_ref, vec_ref, mask_ref, t, 2, rows - 2, columns, store)
 
 
 def encoder_kernel(
-    tc_ref, pv_ref, bc_ref, tp_ref, own_ref, bt_ref, late_ref,
+    tc_ref, pv_ref, bc_ref, tp_ref, own_ref, bt_ref, late_ref, inner_ref,
     k1_ref, vec_ref, mask_ref, k2_ref, w_ref, o_ref, top_ref, bottom_ref, g_ref,
     *, frames, rows, columns
 ):
-    wide = rows + 2
-    bias = vec_ref[:, 0:1]
-    gain = vec_ref[:, 1:2]
     x = tiled([(tc_ref, pv_ref, bc_ref), (tp_ref, own_ref, bt_ref)], frames, 2, rows)
-    span = wide * columns
     for t in range(0, frames, 2):
-        y = tap_sum(x, k1_ref, t, wide, columns, 2) + bias
-        scale = lax.rsqrt(jnp.mean(y * y, axis=0, keepdims=True) + 1e-06)
-        z = y * scale * gain
-        g = z / (1.0 + jnp.exp(-z))
-        for i in range(2):
-            for r in range(wide):
-                lo = i * span + r * columns
-                piece = g[:, lo : lo + columns] * mask_ref[t + i, r]
-                g_ref[t + i, r] = piece.astype(g_ref.dtype)
-    gated = lambda t, r: g_ref[t, r] if t < frames else late_ref[t - frames, r]
+        for r0 in (0, rows):
+
+            def store(i, r, piece, t=t, r0=r0):
+                g_ref[t + i, r0 + r] = (piece * mask_ref[t + i, r0 + r]).astype(g_ref.dtype)
+
+            gate_block(x, k1_ref, vec_ref, mask_ref, t, r0, 2, columns, store)
+
+    def gated(t, r):
+        if t >= frames:
+            return late_ref[t - frames, r]
+        if 2 <= r < rows:
+            return inner_ref[t, r - 2]
+        return g_ref[t, r]
+
     total = None
     width = rows * columns
     for t in range(0, frames, 2):
@@ -209,6 +229,11 @@
         out_shape=jax.ShapeDtypeStruct((2, rows + 2, channels, columns), jnp.bfloat16),
         in_specs=[vmem] * 5 + [smem],
     )(pieces[3], own, pieces[5], k1, vec, mask)
+    inner = pl.pallas_call(
+        functools.partial(inner_gate_kernel, **dims),
+        out_shape=jax.ShapeDtypeStruct((frames, rows - 2, channels, columns), jnp.bfloat16),
+        in_specs=[vmem] * 4 + [smem],
+    )(previous, own, k1, vec, mask)
     latent, lat_top, lat_bottom = pl.pallas_call(
         functools.partial(encoder_kernel, **dims),
         out_shape=(
@@ -216,11 +241,12 @@
             jax.ShapeDtypeStruct((1, z_count, 2, columns), jnp.bfloat16),
             jax.ShapeDtypeStruct((1, z_count, 2, columns), jnp.bfloat16),
         ),
-        in_specs=[vmem] * 9 + [smem, vmem, vmem],
+        in_specs=[vmem] * 10 + [smem, vmem, vmem],
         scratch_shapes=[pltpu.VMEM((frames, rows + 2, channels, columns), jnp.bfloat16)],
     )(
         *pieces,
         late,
+        inner,
         k1,
         vec,
         mask,

time: 88.6 us -> 90.6 us (1.023)
  Pallas kernels: 22.9 us -> 25.6 us
    pallas_call x0 -> x1, Pallas kernels: none -> 3.97 us  [body(): pl.pallas_call(functools.partial(inner_gate_kernel, **dims), out_shape=ja...]
    pallas_call x1, Pallas kernels: 10 us -> 8.71 us  [body(): pl.pallas_call(functools.partial(encoder_kernel, **dims), out_shape=(jax....]
  transfers between devices with their start and end apart: 10 -> 10, of which waited for: 5 -> 5; matrix products, arithmetic and copies ran while one was open for 12% -> 12% of each run, Pallas kernels for 6% -> 10%
where the time goes in v12:
time: 90.6 us; the launch traced here: 89.9 us
  starting transfers between devices  29.1 us (32%)
  Pallas kernels  25.6 us (28%)
  local copies, waits for them, and re-layouts  16.6 us (18%)
  waiting for transfers between devices  16.3 us (18%)
  other arithmetic  1.49 us (2%)
    ppermute x6, starting transfers between devices, shift(): return lax.ppermute(x, 'rows', pairs)  18.6 us
    ppermute x4, waiting for transfers between devices, shift(): return lax.ppermute(x, 'tm', pairs)  12 us
    ppermute x4, starting transfers between devices, shift(): return lax.ppermute(x, 'tm', pairs)  10.5 us
    pallas_call x1, Pallas kernels, body(): pl.pallas_call(functools.partial(encoder_kernel, **dims), out_shape=(jax....  8.71 us
    pallas_call x1, Pallas kernels, body(): pl.pallas_call(functools.partial(decode_kernel_body, **dims), out_shape=j...  7.88 us
    unnamed x33, local copies, waits for them, and re-layouts  6.35 us
    pallas_call x1, Pallas kernels, body(): pl.pallas_call(functools.partial(late_gate_kernel, **dims), out_shape=jax...  5.03 us
    ppermute x6, waiting for transfers between devices, shift(): return lax.ppermute(x, 'rows', pairs)  4.37 us
  transfers between devices with their start and end apart: 10, of which 5 were waited for; matrix products, arithmetic and copies ran while one was open for 12% of the time, Pallas kernels for 10%

profile of v12, /device:TPU:24, one launch (start us, length us, event | category | flops | bytes accessed | tf_op | source)
XLA Modules:
  0.0 89.9 jit_solution(6855268609892658504)
XLA Ops:
  0.6 1.3 %copy.43 = bf16[4,96,4,256]{3,1,2,0:T(8,128)(2,1)S(1)} copy(bf16[4,96,4,256]{3,2,1,0:T(4,128)(2,1)} %param.11) | data formatting | bytes 1572864 | tf_op args[0]
  1.9 0.0 copy-start
  1.9 0.0 copy-start.4
  1.9 3.5 %collective-permute-start = (bf16[4,4,96,256]{3,2,1,0:T(8,128)(2,1)S(1)}, bf16[4,4,96,256]{3,2,1,0:T(8,128)(2,1)S(1)}, u32[]{:S(2)}, u32[]{:S(2)}) collective-permute-start(bf16[4,4,96,256]{3,2,1,0:T(8,128)(2,1)S(1)} %bitcast.13), channel_id=1, source_target_pairs={{0,4},{4,8},{8,12},{12,16},{16,20},{20,24},{24,28},{28,32},{32,36}... | collective-permute-start | bytes 2359304 | tf_op jit(solution)/shard_map/ppermute | solution.py:19
  5.5 1.0 %fusion = (bf16[4,2,96,256]{3,2,1,0:T(8,128)(2,1)}, bf16[4,2,96,256]{3,2,1,0:T(8,128)(2,1)}) fusion(bf16[4,4,96,256]{3,2,1,0:T(8,128)(2,1)S(1)} %bitcast.14), kind=kLoop, calls=%fused_computation.6 | loop fusion | bytes 1572864 | tf_op jit(solution)/shard_map/slice | solution.py:197
  6.4 0.0 copy-done
  6.4 1.9 %collective-permute-start.3 = (bf16[4,2,96,256]{3,2,1,0:T(8,128)(2,1)}, bf16[4,2,96,256]{3,2,1,0:T(8,128)(2,1)S(1)}, u32[]{:S(2)}, u32[]{:S(2)}) collective-permute-start(bf16[4,2,96,256]{3,2,1,0:T(8,128)(2,1)} %get-tuple-element.25), channel_id=1, source_target_pairs={{0,1},{1,2},{2,3},{4,5},{5,6},{6,7},{8,9},{9,10},{10,11},{12,13},{... | collective-permute-start | bytes 1179656 | tf_op jit(solution)/shard_map/ppermute | solution.py:16
  8.3 5.1 %collective-permute-start.4 = (bf16[4,2,96,256]{3,2,1,0:T(8,128)(2,1)}, bf16[4,2,96,256]{3,2,1,0:T(8,128)(2,1)S(1)}, u32[]{:S(2)}, u32[]{:S(2)}) collective-permute-start(bf16[4,2,96,256]{3,2,1,0:T(8,128)(2,1)} %get-tuple-element.24), channel_id=1, source_target_pairs={{1,0},{2,1},{3,2},{5,4},{6,5},{7,6},{9,8},{10,9},{11,10},{13,12},{... | collective-permute-start | bytes 1179656 | tf_op jit(solution)/shard_map/ppermute | solution.py:16
  13.5 0.0 copy-done.4
  13.5 0.5 copy.33
  14.0 1.3 %reshape.16.k1_ref = bf16[288,864]{1,0:T(8,128)(2,1)} reshape(bf16[3,96,3,3,96]{4,3,2,1,0:T(4,128)(2,1)S(1)} %copy.33) | data formatting | bytes 995328 | tf_op jit(solution)/shard_map/reshape | solution.py:31
  15.3 1.5 %copy.34 = bf16[3,96,3,3,96]{4,3,2,1,0:T(4,128)(2,1)S(1)} copy(bf16[3,96,3,3,96]{4,1,0,3,2:T(8,128)(2,1)} %bitcast.19) | data formatting | bytes 995328 | tf_op jit(solution)/shard_map/transpose | solution.py:31
  16.8 0.0 copy-start.8
  16.8 1.3 %reshape.17.k2_ref = bf16[288,864]{1,0:T(8,128)(2,1)} reshape(bf16[3,96,3,3,96]{4,3,2,1,0:T(4,128)(2,1)S(1)} %copy.34) | data formatting | bytes 995328 | tf_op jit(solution)/shard_map/reshape | solution.py:31
  18.1 0.0 copy-done.8
  18.1 0.1 copy.35
  18.2 0.1 reshape.18
  18.3 1.6 %copy.36 = bf16[3,96,3,3,96]{4,3,2,1,0:T(4,128)(2,1)S(1)} copy(bf16[3,96,3,3,96]{4,1,0,3,2:T(8,128)(2,1)} %bitcast.20) | data formatting | bytes 995328 | tf_op jit(solution)/shard_map/transpose | solution.py:31
  19.9 0.0 copy-start.15
  19.9 1.3 %reshape.19.fk_ref = bf16[288,864]{1,0:T(8,128)(2,1)} reshape(bf16[3,96,3,3,96]{4,3,2,1,0:T(4,128)(2,1)S(1)} %copy.36) | data formatting | bytes 995328 | tf_op jit(solution)/shard_map/reshape | solution.py:31
  21.3 0.0 copy-start.12
  21.3 0.0 copy-start.13
  21.3 0.0 copy-start.14
  21.3 0.0 copy-done.15
  21.3 0.6 copy-done.12
  21.9 0.0 copy-done.13
  21.9 0.0 copy-done.14
  22.0 0.7 and_convert_fusion.mask_ref
  22.6 5.4 %collective-permute-done.pv_ref = bf16[4,4,96,256]{3,2,1,0:T(8,128)(2,1)S(1)} collective-permute-done((bf16[4,4,96,256]{3,2,1,0:T(8,128)(2,1)S(1)}, bf16[4,4,96,256]{3,2,1,0:T(8,128)(2,1)S(1)}, u32[]{:S(2)}, u32[]{:S(2)}) %collective-permute-start) | collective-permute-done | bytes 786464 | tf_op jit(solution)/shard_map/ppermute | solution.py:19
  28.0 0.0 copy-start.1
  28.0 0.1 fusion.1
  28.1 0.8 copy-done.1
  28.9 1.9 %collective-permute-start.1 = (bf16[4,2,96,256]{3,2,1,0:T(8,128)(2,1)S(1)}, bf16[4,2,96,256]{3,2,1,0:T(8,128)(2,1)S(1)}, u32[]{:S(2)}, u32[]{:S(2)}) collective-permute-start(bf16[4,2,96,256]{3,2,1,0:T(8,128)(2,1)S(1)} %get-tuple-element.13), channel_id=1, source_target_pairs={{0,1},{1,2},{2,3},{4,5},{5,6},{6,7},{8,9},{9,10},{10,11},{12,13},{... | collective-permute-start | bytes 1179656 | tf_op jit(solution)/shard_map/ppermute | solution.py:16
  30.8 5.3 %collective-permute-start.2 = (bf16[4,2,96,256]{3,2,1,0:T(8,128)(2,1)S(1)}, bf16[4,2,96,256]{3,2,1,0:T(8,128)(2,1)S(1)}, u32[]{:S(2)}, u32[]{:S(2)}) collective-permute-start(bf16[4,2,96,256]{3,2,1,0:T(8,128)(2,1)S(1)} %get-tuple-element.14), channel_id=1, source_target_pairs={{1,0},{2,1},{3,2},{5,4},{6,5},{7,6},{9,8},{10,9},{11,10},{13,12},{... | collective-permute-start | bytes 1179656 | tf_op jit(solution)/shard_map/ppermute | solution.py:16
  36.1 0.7 copy.37.vec_ref
  36.8 4.0 %shard_map.123.inner_ref = bf16[4,2,96,256]{3,2,1,0:T(8,128)(2,1)} custom-call(bf16[4,4,96,256]{3,2,1,0:T(8,128)(2,1)} %copy-done.1, bf16[4,4,96,256]{3,2,1,0:T(8,128)(2,1)} %bitcast.15, bf16[288,864]{1,0:T(8,128)(2,1)} %reshape.16.k1_ref, f32[96,4]{1,0:T(8,128)} %copy.37.vec_ref, f32[6,6]{1,0:T(8,128)} %and_convert_fusion.mask_ref), custom_call_target="tpu_custom_call" | custom-call | tf_op jit(solution)/shard_map/pallas_call | solution.py:232
  40.8 0.0 collective-permute-done.3.tp_ref
  40.8 0.0 collective-permute-done.4.bt_ref
  40.8 0.7 copy-done.2
  41.6 0.7 copy-done.3
  42.3 5.0 %shard_map.122.late_ref = bf16[2,6,96,256]{3,2,1,0:T(8,128)(2,1)} custom-call(bf16[4,2,96,256]{3,2,1,0:T(8,128)(2,1)} %copy-done.2, bf16[4,4,96,256]{3,2,1,0:T(8,128)(2,1)} %bitcast.16, bf16[4,2,96,256]{3,2,1,0:T(8,128)(2,1)} %copy-done.3, bf16[288,864]{1,0:T(8,128)(2,1)} %reshape.16.k1_ref, f32[96,4]{1,0:T(8,128)} %copy.37.vec_ref, ...), custom_call_target="tpu_custom_call" | custom-call | tf_op jit(solution)/shard_map/pallas_call | solution.py:227
  47.3 0.0 collective-permute-done.1.tc_ref
  47.3 0.0 collective-permute-done.2.bc_ref
  47.4 0.7 copy-done.5
  48.1 0.7 copy-done.6
  48.8 8.7 %shard_map.124 = (bf16[1,16,4,256]{3,2,1,0:T(4,128)(2,1)}, bf16[1,16,2,256]{3,2,1,0:T(2,128)(2,1)}, bf16[1,16,2,256]{3,2,1,0:T(2,128)(2,1)}) custom-call(bf16[4,2,96,256]{3,2,1,0:T(8,128)(2,1)} %copy-done.5, bf16[4,4,96,256]{3,2,1,0:T(8,128)(2,1)} %copy-done.1, bf16[4,2,96,256]{3,2,1,0:T(8,128)(2,1)} %copy-done.6, bf16[4,2,96,256]{3,2,1,0:T(8,128)(2,1)} %copy-done.2, ...), custom_call_target="tpu_custom_call" | custom-call | tf_op jit(solution)/shard_map/pallas_call | solution.py:237
  57.5 1.9 %collective-permute-start.6 = (bf16[1,16,2,256]{3,2,1,0:T(2,128)(2,1)}, bf16[1,16,2,256]{3,2,1,0:T(2,128)(2,1)S(1)}, u32[]{:S(2)}, u32[]{:S(2)}) collective-permute-start(bf16[1,16,2,256]{3,2,1,0:T(2,128)(2,1)} %get-tuple-element.21), channel_id=1, source_target_pairs={{1,0},{2,1},{3,2},{5,4},{6,5},{7,6},{9,8},{10,9},{11,10},{13,12},{... | collective-permute-start | bytes 49160 | tf_op jit(solution)/shard_map/ppermute | solution.py:16
  59.5 2.4 %collective-permute-start.5 = (bf16[1,16,2,256]{3,2,1,0:T(2,128)(2,1)}, bf16[1,16,2,256]{3,2,1,0:T(2,128)(2,1)S(1)}, u32[]{:S(2)}, u32[]{:S(2)}) collective-permute-start(bf16[1,16,2,256]{3,2,1,0:T(2,128)(2,1)} %get-tuple-element.20), channel_id=1, source_target_pairs={{0,1},{1,2},{2,3},{4,5},{5,6},{6,7},{8,9},{9,10},{10,11},{12,13},{... | collective-permute-start | bytes 49160 | tf_op jit(solution)/shard_map/ppermute | solution.py:16
  61.9 0.0 collective-permute-done.6
  61.9 4.4 %collective-permute-done.5 = bf16[1,16,2,256]{3,2,1,0:T(2,128)(2,1)S(1)} collective-permute-done((bf16[1,16,2,256]{3,2,1,0:T(2,128)(2,1)}, bf16[1,16,2,256]{3,2,1,0:T(2,128)(2,1)S(1)}, u32[]{:S(2)}, u32[]{:S(2)}) %collective-permute-start.5) | collective-permute-done | bytes 16416 | tf_op jit(solution)/shard_map/ppermute | solution.py:16
  66.2 0.8 pad_maximum_fusion.l0_ref
  67.1 0.0 copy-start.7
  67.1 1.9 %collective-permute-start.7 = (bf16[1,16,8,256]{3,2,1,0:T(8,128)(2,1)S(1)}, bf16[1,16,8,256]{3,2,1,0:T(8,128)(2,1)S(1)}, u32[]{:S(2)}, u32[]{:S(2)}) collective-permute-start(bf16[1,16,8,256]{3,2,1,0:T(8,128)(2,1)S(1)} %pad_maximum_fusion.l0_ref), channel_id=1, source_target_pairs={{0,12},{4,16},{8,20},{12,24},{16,28},{20,32},{24,36},{28,40},{32,4... | collective-permute-start | bytes 196616 | tf_op jit(solution)/shard_map/ppermute | solution.py:19
  69.0 2.0 %collective-permute-start.8 = (bf16[1,16,8,256]{3,2,1,0:T(8,128)(2,1)S(1)}, bf16[1,16,8,256]{3,2,1,0:T(8,128)(2,1)S(1)}, u32[]{:S(2)}, u32[]{:S(2)}) collective-permute-start(bf16[1,16,8,256]{3,2,1,0:T(8,128)(2,1)S(1)} %pad_maximum_fusion.l0_ref), channel_id=1, source_target_pairs={{0,8},{4,12},{8,16},{12,20},{16,24},{20,28},{24,32},{28,36},{32,40... | collective-permute-start | bytes 196616 | tf_op jit(solution)/shard_map/ppermute | solution.py:19
  71.0 3.0 %collective-permute-start.9 = (bf16[1,16,8,256]{3,2,1,0:T(8,128)(2,1)S(1)}, bf16[1,16,8,256]{3,2,1,0:T(8,128)(2,1)S(1)}, u32[]{:S(2)}, u32[]{:S(2)}) collective-permute-start(bf16[1,16,8,256]{3,2,1,0:T(8,128)(2,1)S(1)} %pad_maximum_fusion.l0_ref), channel_id=1, source_target_pairs={{0,4},{4,8},{8,12},{12,16},{16,20},{20,24},{24,28},{28,32},{32,36}... | collective-permute-start | bytes 196616 | tf_op jit(solution)/shard_map/ppermute | solution.py:19
  74.1 0.8 copy.40.dk_ref
  74.8 0.0 copy-done.7
  74.8 1.6 %collective-permute-done.7.l3_ref = bf16[1,16,8,256]{3,2,1,0:T(8,128)(2,1)S(1)} collective-permute-done((bf16[1,16,8,256]{3,2,1,0:T(8,128)(2,1)S(1)}, bf16[1,16,8,256]{3,2,1,0:T(8,128)(2,1)S(1)}, u32[]{:S(2)}, u32[]{:S(2)}) %collective-permute-start.7) | collective-permute-done | bytes 65568 | tf_op jit(solution)/shard_map/ppermute | solution.py:19
  76.4 3.3 %collective-permute-done.8.l2_ref = bf16[1,16,8,256]{3,2,1,0:T(8,128)(2,1)S(1)} collective-permute-done((bf16[1,16,8,256]{3,2,1,0:T(8,128)(2,1)S(1)}, bf16[1,16,8,256]{3,2,1,0:T(8,128)(2,1)S(1)}, u32[]{:S(2)}, u32[]{:S(2)}) %collective-permute-start.8) | collective-permute-done | bytes 65568 | tf_op jit(solution)/shard_map/ppermute | solution.py:19
  79.7 1.8 %collective-permute-done.9.l1_ref = bf16[1,16,8,256]{3,2,1,0:T(8,128)(2,1)S(1)} collective-permute-done((bf16[1,16,8,256]{3,2,1,0:T(8,128)(2,1)S(1)}, bf16[1,16,8,256]{3,2,1,0:T(8,128)(2,1)S(1)}, u32[]{:S(2)}, u32[]{:S(2)}) %collective-permute-start.9) | collective-permute-done | bytes 65568 | tf_op jit(solution)/shard_map/ppermute | solution.py:19
  81.4 0.0 copy-done.9
  81.4 0.0 copy-done.10
  81.4 0.6 copy-done.11
  82.1 7.9 %shard_map.125 = bf16[4,96,4,256]{3,2,1,0:T(4,128)(2,1)} custom-call(bf16[1,16,8,256]{3,2,1,0:T(8,128)(2,1)} %copy-done.9, bf16[1,16,8,256]{3,2,1,0:T(8,128)(2,1)} %copy-done.10, bf16[1,16,8,256]{3,2,1,0:T(8,128)(2,1)} %copy-done.11, bf16[1,16,8,256]{3,2,1,0:T(8,128)(2,1)} %copy-done.7, bf16[288,144]{1,0:T(8,128)(2,1)} %copy.40.dk_ref, ...), custom_call_target="tpu_custom_call" | custom-call | tf_op jit(solution)/shard_map/pallas_call | solution.py:260
  (9 shorter events, 0.0 us)
Async XLA Ops:
  1.9 4.5 %copy-start = (bf16[4,96,4,256]{3,1,2,0:T(8,128)(2,1)}, bf16[4,96,4,256]{3,1,2,0:T(8,128)(2,1)S(1)}, u32[]{:S(2)}) copy-start(bf16[4,96,4,256]{3,1,2,0:T(8,128)(2,1)S(1)} %copy.43) | copy-start | bytes 2359300
  1.9 11.6 %copy-start.4 = (bf16[3,3,3,96,96]{4,3,2,1,0:T(8,128)(2,1)S(1)}, bf16[3,3,3,96,96]{4,3,2,1,0:T(8,128)(2,1)}, u32[]{:S(2)}) copy-start(bf16[3,3,3,96,96]{4,3,2,1,0:T(8,128)(2,1)} %param.12) | copy-start | bytes 1492996
  1.9 26.1 %collective-permute-start = (bf16[4,4,96,256]{3,2,1,0:T(8,128)(2,1)S(1)}, bf16[4,4,96,256]{3,2,1,0:T(8,128)(2,1)S(1)}, u32[]{:S(2)}, u32[]{:S(2)}) collective-permute-start(bf16[4,4,96,256]{3,2,1,0:T(8,128)(2,1)S(1)} %bitcast.13), channel_id=1, source_target_pairs={{0,4},{4,8},{8,12},{12,16},{16,20},{20,24},{24,28},{28,32},{32,36}... | collective-permute-start | bytes 2359304 | tf_op jit(solution)/shard_map/ppermute | solution.py:19
  6.4 34.4 %collective-permute-start.3 = (bf16[4,2,96,256]{3,2,1,0:T(8,128)(2,1)}, bf16[4,2,96,256]{3,2,1,0:T(8,128)(2,1)S(1)}, u32[]{:S(2)}, u32[]{:S(2)}) collective-permute-start(bf16[4,2,96,256]{3,2,1,0:T(8,128)(2,1)} %get-tuple-element.25), channel_id=1, source_target_pairs={{0,1},{1,2},{2,3},{4,5},{5,6},{6,7},{8,9},{9,10},{10,11},{12,13},{... | collective-permute-start | bytes 1179656 | tf_op jit(solution)/shard_map/ppermute | solution.py:16
  8.3 32.5 %collective-permute-start.4 = (bf16[4,2,96,256]{3,2,1,0:T(8,128)(2,1)}, bf16[4,2,96,256]{3,2,1,0:T(8,128)(2,1)S(1)}, u32[]{:S(2)}, u32[]{:S(2)}) collective-permute-start(bf16[4,2,96,256]{3,2,1,0:T(8,128)(2,1)} %get-tuple-element.24), channel_id=1, source_target_pairs={{1,0},{2,1},{3,2},{5,4},{6,5},{7,6},{9,8},{10,9},{11,10},{13,12},{... | collective-permute-start | bytes 1179656 | tf_op jit(solution)/shard_map/ppermute | solution.py:16
  16.8 1.3 %copy-start.8 = (bf16[3,3,3,96,16]{3,4,2,1,0:T(8,128)(2,1)S(1)}, bf16[3,3,3,96,16]{3,4,2,1,0:T(8,128)(2,1)}, u32[]{:S(2)}) copy-start(bf16[3,3,3,96,16]{3,4,2,1,0:T(8,128)(2,1)} %param.17) | copy-start | bytes 248836
  19.9 1.4 %copy-start.15 = (f32[96]{0:T(128)S(1)}, f32[96]{0:T(128)}, u32[]{:S(2)}) copy-start(f32[96]{0:T(128)} %param.13) | copy-start | bytes 1156
  21.3 0.7 copy-start.12
  21.3 0.7 copy-start.13
  21.3 0.7 copy-start.14
  28.0 0.9 copy-start.1
  28.9 18.5 %collective-permute-start.1 = (bf16[4,2,96,256]{3,2,1,0:T(8,128)(2,1)S(1)}, bf16[4,2,96,256]{3,2,1,0:T(8,128)(2,1)S(1)}, u32[]{:S(2)}, u32[]{:S(2)}) collective-permute-start(bf16[4,2,96,256]{3,2,1,0:T(8,128)(2,1)S(1)} %get-tuple-element.13), channel_id=1, source_target_pairs={{0,1},{1,2},{2,3},{4,5},{5,6},{6,7},{8,9},{9,10},{10,11},{12,13},{... | collective-permute-start | bytes 1179656 | tf_op jit(solution)/shard_map/ppermute | solution.py:16
  30.8 16.6 %collective-permute-start.2 = (bf16[4,2,96,256]{3,2,1,0:T(8,128)(2,1)S(1)}, bf16[4,2,96,256]{3,2,1,0:T(8,128)(2,1)S(1)}, u32[]{:S(2)}, u32[]{:S(2)}) collective-permute-start(bf16[4,2,96,256]{3,2,1,0:T(8,128)(2,1)S(1)} %get-tuple-element.14), channel_id=1, source_target_pairs={{1,0},{2,1},{3,2},{5,4},{6,5},{7,6},{9,8},{10,9},{11,10},{13,12},{... | collective-permute-start | bytes 1179656 | tf_op jit(solution)/shard_map/ppermute | solution.py:16
  40.8 0.8 copy-start.2
  41.6 0.7 copy-start.3
  47.3 0.7 copy-start.5
  48.1 0.7 copy-start.6
  57.5 4.3 %collective-permute-start.6 = (bf16[1,16,2,256]{3,2,1,0:T(2,128)(2,1)}, bf16[1,16,2,256]{3,2,1,0:T(2,128)(2,1)S(1)}, u32[]{:S(2)}, u32[]{:S(2)}) collective-permute-start(bf16[1,16,2,256]{3,2,1,0:T(2,128)(2,1)} %get-tuple-element.21), channel_id=1, source_target_pairs={{1,0},{2,1},{3,2},{5,4},{6,5},{7,6},{9,8},{10,9},{11,10},{13,12},{... | collective-permute-start | bytes 49160 | tf_op jit(solution)/shard_map/ppermute | solution.py:16
  59.5 6.8 %collective-permute-start.5 = (bf16[1,16,2,256]{3,2,1,0:T(2,128)(2,1)}, bf16[1,16,2,256]{3,2,1,0:T(2,128)(2,1)S(1)}, u32[]{:S(2)}, u32[]{:S(2)}) collective-permute-start(bf16[1,16,2,256]{3,2,1,0:T(2,128)(2,1)} %get-tuple-element.20), channel_id=1, source_target_pairs={{0,1},{1,2},{2,3},{4,5},{5,6},{6,7},{8,9},{9,10},{10,11},{12,13},{... | collective-permute-start | bytes 49160 | tf_op jit(solution)/shard_map/ppermute | solution.py:16
  67.1 7.8 %copy-start.7 = (bf16[1,16,8,256]{3,2,1,0:T(8,128)(2,1)}, bf16[1,16,8,256]{3,2,1,0:T(8,128)(2,1)S(1)}, u32[]{:S(2)}) copy-start(bf16[1,16,8,256]{3,2,1,0:T(8,128)(2,1)S(1)} %pad_maximum_fusion.l0_ref) | copy-start | bytes 196612
  67.1 9.3 %collective-permute-start.7 = (bf16[1,16,8,256]{3,2,1,0:T(8,128)(2,1)S(1)}, bf16[1,16,8,256]{3,2,1,0:T(8,128)(2,1)S(1)}, u32[]{:S(2)}, u32[]{:S(2)}) collective-permute-start(bf16[1,16,8,256]{3,2,1,0:T(8,128)(2,1)S(1)} %pad_maximum_fusion.l0_ref), channel_id=1, source_target_pairs={{0,12},{4,16},{8,20},{12,24},{16,28},{20,32},{24,36},{28,40},{32,4... | collective-permute-start | bytes 196616 | tf_op jit(solution)/shard_map/ppermute | solution.py:19
  69.0 10.7 %collective-permute-start.8 = (bf16[1,16,8,256]{3,2,1,0:T(8,128)(2,1)S(1)}, bf16[1,16,8,256]{3,2,1,0:T(8,128)(2,1)S(1)}, u32[]{:S(2)}, u32[]{:S(2)}) collective-permute-start(bf16[1,16,8,256]{3,2,1,0:T(8,128)(2,1)S(1)} %pad_maximum_fusion.l0_ref), channel_id=1, source_target_pairs={{0,8},{4,12},{8,16},{12,20},{16,24},{20,28},{24,32},{28,36},{32,40... | collective-permute-start | bytes 196616 | tf_op jit(solution)/shard_map/ppermute | solution.py:19
  71.0 10.4 %collective-permute-start.9 = (bf16[1,16,8,256]{3,2,1,0:T(8,128)(2,1)S(1)}, bf16[1,16,8,256]{3,2,1,0:T(8,128)(2,1)S(1)}, u32[]{:S(2)}, u32[]{:S(2)}) collective-permute-start(bf16[1,16,8,256]{3,2,1,0:T(8,128)(2,1)S(1)} %pad_maximum_fusion.l0_ref), channel_id=1, source_target_pairs={{0,4},{4,8},{8,12},{12,16},{16,20},{20,24},{24,28},{28,32},{32,36}... | collective-permute-start | bytes 196616 | tf_op jit(solution)/shard_map/ppermute | solution.py:19
  76.4 5.0 %copy-start.9 = (bf16[1,16,8,256]{3,2,1,0:T(8,128)(2,1)}, bf16[1,16,8,256]{3,2,1,0:T(8,128)(2,1)S(1)}, u32[]{:S(2)}) copy-start(bf16[1,16,8,256]{3,2,1,0:T(8,128)(2,1)S(1)} %collective-permute-done.7.l3_ref) | copy-start | bytes 196612
  79.7 1.8 %copy-start.10 = (bf16[1,16,8,256]{3,2,1,0:T(8,128)(2,1)}, bf16[1,16,8,256]{3,2,1,0:T(8,128)(2,1)S(1)}, u32[]{:S(2)}) copy-start(bf16[1,16,8,256]{3,2,1,0:T(8,128)(2,1)S(1)} %collective-permute-done.8.l2_ref) | copy-start | bytes 196612
  81.4 0.6 copy-start.11

commit v13 on v11

--- a/solution.py
+++ b/solution.py
@@ -190,25 +190,28 @@
         jnp.stack([first_bias, first_gain, decode_bias, decode_gain], 1),
         inside.astype(jnp.float32),
     )
-    prev_top, prev_bottom, *params = lax.optimization_barrier(
-        (previous[:, -2:], previous[:, :2], *params)
+    vmem = pl.BlockSpec(memory_space=pltpu.VMEM)
+    smem = pl.BlockSpec(memory_space=pltpu.SMEM)
+    k1, k2, dk, fk, vec, mask = params
+    from_above = shift(top, 0, 1)
+    from_below = shift(bottom, 0, -1)
+    late = pl.pallas_call(
+        functools.partial(late_gate_kernel, **dims),
+        out_shape=jax.ShapeDtypeStruct((2, rows + 2, channels, columns), jnp.bfloat16),
+        in_specs=[vmem] * 5 + [smem],
+    )(from_above, own, from_below, k1, vec, mask)
+    prev_top, prev_bottom, late, *params = lax.optimization_barrier(
+        (previous[:, -2:], previous[:, :2], late, *params)
     )
     k1, k2, dk, fk, vec, mask = params
     pieces = [
         shift(prev_top, 0, 1),
         previous,
         shift(prev_bottom, 0, -1),
-        shift(top, 0, 1),
+        from_above,
         own,
-        shift(bottom, 0, -1),
+        from_below,
     ]
-    vmem = pl.BlockSpec(memory_space=pltpu.VMEM)
-    smem = pl.BlockSpec(memory_space=pltpu.SMEM)
-    late = pl.pallas_call(
-        functools.partial(late_gate_kernel, **dims),
-        out_shape=jax.ShapeDtypeStruct((2, rows + 2, channels, columns), jnp.bfloat16),
-        in_specs=[vmem] * 5 + [smem],
-    )(pieces[3], own, pieces[5], k1, vec, mask)
     latent, lat_top, lat_bottom = pl.pallas_call(
         functools.partial(encoder_kernel, **dims),
         out_shape=(

time: 88.6 us -> 94.4 us (1.065)
  the two profiles are of different devices: /device:TPU:24 before, /device:TPU:65 now
where the time goes in v13:
time: 94.4 us; the launch traced here: 93.7 us
  starting transfers between devices  34.3 us (36%)
  Pallas kernels  22.9 us (24%)
  local copies, waits for them, and re-layouts  17.7 us (19%)
  waiting for transfers between devices  16.4 us (17%)
  other arithmetic  1.5 us (2%)
    ppermute x6, starting transfers between devices, shift(): return lax.ppermute(x, 'rows', pairs)  18.9 us
    ppermute x4, starting transfers between devices, shift(): return lax.ppermute(x, 'tm', pairs)  15.3 us
    ppermute x6, waiting for transfers between devices, shift(): return lax.ppermute(x, 'rows', pairs)  12.3 us
    pallas_call x1, Pallas kernels, body(): pl.pallas_call(functools.partial(encoder_kernel, **dims), out_shape=(jax....  10 us
    pallas_call x1, Pallas kernels, body(): pl.pallas_call(functools.partial(decode_kernel_body, **dims), out_shape=j...  7.88 us
    unnamed x31, local copies, waits for them, and re-layouts  5.67 us
    pallas_call x1, Pallas kernels, body(): pl.pallas_call(functools.partial(late_gate_kernel, **dims), out_shape=jax...  5.03 us
    transpose x4, local copies, waits for them, and re-layouts, merged_kernel(): return kernel.transpose(2, 3, 0, 1, 4).reshape(3 * o, 9 * c)  4.7 us
  transfers between devices with their start and end apart: 10, of which 4 were waited for; matrix products, arithmetic and copies ran while one was open for 14% of the time, Pallas kernels for 5%

profile of v13, /device:TPU:65, one launch (start us, length us, event | category | flops | bytes accessed | tf_op | source)
XLA Modules:
  0.0 93.7 jit_solution(4811147208340624467)
XLA Ops:
  0.6 1.3 %copy.42 = bf16[4,96,4,256]{3,1,2,0:T(8,128)(2,1)S(1)} copy(bf16[4,96,4,256]{3,2,1,0:T(4,128)(2,1)} %param.11) | data formatting | bytes 1572864 | tf_op args[0]
  1.9 0.0 copy-start
  1.9 3.1 %collective-permute-start = (bf16[4,4,96,256]{3,2,1,0:T(8,128)(2,1)S(1)}, bf16[4,4,96,256]{3,2,1,0:T(8,128)(2,1)S(1)}, u32[]{:S(2)}, u32[]{:S(2)}) collective-permute-start(bf16[4,4,96,256]{3,2,1,0:T(8,128)(2,1)S(1)} %bitcast.13), channel_id=1, source_target_pairs={{0,4},{4,8},{8,12},{12,16},{16,20},{20,24},{24,28},{28,32},{32,36}... | collective-permute-start | bytes 2359304 | tf_op jit(solution)/shard_map/ppermute | solution.py:19
  5.0 1.0 %fusion = (bf16[4,2,96,256]{3,2,1,0:T(8,128)(2,1)}, bf16[4,2,96,256]{3,2,1,0:T(8,128)(2,1)}) fusion(bf16[4,4,96,256]{3,2,1,0:T(8,128)(2,1)S(1)} %bitcast.14), kind=kLoop, calls=%fused_computation.6 | loop fusion | bytes 1572864 | tf_op jit(solution)/shard_map/slice | solution.py:177
  6.0 0.0 copy-done
  6.0 5.7 %collective-permute-start.1 = (bf16[4,2,96,256]{3,2,1,0:T(8,128)(2,1)}, bf16[4,2,96,256]{3,2,1,0:T(8,128)(2,1)S(1)}, u32[]{:S(2)}, u32[]{:S(2)}) collective-permute-start(bf16[4,2,96,256]{3,2,1,0:T(8,128)(2,1)} %get-tuple-element.27), channel_id=1, source_target_pairs={{0,1},{1,2},{2,3},{4,5},{5,6},{6,7},{8,9},{9,10},{10,11},{12,13},{... | collective-permute-start | bytes 1179656 | tf_op jit(solution)/shard_map/ppermute | solution.py:16
  11.7 1.9 %collective-permute-start.2 = (bf16[4,2,96,256]{3,2,1,0:T(8,128)(2,1)}, bf16[4,2,96,256]{3,2,1,0:T(8,128)(2,1)S(1)}, u32[]{:S(2)}, u32[]{:S(2)}) collective-permute-start(bf16[4,2,96,256]{3,2,1,0:T(8,128)(2,1)} %get-tuple-element.26), channel_id=1, source_target_pairs={{1,0},{2,1},{3,2},{5,4},{6,5},{7,6},{9,8},{10,9},{11,10},{13,12},{... | collective-permute-start | bytes 1179656 | tf_op jit(solution)/shard_map/ppermute | solution.py:16
  13.6 1.6 %copy.33 = bf16[3,96,3,3,96]{4,3,2,1,0:T(4,128)(2,1)S(1)} copy(bf16[3,96,3,3,96]{4,1,0,3,2:T(8,128)(2,1)} %bitcast.17) | data formatting | bytes 995328 | tf_op jit(solution)/shard_map/transpose | solution.py:31
  15.1 0.0 copy-start.14
  15.2 1.3 %reshape.16.k1_ref = bf16[288,864]{1,0:T(8,128)(2,1)} reshape(bf16[3,96,3,3,96]{4,3,2,1,0:T(4,128)(2,1)S(1)} %copy.33) | data formatting | bytes 995328 | tf_op jit(solution)/shard_map/reshape | solution.py:31
  16.5 0.0 copy-start.11
  16.5 0.0 copy-start.12
  16.5 0.0 copy-start.13
  16.5 0.0 copy-done.14
  16.5 0.6 copy-done.11
  17.1 0.0 copy-done.12
  17.1 0.0 copy-done.13
  17.2 0.7 copy.34.vec_ref
  17.9 1.5 %copy.35 = bf16[3,96,3,3,96]{4,3,2,1,0:T(4,128)(2,1)S(1)} copy(bf16[3,96,3,3,96]{4,1,0,3,2:T(8,128)(2,1)} %bitcast.18) | data formatting | bytes 995328 | tf_op jit(solution)/shard_map/transpose | solution.py:31
  19.5 1.3 %reshape.17.k2_ref = bf16[288,864]{1,0:T(8,128)(2,1)} reshape(bf16[3,96,3,3,96]{4,3,2,1,0:T(4,128)(2,1)S(1)} %copy.35) | data formatting | bytes 995328 | tf_op jit(solution)/shard_map/reshape | solution.py:31
  20.8 1.5 %copy.37 = bf16[3,96,3,3,96]{4,3,2,1,0:T(4,128)(2,1)S(1)} copy(bf16[3,96,3,3,96]{4,1,0,3,2:T(8,128)(2,1)} %bitcast.19) | data formatting | bytes 995328 | tf_op jit(solution)/shard_map/transpose | solution.py:31
  22.3 0.0 copy-start.7
  22.3 1.3 %reshape.19.fk_ref = bf16[288,864]{1,0:T(8,128)(2,1)} reshape(bf16[3,96,3,3,96]{4,3,2,1,0:T(4,128)(2,1)S(1)} %copy.37) | data formatting | bytes 995328 | tf_op jit(solution)/shard_map/reshape | solution.py:31
  23.7 0.0 copy-done.7
  23.7 0.1 copy.36
  23.7 0.1 reshape.18
  23.9 0.7 and_convert_fusion.mask_ref
  24.6 0.0 collective-permute-done.1.tp_ref
  24.6 0.0 copy-start.2
  24.6 0.0 collective-permute-done.2.bt_ref
  24.6 0.8 copy-done.2
  25.3 0.0 copy-start.3
  25.3 0.8 copy-done.3
  26.1 5.0 %shard_map.122.late_ref = bf16[2,6,96,256]{3,2,1,0:T(8,128)(2,1)} custom-call(bf16[4,2,96,256]{3,2,1,0:T(8,128)(2,1)} %copy-done.2, bf16[4,4,96,256]{3,2,1,0:T(8,128)(2,1)} %bitcast.15, bf16[4,2,96,256]{3,2,1,0:T(8,128)(2,1)} %copy-done.3, bf16[288,864]{1,0:T(8,128)(2,1)} %reshape.16.k1_ref, f32[96,4]{1,0:T(8,128)} %copy.34.vec_ref, ...), custom_call_target="tpu_custom_call" | custom-call | tf_op jit(solution)/shard_map/pallas_call | solution.py:198
  31.1 0.0 collective-permute-done.pv_ref
  31.1 0.1 fusion.1
  31.2 0.8 copy-done.1
  32.0 5.1 %collective-permute-start.3 = (bf16[4,2,96,256]{3,2,1,0:T(8,128)(2,1)S(1)}, bf16[4,2,96,256]{3,2,1,0:T(8,128)(2,1)S(1)}, u32[]{:S(2)}, u32[]{:S(2)}) collective-permute-start(bf16[4,2,96,256]{3,2,1,0:T(8,128)(2,1)S(1)} %get-tuple-element.14), channel_id=1, source_target_pairs={{0,1},{1,2},{2,3},{4,5},{5,6},{6,7},{8,9},{9,10},{10,11},{12,13},{... | collective-permute-start | bytes 1179656 | tf_op jit(solution)/shard_map/ppermute | solution.py:16
  37.1 1.9 %collective-permute-start.4 = (bf16[4,2,96,256]{3,2,1,0:T(8,128)(2,1)S(1)}, bf16[4,2,96,256]{3,2,1,0:T(8,128)(2,1)S(1)}, u32[]{:S(2)}, u32[]{:S(2)}) collective-permute-start(bf16[4,2,96,256]{3,2,1,0:T(8,128)(2,1)S(1)} %get-tuple-element.15), channel_id=1, source_target_pairs={{1,0},{2,1},{3,2},{5,4},{6,5},{7,6},{9,8},{10,9},{11,10},{13,12},{... | collective-permute-start | bytes 1179656 | tf_op jit(solution)/shard_map/ppermute | solution.py:16
  39.1 0.7 copy.38.vec_ref
  39.8 2.1 %collective-permute-done.3.tc_ref = bf16[4,2,96,256]{3,2,1,0:T(8,128)(2,1)S(1)} collective-permute-done((bf16[4,2,96,256]{3,2,1,0:T(8,128)(2,1)S(1)}, bf16[4,2,96,256]{3,2,1,0:T(8,128)(2,1)S(1)}, u32[]{:S(2)}, u32[]{:S(2)}) %collective-permute-start.3) | collective-permute-done | bytes 393248 | tf_op jit(solution)/shard_map/ppermute | solution.py:16
  41.8 5.9 %collective-permute-done.4.bc_ref = bf16[4,2,96,256]{3,2,1,0:T(8,128)(2,1)S(1)} collective-permute-done((bf16[4,2,96,256]{3,2,1,0:T(8,128)(2,1)S(1)}, bf16[4,2,96,256]{3,2,1,0:T(8,128)(2,1)S(1)}, u32[]{:S(2)}, u32[]{:S(2)}) %collective-permute-start.4) | collective-permute-done | bytes 393248 | tf_op jit(solution)/shard_map/ppermute | solution.py:16
  47.7 0.0 copy-done.4
  47.7 0.8 copy-done.5
  48.5 10.0 %shard_map.123 = (bf16[1,16,4,256]{3,2,1,0:T(4,128)(2,1)}, bf16[1,16,2,256]{3,2,1,0:T(2,128)(2,1)}, bf16[1,16,2,256]{3,2,1,0:T(2,128)(2,1)}) custom-call(bf16[4,2,96,256]{3,2,1,0:T(8,128)(2,1)} %copy-done.4, bf16[4,4,96,256]{3,2,1,0:T(8,128)(2,1)} %copy-done.1, bf16[4,2,96,256]{3,2,1,0:T(8,128)(2,1)} %copy-done.5, bf16[4,2,96,256]{3,2,1,0:T(8,128)(2,1)} %copy-done.2, ...), custom_call_target="tpu_custom_call" | custom-call | tf_op jit(solution)/shard_map/pallas_call | solution.py:215
  58.5 1.9 %collective-permute-start.5 = (bf16[1,16,2,256]{3,2,1,0:T(2,128)(2,1)}, bf16[1,16,2,256]{3,2,1,0:T(2,128)(2,1)S(1)}, u32[]{:S(2)}, u32[]{:S(2)}) collective-permute-start(bf16[1,16,2,256]{3,2,1,0:T(2,128)(2,1)} %get-tuple-element.22), channel_id=1, source_target_pairs={{0,1},{1,2},{2,3},{4,5},{5,6},{6,7},{8,9},{9,10},{10,11},{12,13},{... | collective-permute-start | bytes 49160 | tf_op jit(solution)/shard_map/ppermute | solution.py:16
  60.4 2.4 %collective-permute-start.6 = (bf16[1,16,2,256]{3,2,1,0:T(2,128)(2,1)}, bf16[1,16,2,256]{3,2,1,0:T(2,128)(2,1)S(1)}, u32[]{:S(2)}, u32[]{:S(2)}) collective-permute-start(bf16[1,16,2,256]{3,2,1,0:T(2,128)(2,1)} %get-tuple-element.23), channel_id=1, source_target_pairs={{1,0},{2,1},{3,2},{5,4},{6,5},{7,6},{9,8},{10,9},{11,10},{13,12},{... | collective-permute-start | bytes 49160 | tf_op jit(solution)/shard_map/ppermute | solution.py:16
  62.8 0.0 collective-permute-done.5
  62.9 4.4 %collective-permute-done.6 = bf16[1,16,2,256]{3,2,1,0:T(2,128)(2,1)S(1)} collective-permute-done((bf16[1,16,2,256]{3,2,1,0:T(2,128)(2,1)}, bf16[1,16,2,256]{3,2,1,0:T(2,128)(2,1)S(1)}, u32[]{:S(2)}, u32[]{:S(2)}) %collective-permute-start.6) | collective-permute-done | bytes 16416 | tf_op jit(solution)/shard_map/ppermute | solution.py:16
  67.2 0.8 pad_maximum_fusion.l0_ref
  68.0 0.0 copy-start.6
  68.0 4.6 %collective-permute-start.7 = (bf16[1,16,8,256]{3,2,1,0:T(8,128)(2,1)S(1)}, bf16[1,16,8,256]{3,2,1,0:T(8,128)(2,1)S(1)}, u32[]{:S(2)}, u32[]{:S(2)}) collective-permute-start(bf16[1,16,8,256]{3,2,1,0:T(8,128)(2,1)S(1)} %pad_maximum_fusion.l0_ref), channel_id=1, source_target_pairs={{0,12},{4,16},{8,20},{12,24},{16,28},{20,32},{24,36},{28,40},{32,4... | collective-permute-start | bytes 196616 | tf_op jit(solution)/shard_map/ppermute | solution.py:19
  72.7 3.4 %collective-permute-start.8 = (bf16[1,16,8,256]{3,2,1,0:T(8,128)(2,1)S(1)}, bf16[1,16,8,256]{3,2,1,0:T(8,128)(2,1)S(1)}, u32[]{:S(2)}, u32[]{:S(2)}) collective-permute-start(bf16[1,16,8,256]{3,2,1,0:T(8,128)(2,1)S(1)} %pad_maximum_fusion.l0_ref), channel_id=1, source_target_pairs={{0,8},{4,12},{8,16},{12,20},{16,24},{20,28},{24,32},{28,36},{32,40... | collective-permute-start | bytes 196616 | tf_op jit(solution)/shard_map/ppermute | solution.py:19
  76.1 4.1 %collective-permute-start.9 = (bf16[1,16,8,256]{3,2,1,0:T(8,128)(2,1)S(1)}, bf16[1,16,8,256]{3,2,1,0:T(8,128)(2,1)S(1)}, u32[]{:S(2)}, u32[]{:S(2)}) collective-permute-start(bf16[1,16,8,256]{3,2,1,0:T(8,128)(2,1)S(1)} %pad_maximum_fusion.l0_ref), channel_id=1, source_target_pairs={{0,4},{4,8},{8,12},{12,16},{16,20},{20,24},{24,28},{28,32},{32,36}... | collective-permute-start | bytes 196616 | tf_op jit(solution)/shard_map/ppermute | solution.py:19
  80.3 0.8 copy.39.dk_ref
  81.0 0.0 copy-done.6
  81.0 0.0 collective-permute-done.7.l3_ref
  81.1 0.0 collective-permute-done.8.l2_ref
  81.1 0.0 copy-start.9
  81.1 4.1 %collective-permute-done.9.l1_ref = bf16[1,16,8,256]{3,2,1,0:T(8,128)(2,1)S(1)} collective-permute-done((bf16[1,16,8,256]{3,2,1,0:T(8,128)(2,1)S(1)}, bf16[1,16,8,256]{3,2,1,0:T(8,128)(2,1)S(1)}, u32[]{:S(2)}, u32[]{:S(2)}) %collective-permute-start.9) | collective-permute-done | bytes 65568 | tf_op jit(solution)/shard_map/ppermute | solution.py:19
  85.2 0.0 copy-done.8
  85.2 0.0 copy-done.9
  85.2 0.6 copy-done.10
  85.8 7.9 %shard_map.124 = bf16[4,96,4,256]{3,2,1,0:T(4,128)(2,1)} custom-call(bf16[1,16,8,256]{3,2,1,0:T(8,128)(2,1)} %copy-done.8, bf16[1,16,8,256]{3,2,1,0:T(8,128)(2,1)} %copy-done.9, bf16[1,16,8,256]{3,2,1,0:T(8,128)(2,1)} %copy-done.10, bf16[1,16,8,256]{3,2,1,0:T(8,128)(2,1)} %copy-done.6, bf16[288,144]{1,0:T(8,128)(2,1)} %copy.39.dk_ref, ...), custom_call_target="tpu_custom_call" | custom-call | tf_op jit(solution)/shard_map/pallas_call | solution.py:237
  (7 shorter events, 0.0 us)
Async XLA Ops:
  1.9 4.1 %copy-start = (bf16[4,96,4,256]{3,1,2,0:T(8,128)(2,1)}, bf16[4,96,4,256]{3,1,2,0:T(8,128)(2,1)S(1)}, u32[]{:S(2)}) copy-start(bf16[4,96,4,256]{3,1,2,0:T(8,128)(2,1)S(1)} %copy.42) | copy-start | bytes 2359300
  1.9 29.2 %collective-permute-start = (bf16[4,4,96,256]{3,2,1,0:T(8,128)(2,1)S(1)}, bf16[4,4,96,256]{3,2,1,0:T(8,128)(2,1)S(1)}, u32[]{:S(2)}, u32[]{:S(2)}) collective-permute-start(bf16[4,4,96,256]{3,2,1,0:T(8,128)(2,1)S(1)} %bitcast.13), channel_id=1, source_target_pairs={{0,4},{4,8},{8,12},{12,16},{16,20},{20,24},{24,28},{28,32},{32,36}... | collective-permute-start | bytes 2359304 | tf_op jit(solution)/shard_map/ppermute | solution.py:19
  6.0 18.6 %collective-permute-start.1 = (bf16[4,2,96,256]{3,2,1,0:T(8,128)(2,1)}, bf16[4,2,96,256]{3,2,1,0:T(8,128)(2,1)S(1)}, u32[]{:S(2)}, u32[]{:S(2)}) collective-permute-start(bf16[4,2,96,256]{3,2,1,0:T(8,128)(2,1)} %get-tuple-element.27), channel_id=1, source_target_pairs={{0,1},{1,2},{2,3},{4,5},{5,6},{6,7},{8,9},{9,10},{10,11},{12,13},{... | collective-permute-start | bytes 1179656 | tf_op jit(solution)/shard_map/ppermute | solution.py:16
  11.7 12.9 %collective-permute-start.2 = (bf16[4,2,96,256]{3,2,1,0:T(8,128)(2,1)}, bf16[4,2,96,256]{3,2,1,0:T(8,128)(2,1)S(1)}, u32[]{:S(2)}, u32[]{:S(2)}) collective-permute-start(bf16[4,2,96,256]{3,2,1,0:T(8,128)(2,1)} %get-tuple-element.26), channel_id=1, source_target_pairs={{1,0},{2,1},{3,2},{5,4},{6,5},{7,6},{9,8},{10,9},{11,10},{13,12},{... | collective-permute-start | bytes 1179656 | tf_op jit(solution)/shard_map/ppermute | solution.py:16
  15.1 1.3 %copy-start.14 = (f32[96]{0:T(128)S(1)}, f32[96]{0:T(128)}, u32[]{:S(2)}) copy-start(f32[96]{0:T(128)} %param.13) | copy-start | bytes 1156
  16.5 0.7 copy-start.11
  16.5 0.7 copy-start.12
  16.5 0.7 copy-start.13
  22.3 1.4 %copy-start.7 = (bf16[3,3,3,96,16]{3,4,2,1,0:T(8,128)(2,1)S(1)}, bf16[3,3,3,96,16]{3,4,2,1,0:T(8,128)(2,1)}, u32[]{:S(2)}) copy-start(bf16[3,3,3,96,16]{3,4,2,1,0:T(8,128)(2,1)} %param.17) | copy-start | bytes 248836
  24.6 0.8 copy-start.2
  25.3 0.8 copy-start.3
  31.1 0.9 copy-start.1
  32.0 9.8 %collective-permute-start.3 = (bf16[4,2,96,256]{3,2,1,0:T(8,128)(2,1)S(1)}, bf16[4,2,96,256]{3,2,1,0:T(8,128)(2,1)S(1)}, u32[]{:S(2)}, u32[]{:S(2)}) collective-permute-start(bf16[4,2,96,256]{3,2,1,0:T(8,128)(2,1)S(1)} %get-tuple-element.14), channel_id=1, source_target_pairs={{0,1},{1,2},{2,3},{4,5},{5,6},{6,7},{8,9},{9,10},{10,11},{12,13},{... | collective-permute-start | bytes 1179656 | tf_op jit(solution)/shard_map/ppermute | solution.py:16
  37.1 10.6 %collective-permute-start.4 = (bf16[4,2,96,256]{3,2,1,0:T(8,128)(2,1)S(1)}, bf16[4,2,96,256]{3,2,1,0:T(8,128)(2,1)S(1)}, u32[]{:S(2)}, u32[]{:S(2)}) collective-permute-start(bf16[4,2,96,256]{3,2,1,0:T(8,128)(2,1)S(1)} %get-tuple-element.15), channel_id=1, source_target_pairs={{1,0},{2,1},{3,2},{5,4},{6,5},{7,6},{9,8},{10,9},{11,10},{13,12},{... | collective-permute-start | bytes 1179656 | tf_op jit(solution)/shard_map/ppermute | solution.py:16
  41.8 5.9 %copy-start.4 = (bf16[4,2,96,256]{3,2,1,0:T(8,128)(2,1)}, bf16[4,2,96,256]{3,2,1,0:T(8,128)(2,1)S(1)}, u32[]{:S(2)}) copy-start(bf16[4,2,96,256]{3,2,1,0:T(8,128)(2,1)S(1)} %collective-permute-done.3.tc_ref) | copy-start | bytes 1179652
  47.7 0.8 copy-start.5
  58.5 4.3 %collective-permute-start.5 = (bf16[1,16,2,256]{3,2,1,0:T(2,128)(2,1)}, bf16[1,16,2,256]{3,2,1,0:T(2,128)(2,1)S(1)}, u32[]{:S(2)}, u32[]{:S(2)}) collective-permute-start(bf16[1,16,2,256]{3,2,1,0:T(2,128)(2,1)} %get-tuple-element.22), channel_id=1, source_target_pairs={{0,1},{1,2},{2,3},{4,5},{5,6},{6,7},{8,9},{9,10},{10,11},{12,13},{... | collective-permute-start | bytes 49160 | tf_op jit(solution)/shard_map/ppermute | solution.py:16
  60.4 6.8 %collective-permute-start.6 = (bf16[1,16,2,256]{3,2,1,0:T(2,128)(2,1)}, bf16[1,16,2,256]{3,2,1,0:T(2,128)(2,1)S(1)}, u32[]{:S(2)}, u32[]{:S(2)}) collective-permute-start(bf16[1,16,2,256]{3,2,1,0:T(2,128)(2,1)} %get-tuple-element.23), channel_id=1, source_target_pairs={{1,0},{2,1},{3,2},{5,4},{6,5},{7,6},{9,8},{10,9},{11,10},{13,12},{... | collective-permute-start | bytes 49160 | tf_op jit(solution)/shard_map/ppermute | solution.py:16
  68.0 13.0 %copy-start.6 = (bf16[1,16,8,256]{3,2,1,0:T(8,128)(2,1)}, bf16[1,16,8,256]{3,2,1,0:T(8,128)(2,1)S(1)}, u32[]{:S(2)}) copy-start(bf16[1,16,8,256]{3,2,1,0:T(8,128)(2,1)S(1)} %pad_maximum_fusion.l0_ref) | copy-start | bytes 196612
  68.0 13.0 %collective-permute-start.7 = (bf16[1,16,8,256]{3,2,1,0:T(8,128)(2,1)S(1)}, bf16[1,16,8,256]{3,2,1,0:T(8,128)(2,1)S(1)}, u32[]{:S(2)}, u32[]{:S(2)}) collective-permute-start(bf16[1,16,8,256]{3,2,1,0:T(8,128)(2,1)S(1)} %pad_maximum_fusion.l0_ref), channel_id=1, source_target_pairs={{0,12},{4,16},{8,20},{12,24},{16,28},{20,32},{24,36},{28,40},{32,4... | collective-permute-start | bytes 196616 | tf_op jit(solution)/shard_map/ppermute | solution.py:19
  72.7 8.4 %collective-permute-start.8 = (bf16[1,16,8,256]{3,2,1,0:T(8,128)(2,1)S(1)}, bf16[1,16,8,256]{3,2,1,0:T(8,128)(2,1)S(1)}, u32[]{:S(2)}, u32[]{:S(2)}) collective-permute-start(bf16[1,16,8,256]{3,2,1,0:T(8,128)(2,1)S(1)} %pad_maximum_fusion.l0_ref), channel_id=1, source_target_pairs={{0,8},{4,12},{8,16},{12,20},{16,24},{20,28},{24,32},{28,36},{32,40... | collective-permute-start | bytes 196616 | tf_op jit(solution)/shard_map/ppermute | solution.py:19
  76.1 9.1 %collective-permute-start.9 = (bf16[1,16,8,256]{3,2,1,0:T(8,128)(2,1)S(1)}, bf16[1,16,8,256]{3,2,1,0:T(8,128)(2,1)S(1)}, u32[]{:S(2)}, u32[]{:S(2)}) collective-permute-start(bf16[1,16,8,256]{3,2,1,0:T(8,128)(2,1)S(1)} %pad_maximum_fusion.l0_ref), channel_id=1, source_target_pairs={{0,4},{4,8},{8,12},{12,16},{16,20},{20,24},{24,28},{28,32},{32,36}... | collective-permute-start | bytes 196616 | tf_op jit(solution)/shard_map/ppermute | solution.py:19
  81.1 4.1 %copy-start.8 = (bf16[1,16,8,256]{3,2,1,0:T(8,128)(2,1)}, bf16[1,16,8,256]{3,2,1,0:T(8,128)(2,1)S(1)}, u32[]{:S(2)}) copy-start(bf16[1,16,8,256]{3,2,1,0:T(8,128)(2,1)S(1)} %collective-permute-done.7.l3_ref) | copy-start | bytes 196612
  81.1 4.1 %copy-start.9 = (bf16[1,16,8,256]{3,2,1,0:T(8,128)(2,1)}, bf16[1,16,8,256]{3,2,1,0:T(8,128)(2,1)S(1)}, u32[]{:S(2)}) copy-start(bf16[1,16,8,256]{3,2,1,0:T(8,128)(2,1)S(1)} %collective-permute-done.8.l2_ref) | copy-start | bytes 196612
  85.2 0.6 copy-start.10

commit v14 on v11

--- a/solution.py
+++ b/solution.py
@@ -69,6 +69,10 @@
     left = jnp.where(lane == 0, 0.0, left)
     right = jnp.where(lane == columns - 1, 0.0, right)
     return left + acc[out_channels : 2 * out_channels] + right
+
+
+def at_row(get, r):
+    return lambda t, rr: get(t, rr + r)
 
 
 def late_gate_kernel(
@@ -149,11 +153,10 @@
                 piece = up[:, r * columns : (r + 1) * columns] * mask_ref[slot, r]
                 ext_ref[slot, r] = piece.astype(ext_ref.dtype)
     for t in range(frames):
-        y = tap_sum(from_ref(ext_ref), fk_ref, t, rows, columns)
-        res = frame_rows(from_ref(ext_ref), t + 2, 1, rows)
-        out = (res.astype(jnp.float32) + y).astype(o_ref.dtype)
         for r in range(rows):
-            o_ref[t, :, r, :] = out[:, r * columns : (r + 1) * columns]
+            y = tap_sum(at_row(from_ref(ext_ref), r), fk_ref, t, 1, columns)
+            res = ext_ref[t + 2, r + 1]
+            o_ref[t, :, r, :] = (res.astype(jnp.float32) + y).astype(o_ref.dtype)
 
 
 def body(

time: 88.6 us -> 88.3 us (level)
  no operation moved by 1% of the time
where the time goes in v14:
time: 88.3 us; the launch traced here: 87.7 us
  starting transfers between devices  29.1 us (33%)
  Pallas kernels  22.7 us (26%)
  waiting for transfers between devices  17 us (19%)
  local copies, waits for them, and re-layouts  16.6 us (19%)
  other arithmetic  1.5 us (2%)
    ppermute x6, starting transfers between devices, shift(): return lax.ppermute(x, 'rows', pairs)  18.6 us
    ppermute x4, waiting for transfers between devices, shift(): return lax.ppermute(x, 'tm', pairs)  12.2 us
    ppermute x4, starting transfers between devices, shift(): return lax.ppermute(x, 'tm', pairs)  10.5 us
    pallas_call x1, Pallas kernels, body(): pl.pallas_call(functools.partial(encoder_kernel, **dims), out_shape=(jax....  10 us
    pallas_call x1, Pallas kernels, body(): pl.pallas_call(functools.partial(decode_kernel_body, **dims), out_shape=j...  7.62 us
    unnamed x33, local copies, waits for them, and re-layouts  6.37 us
    pallas_call x1, Pallas kernels, body(): pl.pallas_call(functools.partial(late_gate_kernel, **dims), out_shape=jax...  5.03 us
    ppermute x6, waiting for transfers between devices, shift(): return lax.ppermute(x, 'rows', pairs)  4.85 us
  transfers between devices with their start and end apart: 10, of which 5 were waited for; matrix products, arithmetic and copies ran while one was open for 12% of the time, Pallas kernels for 6%

profile of v14, /device:TPU:24, one launch (start us, length us, event | category | flops | bytes accessed | tf_op | source)
XLA Modules:
  0.0 87.7 jit_solution(5262269566177177824)
XLA Ops:
  0.6 1.3 %copy.42 = bf16[4,96,4,256]{3,1,2,0:T(8,128)(2,1)S(1)} copy(bf16[4,96,4,256]{3,2,1,0:T(4,128)(2,1)} %param.11) | data formatting | bytes 1572864 | tf_op args[0]
  1.9 0.0 copy-start
  1.9 0.0 copy-start.4
  1.9 3.5 %collective-permute-start = (bf16[4,4,96,256]{3,2,1,0:T(8,128)(2,1)S(1)}, bf16[4,4,96,256]{3,2,1,0:T(8,128)(2,1)S(1)}, u32[]{:S(2)}, u32[]{:S(2)}) collective-permute-start(bf16[4,4,96,256]{3,2,1,0:T(8,128)(2,1)S(1)} %bitcast.13), channel_id=1, source_target_pairs={{0,4},{4,8},{8,12},{12,16},{16,20},{20,24},{24,28},{28,32},{32,36}... | collective-permute-start | bytes 2359304 | tf_op jit(solution)/shard_map/ppermute | solution.py:19
  5.5 1.0 %fusion = (bf16[4,2,96,256]{3,2,1,0:T(8,128)(2,1)}, bf16[4,2,96,256]{3,2,1,0:T(8,128)(2,1)}) fusion(bf16[4,4,96,256]{3,2,1,0:T(8,128)(2,1)S(1)} %bitcast.14), kind=kLoop, calls=%fused_computation.6 | loop fusion | bytes 1572864 | tf_op jit(solution)/shard_map/slice | solution.py:180
  6.4 0.0 copy-done
  6.4 1.9 %collective-permute-start.3 = (bf16[4,2,96,256]{3,2,1,0:T(8,128)(2,1)}, bf16[4,2,96,256]{3,2,1,0:T(8,128)(2,1)S(1)}, u32[]{:S(2)}, u32[]{:S(2)}) collective-permute-start(bf16[4,2,96,256]{3,2,1,0:T(8,128)(2,1)} %get-tuple-element.25), channel_id=1, source_target_pairs={{0,1},{1,2},{2,3},{4,5},{5,6},{6,7},{8,9},{9,10},{10,11},{12,13},{... | collective-permute-start | bytes 1179656 | tf_op jit(solution)/shard_map/ppermute | solution.py:16
  8.3 5.1 %collective-permute-start.4 = (bf16[4,2,96,256]{3,2,1,0:T(8,128)(2,1)}, bf16[4,2,96,256]{3,2,1,0:T(8,128)(2,1)S(1)}, u32[]{:S(2)}, u32[]{:S(2)}) collective-permute-start(bf16[4,2,96,256]{3,2,1,0:T(8,128)(2,1)} %get-tuple-element.24), channel_id=1, source_target_pairs={{1,0},{2,1},{3,2},{5,4},{6,5},{7,6},{9,8},{10,9},{11,10},{13,12},{... | collective-permute-start | bytes 1179656 | tf_op jit(solution)/shard_map/ppermute | solution.py:16
  13.5 0.0 copy-done.4
  13.5 0.5 copy.33
  14.0 1.3 %reshape.16.k1_ref = bf16[288,864]{1,0:T(8,128)(2,1)} reshape(bf16[3,96,3,3,96]{4,3,2,1,0:T(4,128)(2,1)S(1)} %copy.33) | data formatting | bytes 995328 | tf_op jit(solution)/shard_map/reshape | solution.py:31
  15.3 1.5 %copy.34 = bf16[3,96,3,3,96]{4,3,2,1,0:T(4,128)(2,1)S(1)} copy(bf16[3,96,3,3,96]{4,1,0,3,2:T(8,128)(2,1)} %bitcast.18) | data formatting | bytes 995328 | tf_op jit(solution)/shard_map/transpose | solution.py:31
  16.8 0.0 copy-start.8
  16.8 1.3 %reshape.17.k2_ref = bf16[288,864]{1,0:T(8,128)(2,1)} reshape(bf16[3,96,3,3,96]{4,3,2,1,0:T(4,128)(2,1)S(1)} %copy.34) | data formatting | bytes 995328 | tf_op jit(solution)/shard_map/reshape | solution.py:31
  18.1 0.0 copy-done.8
  18.1 0.1 copy.35
  18.2 0.1 reshape.18
  18.3 1.6 %copy.36 = bf16[3,96,3,3,96]{4,3,2,1,0:T(4,128)(2,1)S(1)} copy(bf16[3,96,3,3,96]{4,1,0,3,2:T(8,128)(2,1)} %bitcast.19) | data formatting | bytes 995328 | tf_op jit(solution)/shard_map/transpose | solution.py:31
  19.9 0.0 copy-start.15
  19.9 1.3 %reshape.19.fk_ref = bf16[288,864]{1,0:T(8,128)(2,1)} reshape(bf16[3,96,3,3,96]{4,3,2,1,0:T(4,128)(2,1)S(1)} %copy.36) | data formatting | bytes 995328 | tf_op jit(solution)/shard_map/reshape | solution.py:31
  21.2 0.0 copy-start.12
  21.3 0.0 copy-start.13
  21.3 0.0 copy-start.14
  21.3 0.0 copy-done.15
  21.3 0.6 copy-done.12
  21.9 0.0 copy-done.13
  21.9 0.0 copy-done.14
  21.9 0.7 and_convert_fusion.mask_ref
  22.6 5.4 %collective-permute-done.pv_ref = bf16[4,4,96,256]{3,2,1,0:T(8,128)(2,1)S(1)} collective-permute-done((bf16[4,4,96,256]{3,2,1,0:T(8,128)(2,1)S(1)}, bf16[4,4,96,256]{3,2,1,0:T(8,128)(2,1)S(1)}, u32[]{:S(2)}, u32[]{:S(2)}) %collective-permute-start) | collective-permute-done | bytes 786464 | tf_op jit(solution)/shard_map/ppermute | solution.py:19
  28.0 0.0 copy-start.1
  28.0 0.1 fusion.1
  28.1 0.8 copy-done.1
  28.9 1.9 %collective-permute-start.1 = (bf16[4,2,96,256]{3,2,1,0:T(8,128)(2,1)S(1)}, bf16[4,2,96,256]{3,2,1,0:T(8,128)(2,1)S(1)}, u32[]{:S(2)}, u32[]{:S(2)}) collective-permute-start(bf16[4,2,96,256]{3,2,1,0:T(8,128)(2,1)S(1)} %get-tuple-element.13), channel_id=1, source_target_pairs={{0,1},{1,2},{2,3},{4,5},{5,6},{6,7},{8,9},{9,10},{10,11},{12,13},{... | collective-permute-start | bytes 1179656 | tf_op jit(solution)/shard_map/ppermute | solution.py:16
  30.8 5.1 %collective-permute-start.2 = (bf16[4,2,96,256]{3,2,1,0:T(8,128)(2,1)S(1)}, bf16[4,2,96,256]{3,2,1,0:T(8,128)(2,1)S(1)}, u32[]{:S(2)}, u32[]{:S(2)}) collective-permute-start(bf16[4,2,96,256]{3,2,1,0:T(8,128)(2,1)S(1)} %get-tuple-element.14), channel_id=1, source_target_pairs={{1,0},{2,1},{3,2},{5,4},{6,5},{7,6},{9,8},{10,9},{11,10},{13,12},{... | collective-permute-start | bytes 1179656 | tf_op jit(solution)/shard_map/ppermute | solution.py:16
  35.9 0.7 copy.37.vec_ref
  36.7 0.0 collective-permute-done.3.tp_ref
  36.7 0.0 copy-start.2
  36.7 0.0 collective-permute-done.4.bt_ref
  36.7 0.7 copy-done.2
  37.4 0.7 copy-done.3
  38.2 5.0 %shard_map.122.late_ref = bf16[2,6,96,256]{3,2,1,0:T(8,128)(2,1)} custom-call(bf16[4,2,96,256]{3,2,1,0:T(8,128)(2,1)} %copy-done.2, bf16[4,4,96,256]{3,2,1,0:T(8,128)(2,1)} %bitcast.15, bf16[4,2,96,256]{3,2,1,0:T(8,128)(2,1)} %copy-done.3, bf16[288,864]{1,0:T(8,128)(2,1)} %reshape.16.k1_ref, f32[96,4]{1,0:T(8,128)} %copy.37.vec_ref, ...), custom_call_target="tpu_custom_call" | custom-call | tf_op jit(solution)/shard_map/pallas_call | solution.py:210
  43.2 0.0 collective-permute-done.1.tc_ref
  43.2 0.0 collective-permute-done.2.bc_ref
  43.2 0.7 copy-done.5
  44.0 0.7 copy-done.6
  44.7 10.0 %shard_map.123 = (bf16[1,16,4,256]{3,2,1,0:T(4,128)(2,1)}, bf16[1,16,2,256]{3,2,1,0:T(2,128)(2,1)}, bf16[1,16,2,256]{3,2,1,0:T(2,128)(2,1)}) custom-call(bf16[4,2,96,256]{3,2,1,0:T(8,128)(2,1)} %copy-done.5, bf16[4,4,96,256]{3,2,1,0:T(8,128)(2,1)} %copy-done.1, bf16[4,2,96,256]{3,2,1,0:T(8,128)(2,1)} %copy-done.6, bf16[4,2,96,256]{3,2,1,0:T(8,128)(2,1)} %copy-done.2, ...), custom_call_target="tpu_custom_call" | custom-call | tf_op jit(solution)/shard_map/pallas_call | solution.py:215
  54.7 2.6 %collective-permute-start.6 = (bf16[1,16,2,256]{3,2,1,0:T(2,128)(2,1)}, bf16[1,16,2,256]{3,2,1,0:T(2,128)(2,1)S(1)}, u32[]{:S(2)}, u32[]{:S(2)}) collective-permute-start(bf16[1,16,2,256]{3,2,1,0:T(2,128)(2,1)} %get-tuple-element.21), channel_id=1, source_target_pairs={{1,0},{2,1},{3,2},{5,4},{6,5},{7,6},{9,8},{10,9},{11,10},{13,12},{... | collective-permute-start | bytes 49160 | tf_op jit(solution)/shard_map/ppermute | solution.py:16
  57.3 1.9 %collective-permute-start.5 = (bf16[1,16,2,256]{3,2,1,0:T(2,128)(2,1)}, bf16[1,16,2,256]{3,2,1,0:T(2,128)(2,1)S(1)}, u32[]{:S(2)}, u32[]{:S(2)}) collective-permute-start(bf16[1,16,2,256]{3,2,1,0:T(2,128)(2,1)} %get-tuple-element.20), channel_id=1, source_target_pairs={{0,1},{1,2},{2,3},{4,5},{5,6},{6,7},{8,9},{9,10},{10,11},{12,13},{... | collective-permute-start | bytes 49160 | tf_op jit(solution)/shard_map/ppermute | solution.py:16
  59.2 0.0 collective-permute-done.6
  59.2 4.8 %collective-permute-done.5 = bf16[1,16,2,256]{3,2,1,0:T(2,128)(2,1)S(1)} collective-permute-done((bf16[1,16,2,256]{3,2,1,0:T(2,128)(2,1)}, bf16[1,16,2,256]{3,2,1,0:T(2,128)(2,1)S(1)}, u32[]{:S(2)}, u32[]{:S(2)}) %collective-permute-start.5) | collective-permute-done | bytes 16416 | tf_op jit(solution)/shard_map/ppermute | solution.py:16
  64.1 0.8 pad_maximum_fusion.l0_ref
  64.9 0.0 copy-start.7
  64.9 2.1 %collective-permute-start.7 = (bf16[1,16,8,256]{3,2,1,0:T(8,128)(2,1)S(1)}, bf16[1,16,8,256]{3,2,1,0:T(8,128)(2,1)S(1)}, u32[]{:S(2)}, u32[]{:S(2)}) collective-permute-start(bf16[1,16,8,256]{3,2,1,0:T(8,128)(2,1)S(1)} %pad_maximum_fusion.l0_ref), channel_id=1, source_target_pairs={{0,12},{4,16},{8,20},{12,24},{16,28},{20,32},{24,36},{28,40},{32,4... | collective-permute-start | bytes 196616 | tf_op jit(solution)/shard_map/ppermute | solution.py:19
  67.0 2.0 %collective-permute-start.8 = (bf16[1,16,8,256]{3,2,1,0:T(8,128)(2,1)S(1)}, bf16[1,16,8,256]{3,2,1,0:T(8,128)(2,1)S(1)}, u32[]{:S(2)}, u32[]{:S(2)}) collective-permute-start(bf16[1,16,8,256]{3,2,1,0:T(8,128)(2,1)S(1)} %pad_maximum_fusion.l0_ref), channel_id=1, source_target_pairs={{0,8},{4,12},{8,16},{12,20},{16,24},{20,28},{24,32},{28,36},{32,40... | collective-permute-start | bytes 196616 | tf_op jit(solution)/shard_map/ppermute | solution.py:19
  69.1 2.8 %collective-permute-start.9 = (bf16[1,16,8,256]{3,2,1,0:T(8,128)(2,1)S(1)}, bf16[1,16,8,256]{3,2,1,0:T(8,128)(2,1)S(1)}, u32[]{:S(2)}, u32[]{:S(2)}) collective-permute-start(bf16[1,16,8,256]{3,2,1,0:T(8,128)(2,1)S(1)} %pad_maximum_fusion.l0_ref), channel_id=1, source_target_pairs={{0,4},{4,8},{8,12},{12,16},{16,20},{20,24},{24,28},{28,32},{32,36}... | collective-permute-start | bytes 196616 | tf_op jit(solution)/shard_map/ppermute | solution.py:19
  71.9 0.8 copy.39.dk_ref
  72.6 0.0 copy-done.7
  72.6 1.4 %collective-permute-done.7.l3_ref = bf16[1,16,8,256]{3,2,1,0:T(8,128)(2,1)S(1)} collective-permute-done((bf16[1,16,8,256]{3,2,1,0:T(8,128)(2,1)S(1)}, bf16[1,16,8,256]{3,2,1,0:T(8,128)(2,1)S(1)}, u32[]{:S(2)}, u32[]{:S(2)}) %collective-permute-start.7) | collective-permute-done | bytes 65568 | tf_op jit(solution)/shard_map/ppermute | solution.py:19
  74.1 3.6 %collective-permute-done.8.l2_ref = bf16[1,16,8,256]{3,2,1,0:T(8,128)(2,1)S(1)} collective-permute-done((bf16[1,16,8,256]{3,2,1,0:T(8,128)(2,1)S(1)}, bf16[1,16,8,256]{3,2,1,0:T(8,128)(2,1)S(1)}, u32[]{:S(2)}, u32[]{:S(2)}) %collective-permute-start.8) | collective-permute-done | bytes 65568 | tf_op jit(solution)/shard_map/ppermute | solution.py:19
  77.7 1.8 %collective-permute-done.9.l1_ref = bf16[1,16,8,256]{3,2,1,0:T(8,128)(2,1)S(1)} collective-permute-done((bf16[1,16,8,256]{3,2,1,0:T(8,128)(2,1)S(1)}, bf16[1,16,8,256]{3,2,1,0:T(8,128)(2,1)S(1)}, u32[]{:S(2)}, u32[]{:S(2)}) %collective-permute-start.9) | collective-permute-done | bytes 65568 | tf_op jit(solution)/shard_map/ppermute | solution.py:19
  79.5 0.0 copy-done.9
  79.5 0.0 copy-done.10
  79.5 0.6 copy-done.11
  80.1 7.6 %shard_map.124 = bf16[4,96,4,256]{3,2,1,0:T(4,128)(2,1)} custom-call(bf16[1,16,8,256]{3,2,1,0:T(8,128)(2,1)} %copy-done.9, bf16[1,16,8,256]{3,2,1,0:T(8,128)(2,1)} %copy-done.10, bf16[1,16,8,256]{3,2,1,0:T(8,128)(2,1)} %copy-done.11, bf16[1,16,8,256]{3,2,1,0:T(8,128)(2,1)} %copy-done.7, bf16[288,144]{1,0:T(8,128)(2,1)} %copy.39.dk_ref, ...), custom_call_target="tpu_custom_call" | custom-call | tf_op jit(solution)/shard_map/pallas_call | solution.py:237
  (8 shorter events, 0.0 us)
Async XLA Ops:
  1.9 4.5 %copy-start = (bf16[4,96,4,256]{3,1,2,0:T(8,128)(2,1)}, bf16[4,96,4,256]{3,1,2,0:T(8,128)(2,1)S(1)}, u32[]{:S(2)}) copy-start(bf16[4,96,4,256]{3,1,2,0:T(8,128)(2,1)S(1)} %copy.42) | copy-start | bytes 2359300
  1.9 11.6 %copy-start.4 = (bf16[3,3,3,96,96]{4,3,2,1,0:T(8,128)(2,1)S(1)}, bf16[3,3,3,96,96]{4,3,2,1,0:T(8,128)(2,1)}, u32[]{:S(2)}) copy-start(bf16[3,3,3,96,96]{4,3,2,1,0:T(8,128)(2,1)} %param.12) | copy-start | bytes 1492996
  1.9 26.1 %collective-permute-start = (bf16[4,4,96,256]{3,2,1,0:T(8,128)(2,1)S(1)}, bf16[4,4,96,256]{3,2,1,0:T(8,128)(2,1)S(1)}, u32[]{:S(2)}, u32[]{:S(2)}) collective-permute-start(bf16[4,4,96,256]{3,2,1,0:T(8,128)(2,1)S(1)} %bitcast.13), channel_id=1, source_target_pairs={{0,4},{4,8},{8,12},{12,16},{16,20},{20,24},{24,28},{28,32},{32,36}... | collective-permute-start | bytes 2359304 | tf_op jit(solution)/shard_map/ppermute | solution.py:19
  6.4 30.3 %collective-permute-start.3 = (bf16[4,2,96,256]{3,2,1,0:T(8,128)(2,1)}, bf16[4,2,96,256]{3,2,1,0:T(8,128)(2,1)S(1)}, u32[]{:S(2)}, u32[]{:S(2)}) collective-permute-start(bf16[4,2,96,256]{3,2,1,0:T(8,128)(2,1)} %get-tuple-element.25), channel_id=1, source_target_pairs={{0,1},{1,2},{2,3},{4,5},{5,6},{6,7},{8,9},{9,10},{10,11},{12,13},{... | collective-permute-start | bytes 1179656 | tf_op jit(solution)/shard_map/ppermute | solution.py:16
  8.3 28.3 %collective-permute-start.4 = (bf16[4,2,96,256]{3,2,1,0:T(8,128)(2,1)}, bf16[4,2,96,256]{3,2,1,0:T(8,128)(2,1)S(1)}, u32[]{:S(2)}, u32[]{:S(2)}) collective-permute-start(bf16[4,2,96,256]{3,2,1,0:T(8,128)(2,1)} %get-tuple-element.24), channel_id=1, source_target_pairs={{1,0},{2,1},{3,2},{5,4},{6,5},{7,6},{9,8},{10,9},{11,10},{13,12},{... | collective-permute-start | bytes 1179656 | tf_op jit(solution)/shard_map/ppermute | solution.py:16
  16.8 1.3 %copy-start.8 = (bf16[3,3,3,96,16]{3,4,2,1,0:T(8,128)(2,1)S(1)}, bf16[3,3,3,96,16]{3,4,2,1,0:T(8,128)(2,1)}, u32[]{:S(2)}) copy-start(bf16[3,3,3,96,16]{3,4,2,1,0:T(8,128)(2,1)} %param.17) | copy-start | bytes 248836
  19.9 1.4 %copy-start.15 = (f32[96]{0:T(128)S(1)}, f32[96]{0:T(128)}, u32[]{:S(2)}) copy-start(f32[96]{0:T(128)} %param.13) | copy-start | bytes 1156
  21.2 0.7 copy-start.12
  21.3 0.7 copy-start.13
  21.3 0.7 copy-start.14
  28.0 0.9 %copy-start.1 = (bf16[4,4,96,256]{3,2,1,0:T(8,128)(2,1)}, bf16[4,4,96,256]{3,2,1,0:T(8,128)(2,1)S(1)}, u32[]{:S(2)}) copy-start(bf16[4,4,96,256]{3,2,1,0:T(8,128)(2,1)S(1)} %collective-permute-done.pv_ref) | copy-start | bytes 2359300
  28.9 14.3 %collective-permute-start.1 = (bf16[4,2,96,256]{3,2,1,0:T(8,128)(2,1)S(1)}, bf16[4,2,96,256]{3,2,1,0:T(8,128)(2,1)S(1)}, u32[]{:S(2)}, u32[]{:S(2)}) collective-permute-start(bf16[4,2,96,256]{3,2,1,0:T(8,128)(2,1)S(1)} %get-tuple-element.13), channel_id=1, source_target_pairs={{0,1},{1,2},{2,3},{4,5},{5,6},{6,7},{8,9},{9,10},{10,11},{12,13},{... | collective-permute-start | bytes 1179656 | tf_op jit(solution)/shard_map/ppermute | solution.py:16
  30.8 12.4 %collective-permute-start.2 = (bf16[4,2,96,256]{3,2,1,0:T(8,128)(2,1)S(1)}, bf16[4,2,96,256]{3,2,1,0:T(8,128)(2,1)S(1)}, u32[]{:S(2)}, u32[]{:S(2)}) collective-permute-start(bf16[4,2,96,256]{3,2,1,0:T(8,128)(2,1)S(1)} %get-tuple-element.14), channel_id=1, source_target_pairs={{1,0},{2,1},{3,2},{5,4},{6,5},{7,6},{9,8},{10,9},{11,10},{13,12},{... | collective-permute-start | bytes 1179656 | tf_op jit(solution)/shard_map/ppermute | solution.py:16
  36.7 0.8 copy-start.2
  37.4 0.7 copy-start.3
  43.2 0.8 copy-start.5
  44.0 0.7 copy-start.6
  54.7 4.5 %collective-permute-start.6 = (bf16[1,16,2,256]{3,2,1,0:T(2,128)(2,1)}, bf16[1,16,2,256]{3,2,1,0:T(2,128)(2,1)S(1)}, u32[]{:S(2)}, u32[]{:S(2)}) collective-permute-start(bf16[1,16,2,256]{3,2,1,0:T(2,128)(2,1)} %get-tuple-element.21), channel_id=1, source_target_pairs={{1,0},{2,1},{3,2},{5,4},{6,5},{7,6},{9,8},{10,9},{11,10},{13,12},{... | collective-permute-start | bytes 49160 | tf_op jit(solution)/shard_map/ppermute | solution.py:16
  57.3 6.8 %collective-permute-start.5 = (bf16[1,16,2,256]{3,2,1,0:T(2,128)(2,1)}, bf16[1,16,2,256]{3,2,1,0:T(2,128)(2,1)S(1)}, u32[]{:S(2)}, u32[]{:S(2)}) collective-permute-start(bf16[1,16,2,256]{3,2,1,0:T(2,128)(2,1)} %get-tuple-element.20), channel_id=1, source_target_pairs={{0,1},{1,2},{2,3},{4,5},{5,6},{6,7},{8,9},{9,10},{10,11},{12,13},{... | collective-permute-start | bytes 49160 | tf_op jit(solution)/shard_map/ppermute | solution.py:16
  64.9 7.8 %copy-start.7 = (bf16[1,16,8,256]{3,2,1,0:T(8,128)(2,1)}, bf16[1,16,8,256]{3,2,1,0:T(8,128)(2,1)S(1)}, u32[]{:S(2)}) copy-start(bf16[1,16,8,256]{3,2,1,0:T(8,128)(2,1)S(1)} %pad_maximum_fusion.l0_ref) | copy-start | bytes 196612
  64.9 9.2 %collective-permute-start.7 = (bf16[1,16,8,256]{3,2,1,0:T(8,128)(2,1)S(1)}, bf16[1,16,8,256]{3,2,1,0:T(8,128)(2,1)S(1)}, u32[]{:S(2)}, u32[]{:S(2)}) collective-permute-start(bf16[1,16,8,256]{3,2,1,0:T(8,128)(2,1)S(1)} %pad_maximum_fusion.l0_ref), channel_id=1, source_target_pairs={{0,12},{4,16},{8,20},{12,24},{16,28},{20,32},{24,36},{28,40},{32,4... | collective-permute-start | bytes 196616 | tf_op jit(solution)/shard_map/ppermute | solution.py:19
  67.0 10.7 %collective-permute-start.8 = (bf16[1,16,8,256]{3,2,1,0:T(8,128)(2,1)S(1)}, bf16[1,16,8,256]{3,2,1,0:T(8,128)(2,1)S(1)}, u32[]{:S(2)}, u32[]{:S(2)}) collective-permute-start(bf16[1,16,8,256]{3,2,1,0:T(8,128)(2,1)S(1)} %pad_maximum_fusion.l0_ref), channel_id=1, source_target_pairs={{0,8},{4,12},{8,16},{12,20},{16,24},{20,28},{24,32},{28,36},{32,40... | collective-permute-start | bytes 196616 | tf_op jit(solution)/shard_map/ppermute | solution.py:19
  69.1 10.4 %collective-permute-start.9 = (bf16[1,16,8,256]{3,2,1,0:T(8,128)(2,1)S(1)}, bf16[1,16,8,256]{3,2,1,0:T(8,128)(2,1)S(1)}, u32[]{:S(2)}, u32[]{:S(2)}) collective-permute-start(bf16[1,16,8,256]{3,2,1,0:T(8,128)(2,1)S(1)} %pad_maximum_fusion.l0_ref), channel_id=1, source_target_pairs={{0,4},{4,8},{8,12},{12,16},{16,20},{20,24},{24,28},{28,32},{32,36}... | collective-permute-start | bytes 196616 | tf_op jit(solution)/shard_map/ppermute | solution.py:19
  74.1 5.4 %copy-start.9 = (bf16[1,16,8,256]{3,2,1,0:T(8,128)(2,1)}, bf16[1,16,8,256]{3,2,1,0:T(8,128)(2,1)S(1)}, u32[]{:S(2)}) copy-start(bf16[1,16,8,256]{3,2,1,0:T(8,128)(2,1)S(1)} %collective-permute-done.7.l3_ref) | copy-start | bytes 196612
  77.7 1.8 %copy-start.10 = (bf16[1,16,8,256]{3,2,1,0:T(8,128)(2,1)}, bf16[1,16,8,256]{3,2,1,0:T(8,128)(2,1)S(1)}, u32[]{:S(2)}) copy-start(bf16[1,16,8,256]{3,2,1,0:T(8,128)(2,1)S(1)} %collective-permute-done.8.l2_ref) | copy-start | bytes 196612
  79.5 0.6 copy-start.11

commit v15 on v11

--- a/solution.py
+++ b/solution.py
@@ -89,16 +89,24 @@
 
 
 def encoder_kernel(
-    tc_ref, pv_ref, bc_ref, tp_ref, own_ref, bt_ref, late_ref,
+    tc_any, pv_any, bc_any, tp_any, own_any, bt_any, late_any,
     k1_ref, vec_ref, mask_ref, k2_ref, w_ref, o_ref, top_ref, bottom_ref, g_ref,
+    tc_ref, pv_ref, bc_ref, tp_ref, own_ref, bt_ref, late_ref, sems,
     *, frames, rows, columns
 ):
+    sources = (tc_any, pv_any, bc_any, tp_any, own_any, bt_any, late_any)
+    targets = (tc_ref, pv_ref, bc_ref, tp_ref, own_ref, bt_ref, late_ref)
+    copies = [pltpu.make_async_copy(a, b, sems.at[i]) for i, (a, b) in enumerate(zip(sources, targets))]
+    for c in copies:
+        c.start()
     wide = rows + 2
     bias = vec_ref[:, 0:1]
     gain = vec_ref[:, 1:2]
     x = tiled([(tc_ref, pv_ref, bc_ref), (tp_ref, own_ref, bt_ref)], frames, 2, rows)
     span = wide * columns
     for t in range(0, frames, 2):
+        for c in copies[:3] if t == 0 else copies[3:6]:
+            c.wait()
         y = tap_sum(x, k1_ref, t, wide, columns, 2) + bias
         scale = lax.rsqrt(jnp.mean(y * y, axis=0, keepdims=True) + 1e-06)
         z = y * scale * gain
@@ -108,6 +116,7 @@
                 lo = i * span + r * columns
                 piece = g[:, lo : lo + columns] * mask_ref[t + i, r]
                 g_ref[t + i, r] = piece.astype(g_ref.dtype)
+    copies[6].wait()
     gated = lambda t, r: g_ref[t, r] if t < frames else late_ref[t - frames, r]
     total = None
     width = rows * columns
@@ -216,8 +225,10 @@
             jax.ShapeDtypeStruct((1, z_count, 2, columns), jnp.bfloat16),
             jax.ShapeDtypeStruct((1, z_count, 2, columns), jnp.bfloat16),
         ),
-        in_specs=[vmem] * 9 + [smem, vmem, vmem],
-        scratch_shapes=[pltpu.VMEM((frames, rows + 2, channels, columns), jnp.bfloat16)],
+        in_specs=[pl.BlockSpec(memory_space=pl.ANY)] * 7 + [vmem, vmem, smem, vmem, vmem],
+        scratch_shapes=[pltpu.VMEM((frames, rows + 2, channels, columns), jnp.bfloat16)]
+        + [pltpu.VMEM(p.shape, p.dtype) for p in pieces]
+        + [pltpu.VMEM(late.shape, late.dtype), pltpu.SemaphoreType.DMA((7,))],
     )(
         *pieces,
         late,

time: 88.6 us -> 89.7 us (1.012)
  Pallas kernels: 22.9 us -> 24.1 us
    pallas_call x1, Pallas kernels: 10 us -> 11.2 us  [body(): pl.pallas_call(functools.partial(encoder_kernel, **dims), out_shape=(jax....]
where the time goes in v15:
time: 89.7 us; the launch traced here: 89 us
  starting transfers between devices  29.1 us (32%)
  Pallas kernels  24.1 us (27%)
  waiting for transfers between devices  16.8 us (19%)
  local copies, waits for them, and re-layouts  16.6 us (19%)
  other arithmetic  1.5 us (2%)
    ppermute x6, starting transfers between devices, shift(): return lax.ppermute(x, 'rows', pairs)  18.6 us
    ppermute x4, waiting for transfers between devices, shift(): return lax.ppermute(x, 'tm', pairs)  12 us
    pallas_call x1, Pallas kernels, body(): pl.pallas_call(functools.partial(encoder_kernel, **dims), out_shape=(jax....  11.2 us
    ppermute x4, starting transfers between devices, shift(): return lax.ppermute(x, 'tm', pairs)  10.5 us
    pallas_call x1, Pallas kernels, body(): pl.pallas_call(functools.partial(decode_kernel_body, **dims), out_shape=j...  7.88 us
    unnamed x33, local copies, waits for them, and re-layouts  6.37 us
    pallas_call x1, Pallas kernels, body(): pl.pallas_call(functools.partial(late_gate_kernel, **dims), out_shape=jax...  5.03 us
    ppermute x6, waiting for transfers between devices, shift(): return lax.ppermute(x, 'rows', pairs)  4.84 us
  transfers between devices with their start and end apart: 10, of which 5 were waited for; matrix products, arithmetic and copies ran while one was open for 12% of the time, Pallas kernels for 6%

profile of v15, /device:TPU:24, one launch (start us, length us, event | category | flops | bytes accessed | tf_op | source)
XLA Modules:
  0.0 89.0 jit_solution(10335407460003954342)
XLA Ops:
  0.6 1.3 %copy.42 = bf16[4,96,4,256]{3,1,2,0:T(8,128)(2,1)S(1)} copy(bf16[4,96,4,256]{3,2,1,0:T(4,128)(2,1)} %param.11) | data formatting | bytes 1572864 | tf_op args[0]
  1.9 0.0 copy-start
  1.9 0.0 copy-start.4
  1.9 3.5 %collective-permute-start = (bf16[4,4,96,256]{3,2,1,0:T(8,128)(2,1)S(1)}, bf16[4,4,96,256]{3,2,1,0:T(8,128)(2,1)S(1)}, u32[]{:S(2)}, u32[]{:S(2)}) collective-permute-start(bf16[4,4,96,256]{3,2,1,0:T(8,128)(2,1)S(1)} %bitcast.13), channel_id=1, source_target_pairs={{0,4},{4,8},{8,12},{12,16},{16,20},{20,24},{24,28},{28,32},{32,36}... | collective-permute-start | bytes 2359304 | tf_op jit(solution)/shard_map/ppermute | solution.py:19
  5.5 1.0 %fusion = (bf16[4,2,96,256]{3,2,1,0:T(8,128)(2,1)}, bf16[4,2,96,256]{3,2,1,0:T(8,128)(2,1)}) fusion(bf16[4,4,96,256]{3,2,1,0:T(8,128)(2,1)S(1)} %bitcast.14), kind=kLoop, calls=%fused_computation.6 | loop fusion | bytes 1572864 | tf_op jit(solution)/shard_map/slice | solution.py:186
  6.4 0.0 copy-done
  6.4 1.9 %collective-permute-start.3 = (bf16[4,2,96,256]{3,2,1,0:T(8,128)(2,1)}, bf16[4,2,96,256]{3,2,1,0:T(8,128)(2,1)S(1)}, u32[]{:S(2)}, u32[]{:S(2)}) collective-permute-start(bf16[4,2,96,256]{3,2,1,0:T(8,128)(2,1)} %get-tuple-element.25), channel_id=1, source_target_pairs={{0,1},{1,2},{2,3},{4,5},{5,6},{6,7},{8,9},{9,10},{10,11},{12,13},{... | collective-permute-start | bytes 1179656 | tf_op jit(solution)/shard_map/ppermute | solution.py:16
  8.3 5.1 %collective-permute-start.4 = (bf16[4,2,96,256]{3,2,1,0:T(8,128)(2,1)}, bf16[4,2,96,256]{3,2,1,0:T(8,128)(2,1)S(1)}, u32[]{:S(2)}, u32[]{:S(2)}) collective-permute-start(bf16[4,2,96,256]{3,2,1,0:T(8,128)(2,1)} %get-tuple-element.24), channel_id=1, source_target_pairs={{1,0},{2,1},{3,2},{5,4},{6,5},{7,6},{9,8},{10,9},{11,10},{13,12},{... | collective-permute-start | bytes 1179656 | tf_op jit(solution)/shard_map/ppermute | solution.py:16
  13.5 0.0 copy-done.4
  13.5 0.5 copy.33
  14.0 1.3 %reshape.16.k1_ref = bf16[288,864]{1,0:T(8,128)(2,1)} reshape(bf16[3,96,3,3,96]{4,3,2,1,0:T(4,128)(2,1)S(1)} %copy.33) | data formatting | bytes 995328 | tf_op jit(solution)/shard_map/reshape | solution.py:31
  15.3 1.5 %copy.34 = bf16[3,96,3,3,96]{4,3,2,1,0:T(4,128)(2,1)S(1)} copy(bf16[3,96,3,3,96]{4,1,0,3,2:T(8,128)(2,1)} %bitcast.18) | data formatting | bytes 995328 | tf_op jit(solution)/shard_map/transpose | solution.py:31
  16.8 0.0 copy-start.8
  16.8 1.3 %reshape.17.k2_ref = bf16[288,864]{1,0:T(8,128)(2,1)} reshape(bf16[3,96,3,3,96]{4,3,2,1,0:T(4,128)(2,1)S(1)} %copy.34) | data formatting | bytes 995328 | tf_op jit(solution)/shard_map/reshape | solution.py:31
  18.1 0.0 copy-done.8
  18.1 0.1 copy.35
  18.2 0.1 reshape.18
  18.3 1.6 %copy.36 = bf16[3,96,3,3,96]{4,3,2,1,0:T(4,128)(2,1)S(1)} copy(bf16[3,96,3,3,96]{4,1,0,3,2:T(8,128)(2,1)} %bitcast.19) | data formatting | bytes 995328 | tf_op jit(solution)/shard_map/transpose | solution.py:31
  19.9 0.0 copy-start.15
  19.9 1.3 %reshape.19.fk_ref = bf16[288,864]{1,0:T(8,128)(2,1)} reshape(bf16[3,96,3,3,96]{4,3,2,1,0:T(4,128)(2,1)S(1)} %copy.36) | data formatting | bytes 995328 | tf_op jit(solution)/shard_map/reshape | solution.py:31
  21.2 0.0 copy-start.12
  21.3 0.0 copy-start.13
  21.3 0.0 copy-start.14
  21.3 0.0 copy-done.15
  21.3 0.6 copy-done.12
  21.9 0.0 copy-done.13
  21.9 0.0 copy-done.14
  21.9 0.7 and_convert_fusion.mask_ref
  22.6 5.4 %collective-permute-done.pv_any = bf16[4,4,96,256]{3,2,1,0:T(8,128)(2,1)S(1)} collective-permute-done((bf16[4,4,96,256]{3,2,1,0:T(8,128)(2,1)S(1)}, bf16[4,4,96,256]{3,2,1,0:T(8,128)(2,1)S(1)}, u32[]{:S(2)}, u32[]{:S(2)}) %collective-permute-start) | collective-permute-done | bytes 786464 | tf_op jit(solution)/shard_map/ppermute | solution.py:19
  28.0 0.0 copy-start.1
  28.0 0.1 fusion.1
  28.1 0.8 copy-done.1
  28.9 1.9 %collective-permute-start.1 = (bf16[4,2,96,256]{3,2,1,0:T(8,128)(2,1)S(1)}, bf16[4,2,96,256]{3,2,1,0:T(8,128)(2,1)S(1)}, u32[]{:S(2)}, u32[]{:S(2)}) collective-permute-start(bf16[4,2,96,256]{3,2,1,0:T(8,128)(2,1)S(1)} %get-tuple-element.13), channel_id=1, source_target_pairs={{0,1},{1,2},{2,3},{4,5},{5,6},{6,7},{8,9},{9,10},{10,11},{12,13},{... | collective-permute-start | bytes 1179656 | tf_op jit(solution)/shard_map/ppermute | solution.py:16
  30.8 5.3 %collective-permute-start.2 = (bf16[4,2,96,256]{3,2,1,0:T(8,128)(2,1)S(1)}, bf16[4,2,96,256]{3,2,1,0:T(8,128)(2,1)S(1)}, u32[]{:S(2)}, u32[]{:S(2)}) collective-permute-start(bf16[4,2,96,256]{3,2,1,0:T(8,128)(2,1)S(1)} %get-tuple-element.14), channel_id=1, source_target_pairs={{1,0},{2,1},{3,2},{5,4},{6,5},{7,6},{9,8},{10,9},{11,10},{13,12},{... | collective-permute-start | bytes 1179656 | tf_op jit(solution)/shard_map/ppermute | solution.py:16
  36.1 0.7 copy.37.vec_ref
  36.8 0.0 collective-permute-done.3.tp_ref.tp_any
  36.9 0.0 copy-start.2
  36.9 0.0 collective-permute-done.4.bt_ref.bt_any
  36.9 0.7 copy-done.2
  37.6 0.7 copy-done.3
  38.4 5.0 %shard_map.122.late_any = bf16[2,6,96,256]{3,2,1,0:T(8,128)(2,1)} custom-call(bf16[4,2,96,256]{3,2,1,0:T(8,128)(2,1)} %copy-done.2, bf16[4,4,96,256]{3,2,1,0:T(8,128)(2,1)} %bitcast.15, bf16[4,2,96,256]{3,2,1,0:T(8,128)(2,1)} %copy-done.3, bf16[288,864]{1,0:T(8,128)(2,1)} %reshape.16.k1_ref, f32[96,4]{1,0:T(8,128)} %copy.37.vec_ref, ...), custom_call_target="tpu_custom_call" | custom-call | tf_op jit(solution)/shard_map/pallas_call | solution.py:216
  43.4 0.0 collective-permute-done.1.tc_any
  43.4 0.0 collective-permute-done.2.bc_any
  43.4 0.7 copy-done.5
  44.1 0.7 copy-done.6
  44.9 11.2 %shard_map.123 = (bf16[1,16,4,256]{3,2,1,0:T(4,128)(2,1)}, bf16[1,16,2,256]{3,2,1,0:T(2,128)(2,1)}, bf16[1,16,2,256]{3,2,1,0:T(2,128)(2,1)}) custom-call(bf16[4,2,96,256]{3,2,1,0:T(8,128)(2,1)} %copy-done.5, bf16[4,4,96,256]{3,2,1,0:T(8,128)(2,1)} %copy-done.1, bf16[4,2,96,256]{3,2,1,0:T(8,128)(2,1)} %copy-done.6, bf16[4,2,96,256]{3,2,1,0:T(8,128)(2,1)} %copy-done.2, ...), custom_call_target="tpu_custom_call" | custom-call | tf_op jit(solution)/shard_map/pallas_call | solution.py:221
  56.1 2.4 %collective-permute-start.6 = (bf16[1,16,2,256]{3,2,1,0:T(2,128)(2,1)}, bf16[1,16,2,256]{3,2,1,0:T(2,128)(2,1)S(1)}, u32[]{:S(2)}, u32[]{:S(2)}) collective-permute-start(bf16[1,16,2,256]{3,2,1,0:T(2,128)(2,1)} %get-tuple-element.21), channel_id=1, source_target_pairs={{1,0},{2,1},{3,2},{5,4},{6,5},{7,6},{9,8},{10,9},{11,10},{13,12},{... | collective-permute-start | bytes 49160 | tf_op jit(solution)/shard_map/ppermute | solution.py:16
  58.5 1.9 %collective-permute-start.5 = (bf16[1,16,2,256]{3,2,1,0:T(2,128)(2,1)}, bf16[1,16,2,256]{3,2,1,0:T(2,128)(2,1)S(1)}, u32[]{:S(2)}, u32[]{:S(2)}) collective-permute-start(bf16[1,16,2,256]{3,2,1,0:T(2,128)(2,1)} %get-tuple-element.20), channel_id=1, source_target_pairs={{0,1},{1,2},{2,3},{4,5},{5,6},{6,7},{8,9},{9,10},{10,11},{12,13},{... | collective-permute-start | bytes 49160 | tf_op jit(solution)/shard_map/ppermute | solution.py:16
  60.5 0.0 collective-permute-done.6
  60.5 4.8 %collective-permute-done.5 = bf16[1,16,2,256]{3,2,1,0:T(2,128)(2,1)S(1)} collective-permute-done((bf16[1,16,2,256]{3,2,1,0:T(2,128)(2,1)}, bf16[1,16,2,256]{3,2,1,0:T(2,128)(2,1)S(1)}, u32[]{:S(2)}, u32[]{:S(2)}) %collective-permute-start.5) | collective-permute-done | bytes 16416 | tf_op jit(solution)/shard_map/ppermute | solution.py:16
  65.3 0.8 pad_maximum_fusion.l0_ref
  66.1 0.0 copy-start.7
  66.1 1.9 %collective-permute-start.7 = (bf16[1,16,8,256]{3,2,1,0:T(8,128)(2,1)S(1)}, bf16[1,16,8,256]{3,2,1,0:T(8,128)(2,1)S(1)}, u32[]{:S(2)}, u32[]{:S(2)}) collective-permute-start(bf16[1,16,8,256]{3,2,1,0:T(8,128)(2,1)S(1)} %pad_maximum_fusion.l0_ref), channel_id=1, source_target_pairs={{0,12},{4,16},{8,20},{12,24},{16,28},{20,32},{24,36},{28,40},{32,4... | collective-permute-start | bytes 196616 | tf_op jit(solution)/shard_map/ppermute | solution.py:19
  68.0 2.0 %collective-permute-start.8 = (bf16[1,16,8,256]{3,2,1,0:T(8,128)(2,1)S(1)}, bf16[1,16,8,256]{3,2,1,0:T(8,128)(2,1)S(1)}, u32[]{:S(2)}, u32[]{:S(2)}) collective-permute-start(bf16[1,16,8,256]{3,2,1,0:T(8,128)(2,1)S(1)} %pad_maximum_fusion.l0_ref), channel_id=1, source_target_pairs={{0,8},{4,12},{8,16},{12,20},{16,24},{20,28},{24,32},{28,36},{32,40... | collective-permute-start | bytes 196616 | tf_op jit(solution)/shard_map/ppermute | solution.py:19
  70.1 3.0 %collective-permute-start.9 = (bf16[1,16,8,256]{3,2,1,0:T(8,128)(2,1)S(1)}, bf16[1,16,8,256]{3,2,1,0:T(8,128)(2,1)S(1)}, u32[]{:S(2)}, u32[]{:S(2)}) collective-permute-start(bf16[1,16,8,256]{3,2,1,0:T(8,128)(2,1)S(1)} %pad_maximum_fusion.l0_ref), channel_id=1, source_target_pairs={{0,4},{4,8},{8,12},{12,16},{16,20},{20,24},{24,28},{28,32},{32,36}... | collective-permute-start | bytes 196616 | tf_op jit(solution)/shard_map/ppermute | solution.py:19
  73.1 0.8 copy.39.dk_ref
  73.9 0.0 copy-done.7
  73.9 1.5 %collective-permute-done.7.l3_ref = bf16[1,16,8,256]{3,2,1,0:T(8,128)(2,1)S(1)} collective-permute-done((bf16[1,16,8,256]{3,2,1,0:T(8,128)(2,1)S(1)}, bf16[1,16,8,256]{3,2,1,0:T(8,128)(2,1)S(1)}, u32[]{:S(2)}, u32[]{:S(2)}) %collective-permute-start.7) | collective-permute-done | bytes 65568 | tf_op jit(solution)/shard_map/ppermute | solution.py:19
  75.4 3.4 %collective-permute-done.8.l2_ref = bf16[1,16,8,256]{3,2,1,0:T(8,128)(2,1)S(1)} collective-permute-done((bf16[1,16,8,256]{3,2,1,0:T(8,128)(2,1)S(1)}, bf16[1,16,8,256]{3,2,1,0:T(8,128)(2,1)S(1)}, u32[]{:S(2)}, u32[]{:S(2)}) %collective-permute-start.8) | collective-permute-done | bytes 65568 | tf_op jit(solution)/shard_map/ppermute | solution.py:19
  78.7 1.8 %collective-permute-done.9.l1_ref = bf16[1,16,8,256]{3,2,1,0:T(8,128)(2,1)S(1)} collective-permute-done((bf16[1,16,8,256]{3,2,1,0:T(8,128)(2,1)S(1)}, bf16[1,16,8,256]{3,2,1,0:T(8,128)(2,1)S(1)}, u32[]{:S(2)}, u32[]{:S(2)}) %collective-permute-start.9) | collective-permute-done | bytes 65568 | tf_op jit(solution)/shard_map/ppermute | solution.py:19
  80.5 0.0 copy-done.9
  80.5 0.0 copy-done.10
  80.5 0.6 copy-done.11
  81.1 7.9 %shard_map.124 = bf16[4,96,4,256]{3,2,1,0:T(4,128)(2,1)} custom-call(bf16[1,16,8,256]{3,2,1,0:T(8,128)(2,1)} %copy-done.9, bf16[1,16,8,256]{3,2,1,0:T(8,128)(2,1)} %copy-done.10, bf16[1,16,8,256]{3,2,1,0:T(8,128)(2,1)} %copy-done.11, bf16[1,16,8,256]{3,2,1,0:T(8,128)(2,1)} %copy-done.7, bf16[288,144]{1,0:T(8,128)(2,1)} %copy.39.dk_ref, ...), custom_call_target="tpu_custom_call" | custom-call | tf_op jit(solution)/shard_map/pallas_call | solution.py:245
  (8 shorter events, 0.0 us)
Async XLA Ops:
  1.9 4.5 %copy-start = (bf16[4,96,4,256]{3,1,2,0:T(8,128)(2,1)}, bf16[4,96,4,256]{3,1,2,0:T(8,128)(2,1)S(1)}, u32[]{:S(2)}) copy-start(bf16[4,96,4,256]{3,1,2,0:T(8,128)(2,1)S(1)} %copy.42) | copy-start | bytes 2359300
  1.9 11.6 %copy-start.4 = (bf16[3,3,3,96,96]{4,3,2,1,0:T(8,128)(2,1)S(1)}, bf16[3,3,3,96,96]{4,3,2,1,0:T(8,128)(2,1)}, u32[]{:S(2)}) copy-start(bf16[3,3,3,96,96]{4,3,2,1,0:T(8,128)(2,1)} %param.12) | copy-start | bytes 1492996
  1.9 26.1 %collective-permute-start = (bf16[4,4,96,256]{3,2,1,0:T(8,128)(2,1)S(1)}, bf16[4,4,96,256]{3,2,1,0:T(8,128)(2,1)S(1)}, u32[]{:S(2)}, u32[]{:S(2)}) collective-permute-start(bf16[4,4,96,256]{3,2,1,0:T(8,128)(2,1)S(1)} %bitcast.13), channel_id=1, source_target_pairs={{0,4},{4,8},{8,12},{12,16},{16,20},{20,24},{24,28},{28,32},{32,36}... | collective-permute-start | bytes 2359304 | tf_op jit(solution)/shard_map/ppermute | solution.py:19
  6.4 30.4 %collective-permute-start.3 = (bf16[4,2,96,256]{3,2,1,0:T(8,128)(2,1)}, bf16[4,2,96,256]{3,2,1,0:T(8,128)(2,1)S(1)}, u32[]{:S(2)}, u32[]{:S(2)}) collective-permute-start(bf16[4,2,96,256]{3,2,1,0:T(8,128)(2,1)} %get-tuple-element.25), channel_id=1, source_target_pairs={{0,1},{1,2},{2,3},{4,5},{5,6},{6,7},{8,9},{9,10},{10,11},{12,13},{... | collective-permute-start | bytes 1179656 | tf_op jit(solution)/shard_map/ppermute | solution.py:16
  8.3 28.5 %collective-permute-start.4 = (bf16[4,2,96,256]{3,2,1,0:T(8,128)(2,1)}, bf16[4,2,96,256]{3,2,1,0:T(8,128)(2,1)S(1)}, u32[]{:S(2)}, u32[]{:S(2)}) collective-permute-start(bf16[4,2,96,256]{3,2,1,0:T(8,128)(2,1)} %get-tuple-element.24), channel_id=1, source_target_pairs={{1,0},{2,1},{3,2},{5,4},{6,5},{7,6},{9,8},{10,9},{11,10},{13,12},{... | collective-permute-start | bytes 1179656 | tf_op jit(solution)/shard_map/ppermute | solution.py:16
  16.8 1.3 %copy-start.8 = (bf16[3,3,3,96,16]{3,4,2,1,0:T(8,128)(2,1)S(1)}, bf16[3,3,3,96,16]{3,4,2,1,0:T(8,128)(2,1)}, u32[]{:S(2)}) copy-start(bf16[3,3,3,96,16]{3,4,2,1,0:T(8,128)(2,1)} %param.17) | copy-start | bytes 248836
  19.9 1.4 %copy-start.15 = (f32[96]{0:T(128)S(1)}, f32[96]{0:T(128)}, u32[]{:S(2)}) copy-start(f32[96]{0:T(128)} %param.13) | copy-start | bytes 1156
  21.2 0.7 copy-start.12
  21.3 0.7 copy-start.13
  21.3 0.7 copy-start.14
  28.0 0.9 copy-start.1
  28.9 14.5 %collective-permute-start.1 = (bf16[4,2,96,256]{3,2,1,0:T(8,128)(2,1)S(1)}, bf16[4,2,96,256]{3,2,1,0:T(8,128)(2,1)S(1)}, u32[]{:S(2)}, u32[]{:S(2)}) collective-permute-start(bf16[4,2,96,256]{3,2,1,0:T(8,128)(2,1)S(1)} %get-tuple-element.13), channel_id=1, source_target_pairs={{0,1},{1,2},{2,3},{4,5},{5,6},{6,7},{8,9},{9,10},{10,11},{12,13},{... | collective-permute-start | bytes 1179656 | tf_op jit(solution)/shard_map/ppermute | solution.py:16
  30.8 12.6 %collective-permute-start.2 = (bf16[4,2,96,256]{3,2,1,0:T(8,128)(2,1)S(1)}, bf16[4,2,96,256]{3,2,1,0:T(8,128)(2,1)S(1)}, u32[]{:S(2)}, u32[]{:S(2)}) collective-permute-start(bf16[4,2,96,256]{3,2,1,0:T(8,128)(2,1)S(1)} %get-tuple-element.14), channel_id=1, source_target_pairs={{1,0},{2,1},{3,2},{5,4},{6,5},{7,6},{9,8},{10,9},{11,10},{13,12},{... | collective-permute-start | bytes 1179656 | tf_op jit(solution)/shard_map/ppermute | solution.py:16
  36.9 0.8 copy-start.2
  37.6 0.7 copy-start.3
  43.4 0.8 copy-start.5
  44.1 0.7 copy-start.6
  56.1 4.3 %collective-permute-start.6 = (bf16[1,16,2,256]{3,2,1,0:T(2,128)(2,1)}, bf16[1,16,2,256]{3,2,1,0:T(2,128)(2,1)S(1)}, u32[]{:S(2)}, u32[]{:S(2)}) collective-permute-start(bf16[1,16,2,256]{3,2,1,0:T(2,128)(2,1)} %get-tuple-element.21), channel_id=1, source_target_pairs={{1,0},{2,1},{3,2},{5,4},{6,5},{7,6},{9,8},{10,9},{11,10},{13,12},{... | collective-permute-start | bytes 49160 | tf_op jit(solution)/shard_map/ppermute | solution.py:16
  58.5 6.8 %collective-permute-start.5 = (bf16[1,16,2,256]{3,2,1,0:T(2,128)(2,1)}, bf16[1,16,2,256]{3,2,1,0:T(2,128)(2,1)S(1)}, u32[]{:S(2)}, u32[]{:S(2)}) collective-permute-start(bf16[1,16,2,256]{3,2,1,0:T(2,128)(2,1)} %get-tuple-element.20), channel_id=1, source_target_pairs={{0,1},{1,2},{2,3},{4,5},{5,6},{6,7},{8,9},{9,10},{10,11},{12,13},{... | collective-permute-start | bytes 49160 | tf_op jit(solution)/shard_map/ppermute | solution.py:16
  66.1 7.8 %copy-start.7 = (bf16[1,16,8,256]{3,2,1,0:T(8,128)(2,1)}, bf16[1,16,8,256]{3,2,1,0:T(8,128)(2,1)S(1)}, u32[]{:S(2)}) copy-start(bf16[1,16,8,256]{3,2,1,0:T(8,128)(2,1)S(1)} %pad_maximum_fusion.l0_ref) | copy-start | bytes 196612
  66.1 9.2 %collective-permute-start.7 = (bf16[1,16,8,256]{3,2,1,0:T(8,128)(2,1)S(1)}, bf16[1,16,8,256]{3,2,1,0:T(8,128)(2,1)S(1)}, u32[]{:S(2)}, u32[]{:S(2)}) collective-permute-start(bf16[1,16,8,256]{3,2,1,0:T(8,128)(2,1)S(1)} %pad_maximum_fusion.l0_ref), channel_id=1, source_target_pairs={{0,12},{4,16},{8,20},{12,24},{16,28},{20,32},{24,36},{28,40},{32,4... | collective-permute-start | bytes 196616 | tf_op jit(solution)/shard_map/ppermute | solution.py:19
  68.0 10.7 %collective-permute-start.8 = (bf16[1,16,8,256]{3,2,1,0:T(8,128)(2,1)S(1)}, bf16[1,16,8,256]{3,2,1,0:T(8,128)(2,1)S(1)}, u32[]{:S(2)}, u32[]{:S(2)}) collective-permute-start(bf16[1,16,8,256]{3,2,1,0:T(8,128)(2,1)S(1)} %pad_maximum_fusion.l0_ref), channel_id=1, source_target_pairs={{0,8},{4,12},{8,16},{12,20},{16,24},{20,28},{24,32},{28,36},{32,40... | collective-permute-start | bytes 196616 | tf_op jit(solution)/shard_map/ppermute | solution.py:19
  70.1 10.4 %collective-permute-start.9 = (bf16[1,16,8,256]{3,2,1,0:T(8,128)(2,1)S(1)}, bf16[1,16,8,256]{3,2,1,0:T(8,128)(2,1)S(1)}, u32[]{:S(2)}, u32[]{:S(2)}) collective-permute-start(bf16[1,16,8,256]{3,2,1,0:T(8,128)(2,1)S(1)} %pad_maximum_fusion.l0_ref), channel_id=1, source_target_pairs={{0,4},{4,8},{8,12},{12,16},{16,20},{20,24},{24,28},{28,32},{32,36}... | collective-permute-start | bytes 196616 | tf_op jit(solution)/shard_map/ppermute | solution.py:19
  75.4 5.1 %copy-start.9 = (bf16[1,16,8,256]{3,2,1,0:T(8,128)(2,1)}, bf16[1,16,8,256]{3,2,1,0:T(8,128)(2,1)S(1)}, u32[]{:S(2)}) copy-start(bf16[1,16,8,256]{3,2,1,0:T(8,128)(2,1)S(1)} %collective-permute-done.7.l3_ref) | copy-start | bytes 196612
  78.7 1.8 %copy-start.10 = (bf16[1,16,8,256]{3,2,1,0:T(8,128)(2,1)}, bf16[1,16,8,256]{3,2,1,0:T(8,128)(2,1)S(1)}, u32[]{:S(2)}) copy-start(bf16[1,16,8,256]{3,2,1,0:T(8,128)(2,1)S(1)} %collective-permute-done.8.l2_ref) | copy-start | bytes 196612
  80.5 0.6 copy-start.11

commit v16 on v11

--- a/solution.py
+++ b/solution.py
@@ -136,11 +136,13 @@
     gain = vec_ref[:, 3:4]
     lat_refs = (l3_ref, l2_ref, l1_ref, l0_ref)
     lat = lambda t, r: lat_refs[t][0, :, r, :]
+    both = tap_sum(lat, dk_ref, 0, wide, columns, 2) + bias
+    scale = lax.rsqrt(jnp.mean(both * both, axis=0, keepdims=True) + 1e-06)
+    z = both * scale * gain
+    acts = (z / (1.0 + jnp.exp(-z))).astype(jnp.bfloat16)
+    span = wide * columns
     for f in range(2):
-        y = tap_sum(lat, dk_ref, f, wide, columns) + bias
-        scale = lax.rsqrt(jnp.mean(y * y, axis=0, keepdims=True) + 1e-06)
-        z = y * scale * gain
-        act = (z / (1.0 + jnp.exp(-z))).astype(jnp.bfloat16)
+        act = acts[:, f * span : (f + 1) * span]
         first_j = frames - 2 if f == 0 else 0
         for j in range(first_j, frames):
             up = jnp.dot(up_ref[j], act, preferred_element_type=jnp.float32)

time: 88.6 us -> 88.1 us (level)
  no operation moved by 1% of the time
where the time goes in v16:
time: 88.1 us; the launch traced here: 87.5 us
  starting transfers between devices  29.1 us (33%)
  Pallas kernels  22.4 us (25%)
  waiting for transfers between devices  17 us (19%)
  local copies, waits for them, and re-layouts  16.6 us (19%)
  other arithmetic  1.5 us (2%)
    ppermute x6, starting transfers between devices, shift(): return lax.ppermute(x, 'rows', pairs)  18.6 us
    ppermute x4, waiting for transfers between devices, shift(): return lax.ppermute(x, 'tm', pairs)  12.2 us
    ppermute x4, starting transfers between devices, shift(): return lax.ppermute(x, 'tm', pairs)  10.5 us
    pallas_call x1, Pallas kernels, body(): pl.pallas_call(functools.partial(encoder_kernel, **dims), out_shape=(jax....  10 us
    pallas_call x1, Pallas kernels, body(): pl.pallas_call(functools.partial(decode_kernel_body, **dims), out_shape=j...  7.39 us
    unnamed x33, local copies, waits for them, and re-layouts  6.37 us
    pallas_call x1, Pallas kernels, body(): pl.pallas_call(functools.partial(late_gate_kernel, **dims), out_shape=jax...  5.03 us
    ppermute x6, waiting for transfers between devices, shift(): return lax.ppermute(x, 'rows', pairs)  4.85 us
  transfers between devices with their start and end apart: 10, of which 5 were waited for; matrix products, arithmetic and copies ran while one was open for 12% of the time, Pallas kernels for 6%

profile of v16, /device:TPU:24, one launch (start us, length us, event | category | flops | bytes accessed | tf_op | source)
XLA Modules:
  0.0 87.5 jit_solution(2100716926184808298)
XLA Ops:
  0.6 1.3 %copy.42 = bf16[4,96,4,256]{3,1,2,0:T(8,128)(2,1)S(1)} copy(bf16[4,96,4,256]{3,2,1,0:T(4,128)(2,1)} %param.11) | data formatting | bytes 1572864 | tf_op args[0]
  1.9 0.0 copy-start
  1.9 0.0 copy-start.4
  1.9 3.5 %collective-permute-start = (bf16[4,4,96,256]{3,2,1,0:T(8,128)(2,1)S(1)}, bf16[4,4,96,256]{3,2,1,0:T(8,128)(2,1)S(1)}, u32[]{:S(2)}, u32[]{:S(2)}) collective-permute-start(bf16[4,4,96,256]{3,2,1,0:T(8,128)(2,1)S(1)} %bitcast.13), channel_id=1, source_target_pairs={{0,4},{4,8},{8,12},{12,16},{16,20},{20,24},{24,28},{28,32},{32,36}... | collective-permute-start | bytes 2359304 | tf_op jit(solution)/shard_map/ppermute | solution.py:19
  5.5 1.0 %fusion = (bf16[4,2,96,256]{3,2,1,0:T(8,128)(2,1)}, bf16[4,2,96,256]{3,2,1,0:T(8,128)(2,1)}) fusion(bf16[4,4,96,256]{3,2,1,0:T(8,128)(2,1)S(1)} %bitcast.14), kind=kLoop, calls=%fused_computation.6 | loop fusion | bytes 1572864 | tf_op jit(solution)/shard_map/slice | solution.py:179
  6.4 0.0 copy-done
  6.4 1.9 %collective-permute-start.3 = (bf16[4,2,96,256]{3,2,1,0:T(8,128)(2,1)}, bf16[4,2,96,256]{3,2,1,0:T(8,128)(2,1)S(1)}, u32[]{:S(2)}, u32[]{:S(2)}) collective-permute-start(bf16[4,2,96,256]{3,2,1,0:T(8,128)(2,1)} %get-tuple-element.25), channel_id=1, source_target_pairs={{0,1},{1,2},{2,3},{4,5},{5,6},{6,7},{8,9},{9,10},{10,11},{12,13},{... | collective-permute-start | bytes 1179656 | tf_op jit(solution)/shard_map/ppermute | solution.py:16
  8.3 5.1 %collective-permute-start.4 = (bf16[4,2,96,256]{3,2,1,0:T(8,128)(2,1)}, bf16[4,2,96,256]{3,2,1,0:T(8,128)(2,1)S(1)}, u32[]{:S(2)}, u32[]{:S(2)}) collective-permute-start(bf16[4,2,96,256]{3,2,1,0:T(8,128)(2,1)} %get-tuple-element.24), channel_id=1, source_target_pairs={{1,0},{2,1},{3,2},{5,4},{6,5},{7,6},{9,8},{10,9},{11,10},{13,12},{... | collective-permute-start | bytes 1179656 | tf_op jit(solution)/shard_map/ppermute | solution.py:16
  13.5 0.0 copy-done.4
  13.5 0.5 copy.33
  14.0 1.3 %reshape.16.k1_ref = bf16[288,864]{1,0:T(8,128)(2,1)} reshape(bf16[3,96,3,3,96]{4,3,2,1,0:T(4,128)(2,1)S(1)} %copy.33) | data formatting | bytes 995328 | tf_op jit(solution)/shard_map/reshape | solution.py:31
  15.3 1.5 %copy.34 = bf16[3,96,3,3,96]{4,3,2,1,0:T(4,128)(2,1)S(1)} copy(bf16[3,96,3,3,96]{4,1,0,3,2:T(8,128)(2,1)} %bitcast.18) | data formatting | bytes 995328 | tf_op jit(solution)/shard_map/transpose | solution.py:31
  16.8 0.0 copy-start.8
  16.8 1.3 %reshape.17.k2_ref = bf16[288,864]{1,0:T(8,128)(2,1)} reshape(bf16[3,96,3,3,96]{4,3,2,1,0:T(4,128)(2,1)S(1)} %copy.34) | data formatting | bytes 995328 | tf_op jit(solution)/shard_map/reshape | solution.py:31
  18.1 0.0 copy-done.8
  18.1 0.1 copy.35
  18.2 0.1 reshape.18
  18.3 1.6 %copy.36 = bf16[3,96,3,3,96]{4,3,2,1,0:T(4,128)(2,1)S(1)} copy(bf16[3,96,3,3,96]{4,1,0,3,2:T(8,128)(2,1)} %bitcast.19) | data formatting | bytes 995328 | tf_op jit(solution)/shard_map/transpose | solution.py:31
  19.9 0.0 copy-start.15
  19.9 1.3 %reshape.19.fk_ref = bf16[288,864]{1,0:T(8,128)(2,1)} reshape(bf16[3,96,3,3,96]{4,3,2,1,0:T(4,128)(2,1)S(1)} %copy.36) | data formatting | bytes 995328 | tf_op jit(solution)/shard_map/reshape | solution.py:31
  21.2 0.0 copy-start.12
  21.3 0.0 copy-start.13
  21.3 0.0 copy-start.14
  21.3 0.0 copy-done.15
  21.3 0.6 copy-done.12
  21.9 0.0 copy-done.13
  21.9 0.0 copy-done.14
  21.9 0.7 and_convert_fusion.mask_ref
  22.6 5.4 %collective-permute-done.pv_ref = bf16[4,4,96,256]{3,2,1,0:T(8,128)(2,1)S(1)} collective-permute-done((bf16[4,4,96,256]{3,2,1,0:T(8,128)(2,1)S(1)}, bf16[4,4,96,256]{3,2,1,0:T(8,128)(2,1)S(1)}, u32[]{:S(2)}, u32[]{:S(2)}) %collective-permute-start) | collective-permute-done | bytes 786464 | tf_op jit(solution)/shard_map/ppermute | solution.py:19
  28.0 0.0 copy-start.1
  28.0 0.1 fusion.1
  28.1 0.8 copy-done.1
  28.9 1.9 %collective-permute-start.1 = (bf16[4,2,96,256]{3,2,1,0:T(8,128)(2,1)S(1)}, bf16[4,2,96,256]{3,2,1,0:T(8,128)(2,1)S(1)}, u32[]{:S(2)}, u32[]{:S(2)}) collective-permute-start(bf16[4,2,96,256]{3,2,1,0:T(8,128)(2,1)S(1)} %get-tuple-element.13), channel_id=1, source_target_pairs={{0,1},{1,2},{2,3},{4,5},{5,6},{6,7},{8,9},{9,10},{10,11},{12,13},{... | collective-permute-start | bytes 1179656 | tf_op jit(solution)/shard_map/ppermute | solution.py:16
  30.8 5.1 %collective-permute-start.2 = (bf16[4,2,96,256]{3,2,1,0:T(8,128)(2,1)S(1)}, bf16[4,2,96,256]{3,2,1,0:T(8,128)(2,1)S(1)}, u32[]{:S(2)}, u32[]{:S(2)}) collective-permute-start(bf16[4,2,96,256]{3,2,1,0:T(8,128)(2,1)S(1)} %get-tuple-element.14), channel_id=1, source_target_pairs={{1,0},{2,1},{3,2},{5,4},{6,5},{7,6},{9,8},{10,9},{11,10},{13,12},{... | collective-permute-start | bytes 1179656 | tf_op jit(solution)/shard_map/ppermute | solution.py:16
  35.9 0.7 copy.37.vec_ref
  36.7 0.0 collective-permute-done.3.tp_ref
  36.7 0.0 copy-start.2
  36.7 0.0 collective-permute-done.4.bt_ref
  36.7 0.7 copy-done.2
  37.4 0.7 copy-done.3
  38.2 5.0 %shard_map.122.late_ref = bf16[2,6,96,256]{3,2,1,0:T(8,128)(2,1)} custom-call(bf16[4,2,96,256]{3,2,1,0:T(8,128)(2,1)} %copy-done.2, bf16[4,4,96,256]{3,2,1,0:T(8,128)(2,1)} %bitcast.15, bf16[4,2,96,256]{3,2,1,0:T(8,128)(2,1)} %copy-done.3, bf16[288,864]{1,0:T(8,128)(2,1)} %reshape.16.k1_ref, f32[96,4]{1,0:T(8,128)} %copy.37.vec_ref, ...), custom_call_target="tpu_custom_call" | custom-call | tf_op jit(solution)/shard_map/pallas_call | solution.py:209
  43.2 0.0 collective-permute-done.1.tc_ref
  43.2 0.0 collective-permute-done.2.bc_ref
  43.2 0.7 copy-done.5
  44.0 0.7 copy-done.6
  44.7 10.0 %shard_map.123 = (bf16[1,16,4,256]{3,2,1,0:T(4,128)(2,1)}, bf16[1,16,2,256]{3,2,1,0:T(2,128)(2,1)}, bf16[1,16,2,256]{3,2,1,0:T(2,128)(2,1)}) custom-call(bf16[4,2,96,256]{3,2,1,0:T(8,128)(2,1)} %copy-done.5, bf16[4,4,96,256]{3,2,1,0:T(8,128)(2,1)} %copy-done.1, bf16[4,2,96,256]{3,2,1,0:T(8,128)(2,1)} %copy-done.6, bf16[4,2,96,256]{3,2,1,0:T(8,128)(2,1)} %copy-done.2, ...), custom_call_target="tpu_custom_call" | custom-call | tf_op jit(solution)/shard_map/pallas_call | solution.py:214
  54.7 2.6 %collective-permute-start.6 = (bf16[1,16,2,256]{3,2,1,0:T(2,128)(2,1)}, bf16[1,16,2,256]{3,2,1,0:T(2,128)(2,1)S(1)}, u32[]{:S(2)}, u32[]{:S(2)}) collective-permute-start(bf16[1,16,2,256]{3,2,1,0:T(2,128)(2,1)} %get-tuple-element.21), channel_id=1, source_target_pairs={{1,0},{2,1},{3,2},{5,4},{6,5},{7,6},{9,8},{10,9},{11,10},{13,12},{... | collective-permute-start | bytes 49160 | tf_op jit(solution)/shard_map/ppermute | solution.py:16
  57.3 1.9 %collective-permute-start.5 = (bf16[1,16,2,256]{3,2,1,0:T(2,128)(2,1)}, bf16[1,16,2,256]{3,2,1,0:T(2,128)(2,1)S(1)}, u32[]{:S(2)}, u32[]{:S(2)}) collective-permute-start(bf16[1,16,2,256]{3,2,1,0:T(2,128)(2,1)} %get-tuple-element.20), channel_id=1, source_target_pairs={{0,1},{1,2},{2,3},{4,5},{5,6},{6,7},{8,9},{9,10},{10,11},{12,13},{... | collective-permute-start | bytes 49160 | tf_op jit(solution)/shard_map/ppermute | solution.py:16
  59.2 0.0 collective-permute-done.6
  59.2 4.8 %collective-permute-done.5 = bf16[1,16,2,256]{3,2,1,0:T(2,128)(2,1)S(1)} collective-permute-done((bf16[1,16,2,256]{3,2,1,0:T(2,128)(2,1)}, bf16[1,16,2,256]{3,2,1,0:T(2,128)(2,1)S(1)}, u32[]{:S(2)}, u32[]{:S(2)}) %collective-permute-start.5) | collective-permute-done | bytes 16416 | tf_op jit(solution)/shard_map/ppermute | solution.py:16
  64.1 0.8 pad_maximum_fusion.l0_ref
  64.9 0.0 copy-start.7
  64.9 2.1 %collective-permute-start.7 = (bf16[1,16,8,256]{3,2,1,0:T(8,128)(2,1)S(1)}, bf16[1,16,8,256]{3,2,1,0:T(8,128)(2,1)S(1)}, u32[]{:S(2)}, u32[]{:S(2)}) collective-permute-start(bf16[1,16,8,256]{3,2,1,0:T(8,128)(2,1)S(1)} %pad_maximum_fusion.l0_ref), channel_id=1, source_target_pairs={{0,12},{4,16},{8,20},{12,24},{16,28},{20,32},{24,36},{28,40},{32,4... | collective-permute-start | bytes 196616 | tf_op jit(solution)/shard_map/ppermute | solution.py:19
  67.0 2.0 %collective-permute-start.8 = (bf16[1,16,8,256]{3,2,1,0:T(8,128)(2,1)S(1)}, bf16[1,16,8,256]{3,2,1,0:T(8,128)(2,1)S(1)}, u32[]{:S(2)}, u32[]{:S(2)}) collective-permute-start(bf16[1,16,8,256]{3,2,1,0:T(8,128)(2,1)S(1)} %pad_maximum_fusion.l0_ref), channel_id=1, source_target_pairs={{0,8},{4,12},{8,16},{12,20},{16,24},{20,28},{24,32},{28,36},{32,40... | collective-permute-start | bytes 196616 | tf_op jit(solution)/shard_map/ppermute | solution.py:19
  69.1 2.8 %collective-permute-start.9 = (bf16[1,16,8,256]{3,2,1,0:T(8,128)(2,1)S(1)}, bf16[1,16,8,256]{3,2,1,0:T(8,128)(2,1)S(1)}, u32[]{:S(2)}, u32[]{:S(2)}) collective-permute-start(bf16[1,16,8,256]{3,2,1,0:T(8,128)(2,1)S(1)} %pad_maximum_fusion.l0_ref), channel_id=1, source_target_pairs={{0,4},{4,8},{8,12},{12,16},{16,20},{20,24},{24,28},{28,32},{32,36}... | collective-permute-start | bytes 196616 | tf_op jit(solution)/shard_map/ppermute | solution.py:19
  71.9 0.8 copy.39.dk_ref
  72.6 0.0 copy-done.7
  72.6 1.4 %collective-permute-done.7.l3_ref = bf16[1,16,8,256]{3,2,1,0:T(8,128)(2,1)S(1)} collective-permute-done((bf16[1,16,8,256]{3,2,1,0:T(8,128)(2,1)S(1)}, bf16[1,16,8,256]{3,2,1,0:T(8,128)(2,1)S(1)}, u32[]{:S(2)}, u32[]{:S(2)}) %collective-permute-start.7) | collective-permute-done | bytes 65568 | tf_op jit(solution)/shard_map/ppermute | solution.py:19
  74.1 3.6 %collective-permute-done.8.l2_ref = bf16[1,16,8,256]{3,2,1,0:T(8,128)(2,1)S(1)} collective-permute-done((bf16[1,16,8,256]{3,2,1,0:T(8,128)(2,1)S(1)}, bf16[1,16,8,256]{3,2,1,0:T(8,128)(2,1)S(1)}, u32[]{:S(2)}, u32[]{:S(2)}) %collective-permute-start.8) | collective-permute-done | bytes 65568 | tf_op jit(solution)/shard_map/ppermute | solution.py:19
  77.7 1.8 %collective-permute-done.9.l1_ref = bf16[1,16,8,256]{3,2,1,0:T(8,128)(2,1)S(1)} collective-permute-done((bf16[1,16,8,256]{3,2,1,0:T(8,128)(2,1)S(1)}, bf16[1,16,8,256]{3,2,1,0:T(8,128)(2,1)S(1)}, u32[]{:S(2)}, u32[]{:S(2)}) %collective-permute-start.9) | collective-permute-done | bytes 65568 | tf_op jit(solution)/shard_map/ppermute | solution.py:19
  79.5 0.0 copy-done.9
  79.5 0.0 copy-done.10
  79.5 0.6 copy-done.11
  80.1 7.4 %shard_map.124 = bf16[4,96,4,256]{3,2,1,0:T(4,128)(2,1)} custom-call(bf16[1,16,8,256]{3,2,1,0:T(8,128)(2,1)} %copy-done.9, bf16[1,16,8,256]{3,2,1,0:T(8,128)(2,1)} %copy-done.10, bf16[1,16,8,256]{3,2,1,0:T(8,128)(2,1)} %copy-done.11, bf16[1,16,8,256]{3,2,1,0:T(8,128)(2,1)} %copy-done.7, bf16[288,144]{1,0:T(8,128)(2,1)} %copy.39.dk_ref, ...), custom_call_target="tpu_custom_call" | custom-call | tf_op jit(solution)/shard_map/pallas_call | solution.py:236
  (8 shorter events, 0.0 us)
Async XLA Ops:
  1.9 4.5 %copy-start = (bf16[4,96,4,256]{3,1,2,0:T(8,128)(2,1)}, bf16[4,96,4,256]{3,1,2,0:T(8,128)(2,1)S(1)}, u32[]{:S(2)}) copy-start(bf16[4,96,4,256]{3,1,2,0:T(8,128)(2,1)S(1)} %copy.42) | copy-start | bytes 2359300
  1.9 11.6 %copy-start.4 = (bf16[3,3,3,96,96]{4,3,2,1,0:T(8,128)(2,1)S(1)}, bf16[3,3,3,96,96]{4,3,2,1,0:T(8,128)(2,1)}, u32[]{:S(2)}) copy-start(bf16[3,3,3,96,96]{4,3,2,1,0:T(8,128)(2,1)} %param.12) | copy-start | bytes 1492996
  1.9 26.1 %collective-permute-start = (bf16[4,4,96,256]{3,2,1,0:T(8,128)(2,1)S(1)}, bf16[4,4,96,256]{3,2,1,0:T(8,128)(2,1)S(1)}, u32[]{:S(2)}, u32[]{:S(2)}) collective-permute-start(bf16[4,4,96,256]{3,2,1,0:T(8,128)(2,1)S(1)} %bitcast.13), channel_id=1, source_target_pairs={{0,4},{4,8},{8,12},{12,16},{16,20},{20,24},{24,28},{28,32},{32,36}... | collective-permute-start | bytes 2359304 | tf_op jit(solution)/shard_map/ppermute | solution.py:19
  6.4 30.3 %collective-permute-start.3 = (bf16[4,2,96,256]{3,2,1,0:T(8,128)(2,1)}, bf16[4,2,96,256]{3,2,1,0:T(8,128)(2,1)S(1)}, u32[]{:S(2)}, u32[]{:S(2)}) collective-permute-start(bf16[4,2,96,256]{3,2,1,0:T(8,128)(2,1)} %get-tuple-element.25), channel_id=1, source_target_pairs={{0,1},{1,2},{2,3},{4,5},{5,6},{6,7},{8,9},{9,10},{10,11},{12,13},{... | collective-permute-start | bytes 1179656 | tf_op jit(solution)/shard_map/ppermute | solution.py:16
  8.3 28.3 %collective-permute-start.4 = (bf16[4,2,96,256]{3,2,1,0:T(8,128)(2,1)}, bf16[4,2,96,256]{3,2,1,0:T(8,128)(2,1)S(1)}, u32[]{:S(2)}, u32[]{:S(2)}) collective-permute-start(bf16[4,2,96,256]{3,2,1,0:T(8,128)(2,1)} %get-tuple-element.24), channel_id=1, source_target_pairs={{1,0},{2,1},{3,2},{5,4},{6,5},{7,6},{9,8},{10,9},{11,10},{13,12},{... | collective-permute-start | bytes 1179656 | tf_op jit(solution)/shard_map/ppermute | solution.py:16
  16.8 1.3 %copy-start.8 = (bf16[3,3,3,96,16]{3,4,2,1,0:T(8,128)(2,1)S(1)}, bf16[3,3,3,96,16]{3,4,2,1,0:T(8,128)(2,1)}, u32[]{:S(2)}) copy-start(bf16[3,3,3,96,16]{3,4,2,1,0:T(8,128)(2,1)} %param.17) | copy-start | bytes 248836
  19.9 1.4 %copy-start.15 = (f32[96]{0:T(128)S(1)}, f32[96]{0:T(128)}, u32[]{:S(2)}) copy-start(f32[96]{0:T(128)} %param.13) | copy-start | bytes 1156
  21.2 0.7 copy-start.12
  21.3 0.7 copy-start.13
  21.3 0.7 copy-start.14
  28.0 0.9 %copy-start.1 = (bf16[4,4,96,256]{3,2,1,0:T(8,128)(2,1)}, bf16[4,4,96,256]{3,2,1,0:T(8,128)(2,1)S(1)}, u32[]{:S(2)}) copy-start(bf16[4,4,96,256]{3,2,1,0:T(8,128)(2,1)S(1)} %collective-permute-done.pv_ref) | copy-start | bytes 2359300
  28.9 14.3 %collective-permute-start.1 = (bf16[4,2,96,256]{3,2,1,0:T(8,128)(2,1)S(1)}, bf16[4,2,96,256]{3,2,1,0:T(8,128)(2,1)S(1)}, u32[]{:S(2)}, u32[]{:S(2)}) collective-permute-start(bf16[4,2,96,256]{3,2,1,0:T(8,128)(2,1)S(1)} %get-tuple-element.13), channel_id=1, source_target_pairs={{0,1},{1,2},{2,3},{4,5},{5,6},{6,7},{8,9},{9,10},{10,11},{12,13},{... | collective-permute-start | bytes 1179656 | tf_op jit(solution)/shard_map/ppermute | solution.py:16
  30.8 12.4 %collective-permute-start.2 = (bf16[4,2,96,256]{3,2,1,0:T(8,128)(2,1)S(1)}, bf16[4,2,96,256]{3,2,1,0:T(8,128)(2,1)S(1)}, u32[]{:S(2)}, u32[]{:S(2)}) collective-permute-start(bf16[4,2,96,256]{3,2,1,0:T(8,128)(2,1)S(1)} %get-tuple-element.14), channel_id=1, source_target_pairs={{1,0},{2,1},{3,2},{5,4},{6,5},{7,6},{9,8},{10,9},{11,10},{13,12},{... | collective-permute-start | bytes 1179656 | tf_op jit(solution)/shard_map/ppermute | solution.py:16
  36.7 0.8 copy-start.2
  37.4 0.7 copy-start.3
  43.2 0.8 copy-start.5
  44.0 0.7 copy-start.6
  54.7 4.5 %collective-permute-start.6 = (bf16[1,16,2,256]{3,2,1,0:T(2,128)(2,1)}, bf16[1,16,2,256]{3,2,1,0:T(2,128)(2,1)S(1)}, u32[]{:S(2)}, u32[]{:S(2)}) collective-permute-start(bf16[1,16,2,256]{3,2,1,0:T(2,128)(2,1)} %get-tuple-element.21), channel_id=1, source_target_pairs={{1,0},{2,1},{3,2},{5,4},{6,5},{7,6},{9,8},{10,9},{11,10},{13,12},{... | collective-permute-start | bytes 49160 | tf_op jit(solution)/shard_map/ppermute | solution.py:16
  57.3 6.8 %collective-permute-start.5 = (bf16[1,16,2,256]{3,2,1,0:T(2,128)(2,1)}, bf16[1,16,2,256]{3,2,1,0:T(2,128)(2,1)S(1)}, u32[]{:S(2)}, u32[]{:S(2)}) collective-permute-start(bf16[1,16,2,256]{3,2,1,0:T(2,128)(2,1)} %get-tuple-element.20), channel_id=1, source_target_pairs={{0,1},{1,2},{2,3},{4,5},{5,6},{6,7},{8,9},{9,10},{10,11},{12,13},{... | collective-permute-start | bytes 49160 | tf_op jit(solution)/shard_map/ppermute | solution.py:16
  64.9 7.8 %copy-start.7 = (bf16[1,16,8,256]{3,2,1,0:T(8,128)(2,1)}, bf16[1,16,8,256]{3,2,1,0:T(8,128)(2,1)S(1)}, u32[]{:S(2)}) copy-start(bf16[1,16,8,256]{3,2,1,0:T(8,128)(2,1)S(1)} %pad_maximum_fusion.l0_ref) | copy-start | bytes 196612
  64.9 9.2 %collective-permute-start.7 = (bf16[1,16,8,256]{3,2,1,0:T(8,128)(2,1)S(1)}, bf16[1,16,8,256]{3,2,1,0:T(8,128)(2,1)S(1)}, u32[]{:S(2)}, u32[]{:S(2)}) collective-permute-start(bf16[1,16,8,256]{3,2,1,0:T(8,128)(2,1)S(1)} %pad_maximum_fusion.l0_ref), channel_id=1, source_target_pairs={{0,12},{4,16},{8,20},{12,24},{16,28},{20,32},{24,36},{28,40},{32,4... | collective-permute-start | bytes 196616 | tf_op jit(solution)/shard_map/ppermute | solution.py:19
  67.0 10.7 %collective-permute-start.8 = (bf16[1,16,8,256]{3,2,1,0:T(8,128)(2,1)S(1)}, bf16[1,16,8,256]{3,2,1,0:T(8,128)(2,1)S(1)}, u32[]{:S(2)}, u32[]{:S(2)}) collective-permute-start(bf16[1,16,8,256]{3,2,1,0:T(8,128)(2,1)S(1)} %pad_maximum_fusion.l0_ref), channel_id=1, source_target_pairs={{0,8},{4,12},{8,16},{12,20},{16,24},{20,28},{24,32},{28,36},{32,40... | collective-permute-start | bytes 196616 | tf_op jit(solution)/shard_map/ppermute | solution.py:19
  69.1 10.4 %collective-permute-start.9 = (bf16[1,16,8,256]{3,2,1,0:T(8,128)(2,1)S(1)}, bf16[1,16,8,256]{3,2,1,0:T(8,128)(2,1)S(1)}, u32[]{:S(2)}, u32[]{:S(2)}) collective-permute-start(bf16[1,16,8,256]{3,2,1,0:T(8,128)(2,1)S(1)} %pad_maximum_fusion.l0_ref), channel_id=1, source_target_pairs={{0,4},{4,8},{8,12},{12,16},{16,20},{20,24},{24,28},{28,32},{32,36}... | collective-permute-start | bytes 196616 | tf_op jit(solution)/shard_map/ppermute | solution.py:19
  74.1 5.4 %copy-start.9 = (bf16[1,16,8,256]{3,2,1,0:T(8,128)(2,1)}, bf16[1,16,8,256]{3,2,1,0:T(8,128)(2,1)S(1)}, u32[]{:S(2)}) copy-start(bf16[1,16,8,256]{3,2,1,0:T(8,128)(2,1)S(1)} %collective-permute-done.7.l3_ref) | copy-start | bytes 196612
  77.7 1.8 %copy-start.10 = (bf16[1,16,8,256]{3,2,1,0:T(8,128)(2,1)}, bf16[1,16,8,256]{3,2,1,0:T(8,128)(2,1)S(1)}, u32[]{:S(2)}) copy-start(bf16[1,16,8,256]{3,2,1,0:T(8,128)(2,1)S(1)} %collective-permute-done.8.l2_ref) | copy-start | bytes 196612
  79.5 0.6 copy-start.11

commit v17 on v16

--- a/solution.py
+++ b/solution.py
@@ -150,12 +150,14 @@
             for r in range(wide):
                 piece = up[:, r * columns : (r + 1) * columns] * mask_ref[slot, r]
                 ext_ref[slot, r] = piece.astype(ext_ref.dtype)
-    for t in range(frames):
-        y = tap_sum(from_ref(ext_ref), fk_ref, t, rows, columns)
-        res = frame_rows(from_ref(ext_ref), t + 2, 1, rows)
-        out = (res.astype(jnp.float32) + y).astype(o_ref.dtype)
-        for r in range(rows):
-            o_ref[t, :, r, :] = out[:, r * columns : (r + 1) * columns]
+    width = rows * columns
+    for t in range(0, frames, 2):
+        y = tap_sum(from_ref(ext_ref), fk_ref, t, rows, columns, 2)
+        for i in range(2):
+            res = frame_rows(from_ref(ext_ref), t + i + 2, 1, rows)
+            out = (res.astype(jnp.float32) + y[:, i * width : (i + 1) * width]).astype(o_ref.dtype)
+            for r in range(rows):
+                o_ref[t + i, :, r, :] = out[:, r * columns : (r + 1) * columns]
 
 
 def body(

time: 88.1 us -> 88 us (level)
  no operation moved by 1% of the time
where the time goes in v17:
time: 88 us; the launch traced here: 87.3 us
  starting transfers between devices  29.1 us (33%)
  Pallas kernels  22.3 us (25%)
  waiting for transfers between devices  17 us (19%)
  local copies, waits for them, and re-layouts  16.6 us (19%)
  other arithmetic  1.5 us (2%)
    ppermute x6, starting transfers between devices, shift(): return lax.ppermute(x, 'rows', pairs)  18.6 us
    ppermute x4, waiting for transfers between devices, shift(): return lax.ppermute(x, 'tm', pairs)  12.2 us
    ppermute x4, starting transfers between devices, shift(): return lax.ppermute(x, 'tm', pairs)  10.5 us
    pallas_call x1, Pallas kernels, body(): pl.pallas_call(functools.partial(encoder_kernel, **dims), out_shape=(jax....  10 us
    pallas_call x1, Pallas kernels, body(): pl.pallas_call(functools.partial(decode_kernel_body, **dims), out_shape=j...  7.24 us
    unnamed x33, local copies, waits for them, and re-layouts  6.37 us
    pallas_call x1, Pallas kernels, body(): pl.pallas_call(functools.partial(late_gate_kernel, **dims), out_shape=jax...  5.03 us
    ppermute x6, waiting for transfers between devices, shift(): return lax.ppermute(x, 'rows', pairs)  4.85 us
  transfers between devices with their start and end apart: 10, of which 5 were waited for; matrix products, arithmetic and copies ran while one was open for 12% of the time, Pallas kernels for 6%

profile of v17, /device:TPU:24, one launch (start us, length us, event | category | flops | bytes accessed | tf_op | source)
XLA Modules:
  0.0 87.3 jit_solution(7926987016303781271)
XLA Ops:
  0.6 1.3 %copy.42 = bf16[4,96,4,256]{3,1,2,0:T(8,128)(2,1)S(1)} copy(bf16[4,96,4,256]{3,2,1,0:T(4,128)(2,1)} %param.11) | data formatting | bytes 1572864 | tf_op args[0]
  1.9 0.0 copy-start
  1.9 0.0 copy-start.4
  1.9 3.5 %collective-permute-start = (bf16[4,4,96,256]{3,2,1,0:T(8,128)(2,1)S(1)}, bf16[4,4,96,256]{3,2,1,0:T(8,128)(2,1)S(1)}, u32[]{:S(2)}, u32[]{:S(2)}) collective-permute-start(bf16[4,4,96,256]{3,2,1,0:T(8,128)(2,1)S(1)} %bitcast.13), channel_id=1, source_target_pairs={{0,4},{4,8},{8,12},{12,16},{16,20},{20,24},{24,28},{28,32},{32,36}... | collective-permute-start | bytes 2359304 | tf_op jit(solution)/shard_map/ppermute | solution.py:19
  5.5 1.0 %fusion = (bf16[4,2,96,256]{3,2,1,0:T(8,128)(2,1)}, bf16[4,2,96,256]{3,2,1,0:T(8,128)(2,1)}) fusion(bf16[4,4,96,256]{3,2,1,0:T(8,128)(2,1)S(1)} %bitcast.14), kind=kLoop, calls=%fused_computation.6 | loop fusion | bytes 1572864 | tf_op jit(solution)/shard_map/slice | solution.py:181
  6.4 0.0 copy-done
  6.4 1.9 %collective-permute-start.3 = (bf16[4,2,96,256]{3,2,1,0:T(8,128)(2,1)}, bf16[4,2,96,256]{3,2,1,0:T(8,128)(2,1)S(1)}, u32[]{:S(2)}, u32[]{:S(2)}) collective-permute-start(bf16[4,2,96,256]{3,2,1,0:T(8,128)(2,1)} %get-tuple-element.25), channel_id=1, source_target_pairs={{0,1},{1,2},{2,3},{4,5},{5,6},{6,7},{8,9},{9,10},{10,11},{12,13},{... | collective-permute-start | bytes 1179656 | tf_op jit(solution)/shard_map/ppermute | solution.py:16
  8.3 5.1 %collective-permute-start.4 = (bf16[4,2,96,256]{3,2,1,0:T(8,128)(2,1)}, bf16[4,2,96,256]{3,2,1,0:T(8,128)(2,1)S(1)}, u32[]{:S(2)}, u32[]{:S(2)}) collective-permute-start(bf16[4,2,96,256]{3,2,1,0:T(8,128)(2,1)} %get-tuple-element.24), channel_id=1, source_target_pairs={{1,0},{2,1},{3,2},{5,4},{6,5},{7,6},{9,8},{10,9},{11,10},{13,12},{... | collective-permute-start | bytes 1179656 | tf_op jit(solution)/shard_map/ppermute | solution.py:16
  13.5 0.0 copy-done.4
  13.5 0.5 copy.33
  14.0 1.3 %reshape.16.k1_ref = bf16[288,864]{1,0:T(8,128)(2,1)} reshape(bf16[3,96,3,3,96]{4,3,2,1,0:T(4,128)(2,1)S(1)} %copy.33) | data formatting | bytes 995328 | tf_op jit(solution)/shard_map/reshape | solution.py:31
  15.3 1.5 %copy.34 = bf16[3,96,3,3,96]{4,3,2,1,0:T(4,128)(2,1)S(1)} copy(bf16[3,96,3,3,96]{4,1,0,3,2:T(8,128)(2,1)} %bitcast.18) | data formatting | bytes 995328 | tf_op jit(solution)/shard_map/transpose | solution.py:31
  16.8 0.0 copy-start.8
  16.8 1.3 %reshape.17.k2_ref = bf16[288,864]{1,0:T(8,128)(2,1)} reshape(bf16[3,96,3,3,96]{4,3,2,1,0:T(4,128)(2,1)S(1)} %copy.34) | data formatting | bytes 995328 | tf_op jit(solution)/shard_map/reshape | solution.py:31
  18.1 0.0 copy-done.8
  18.1 0.1 copy.35
  18.2 0.1 reshape.18
  18.3 1.6 %copy.36 = bf16[3,96,3,3,96]{4,3,2,1,0:T(4,128)(2,1)S(1)} copy(bf16[3,96,3,3,96]{4,1,0,3,2:T(8,128)(2,1)} %bitcast.19) | data formatting | bytes 995328 | tf_op jit(solution)/shard_map/transpose | solution.py:31
  19.9 0.0 copy-start.15
  19.9 1.3 %reshape.19.fk_ref = bf16[288,864]{1,0:T(8,128)(2,1)} reshape(bf16[3,96,3,3,96]{4,3,2,1,0:T(4,128)(2,1)S(1)} %copy.36) | data formatting | bytes 995328 | tf_op jit(solution)/shard_map/reshape | solution.py:31
  21.2 0.0 copy-start.12
  21.3 0.0 copy-start.13
  21.3 0.0 copy-start.14
  21.3 0.0 copy-done.15
  21.3 0.6 copy-done.12
  21.9 0.0 copy-done.13
  21.9 0.0 copy-done.14
  21.9 0.7 and_convert_fusion.mask_ref
  22.6 5.4 %collective-permute-done.pv_ref = bf16[4,4,96,256]{3,2,1,0:T(8,128)(2,1)S(1)} collective-permute-done((bf16[4,4,96,256]{3,2,1,0:T(8,128)(2,1)S(1)}, bf16[4,4,96,256]{3,2,1,0:T(8,128)(2,1)S(1)}, u32[]{:S(2)}, u32[]{:S(2)}) %collective-permute-start) | collective-permute-done | bytes 786464 | tf_op jit(solution)/shard_map/ppermute | solution.py:19
  28.0 0.0 copy-start.1
  28.0 0.1 fusion.1
  28.1 0.8 copy-done.1
  28.9 1.9 %collective-permute-start.1 = (bf16[4,2,96,256]{3,2,1,0:T(8,128)(2,1)S(1)}, bf16[4,2,96,256]{3,2,1,0:T(8,128)(2,1)S(1)}, u32[]{:S(2)}, u32[]{:S(2)}) collective-permute-start(bf16[4,2,96,256]{3,2,1,0:T(8,128)(2,1)S(1)} %get-tuple-element.13), channel_id=1, source_target_pairs={{0,1},{1,2},{2,3},{4,5},{5,6},{6,7},{8,9},{9,10},{10,11},{12,13},{... | collective-permute-start | bytes 1179656 | tf_op jit(solution)/shard_map/ppermute | solution.py:16
  30.8 5.1 %collective-permute-start.2 = (bf16[4,2,96,256]{3,2,1,0:T(8,128)(2,1)S(1)}, bf16[4,2,96,256]{3,2,1,0:T(8,128)(2,1)S(1)}, u32[]{:S(2)}, u32[]{:S(2)}) collective-permute-start(bf16[4,2,96,256]{3,2,1,0:T(8,128)(2,1)S(1)} %get-tuple-element.14), channel_id=1, source_target_pairs={{1,0},{2,1},{3,2},{5,4},{6,5},{7,6},{9,8},{10,9},{11,10},{13,12},{... | collective-permute-start | bytes 1179656 | tf_op jit(solution)/shard_map/ppermute | solution.py:16
  35.9 0.7 copy.37.vec_ref
  36.7 0.0 collective-permute-done.3.tp_ref
  36.7 0.0 copy-start.2
  36.7 0.0 collective-permute-done.4.bt_ref
  36.7 0.7 copy-done.2
  37.4 0.7 copy-done.3
  38.2 5.0 %shard_map.122.late_ref = bf16[2,6,96,256]{3,2,1,0:T(8,128)(2,1)} custom-call(bf16[4,2,96,256]{3,2,1,0:T(8,128)(2,1)} %copy-done.2, bf16[4,4,96,256]{3,2,1,0:T(8,128)(2,1)} %bitcast.15, bf16[4,2,96,256]{3,2,1,0:T(8,128)(2,1)} %copy-done.3, bf16[288,864]{1,0:T(8,128)(2,1)} %reshape.16.k1_ref, f32[96,4]{1,0:T(8,128)} %copy.37.vec_ref, ...), custom_call_target="tpu_custom_call" | custom-call | tf_op jit(solution)/shard_map/pallas_call | solution.py:211
  43.2 0.0 collective-permute-done.1.tc_ref
  43.2 0.0 collective-permute-done.2.bc_ref
  43.2 0.7 copy-done.5
  44.0 0.7 copy-done.6
  44.7 10.0 %shard_map.123 = (bf16[1,16,4,256]{3,2,1,0:T(4,128)(2,1)}, bf16[1,16,2,256]{3,2,1,0:T(2,128)(2,1)}, bf16[1,16,2,256]{3,2,1,0:T(2,128)(2,1)}) custom-call(bf16[4,2,96,256]{3,2,1,0:T(8,128)(2,1)} %copy-done.5, bf16[4,4,96,256]{3,2,1,0:T(8,128)(2,1)} %copy-done.1, bf16[4,2,96,256]{3,2,1,0:T(8,128)(2,1)} %copy-done.6, bf16[4,2,96,256]{3,2,1,0:T(8,128)(2,1)} %copy-done.2, ...), custom_call_target="tpu_custom_call" | custom-call | tf_op jit(solution)/shard_map/pallas_call | solution.py:216
  54.7 2.6 %collective-permute-start.6 = (bf16[1,16,2,256]{3,2,1,0:T(2,128)(2,1)}, bf16[1,16,2,256]{3,2,1,0:T(2,128)(2,1)S(1)}, u32[]{:S(2)}, u32[]{:S(2)}) collective-permute-start(bf16[1,16,2,256]{3,2,1,0:T(2,128)(2,1)} %get-tuple-element.21), channel_id=1, source_target_pairs={{1,0},{2,1},{3,2},{5,4},{6,5},{7,6},{9,8},{10,9},{11,10},{13,12},{... | collective-permute-start | bytes 49160 | tf_op jit(solution)/shard_map/ppermute | solution.py:16
  57.3 1.9 %collective-permute-start.5 = (bf16[1,16,2,256]{3,2,1,0:T(2,128)(2,1)}, bf16[1,16,2,256]{3,2,1,0:T(2,128)(2,1)S(1)}, u32[]{:S(2)}, u32[]{:S(2)}) collective-permute-start(bf16[1,16,2,256]{3,2,1,0:T(2,128)(2,1)} %get-tuple-element.20), channel_id=1, source_target_pairs={{0,1},{1,2},{2,3},{4,5},{5,6},{6,7},{8,9},{9,10},{10,11},{12,13},{... | collective-permute-start | bytes 49160 | tf_op jit(solution)/shard_map/ppermute | solution.py:16
  59.2 0.0 collective-permute-done.6
  59.2 4.8 %collective-permute-done.5 = bf16[1,16,2,256]{3,2,1,0:T(2,128)(2,1)S(1)} collective-permute-done((bf16[1,16,2,256]{3,2,1,0:T(2,128)(2,1)}, bf16[1,16,2,256]{3,2,1,0:T(2,128)(2,1)S(1)}, u32[]{:S(2)}, u32[]{:S(2)}) %collective-permute-start.5) | collective-permute-done | bytes 16416 | tf_op jit(solution)/shard_map/ppermute | solution.py:16
  64.1 0.8 pad_maximum_fusion.l0_ref
  64.9 0.0 copy-start.7
  64.9 2.1 %collective-permute-start.7 = (bf16[1,16,8,256]{3,2,1,0:T(8,128)(2,1)S(1)}, bf16[1,16,8,256]{3,2,1,0:T(8,128)(2,1)S(1)}, u32[]{:S(2)}, u32[]{:S(2)}) collective-permute-start(bf16[1,16,8,256]{3,2,1,0:T(8,128)(2,1)S(1)} %pad_maximum_fusion.l0_ref), channel_id=1, source_target_pairs={{0,12},{4,16},{8,20},{12,24},{16,28},{20,32},{24,36},{28,40},{32,4... | collective-permute-start | bytes 196616 | tf_op jit(solution)/shard_map/ppermute | solution.py:19
  67.0 2.0 %collective-permute-start.8 = (bf16[1,16,8,256]{3,2,1,0:T(8,128)(2,1)S(1)}, bf16[1,16,8,256]{3,2,1,0:T(8,128)(2,1)S(1)}, u32[]{:S(2)}, u32[]{:S(2)}) collective-permute-start(bf16[1,16,8,256]{3,2,1,0:T(8,128)(2,1)S(1)} %pad_maximum_fusion.l0_ref), channel_id=1, source_target_pairs={{0,8},{4,12},{8,16},{12,20},{16,24},{20,28},{24,32},{28,36},{32,40... | collective-permute-start | bytes 196616 | tf_op jit(solution)/shard_map/ppermute | solution.py:19
  69.1 2.8 %collective-permute-start.9 = (bf16[1,16,8,256]{3,2,1,0:T(8,128)(2,1)S(1)}, bf16[1,16,8,256]{3,2,1,0:T(8,128)(2,1)S(1)}, u32[]{:S(2)}, u32[]{:S(2)}) collective-permute-start(bf16[1,16,8,256]{3,2,1,0:T(8,128)(2,1)S(1)} %pad_maximum_fusion.l0_ref), channel_id=1, source_target_pairs={{0,4},{4,8},{8,12},{12,16},{16,20},{20,24},{24,28},{28,32},{32,36}... | collective-permute-start | bytes 196616 | tf_op jit(solution)/shard_map/ppermute | solution.py:19
  71.9 0.8 copy.39.dk_ref
  72.6 0.0 copy-done.7
  72.6 1.4 %collective-permute-done.7.l3_ref = bf16[1,16,8,256]{3,2,1,0:T(8,128)(2,1)S(1)} collective-permute-done((bf16[1,16,8,256]{3,2,1,0:T(8,128)(2,1)S(1)}, bf16[1,16,8,256]{3,2,1,0:T(8,128)(2,1)S(1)}, u32[]{:S(2)}, u32[]{:S(2)}) %collective-permute-start.7) | collective-permute-done | bytes 65568 | tf_op jit(solution)/shard_map/ppermute | solution.py:19
  74.1 3.6 %collective-permute-done.8.l2_ref = bf16[1,16,8,256]{3,2,1,0:T(8,128)(2,1)S(1)} collective-permute-done((bf16[1,16,8,256]{3,2,1,0:T(8,128)(2,1)S(1)}, bf16[1,16,8,256]{3,2,1,0:T(8,128)(2,1)S(1)}, u32[]{:S(2)}, u32[]{:S(2)}) %collective-permute-start.8) | collective-permute-done | bytes 65568 | tf_op jit(solution)/shard_map/ppermute | solution.py:19
  77.7 1.8 %collective-permute-done.9.l1_ref = bf16[1,16,8,256]{3,2,1,0:T(8,128)(2,1)S(1)} collective-permute-done((bf16[1,16,8,256]{3,2,1,0:T(8,128)(2,1)S(1)}, bf16[1,16,8,256]{3,2,1,0:T(8,128)(2,1)S(1)}, u32[]{:S(2)}, u32[]{:S(2)}) %collective-permute-start.9) | collective-permute-done | bytes 65568 | tf_op jit(solution)/shard_map/ppermute | solution.py:19
  79.5 0.0 copy-done.9
  79.5 0.0 copy-done.10
  79.5 0.6 copy-done.11
  80.1 7.2 %shard_map.124 = bf16[4,96,4,256]{3,2,1,0:T(4,128)(2,1)} custom-call(bf16[1,16,8,256]{3,2,1,0:T(8,128)(2,1)} %copy-done.9, bf16[1,16,8,256]{3,2,1,0:T(8,128)(2,1)} %copy-done.10, bf16[1,16,8,256]{3,2,1,0:T(8,128)(2,1)} %copy-done.11, bf16[1,16,8,256]{3,2,1,0:T(8,128)(2,1)} %copy-done.7, bf16[288,144]{1,0:T(8,128)(2,1)} %copy.39.dk_ref, ...), custom_call_target="tpu_custom_call" | custom-call | tf_op jit(solution)/shard_map/pallas_call | solution.py:238
  (8 shorter events, 0.0 us)
Async XLA Ops:
  1.9 4.5 %copy-start = (bf16[4,96,4,256]{3,1,2,0:T(8,128)(2,1)}, bf16[4,96,4,256]{3,1,2,0:T(8,128)(2,1)S(1)}, u32[]{:S(2)}) copy-start(bf16[4,96,4,256]{3,1,2,0:T(8,128)(2,1)S(1)} %copy.42) | copy-start | bytes 2359300
  1.9 11.6 %copy-start.4 = (bf16[3,3,3,96,96]{4,3,2,1,0:T(8,128)(2,1)S(1)}, bf16[3,3,3,96,96]{4,3,2,1,0:T(8,128)(2,1)}, u32[]{:S(2)}) copy-start(bf16[3,3,3,96,96]{4,3,2,1,0:T(8,128)(2,1)} %param.12) | copy-start | bytes 1492996
  1.9 26.1 %collective-permute-start = (bf16[4,4,96,256]{3,2,1,0:T(8,128)(2,1)S(1)}, bf16[4,4,96,256]{3,2,1,0:T(8,128)(2,1)S(1)}, u32[]{:S(2)}, u32[]{:S(2)}) collective-permute-start(bf16[4,4,96,256]{3,2,1,0:T(8,128)(2,1)S(1)} %bitcast.13), channel_id=1, source_target_pairs={{0,4},{4,8},{8,12},{12,16},{16,20},{20,24},{24,28},{28,32},{32,36}... | collective-permute-start | bytes 2359304 | tf_op jit(solution)/shard_map/ppermute | solution.py:19
  6.4 30.3 %collective-permute-start.3 = (bf16[4,2,96,256]{3,2,1,0:T(8,128)(2,1)}, bf16[4,2,96,256]{3,2,1,0:T(8,128)(2,1)S(1)}, u32[]{:S(2)}, u32[]{:S(2)}) collective-permute-start(bf16[4,2,96,256]{3,2,1,0:T(8,128)(2,1)} %get-tuple-element.25), channel_id=1, source_target_pairs={{0,1},{1,2},{2,3},{4,5},{5,6},{6,7},{8,9},{9,10},{10,11},{12,13},{... | collective-permute-start | bytes 1179656 | tf_op jit(solution)/shard_map/ppermute | solution.py:16
  8.3 28.3 %collective-permute-start.4 = (bf16[4,2,96,256]{3,2,1,0:T(8,128)(2,1)}, bf16[4,2,96,256]{3,2,1,0:T(8,128)(2,1)S(1)}, u32[]{:S(2)}, u32[]{:S(2)}) collective-permute-start(bf16[4,2,96,256]{3,2,1,0:T(8,128)(2,1)} %get-tuple-element.24), channel_id=1, source_target_pairs={{1,0},{2,1},{3,2},{5,4},{6,5},{7,6},{9,8},{10,9},{11,10},{13,12},{... | collective-permute-start | bytes 1179656 | tf_op jit(solution)/shard_map/ppermute | solution.py:16
  16.8 1.3 %copy-start.8 = (bf16[3,3,3,96,16]{3,4,2,1,0:T(8,128)(2,1)S(1)}, bf16[3,3,3,96,16]{3,4,2,1,0:T(8,128)(2,1)}, u32[]{:S(2)}) copy-start(bf16[3,3,3,96,16]{3,4,2,1,0:T(8,128)(2,1)} %param.17) | copy-start | bytes 248836
  19.9 1.4 %copy-start.15 = (f32[96]{0:T(128)S(1)}, f32[96]{0:T(128)}, u32[]{:S(2)}) copy-start(f32[96]{0:T(128)} %param.13) | copy-start | bytes 1156
  21.2 0.7 copy-start.12
  21.3 0.7 copy-start.13
  21.3 0.7 copy-start.14
  28.0 0.9 %copy-start.1 = (bf16[4,4,96,256]{3,2,1,0:T(8,128)(2,1)}, bf16[4,4,96,256]{3,2,1,0:T(8,128)(2,1)S(1)}, u32[]{:S(2)}) copy-start(bf16[4,4,96,256]{3,2,1,0:T(8,128)(2,1)S(1)} %collective-permute-done.pv_ref) | copy-start | bytes 2359300
  28.9 14.3 %collective-permute-start.1 = (bf16[4,2,96,256]{3,2,1,0:T(8,128)(2,1)S(1)}, bf16[4,2,96,256]{3,2,1,0:T(8,128)(2,1)S(1)}, u32[]{:S(2)}, u32[]{:S(2)}) collective-permute-start(bf16[4,2,96,256]{3,2,1,0:T(8,128)(2,1)S(1)} %get-tuple-element.13), channel_id=1, source_target_pairs={{0,1},{1,2},{2,3},{4,5},{5,6},{6,7},{8,9},{9,10},{10,11},{12,13},{... | collective-permute-start | bytes 1179656 | tf_op jit(solution)/shard_map/ppermute | solution.py:16
  30.8 12.4 %collective-permute-start.2 = (bf16[4,2,96,256]{3,2,1,0:T(8,128)(2,1)S(1)}, bf16[4,2,96,256]{3,2,1,0:T(8,128)(2,1)S(1)}, u32[]{:S(2)}, u32[]{:S(2)}) collective-permute-start(bf16[4,2,96,256]{3,2,1,0:T(8,128)(2,1)S(1)} %get-tuple-element.14), channel_id=1, source_target_pairs={{1,0},{2,1},{3,2},{5,4},{6,5},{7,6},{9,8},{10,9},{11,10},{13,12},{... | collective-permute-start | bytes 1179656 | tf_op jit(solution)/shard_map/ppermute | solution.py:16
  36.7 0.8 copy-start.2
  37.4 0.7 copy-start.3
  43.2 0.8 copy-start.5
  44.0 0.7 copy-start.6
  54.7 4.5 %collective-permute-start.6 = (bf16[1,16,2,256]{3,2,1,0:T(2,128)(2,1)}, bf16[1,16,2,256]{3,2,1,0:T(2,128)(2,1)S(1)}, u32[]{:S(2)}, u32[]{:S(2)}) collective-permute-start(bf16[1,16,2,256]{3,2,1,0:T(2,128)(2,1)} %get-tuple-element.21), channel_id=1, source_target_pairs={{1,0},{2,1},{3,2},{5,4},{6,5},{7,6},{9,8},{10,9},{11,10},{13,12},{... | collective-permute-start | bytes 49160 | tf_op jit(solution)/shard_map/ppermute | solution.py:16
  57.3 6.8 %collective-permute-start.5 = (bf16[1,16,2,256]{3,2,1,0:T(2,128)(2,1)}, bf16[1,16,2,256]{3,2,1,0:T(2,128)(2,1)S(1)}, u32[]{:S(2)}, u32[]{:S(2)}) collective-permute-start(bf16[1,16,2,256]{3,2,1,0:T(2,128)(2,1)} %get-tuple-element.20), channel_id=1, source_target_pairs={{0,1},{1,2},{2,3},{4,5},{5,6},{6,7},{8,9},{9,10},{10,11},{12,13},{... | collective-permute-start | bytes 49160 | tf_op jit(solution)/shard_map/ppermute | solution.py:16
  64.9 7.8 %copy-start.7 = (bf16[1,16,8,256]{3,2,1,0:T(8,128)(2,1)}, bf16[1,16,8,256]{3,2,1,0:T(8,128)(2,1)S(1)}, u32[]{:S(2)}) copy-start(bf16[1,16,8,256]{3,2,1,0:T(8,128)(2,1)S(1)} %pad_maximum_fusion.l0_ref) | copy-start | bytes 196612
  64.9 9.2 %collective-permute-start.7 = (bf16[1,16,8,256]{3,2,1,0:T(8,128)(2,1)S(1)}, bf16[1,16,8,256]{3,2,1,0:T(8,128)(2,1)S(1)}, u32[]{:S(2)}, u32[]{:S(2)}) collective-permute-start(bf16[1,16,8,256]{3,2,1,0:T(8,128)(2,1)S(1)} %pad_maximum_fusion.l0_ref), channel_id=1, source_target_pairs={{0,12},{4,16},{8,20},{12,24},{16,28},{20,32},{24,36},{28,40},{32,4... | collective-permute-start | bytes 196616 | tf_op jit(solution)/shard_map/ppermute | solution.py:19
  67.0 10.7 %collective-permute-start.8 = (bf16[1,16,8,256]{3,2,1,0:T(8,128)(2,1)S(1)}, bf16[1,16,8,256]{3,2,1,0:T(8,128)(2,1)S(1)}, u32[]{:S(2)}, u32[]{:S(2)}) collective-permute-start(bf16[1,16,8,256]{3,2,1,0:T(8,128)(2,1)S(1)} %pad_maximum_fusion.l0_ref), channel_id=1, source_target_pairs={{0,8},{4,12},{8,16},{12,20},{16,24},{20,28},{24,32},{28,36},{32,40... | collective-permute-start | bytes 196616 | tf_op jit(solution)/shard_map/ppermute | solution.py:19
  69.1 10.4 %collective-permute-start.9 = (bf16[1,16,8,256]{3,2,1,0:T(8,128)(2,1)S(1)}, bf16[1,16,8,256]{3,2,1,0:T(8,128)(2,1)S(1)}, u32[]{:S(2)}, u32[]{:S(2)}) collective-permute-start(bf16[1,16,8,256]{3,2,1,0:T(8,128)(2,1)S(1)} %pad_maximum_fusion.l0_ref), channel_id=1, source_target_pairs={{0,4},{4,8},{8,12},{12,16},{16,20},{20,24},{24,28},{28,32},{32,36}... | collective-permute-start | bytes 196616 | tf_op jit(solution)/shard_map/ppermute | solution.py:19
  74.1 5.4 %copy-start.9 = (bf16[1,16,8,256]{3,2,1,0:T(8,128)(2,1)}, bf16[1,16,8,256]{3,2,1,0:T(8,128)(2,1)S(1)}, u32[]{:S(2)}) copy-start(bf16[1,16,8,256]{3,2,1,0:T(8,128)(2,1)S(1)} %collective-permute-done.7.l3_ref) | copy-start | bytes 196612
  77.7 1.8 %copy-start.10 = (bf16[1,16,8,256]{3,2,1,0:T(8,128)(2,1)}, bf16[1,16,8,256]{3,2,1,0:T(8,128)(2,1)S(1)}, u32[]{:S(2)}) copy-start(bf16[1,16,8,256]{3,2,1,0:T(8,128)(2,1)S(1)} %collective-permute-done.8.l2_ref) | copy-start | bytes 196612
  79.5 0.6 copy-start.11
